TPU v7x, 32 devices: a whole 2x2x4 slice. The times are simulated.
32 devices in a mesh: crop: 8 (over z, y), head: 4 (over x, core).
Axes of the slice: x: 2, y: 2, z: 4, core: 2. Of those that a mesh axis runs over, the one named last changes fastest.
Arguments:
- global_rows: bfloat16 [4096, 4096], P('crop', 'head'), may hold values from -6 to 6
- crop_tokens: bfloat16 [8192, 4096], P('crop', 'head'), may hold values from -6 to 6
- query_weight: bfloat16 [4096, 4096], P('crop', 'head'), may hold values from -0.125 to 0.125
- key_weight: bfloat16 [4096, 4096], P('crop', 'head'), may hold values from -0.125 to 0.125
- value_weight: bfloat16 [4096, 4096], P('crop', 'head'), may hold values from -0.09375 to 0.09375
- fetch_slots: int32 [8, 8, 2], P('crop'), may hold values from 0 to 63
- region_slots: int32 [128, 8], P('crop'), may hold values from 0 to 15, as said below
- region_len: int32 [128], P('crop'), may hold values from 4 to 8
Outputs:
- attended: bfloat16 [4096, 4096], P('crop', 'head')
Inputs may be any that keep to these rules, and one draw needn't show every extreme that they name: `fetch_slots`: entry [s, o, c] numbers one of the 64 crop blocks of index s of crop. `region_slots`: the blocks listed for one page-row are distinct; the lists of the 16 page-rows of one index of crop together name all 16 delivered blocks. page-row r uses its first region_len[r] listed blocks.
All inputs are finite; a program needn't handle non-finite values.
Results may differ from a plain program's by a relative error of at most 0.008.
Values may be sent and summed in bfloat16 or wider, within the bound.
No kernel may reach another device: no remote copies, remote signals or barrier semaphores. Data moves between devices by JAX's collectives and lax.ppermute only.
A program may use at most 128 MiB of HBM per device.

v0:
```python
import jax
import jax.numpy as jnp
from jax import lax
from jax.sharding import PartitionSpec as P

HD = 128
CT = 16
CAP = 2
NB = 8
GR = 32


def add_rows(left, piece):
    return jnp.dot(left, piece, preferred_element_type=jnp.float32)


def body(
    global_rows,
    crop_tokens,
    query_weight,
    key_weight,
    value_weight,
    fetch_slots,
    region_slots,
    region_len,
):
    width = key_weight.shape[1]
    heads_here = width // HD
    ncrop = lax.axis_size("crop")
    rows_here = region_slots.shape[0]
    queries_in = lax.all_gather(global_rows, "head", axis=1, tiled=True)
    query = add_rows(queries_in, lax.all_gather(query_weight, "crop", axis=0, tiled=True)).astype(
        jnp.bfloat16
    )
    picks = fetch_slots[0]
    tokens_all = lax.all_gather(crop_tokens, "head", axis=1, tiled=True)

    def add_one(piece):
        return add_rows(tokens_all, piece)

    keys_full = add_one(lax.all_gather(key_weight, "crop", axis=0, tiled=True))
    vals_full = add_one(lax.all_gather(value_weight, "crop", axis=0, tiled=True))
    packed = jnp.concatenate(
        [keys_full.astype(jnp.bfloat16), vals_full.astype(jnp.bfloat16)], axis=1
    )
    packed = packed.reshape(-1, CT, 2 * width)
    outgoing = packed[picks]
    incoming = lax.all_to_all(outgoing, "crop", split_axis=0, concat_axis=0, tiled=True)
    slotted = incoming.reshape(ncrop * CAP, CT, 2 * width)
    listed = slotted[region_slots].reshape(rows_here, NB * CT, 2 * width)
    keys_row = listed[:, :, :width].reshape(rows_here, NB * CT, heads_here, HD)
    vals_row = listed[:, :, width:].reshape(rows_here, NB * CT, heads_here, HD)
    query_row = query.reshape(rows_here, GR, heads_here, HD)
    scale = 1.0 / HD**0.5
    scores = (
        jnp.einsum("rghe,rkhe->rhgk", query_row, keys_row, preferred_element_type=jnp.float32)
        * scale
    )
    used = (jnp.arange(NB * CT, dtype=jnp.int32) // CT)[None, :] < region_len[:, None]
    scores = jnp.where(used[:, None, None, :], scores, jnp.float32(-1e30))
    top = jnp.max(scores, axis=-1, keepdims=True)
    expo = jnp.exp(scores - top)
    weights = (expo / jnp.sum(expo, axis=-1, keepdims=True)).astype(jnp.bfloat16)
    result = jnp.einsum("rhgk,rkhe->rghe", weights, vals_row, preferred_element_type=jnp.float32)
    return result.astype(jnp.bfloat16).reshape(rows_here * GR, width)


def solution(mesh):
    placed = (
        P("crop", "head"),
        P("crop", "head"),
        P("crop", "head"),
        P("crop", "head"),
        P("crop", "head"),
        P("crop", None, None),
        P("crop", None),
        P("crop"),
    )
    return jax.shard_map(
        body, mesh=mesh, in_specs=placed, out_specs=P("crop", "head"), check_vma=False
    )
```

profile of v0, /device:TPU:0, one launch (start us, length us, event | category | flops | bytes accessed | tf_op | source)
XLA Modules:
  0.0 549.0 jit_solution(13589215673044014440)
XLA Ops:
  6.5 0.7 all-gather.6.cloned.1.call-update
  7.3 0.7 all-gather.8.cloned.1.call-update
  8.1 0.7 all-gather.10.cloned.1.call-update
  8.8 0.5 all-gather.12.cloned.1.call-update
  9.4 0.5 all-gather.14.cloned.1.call-update
  9.9 0.1 copy.13
  10.0 0.1 reshape.96
  10.2 0.1 reshape.104
  10.3 59.6 %all-gather.6.cloned.1.call-done = bf16[1024,4096]{1,0:T(8,128)(2,1)} async-done(((bf16[1024,1024]{1,0:T(8,128)(2,1)}), bf16[1024,4096]{1,0:T(8,128)(2,1)}) %all-gather.6.cloned.1.call-update) | async-done | bytes 8388624 | tf_op jit(solution)/shard_map/all_gather | solution.py:36
  69.9 127.1 %all-gather.8.cloned.1.call-done = bf16[4096,1024]{1,0:T(8,128)(2,1)} async-done(((bf16[512,1024]{1,0:T(8,128)(2,1)}), bf16[4096,1024]{1,0:T(8,128)(2,1)}) %all-gather.8.cloned.1.call-update) | async-done | bytes 8388624 | tf_op jit(solution)/shard_map/all_gather | solution.py:41
  197.0 13.7 %convolution_convert_fusion.1 = bf16[1024,1024]{0,1:T(8,128)(2,1)S(1)} fusion(bf16[1024,4096]{1,0:T(8,128)(2,1)} %all-gather.6.cloned.1.call-done, bf16[4096,1024]{1,0:T(8,128)(2,1)} %all-gather.8.cloned.1.call-done), kind=kOutput, calls=%fused_computation.8 | convolution fusion | flops 8590983168 | bytes 18874368 | tf_op jit(solution)/shard_map/dot_general | solution.py:14
  210.8 111.5 %all-gather.10.cloned.1.call-done = bf16[4096,1024]{1,0:T(8,128)(2,1)} async-done(((bf16[512,1024]{1,0:T(8,128)(2,1)}), bf16[4096,1024]{1,0:T(8,128)(2,1)}) %all-gather.10.cloned.1.call-update) | async-done | bytes 8388624 | tf_op jit(solution)/shard_map/all_gather | solution.py:42
  322.3 13.7 %convolution_convert_fusion = bf16[1024,1024]{0,1:T(8,128)(2,1)S(1)} fusion(bf16[1024,4096]{1,0:T(8,128)(2,1)} %all-gather.6.cloned.1.call-done, bf16[4096,1024]{1,0:T(8,128)(2,1)} %all-gather.10.cloned.1.call-done), kind=kOutput, calls=%fused_computation.7 | convolution fusion | flops 8590983168 | bytes 18874368 | tf_op jit(solution)/shard_map/dot_general | solution.py:14
  336.1 2.4 pad_maximum_fusion
  338.5 6.6 %copy.12 = bf16[1024,2048]{1,0:T(8,128)(2,1)} copy(bf16[1024,2048]{0,1:T(8,128)(2,1)} %pad_maximum_fusion) | data formatting | bytes 8388608 | tf_op jit(solution)/shard_map/concatenate | solution.py:43
  345.1 3.8 gather_fusion
  348.9 3.7 all-to-all-start
  352.6 0.1 broadcast_compare_fusion
  352.7 3.7 all-gather.12.cloned.1.call-done
  356.4 133.9 %all-gather.14.cloned.1.call-done = bf16[4096,1024]{1,0:T(8,128)(2,1)} async-done(((bf16[512,1024]{1,0:T(8,128)(2,1)}), bf16[4096,1024]{1,0:T(8,128)(2,1)}) %all-gather.14.cloned.1.call-update) | async-done | bytes 8388624 | tf_op jit(solution)/shard_map/all_gather | solution.py:32
  490.3 9.1 %fusion.3 = bf16[64,8,8,128]{3,1,2,0:T(8,128)(2,1)S(1)} fusion(bf16[512,4096]{1,0:T(8,128)(2,1)} %all-gather.12.cloned.1.call-done, bf16[4096,1024]{1,0:T(8,128)(2,1)} %all-gather.14.cloned.1.call-done), kind=kOutput, calls=%fused_computation.13 | convolution fusion | flops 4295491584 | bytes 13631488 | tf_op jit(solution)/shard_map/dot_general | solution.py:14
  499.4 0.3 copy.23
  499.7 6.2 %gather_fusion.1 = bf16[128,16,2048]{2,1,0:T(8,128)(2,1)} fusion(bf16[16,16,2048]{2,1,0:T(8,128)(2,1)S(1)} %bitcast.29, s32[1024]{0:T(1024)S(1)} %pad_clamp_fusion), kind=kCustom, calls=%fused_computation.1 | custom fusion | bytes 16777728 | tf_op jit(solution)/shard_map/gather | solution.py:50
  506.0 6.0 %fusion.17 = (bf16[16,128,1024]{2,1,0:T(8,128)(2,1)}, bf16[16,128,1024]{2,1,0:T(8,128)(2,1)}) fusion(bf16[16,128,2048]{2,1,0:T(8,128)(2,1)} %bitcast.30), kind=kLoop, calls=%fused_computation.35 | loop fusion | bytes 16777216 | tf_op jit(solution)/shard_map/slice | solution.py:51
  512.0 6.4 %copy.16 = bf16[16,128,1024]{1,2,0:T(8,128)(2,1)} copy(bf16[16,128,1024]{2,1,0:T(8,128)(2,1)} %get-tuple-element.5) | data formatting | bytes 8388608 | tf_op jit(solution)/shard_map/slice | solution.py:51
  518.4 6.4 %copy.15 = bf16[16,128,1024]{1,2,0:T(8,128)(2,1)} copy(bf16[16,128,1024]{2,1,0:T(8,128)(2,1)} %get-tuple-element.6) | data formatting | bytes 8388608 | tf_op jit(solution)/shard_map/slice | solution.py:52
  524.8 3.4 fusion.4
  528.2 1.3 copy-done
  529.5 1.2 fusion.18
  530.7 10.1 %fusion.2 = bf16[16,32,8,128]{3,1,2,0:T(8,128)(2,1)S(1)} fusion(bf16[16,128,8,128]{1,3,2,0:T(8,128)(2,1)} %bitcast.34, f32[16,8,32]{2,1,0:T(8,128)S(1)} %fusion.18, f32[16,8,32,128]{3,2,1,0:T(8,128)} %copy-done, pred[16,128]{1,0:T(8,128)(4,1)S(1)} %broadcast_compare_fusion), kind=kOutput, calls=%fused_computation.12 | convolution fusion | flops 137367680 | bytes 7358464 | tf_op jit(solution)/shard_map/rhgk,rkhe->rghe/dot_general | solution.py:64
  540.8 0.5 copy.20
  541.2 1.2 copy.28
  (19 shorter events, 0.3 us)
Async XLA Ops:
  6.5 3.4 copy-start.2
  6.5 3.6 copy-start.1
  6.5 63.4 %all-gather.6.cloned.1.call-start = ((), (), s32[]{:S(2)}) async-start(), calls=%async_computation.1 | async-start | bytes 10485760 | tf_op jit(solution)/shard_map/all_gather | solution.py:36
  7.3 189.8 %all-gather.8.cloned.1.call-start = ((), (), s32[]{:S(2)}) async-start(), calls=%async_computation.2 | async-start | bytes 9437184 | tf_op jit(solution)/shard_map/all_gather | solution.py:41
  8.0 314.3 %all-gather.10.cloned.1.call-start = ((), (), s32[]{:S(2)}) async-start(), calls=%async_computation.3 | async-start | bytes 9437184 | tf_op jit(solution)/shard_map/all_gather | solution.py:42
  8.7 347.7 %all-gather.12.cloned.1.call-start = ((), (), s32[]{:S(2)}) async-start(), calls=%async_computation.4 | async-start | bytes 5242880 | tf_op jit(solution)/shard_map/all_gather | solution.py:31
  9.3 481.0 %all-gather.14.cloned.1.call-start = ((), (), s32[]{:S(2)}) async-start(), calls=%async_computation.5 | async-start | bytes 9437184 | tf_op jit(solution)/shard_map/all_gather | solution.py:32
  345.1 7.5 %copy-start.3 = (s32[16]{0:T(128)S(1)}, s32[16]{0:T(128)}, u32[]{:S(2)}) copy-start(s32[16]{0:T(128)} %param.15) | copy-start | bytes 196
  348.9 150.9 %all-to-all-start = ((bf16[8,2,16,2048]{3,2,1,0:T(8,128)(2,1)}), bf16[8,2,16,2048]{3,2,1,0:T(8,128)(2,1)S(1)}, u32[]{:S(2)}, u32[]{:S(2)}) async-start(bf16[8,2,16,2048]{3,2,1,0:T(8,128)(2,1)} %bitcast.2), calls=%async_computation | async-start | bytes 2097152 | tf_op jit(solution)/shard_map/all_to_all | solution.py:48
  528.2 1.3 copy-start
Sparse Core Ops, SparseCore 0:
  8.9 60.9 all-gather.5
  72.1 124.9 all-gather.7
  199.2 123.1 all-gather.9
  323.7 32.6 all-gather.11
  358.4 131.8 all-gather.13
where the time goes:
time: 550 us; the launch traced here: 549 us
  waiting for transfers between devices  439 us (80%)
  matrix products  50.1 us (9%)
  local copies, waits for them, and re-layouts  39.1 us (7%)
  between operations  13.3 us (2%)
    all_gather x1, waiting for transfers between devices, body(): lax.all_gather(query_weight, 'crop', axis=0, tiled=True)  134 us
    all_gather x1, waiting for transfers between devices, body(): keys_full = add_one(lax.all_gather(key_weight, 'crop', axis=0, tiled=True))  127 us
    all_gather x1, waiting for transfers between devices, body(): lax.all_gather(value_weight, 'crop', axis=0, tiled=True)  112 us
    all_gather x1, waiting for transfers between devices, body(): tokens_all = lax.all_gather(crop_tokens, 'head', axis=1, tiled=True)  59.6 us
    dot_general x3, matrix products, add_rows(): return jnp.dot(left, piece, preferred_element_type=jnp.float32)  36.6 us
    slice x2, local copies, waits for them, and re-layouts, body(): keys_row = listed[:, :, :width].reshape(rows_here, NB * CT, heads_here, HD)  12.4 us
  transfers between devices with their start and end apart: 6, of which 5 were waited for; matrix products, arithmetic and copies ran while one was open for 9% of the time, Pallas kernels for 0%

commit v1 on v0

--- a/solution.py
+++ b/solution.py
@@ -10,8 +10,9 @@
 GR = 32
 
 
-def add_rows(left, piece):
-    return jnp.dot(left, piece, preferred_element_type=jnp.float32)
+def ring_order(n):
+    half = n // 2
+    return [2 * i for i in range(half)] + [2 * i + 1 for i in reversed(range(half))]
 
 
 def body(
@@ -25,27 +26,67 @@
     region_len,
 ):
     width = key_weight.shape[1]
+    wrows = key_weight.shape[0]
     heads_here = width // HD
     ncrop = lax.axis_size("crop")
     rows_here = region_slots.shape[0]
+
+    ring = ring_order(ncrop)
+    pos_of = [0] * ncrop
+    for i, c in enumerate(ring):
+        pos_of[c] = i
+    me = lax.axis_index("crop")
+    pos = jnp.array(pos_of, jnp.int32)[me]
+    ring_arr = jnp.array(ring, jnp.int32)
+    fwd_perm = [(ring[i], ring[(i + 1) % ncrop]) for i in range(ncrop)]
+    bwd_perm = [(ring[i], ring[(i - 1) % ncrop]) for i in range(ncrop)]
+
     queries_in = lax.all_gather(global_rows, "head", axis=1, tiled=True)
-    query = add_rows(queries_in, lax.all_gather(query_weight, "crop", axis=0, tiled=True)).astype(
-        jnp.bfloat16
+    picks = fetch_slots[0]
+    blocks = crop_tokens.reshape(-1, CT, crop_tokens.shape[1])
+    chosen = blocks[picks].reshape(-1, crop_tokens.shape[1])
+    tokens_in = lax.all_gather(chosen, "head", axis=1, tiled=True)
+
+    stacked = jnp.concatenate([query_weight, key_weight, value_weight], axis=1)
+
+    acc_q = jnp.zeros((queries_in.shape[0], width), jnp.float32)
+    acc_kv = jnp.zeros((tokens_in.shape[0], 2 * width), jnp.float32)
+
+    def contrib(acc_q, acc_kv, piece, src, lo, n):
+        start = src * wrows + lo
+        fq = lax.dynamic_slice_in_dim(queries_in, start, n, 1)
+        ft = lax.dynamic_slice_in_dim(tokens_in, start, n, 1)
+        acc_q = acc_q + jnp.dot(fq, piece[:, :width], preferred_element_type=jnp.float32)
+        acc_kv = acc_kv + jnp.dot(ft, piece[:, width:], preferred_element_type=jnp.float32)
+        return acc_q, acc_kv
+
+    acc_q, acc_kv = contrib(acc_q, acc_kv, stacked, me, 0, wrows)
+    steps_fwd = ncrop // 2
+    steps_bwd = (ncrop - 1) // 2
+    split = wrows // 2
+
+    def ring_step(k, carry):
+        fwd, bwd, acc_q, acc_kv = carry
+        fwd = lax.ppermute(fwd, "crop", fwd_perm)
+        bwd = lax.ppermute(bwd, "crop", bwd_perm)
+        acc_q, acc_kv = contrib(acc_q, acc_kv, fwd, ring_arr[(pos - k) % ncrop], 0, wrows)
+        acc_q, acc_kv = contrib(acc_q, acc_kv, bwd, ring_arr[(pos + k) % ncrop], 0, wrows)
+        return fwd, bwd, acc_q, acc_kv
+
+    fwd, bwd, acc_q, acc_kv = lax.fori_loop(
+        1, steps_bwd + 1, ring_step, (stacked, stacked, acc_q, acc_kv)
     )
-    picks = fetch_slots[0]
-    tokens_all = lax.all_gather(crop_tokens, "head", axis=1, tiled=True)
+    if steps_fwd > steps_bwd:
+        src = ring_arr[(pos - steps_fwd) % ncrop]
+        fwd_piece = lax.ppermute(fwd[:split], "crop", fwd_perm)
+        bwd_piece = lax.ppermute(bwd[split:], "crop", bwd_perm)
+        acc_q, acc_kv = contrib(acc_q, acc_kv, fwd_piece, src, 0, split)
+        acc_q, acc_kv = contrib(acc_q, acc_kv, bwd_piece, src, split, wrows - split)
 
-    def add_one(piece):
-        return add_rows(tokens_all, piece)
-
-    keys_full = add_one(lax.all_gather(key_weight, "crop", axis=0, tiled=True))
-    vals_full = add_one(lax.all_gather(value_weight, "crop", axis=0, tiled=True))
-    packed = jnp.concatenate(
-        [keys_full.astype(jnp.bfloat16), vals_full.astype(jnp.bfloat16)], axis=1
-    )
-    packed = packed.reshape(-1, CT, 2 * width)
-    outgoing = packed[picks]
-    incoming = lax.all_to_all(outgoing, "crop", split_axis=0, concat_axis=0, tiled=True)
+    query = acc_q.astype(jnp.bfloat16)
+    kv = acc_kv.astype(jnp.bfloat16)
+    packed = kv.reshape(ncrop, CAP, CT, 2 * width)
+    incoming = lax.all_to_all(packed, "crop", split_axis=0, concat_axis=0, tiled=True)
     slotted = incoming.reshape(ncrop * CAP, CT, 2 * width)
     listed = slotted[region_slots].reshape(rows_here, NB * CT, 2 * width)
     keys_row = listed[:, :, :width].reshape(rows_here, NB * CT, heads_here, HD)

time: 550 us -> 458 us (0.83)
  waiting for transfers between devices: 439 us -> 293 us
  local copies, waits for them, and re-layouts: 39.1 us -> 60.6 us
  matrix products: 50.1 us -> 62.1 us
  starting transfers between devices: 3.89 us -> 12.9 us
  loops' own time: 0 us -> 8.08 us
    all_gather x4 -> x1, waiting for transfers between devices: 432 us -> 16.8 us  [body(): tokens_in = lax.all_gather(chosen, 'head', axis=1, tiled=True)]
    ppermute x0 -> x8, waiting for transfers between devices: none -> 223 us  [the longest x3 193 us: ring_step(): fwd = lax.ppermute(fwd, 'crop', fwd_perm)]
    all_gather x1, waiting for transfers between devices: 3.73 us -> 33.1 us  [body(): queries_in = lax.all_gather(global_rows, 'head', axis=1, tiled=True)]
    all_to_all x1, waiting for transfers between devices: 0.01 us -> 19.1 us  [body(): lax.all_to_all(packed, 'crop', split_axis=0, concat_axis=0, tiled=True)]
    while x0 -> x18, local copies, waits for them, and re-layouts: none -> 16.9 us
    dot_general x3 -> x18, matrix products: 36.6 us -> 48.5 us  [the longest x9 29.3 us: contrib(): jnp.dot(ft, piece[:, width:], preferred_element_type=jnp.float32)]
    ppermute x0 -> x8, starting transfers between devices: none -> 8.1 us  [the longest x3 4.46 us: ring_step(): fwd = lax.ppermute(fwd, 'crop', fwd_perm)]
    another operation x0 -> x1, loops' own time: none -> 8.08 us  [body(): lax.fori_loop(1, steps_bwd + 1, ring_step, (stacked, stacked, acc_q, acc_...]
  transfers between devices with their start and end apart: 6 -> 11, of which waited for: 5 -> 8; matrix products, arithmetic and copies ran while one was open for 9% -> 6% of each run, Pallas kernels for 0% -> 0%
where the time goes in v1:
time: 458 us; the launch traced here: 457 us
  waiting for transfers between devices  293 us (64%)
  matrix products  62.1 us (14%)
  local copies, waits for them, and re-layouts  60.6 us (13%)
  between operations  14.9 us (3%)
  starting transfers between devices  12.9 us (3%)
  loops' own time  8.08 us (2%)
  other arithmetic  4.99 us (1%)
    ppermute x3, waiting for transfers between devices, ring_step(): fwd = lax.ppermute(fwd, 'crop', fwd_perm)  193 us
    all_gather x1, waiting for transfers between devices, body(): queries_in = lax.all_gather(global_rows, 'head', axis=1, tiled=True)  33.1 us
    dot_general x9, matrix products, contrib(): jnp.dot(ft, piece[:, width:], preferred_element_type=jnp.float32)  29.3 us
    ppermute x1, waiting for transfers between devices, body(): bwd_piece = lax.ppermute(bwd[split:], 'crop', bwd_perm)  27.8 us
    dot_general x9, matrix products, contrib(): jnp.dot(fq, piece[:, :width], preferred_element_type=jnp.float32)  19.2 us
    all_to_all x1, waiting for transfers between devices, body(): lax.all_to_all(packed, 'crop', split_axis=0, concat_axis=0, tiled=True)  19.1 us
    while x18, local copies, waits for them, and re-layouts  16.9 us
    all_gather x1, waiting for transfers between devices, body(): tokens_in = lax.all_gather(chosen, 'head', axis=1, tiled=True)  16.8 us
  transfers between devices with their start and end apart: 11, of which 8 were waited for; matrix products, arithmetic and copies ran while one was open for 6% of the time, Pallas kernels for 0%

profile of v1, /device:TPU:0, one launch (start us, length us, event | category | flops | bytes accessed | tf_op | source)
XLA Modules:
  0.0 456.6 jit_solution(456569816746212066)
XLA Ops:
  10.7 2.9 pad_maximum_fusion
  13.6 4.0 copy.38
  18.2 16.8 %all-gather.5.cloned.1.call-done = bf16[256,4096]{1,0:T(8,128)(2,1)} async-done(((bf16[256,1024]{1,0:T(8,128)(2,1)}), bf16[256,4096]{1,0:T(8,128)(2,1)}) %all-gather.5.cloned.1.call-update) | async-done | bytes 2097168 | tf_op jit(solution)/shard_map/all_gather | solution.py:48
  35.0 3.0 fusion.21
  37.9 33.1 %all-gather.3.cloned.1.call-done = bf16[512,4096]{1,0:T(8,128)(2,1)} async-done(((bf16[512,1024]{1,0:T(8,128)(2,1)}), bf16[512,4096]{1,0:T(8,128)(2,1)}) %all-gather.3.cloned.1.call-update) | async-done | bytes 4194320 | tf_op jit(solution)/shard_map/all_gather | solution.py:44
  71.1 3.1 fusion.43
  74.1 260.3 %while.22 = (s32[]{:T(128)}, bf16[512,3072]{1,0:T(8,128)(2,1)}, bf16[512,3072]{1,0:T(8,128)(2,1)}, f32[512,1024]{1,0:T(8,128)}, f32[256,2048]{1,0:T(8,128)}, /*i...) while((s32[]{:T(128)}, bf16[512,3072]{1,0:T(8,128)(2,1)}, ...), condition=%wide.region_1.2_spmd.clone, body=%wide.region_0.1_spmd.sunk.clone.sunk | while | flops 2149580800 | bytes 79168192 | solution.py:76
  79.5 65.1 %collective-permute-done = bf16[512,3072]{1,0:T(8,128)(2,1)S(1)} collective-permute-done((bf16[512,3072]{1,0:T(8,128)(2,1)}, bf16[512,3072]{1,0:T(8,128)(2,1)S(1)}, u32[]{:S(2)}, u32[]{:S(2)}) %collective-permute-start) | collective-permute-done | bytes 3145760 | tf_op jit(solution)/shard_map/while/body/eval_jaxpr/ppermute | solution.py:70
  146.3 3.9 copy.48
  154.5 2.6 add_add_fusion.2
  157.1 4.5 fusion.93
  167.0 64.4 %collective-permute-done = bf16[512,3072]{1,0:T(8,128)(2,1)S(1)} collective-permute-done((bf16[512,3072]{1,0:T(8,128)(2,1)}, bf16[512,3072]{1,0:T(8,128)(2,1)S(1)}, u32[]{:S(2)}, u32[]{:S(2)}) %collective-permute-start) | collective-permute-done | bytes 3145760 | tf_op jit(solution)/shard_map/while/body/eval_jaxpr/ppermute | solution.py:70
  233.1 3.9 copy.48
  238.8 2.5 fusion.92
  241.3 2.6 add_add_fusion.2
  243.9 4.5 fusion.93
  253.8 63.6 %collective-permute-done = bf16[512,3072]{1,0:T(8,128)(2,1)S(1)} collective-permute-done((bf16[512,3072]{1,0:T(8,128)(2,1)}, bf16[512,3072]{1,0:T(8,128)(2,1)S(1)}, u32[]{:S(2)}, u32[]{:S(2)}) %collective-permute-start) | collective-permute-done | bytes 3145760 | tf_op jit(solution)/shard_map/while/body/eval_jaxpr/ppermute | solution.py:70
  319.1 3.9 copy.48
  327.3 2.6 add_add_fusion.2
  329.9 4.5 fusion.93
  334.4 2.7 slice.68
  338.6 2.7 slice.66
  343.8 27.8 %collective-permute-done.3 = bf16[256,3072]{1,0:T(8,128)(2,1)S(1)} collective-permute-done((bf16[256,3072]{1,0:T(8,128)(2,1)}, bf16[256,3072]{1,0:T(8,128)(2,1)S(1)}, u32[]{:S(2)}, u32[]{:S(2)}) %collective-permute-start.3) | collective-permute-done | bytes 1572896 | tf_op jit(solution)/shard_map/ppermute | solution.py:82
  375.5 3.7 fusion.20
  379.2 4.7 %all-to-all-start = ((bf16[8,2,16,2048]{3,2,1,0:T(8,128)(2,1)}), bf16[8,2,16,2048]{3,2,1,0:T(8,128)(2,1)S(1)}, u32[]{:S(2)}, u32[]{:S(2)}) async-start(bf16[8,2,16,2048]{3,2,1,0:T(8,128)(2,1)} %bitcast.37), calls=%async_computation | async-start | bytes 2097152 | tf_op jit(solution)/shard_map/all_to_all | solution.py:89
  387.7 19.1 %all-to-all-done = bf16[8,2,16,2048]{3,2,1,0:T(8,128)(2,1)S(1)} async-done(((bf16[8,2,16,2048]{3,2,1,0:T(8,128)(2,1)}), bf16[8,2,16,2048]{3,2,1,0:T(8,128)(2,1)S(1)}, u32[]{:S(2)}, u32[]{:S(2)}) %all-to-all-start) | async-done | bytes 1048608 | tf_op jit(solution)/shard_map/all_to_all | solution.py:89
  406.8 6.3 %gather_fusion.1 = bf16[128,16,2048]{2,1,0:T(8,128)(2,1)} fusion(bf16[16,16,2048]{2,1,0:T(8,128)(2,1)S(1)} %bitcast.34, s32[1024]{0:T(1024)S(1)} %pad_clamp_fusion), kind=kCustom, calls=%fused_computation.1 | custom fusion | bytes 16777728 | tf_op jit(solution)/shard_map/gather | solution.py:91
  413.0 6.0 %fusion.65 = (bf16[16,128,1024]{2,1,0:T(8,128)(2,1)}, bf16[16,128,1024]{2,1,0:T(8,128)(2,1)}) fusion(bf16[16,128,2048]{2,1,0:T(8,128)(2,1)} %bitcast.35), kind=kLoop, calls=%fused_computation.80 | loop fusion | bytes 16777216 | tf_op jit(solution)/shard_map/slice | solution.py:92
  419.1 6.4 %copy.22 = bf16[16,128,1024]{1,2,0:T(8,128)(2,1)} copy(bf16[16,128,1024]{2,1,0:T(8,128)(2,1)} %get-tuple-element.279) | data formatting | bytes 8388608 | tf_op jit(solution)/shard_map/slice | solution.py:93
  425.4 6.4 %copy.23 = bf16[16,128,1024]{1,2,0:T(8,128)(2,1)} copy(bf16[16,128,1024]{2,1,0:T(8,128)(2,1)} %get-tuple-element.278) | data formatting | bytes 8388608 | tf_op jit(solution)/shard_map/slice | solution.py:92
  431.9 3.4 fusion.31
  437.8 10.2 %fusion.26 = bf16[16,32,8,128]{3,1,2,0:T(8,128)(2,1)S(1)} fusion(bf16[16,128,8,128]{1,3,2,0:T(8,128)(2,1)} %bitcast.39, f32[16,8,32]{2,1,0:T(8,128)S(1)} %fusion.66, f32[16,8,32,128]{3,2,1,0:T(8,128)} %copy-done.6, pred[16,128]{1,0:T(8,128)(4,1)S(1)} %broadcast_compare_fusion), kind=kOutput, calls=%fused_computation.35 | convolution fusion | flops 137367680 | bytes 7358464 | tf_op jit(solution)/shard_map/rhgk,rkhe->rghe/dot_general | solution.py:105
  (85 shorter events, 42.9 us)
Async XLA Ops:
  6.5 1.6 copy-start
  6.5 3.8 copy-start.5
  6.5 28.4 %all-gather.5.cloned.1.call-start = ((), (), s32[]{:S(2)}) async-start(), calls=%async_computation.2 | async-start | bytes 2621440 | tf_op jit(solution)/shard_map/all_gather | solution.py:48
  9.5 1.2 copy-start.9
  9.5 61.5 %all-gather.3.cloned.1.call-start = ((), (), s32[]{:S(2)}) async-start(), calls=%async_computation.1 | async-start | bytes 5242880 | tf_op jit(solution)/shard_map/all_gather | solution.py:44
  13.6 4.0 copy-start.14
  13.6 21.3 %copy-start.10 = (bf16[512,1024]{1,0:T(8,128)(2,1)S(1)}, bf16[512,1024]{1,0:T(8,128)(2,1)}, u32[]{:S(2)}) copy-start(bf16[512,1024]{1,0:T(8,128)(2,1)} %param.15) | copy-start | bytes 3145732
  37.9 36.2 %copy-start.11 = (s32[8]{0:T(128)S(1)}, s32[8]{0:T(128)}, u32[]{:S(2)}) copy-start(s32[8]{0:T(128)} %constant.139.clone) | copy-start | bytes 100
  74.1 70.5 %collective-permute-start = (bf16[512,3072]{1,0:T(8,128)(2,1)}, bf16[512,3072]{1,0:T(8,128)(2,1)S(1)}, u32[]{:S(2)}, u32[]{:S(2)}) collective-permute-start(bf16[512,3072]{1,0:T(8,128)(2,1)} %get-tuple-element.349), channel_id=1, source_target_pairs={{0,8},{8,16},{16,24},{24,28},{28,20},{20,12},{12,4},{4,0},{1,9},{9... | collective-permute-start | bytes 9437192 | tf_op jit(solution)/shard_map/while/body/eval_jaxpr/ppermute | solution.py:70
  75.6 70.7 %collective-permute-start.1 = (bf16[512,3072]{1,0:T(8,128)(2,1)}, bf16[512,3072]{1,0:T(8,128)(2,1)}, u32[]{:S(2)}, u32[]{:S(2)}) collective-permute-start(bf16[512,3072]{1,0:T(8,128)(2,1)} %get-tuple-element.350), channel_id=1, source_target_pairs={{0,4},{8,0},{16,8},{24,16},{28,24},{20,28},{12,20},{4,12},{1,5},{9... | collective-permute-start | bytes 9437192 | tf_op jit(solution)/shard_map/while/body/eval_jaxpr/ppermute | solution.py:71
  152.0 2.6 copy-start.2
  157.1 4.5 copy-start.3
  161.6 69.8 %collective-permute-start = (bf16[512,3072]{1,0:T(8,128)(2,1)}, bf16[512,3072]{1,0:T(8,128)(2,1)S(1)}, u32[]{:S(2)}, u32[]{:S(2)}) collective-permute-start(bf16[512,3072]{1,0:T(8,128)(2,1)} %get-tuple-element.349), channel_id=1, source_target_pairs={{0,8},{8,16},{16,24},{24,28},{28,20},{20,12},{12,4},{4,0},{1,9},{9... | collective-permute-start | bytes 9437192 | tf_op jit(solution)/shard_map/while/body/eval_jaxpr/ppermute | solution.py:70
  163.1 70.0 %collective-permute-start.1 = (bf16[512,3072]{1,0:T(8,128)(2,1)}, bf16[512,3072]{1,0:T(8,128)(2,1)}, u32[]{:S(2)}, u32[]{:S(2)}) collective-permute-start(bf16[512,3072]{1,0:T(8,128)(2,1)} %get-tuple-element.350), channel_id=1, source_target_pairs={{0,4},{8,0},{16,8},{24,16},{28,24},{20,28},{12,20},{4,12},{1,5},{9... | collective-permute-start | bytes 9437192 | tf_op jit(solution)/shard_map/while/body/eval_jaxpr/ppermute | solution.py:71
  238.8 2.6 copy-start.2
  243.9 4.5 copy-start.3
  248.4 68.9 %collective-permute-start = (bf16[512,3072]{1,0:T(8,128)(2,1)}, bf16[512,3072]{1,0:T(8,128)(2,1)S(1)}, u32[]{:S(2)}, u32[]{:S(2)}) collective-permute-start(bf16[512,3072]{1,0:T(8,128)(2,1)} %get-tuple-element.349), channel_id=1, source_target_pairs={{0,8},{8,16},{16,24},{24,28},{28,20},{20,12},{12,4},{4,0},{1,9},{9... | collective-permute-start | bytes 9437192 | tf_op jit(solution)/shard_map/while/body/eval_jaxpr/ppermute | solution.py:70
  249.9 69.2 %collective-permute-start.1 = (bf16[512,3072]{1,0:T(8,128)(2,1)}, bf16[512,3072]{1,0:T(8,128)(2,1)}, u32[]{:S(2)}, u32[]{:S(2)}) collective-permute-start(bf16[512,3072]{1,0:T(8,128)(2,1)} %get-tuple-element.350), channel_id=1, source_target_pairs={{0,4},{8,0},{16,8},{24,16},{28,24},{20,28},{12,20},{4,12},{1,5},{9... | collective-permute-start | bytes 9437192 | tf_op jit(solution)/shard_map/while/body/eval_jaxpr/ppermute | solution.py:71
  324.8 2.6 copy-start.2
  329.9 4.5 copy-start.3
  337.1 34.4 %collective-permute-start.3 = (bf16[256,3072]{1,0:T(8,128)(2,1)}, bf16[256,3072]{1,0:T(8,128)(2,1)S(1)}, u32[]{:S(2)}, u32[]{:S(2)}) collective-permute-start(bf16[256,3072]{1,0:T(8,128)(2,1)} %slice.68), channel_id=1, source_target_pairs={{0,4},{8,0},{16,8},{24,16},{28,24},{20,28},{12,20},{4,12},{1,5},{9... | collective-permute-start | bytes 4718600 | tf_op jit(solution)/shard_map/ppermute | solution.py:82
  341.3 34.1 %collective-permute-start.2 = (bf16[256,3072]{1,0:T(8,128)(2,1)}, bf16[256,3072]{1,0:T(8,128)(2,1)S(1)}, u32[]{:S(2)}, u32[]{:S(2)}) collective-permute-start(bf16[256,3072]{1,0:T(8,128)(2,1)} %slice.66), channel_id=1, source_target_pairs={{0,8},{8,16},{16,24},{24,28},{28,20},{20,12},{12,4},{4,0},{1,9},{9... | collective-permute-start | bytes 4718600 | tf_op jit(solution)/shard_map/ppermute | solution.py:81
  371.5 7.6 %copy-start.7 = (bf16[256,3072]{1,0:T(8,128)(2,1)}, bf16[256,3072]{1,0:T(8,128)(2,1)S(1)}, u32[]{:S(2)}) copy-start(bf16[256,3072]{1,0:T(8,128)(2,1)S(1)} %collective-permute-done.3) | copy-start | bytes 4718596
  375.5 3.7 copy-start.8
  379.2 4.8 %copy-start.12 = (s32[16,8]{0,1:T(8,128)S(1)}, s32[16,8]{0,1:T(8,128)}, u32[]{:S(2)}) copy-start(s32[16,8]{0,1:T(8,128)} %param.18) | copy-start | bytes 1540
  379.2 5.0 %copy-start.13 = (s32[16]{0:T(128)S(1)}, s32[16]{0:T(128)}, u32[]{:S(2)}) copy-start(s32[16]{0:T(128)} %param.19) | copy-start | bytes 196
  379.2 6.6 %copy-start.4 = (f32[512,1024]{1,0:T(8,128)S(1)}, f32[512,1024]{1,0:T(8,128)}, u32[]{:S(2)}) copy-start(f32[512,1024]{1,0:T(8,128)} %get-tuple-element.232) | copy-start | bytes 6291460
  379.2 27.6 %all-to-all-start = ((bf16[8,2,16,2048]{3,2,1,0:T(8,128)(2,1)}), bf16[8,2,16,2048]{3,2,1,0:T(8,128)(2,1)S(1)}, u32[]{:S(2)}, u32[]{:S(2)}) async-start(bf16[8,2,16,2048]{3,2,1,0:T(8,128)(2,1)} %bitcast.37), calls=%async_computation | async-start | bytes 2097152 | tf_op jit(solution)/shard_map/all_to_all | solution.py:89
  435.3 1.4 copy-start.6
  437.8 11.9 %copy-start.1 = (bf16[1024,1024]{1,0:T(8,128)(2,1)S(1)}, bf16[1024,1024]{1,0:T(8,128)(2,1)}, u32[]{:S(2)}) copy-start(bf16[1024,1024]{1,0:T(8,128)(2,1)} %param.13) | copy-start | bytes 6291460
Sparse Core Ops, SparseCore 0:
  9.7 25.2 all-gather.4
  36.5 34.4 all-gather.2

commit v2 on v1

--- a/solution.py
+++ b/solution.py
@@ -47,46 +47,37 @@
     chosen = blocks[picks].reshape(-1, crop_tokens.shape[1])
     tokens_in = lax.all_gather(chosen, "head", axis=1, tiled=True)
 
-    stacked = jnp.concatenate([query_weight, key_weight, value_weight], axis=1)
-
-    acc_q = jnp.zeros((queries_in.shape[0], width), jnp.float32)
-    acc_kv = jnp.zeros((tokens_in.shape[0], 2 * width), jnp.float32)
-
-    def contrib(acc_q, acc_kv, piece, src, lo, n):
-        start = src * wrows + lo
-        fq = lax.dynamic_slice_in_dim(queries_in, start, n, 1)
-        ft = lax.dynamic_slice_in_dim(tokens_in, start, n, 1)
-        acc_q = acc_q + jnp.dot(fq, piece[:, :width], preferred_element_type=jnp.float32)
-        acc_kv = acc_kv + jnp.dot(ft, piece[:, width:], preferred_element_type=jnp.float32)
-        return acc_q, acc_kv
-
-    acc_q, acc_kv = contrib(acc_q, acc_kv, stacked, me, 0, wrows)
     steps_fwd = ncrop // 2
     steps_bwd = (ncrop - 1) // 2
     split = wrows // 2
 
-    def ring_step(k, carry):
-        fwd, bwd, acc_q, acc_kv = carry
-        fwd = lax.ppermute(fwd, "crop", fwd_perm)
-        bwd = lax.ppermute(bwd, "crop", bwd_perm)
-        acc_q, acc_kv = contrib(acc_q, acc_kv, fwd, ring_arr[(pos - k) % ncrop], 0, wrows)
-        acc_q, acc_kv = contrib(acc_q, acc_kv, bwd, ring_arr[(pos + k) % ncrop], 0, wrows)
-        return fwd, bwd, acc_q, acc_kv
+    def ring_gather(piece):
+        buf = jnp.zeros((ncrop,) + piece.shape, piece.dtype)
+        buf = lax.dynamic_update_slice(buf, piece[None], (me, 0, 0))
 
-    fwd, bwd, acc_q, acc_kv = lax.fori_loop(
-        1, steps_bwd + 1, ring_step, (stacked, stacked, acc_q, acc_kv)
-    )
-    if steps_fwd > steps_bwd:
-        src = ring_arr[(pos - steps_fwd) % ncrop]
-        fwd_piece = lax.ppermute(fwd[:split], "crop", fwd_perm)
-        bwd_piece = lax.ppermute(bwd[split:], "crop", bwd_perm)
-        acc_q, acc_kv = contrib(acc_q, acc_kv, fwd_piece, src, 0, split)
-        acc_q, acc_kv = contrib(acc_q, acc_kv, bwd_piece, src, split, wrows - split)
+        def ring_step(k, carry):
+            fwd, bwd, buf = carry
+            fwd = lax.ppermute(fwd, "crop", fwd_perm)
+            bwd = lax.ppermute(bwd, "crop", bwd_perm)
+            buf = lax.dynamic_update_slice(buf, fwd[None], (ring_arr[(pos - k) % ncrop], 0, 0))
+            buf = lax.dynamic_update_slice(buf, bwd[None], (ring_arr[(pos + k) % ncrop], 0, 0))
+            return fwd, bwd, buf
 
-    query = acc_q.astype(jnp.bfloat16)
-    kv = acc_kv.astype(jnp.bfloat16)
+        fwd, bwd, buf = lax.fori_loop(1, steps_bwd + 1, ring_step, (piece, piece, buf))
+        if steps_fwd > steps_bwd:
+            src = ring_arr[(pos - steps_fwd) % ncrop]
+            top = lax.ppermute(fwd[:split], "crop", fwd_perm)
+            bottom = lax.ppermute(bwd[split:], "crop", bwd_perm)
+            buf = lax.dynamic_update_slice(buf, top[None], (src, 0, 0))
+            buf = lax.dynamic_update_slice(buf, bottom[None], (src, split, 0))
+        return buf.reshape(ncrop * wrows, piece.shape[1])
+
+    kv_weight = ring_gather(jnp.concatenate([key_weight, value_weight], axis=1))
+    kv = jnp.dot(tokens_in, kv_weight, preferred_element_type=jnp.float32).astype(jnp.bfloat16)
     packed = kv.reshape(ncrop, CAP, CT, 2 * width)
     incoming = lax.all_to_all(packed, "crop", split_axis=0, concat_axis=0, tiled=True)
+    q_weight = ring_gather(query_weight)
+    query = jnp.dot(queries_in, q_weight, preferred_element_type=jnp.float32).astype(jnp.bfloat16)
     slotted = incoming.reshape(ncrop * CAP, CT, 2 * width)
     listed = slotted[region_slots].reshape(rows_here, NB * CT, 2 * width)
     keys_row = listed[:, :, :width].reshape(rows_here, NB * CT, heads_here, HD)

time: 458 us -> 419 us (0.915)
  waiting for transfers between devices: 293 us -> 194 us
  local copies, waits for them, and re-layouts: 60.6 us -> 112 us
  matrix products: 62.1 us -> 34.7 us
  loops' own time: 8.08 us -> 30.8 us
  starting transfers between devices: 12.9 us -> 28.1 us
    all_gather x1, waiting for transfers between devices: 33.1 us -> 0.01 us  [body(): queries_in = lax.all_gather(global_rows, 'head', axis=1, tiled=True)]
    dynamic_update_slice x0 -> x18, local copies, waits for them, and re-layouts: none -> 27.5 us  [the longest x6 13.2 us: ring_step(): lax.dynamic_update_slice(buf, bwd[None], (ring_arr[(pos + k) % ncrop], 0,...]
    dot_general x18 -> x2, matrix products: 48.5 us -> 21.1 us  [the longest x1 12 us: body(): jnp.dot(tokens_in, kv_weight, preferred_element_type=jnp.float32)]
    another operation x1 -> x2, loops' own time: 8.08 us -> 30.8 us  [ring_gather(): lax.fori_loop(1, steps_bwd + 1, ring_step, (piece, piece, buf))]
    all_to_all x1, waiting for transfers between devices: 19.1 us -> 0.01 us  [body(): lax.all_to_all(packed, 'crop', split_axis=0, concat_axis=0, tiled=True)]
    ppermute x3 -> x6, waiting for transfers between devices: 193 us -> 175 us  [ring_step(): fwd = lax.ppermute(fwd, 'crop', fwd_perm)]
    all_gather x1, waiting for transfers between devices: 16.8 us -> 0.01 us  [body(): tokens_in = lax.all_gather(chosen, 'head', axis=1, tiled=True)]
    ppermute x2 -> x4, waiting for transfers between devices: 30.2 us -> 15.7 us  [the longest x2 12.4 us: ring_gather(): top = lax.ppermute(fwd[:split], 'crop', fwd_perm)]
  transfers between devices with their start and end apart: 11 -> 19, of which waited for: 8 -> 15; matrix products, arithmetic and copies ran while one was open for 6% -> 25% of each run, Pallas kernels for 0% -> 0%
where the time goes in v2:
time: 419 us; the launch traced here: 418 us
  waiting for transfers between devices  194 us (46%)
  local copies, waits for them, and re-layouts  112 us (27%)
  matrix products  34.7 us (8%)
  loops' own time  30.8 us (7%)
  starting transfers between devices  28.1 us (7%)
  between operations  16.2 us (4%)
    ppermute x6, waiting for transfers between devices, ring_step(): fwd = lax.ppermute(fwd, 'crop', fwd_perm)  175 us
    another operation x2, loops' own time, ring_gather(): lax.fori_loop(1, steps_bwd + 1, ring_step, (piece, piece, buf))  30.8 us
    while x24, local copies, waits for them, and re-layouts  23.3 us
    ppermute x6, starting transfers between devices, ring_step(): fwd = lax.ppermute(fwd, 'crop', fwd_perm)  17.2 us
    unnamed x24, local copies, waits for them, and re-layouts  15.3 us
    dynamic_update_slice x6, local copies, waits for them, and re-layouts, ring_step(): lax.dynamic_update_slice(buf, bwd[None], (ring_arr[(pos + k) % ncrop], 0,...  13.2 us
    slice x2, local copies, waits for them, and re-layouts, body(): keys_row = listed[:, :, :width].reshape(rows_here, NB * CT, heads_here, HD)  12.5 us
    ppermute x2, waiting for transfers between devices, ring_gather(): top = lax.ppermute(fwd[:split], 'crop', fwd_perm)  12.4 us
  transfers between devices with their start and end apart: 19, of which 15 were waited for; matrix products, arithmetic and copies ran while one was open for 25% of the time, Pallas kernels for 0%

profile of v2, /device:TPU:0, one launch (start us, length us, event | category | flops | bytes accessed | tf_op | source)
XLA Modules:
  0.0 417.8 jit_solution(17229685045506051336)
XLA Ops:
  6.5 2.4 copy.74
  17.1 6.2 %copy-done.4 = bf16[8,512,2048]{2,1,0:T(8,128)(2,1)} copy-done((bf16[8,512,2048]{2,1,0:T(8,128)(2,1)}, bf16[8,512,2048]{2,1,0:T(8,128)(2,1)S(1)}, u32[]{:S(2)}) %copy-start.4) | copy-done | bytes 16777240
  23.3 174.1 %while.40 = (s32[]{:T(128)}, bf16[512,2048]{1,0:T(8,128)(2,1)S(1)}, bf16[512,2048]{1,0:T(8,128)(2,1)}, bf16[8,512,2048]{2,1,0:T(8,128)(2,1)}, s32[]{:T(128)}, /*...) while((s32[]{:T(128)}, bf16[512,2048]{1,0:T(8,128)(2,1)S(1)}, ...), condition=%wide.region_1.2_spmd.clone, body=%wide.region_0.1_spmd.sunk.clone.sunk | while | flops 38 | bytes 50332276 | solution.py:66
  24.6 3.0 collective-permute-start
  33.2 40.2 %collective-permute-done = bf16[512,2048]{1,0:T(8,128)(2,1)S(1)} collective-permute-done((bf16[512,2048]{1,0:T(8,128)(2,1)}, bf16[512,2048]{1,0:T(8,128)(2,1)S(1)}, u32[]{:S(2)}, u32[]{:S(2)}) %collective-permute-start) | collective-permute-done | bytes 2097184 | tf_op jit(solution)/shard_map/while/body/eval_jaxpr/ppermute | solution.py:60
  75.1 3.2 copy.54
  79.8 3.3 bitcast_dynamic-update-slice_fusion.15
  92.0 39.2 %collective-permute-done = bf16[512,2048]{1,0:T(8,128)(2,1)S(1)} collective-permute-done((bf16[512,2048]{1,0:T(8,128)(2,1)}, bf16[512,2048]{1,0:T(8,128)(2,1)S(1)}, u32[]{:S(2)}, u32[]{:S(2)}) %collective-permute-start) | collective-permute-done | bytes 2097184 | tf_op jit(solution)/shard_map/while/body/eval_jaxpr/ppermute | solution.py:60
  132.6 3.2 copy.54
  137.4 3.4 bitcast_dynamic-update-slice_fusion.15
  149.7 38.3 %collective-permute-done = bf16[512,2048]{1,0:T(8,128)(2,1)S(1)} collective-permute-done((bf16[512,2048]{1,0:T(8,128)(2,1)}, bf16[512,2048]{1,0:T(8,128)(2,1)S(1)}, u32[]{:S(2)}, u32[]{:S(2)}) %collective-permute-start) | collective-permute-done | bytes 2097184 | tf_op jit(solution)/shard_map/while/body/eval_jaxpr/ppermute | solution.py:60
  189.3 3.2 copy.54
  194.1 3.3 bitcast_dynamic-update-slice_fusion.15
  204.5 2.3 copy.61
  207.4 5.1 %broadcast_in_dim.91 = bf16[8,512,1024]{2,1,0:T(8,128)(2,1)} broadcast(bf16[]{:T(256)} %constant.148.clone.1), dimensions={} | broadcast | bytes 8388610 | tf_op jit(solution)/shard_map/broadcast_in_dim | solution.py:55
  212.5 2.4 bitcast_dynamic-update-slice_fusion.5
  214.8 6.2 %collective-permute-done.4 = bf16[256,2048]{1,0:T(8,128)(2,1)S(1)} collective-permute-done((bf16[256,2048]{1,0:T(8,128)(2,1)}, bf16[256,2048]{1,0:T(8,128)(2,1)S(1)}, u32[]{:S(2)}, u32[]{:S(2)}) %collective-permute-start.4) | collective-permute-done | bytes 1048608 | tf_op jit(solution)/shard_map/ppermute | solution.py:69
  224.3 12.0 %convolution_convert_fusion = bf16[256,2048]{1,0:T(8,128)(2,1)} fusion(bf16[256,4096]{1,0:T(8,128)(2,1)} %all-gather.3.cloned.1.call-done, bf16[4096,2048]{1,0:T(8,128)(2,1)} %bitcast.76), kind=kOutput, calls=%fused_computation.7 | convolution fusion | flops 4295491584 | bytes 19922944 | tf_op jit(solution)/shard_map/dot_general | solution.py:76
  236.3 5.1 %all-to-all-start = ((bf16[8,2,16,2048]{3,2,1,0:T(8,128)(2,1)}), bf16[8,2,16,2048]{3,2,1,0:T(8,128)(2,1)S(1)}, u32[]{:S(2)}, u32[]{:S(2)}) async-start(bf16[8,2,16,2048]{3,2,1,0:T(8,128)(2,1)} %bitcast.9), calls=%async_computation | async-start | bytes 2097152 | tf_op jit(solution)/shard_map/all_to_all | solution.py:78
  241.4 101.6 %while.41 = (s32[]{:T(128)}, bf16[512,1024]{1,0:T(8,128)(2,1)}, bf16[512,1024]{1,0:T(8,128)(2,1)}, bf16[8,512,1024]{2,1,0:T(8,128)(2,1)}, s32[]{:T(128)}, /*inde...) while((s32[]{:T(128)}, bf16[512,1024]{1,0:T(8,128)(2,1)}, ...), condition=%wide.region_3.4_spmd.clone, body=%wide.region_2.3_spmd.sunk.clone.sunk | while | flops 38 | bytes 16777808 | solution.py:66
  249.5 28.5 %collective-permute-done.2 = bf16[512,1024]{1,0:T(8,128)(2,1)S(1)} collective-permute-done((bf16[512,1024]{1,0:T(8,128)(2,1)}, bf16[512,1024]{1,0:T(8,128)(2,1)S(1)}, u32[]{:S(2)}, u32[]{:S(2)}) %collective-permute-start.2) | collective-permute-done | bytes 1048608 | tf_op jit(solution)/shard_map/while/body/eval_jaxpr/ppermute | solution.py:60
  282.7 7.3 %collective-permute-start.2 = (bf16[512,1024]{1,0:T(8,128)(2,1)}, bf16[512,1024]{1,0:T(8,128)(2,1)S(1)}, u32[]{:S(2)}, u32[]{:S(2)}) collective-permute-start(bf16[512,1024]{1,0:T(8,128)(2,1)} %get-tuple-element.498), channel_id=1, source_target_pairs={{0,8},{8,16},{16,24},{24,28},{28,20},{20,12},{12,4},{4,0},{1,9},{9... | collective-permute-start | bytes 3145736 | tf_op jit(solution)/shard_map/while/body/eval_jaxpr/ppermute | solution.py:60
  296.0 14.3 %collective-permute-done.2 = bf16[512,1024]{1,0:T(8,128)(2,1)S(1)} collective-permute-done((bf16[512,1024]{1,0:T(8,128)(2,1)}, bf16[512,1024]{1,0:T(8,128)(2,1)S(1)}, u32[]{:S(2)}, u32[]{:S(2)}) %collective-permute-start.2) | collective-permute-done | bytes 1048608 | tf_op jit(solution)/shard_map/while/body/eval_jaxpr/ppermute | solution.py:60
  324.0 14.1 %collective-permute-done.2 = bf16[512,1024]{1,0:T(8,128)(2,1)S(1)} collective-permute-done((bf16[512,1024]{1,0:T(8,128)(2,1)}, bf16[512,1024]{1,0:T(8,128)(2,1)S(1)}, u32[]{:S(2)}, u32[]{:S(2)}) %collective-permute-start.2) | collective-permute-done | bytes 1048608 | tf_op jit(solution)/shard_map/while/body/eval_jaxpr/ppermute | solution.py:60
  347.7 6.1 %collective-permute-done.6 = bf16[256,1024]{1,0:T(8,128)(2,1)S(1)} collective-permute-done((bf16[256,1024]{1,0:T(8,128)(2,1)S(1)}, bf16[256,1024]{1,0:T(8,128)(2,1)S(1)}, u32[]{:S(2)}, u32[]{:S(2)}) %collective-permute-start.6) | collective-permute-done | bytes 524320 | tf_op jit(solution)/shard_map/ppermute | solution.py:69
  357.8 6.3 %gather_fusion.1 = bf16[128,16,2048]{2,1,0:T(8,128)(2,1)} fusion(bf16[16,16,2048]{2,1,0:T(8,128)(2,1)S(1)} %bitcast.74, s32[1024]{0:T(1024)S(1)} %pad_clamp_fusion), kind=kCustom, calls=%fused_computation.1 | custom fusion | bytes 16777728 | tf_op jit(solution)/shard_map/gather | solution.py:82
  364.1 6.1 %fusion.19 = (bf16[16,128,1024]{2,1,0:T(8,128)(2,1)}, bf16[16,128,1024]{2,1,0:T(8,128)(2,1)}) fusion(bf16[16,128,2048]{2,1,0:T(8,128)(2,1)} %bitcast.75), kind=kLoop, calls=%fused_computation.47 | loop fusion | bytes 16777216 | tf_op jit(solution)/shard_map/slice | solution.py:83
  370.1 6.4 %copy.25 = bf16[16,128,1024]{1,2,0:T(8,128)(2,1)} copy(bf16[16,128,1024]{2,1,0:T(8,128)(2,1)} %get-tuple-element.385) | data formatting | bytes 8388608 | tf_op jit(solution)/shard_map/slice | solution.py:83
  376.6 6.4 %copy.23 = bf16[16,128,1024]{1,2,0:T(8,128)(2,1)} copy(bf16[16,128,1024]{2,1,0:T(8,128)(2,1)} %get-tuple-element.386) | data formatting | bytes 8388608 | tf_op jit(solution)/shard_map/slice | solution.py:84
  383.0 9.1 %fusion.3 = bf16[512,1024]{0,1:T(8,128)(2,1)S(1)} fusion(bf16[4096,1024]{1,0:T(8,128)(2,1)} %bitcast.16, bf16[512,4096]{1,0:T(8,128)(2,1)} %all-gather.5.cloned.1.call-done), kind=kOutput, calls=%fused_computation.16 | convolution fusion | flops 4295491584 | bytes 13631488 | tf_op jit(solution)/shard_map/dot_general | solution.py:80
  393.1 3.4 fusion.4
  399.0 10.2 %fusion.2 = bf16[16,32,8,128]{3,1,2,0:T(8,128)(2,1)S(1)} fusion(bf16[16,128,8,128]{1,3,2,0:T(8,128)(2,1)} %bitcast.79, f32[16,8,32]{2,1,0:T(8,128)S(1)} %fusion.20, f32[16,8,32,128]{3,2,1,0:T(8,128)} %copy-done.5, pred[16,128]{1,0:T(8,128)(4,1)S(1)} %broadcast_compare_fusion), kind=kOutput, calls=%fused_computation.15 | convolution fusion | flops 137367680 | bytes 7358464 | tf_op jit(solution)/shard_map/rhgk,rkhe->rghe/dot_general | solution.py:96
  (113 shorter events, 70.6 us)
Async XLA Ops:
  6.5 3.3 copy-start
  6.5 4.8 %copy-start.6 = (bf16[512,1024]{1,0:T(8,128)(2,1)S(1)}, bf16[512,1024]{1,0:T(8,128)(2,1)}, u32[]{:S(2)}) copy-start(bf16[512,1024]{1,0:T(8,128)(2,1)} %param.17) | copy-start | bytes 3145732
  6.5 217.8 %all-gather.3.cloned.1.call-start = ((), (), s32[]{:S(2)}) async-start(), calls=%async_computation.1 | async-start | bytes 2621440 | tf_op jit(solution)/shard_map/all_gather | solution.py:48
  11.2 371.7 %all-gather.5.cloned.1.call-start = ((), (), s32[]{:S(2)}) async-start(), calls=%async_computation.2 | async-start | bytes 5242880 | tf_op jit(solution)/shard_map/all_gather | solution.py:44
  11.3 2.8 copy-start.10
  16.8 6.5 %copy-start.7 = (s32[8]{0:T(128)S(1)}, s32[8]{0:T(128)}, u32[]{:S(2)}) copy-start(s32[8]{0:T(128)} %constant.165.clone) | copy-start | bytes 100
  17.1 6.3 %copy-start.4 = (bf16[8,512,2048]{2,1,0:T(8,128)(2,1)}, bf16[8,512,2048]{2,1,0:T(8,128)(2,1)S(1)}, u32[]{:S(2)}) copy-start(bf16[8,512,2048]{2,1,0:T(8,128)(2,1)S(1)} %bitcast_dynamic-update-slice_fusion.4) | copy-start | bytes 50331652
  23.3 1.3 copy-start.2
  24.6 48.8 %collective-permute-start = (bf16[512,2048]{1,0:T(8,128)(2,1)}, bf16[512,2048]{1,0:T(8,128)(2,1)S(1)}, u32[]{:S(2)}, u32[]{:S(2)}) collective-permute-start(bf16[512,2048]{1,0:T(8,128)(2,1)} %copy-done.2), channel_id=1, source_target_pairs={{0,8},{8,16},{16,24},{24,28},{28,20},{20,12},{12,4},{4,0},{1,9},{9... | collective-permute-start | bytes 6291464 | tf_op jit(solution)/shard_map/while/body/eval_jaxpr/ppermute | solution.py:60
  27.7 47.4 %collective-permute-start.1 = (bf16[512,2048]{1,0:T(8,128)(2,1)}, bf16[512,2048]{1,0:T(8,128)(2,1)}, u32[]{:S(2)}, u32[]{:S(2)}) collective-permute-start(bf16[512,2048]{1,0:T(8,128)(2,1)} %get-tuple-element.469), channel_id=1, source_target_pairs={{0,4},{8,0},{16,8},{24,16},{28,24},{20,28},{12,20},{4,12},{1,5},{9... | collective-permute-start | bytes 6291464 | tf_op jit(solution)/shard_map/while/body/eval_jaxpr/ppermute | solution.py:61
  79.8 3.3 copy-start.3
  84.4 46.8 %collective-permute-start = (bf16[512,2048]{1,0:T(8,128)(2,1)}, bf16[512,2048]{1,0:T(8,128)(2,1)S(1)}, u32[]{:S(2)}, u32[]{:S(2)}) collective-permute-start(bf16[512,2048]{1,0:T(8,128)(2,1)} %copy-done.2), channel_id=1, source_target_pairs={{0,8},{8,16},{16,24},{24,28},{28,20},{20,12},{12,4},{4,0},{1,9},{9... | collective-permute-start | bytes 6291464 | tf_op jit(solution)/shard_map/while/body/eval_jaxpr/ppermute | solution.py:60
  86.1 46.5 %collective-permute-start.1 = (bf16[512,2048]{1,0:T(8,128)(2,1)}, bf16[512,2048]{1,0:T(8,128)(2,1)}, u32[]{:S(2)}, u32[]{:S(2)}) collective-permute-start(bf16[512,2048]{1,0:T(8,128)(2,1)} %get-tuple-element.469), channel_id=1, source_target_pairs={{0,4},{8,0},{16,8},{24,16},{28,24},{20,28},{12,20},{4,12},{1,5},{9... | collective-permute-start | bytes 6291464 | tf_op jit(solution)/shard_map/while/body/eval_jaxpr/ppermute | solution.py:61
  137.4 3.4 copy-start.3
  142.1 45.9 %collective-permute-start = (bf16[512,2048]{1,0:T(8,128)(2,1)}, bf16[512,2048]{1,0:T(8,128)(2,1)S(1)}, u32[]{:S(2)}, u32[]{:S(2)}) collective-permute-start(bf16[512,2048]{1,0:T(8,128)(2,1)} %copy-done.2), channel_id=1, source_target_pairs={{0,8},{8,16},{16,24},{24,28},{28,20},{20,12},{12,4},{4,0},{1,9},{9... | collective-permute-start | bytes 6291464 | tf_op jit(solution)/shard_map/while/body/eval_jaxpr/ppermute | solution.py:60
  143.5 45.8 %collective-permute-start.1 = (bf16[512,2048]{1,0:T(8,128)(2,1)}, bf16[512,2048]{1,0:T(8,128)(2,1)}, u32[]{:S(2)}, u32[]{:S(2)}) collective-permute-start(bf16[512,2048]{1,0:T(8,128)(2,1)} %get-tuple-element.469), channel_id=1, source_target_pairs={{0,4},{8,0},{16,8},{24,16},{28,24},{20,28},{12,20},{4,12},{1,5},{9... | collective-permute-start | bytes 6291464 | tf_op jit(solution)/shard_map/while/body/eval_jaxpr/ppermute | solution.py:61
  194.1 3.3 copy-start.3
  198.5 22.6 %collective-permute-start.4 = (bf16[256,2048]{1,0:T(8,128)(2,1)}, bf16[256,2048]{1,0:T(8,128)(2,1)S(1)}, u32[]{:S(2)}, u32[]{:S(2)}) collective-permute-start(bf16[256,2048]{1,0:T(8,128)(2,1)} %slice.18), channel_id=1, source_target_pairs={{0,8},{8,16},{16,24},{24,28},{28,20},{20,12},{12,4},{4,0},{1,9},{9... | collective-permute-start | bytes 3145736 | tf_op jit(solution)/shard_map/ppermute | solution.py:69
  201.2 22.1 %collective-permute-start.5 = (bf16[256,2048]{1,0:T(8,128)(2,1)S(1)}, bf16[256,2048]{1,0:T(8,128)(2,1)S(1)}, u32[]{:S(2)}, u32[]{:S(2)}) collective-permute-start(bf16[256,2048]{1,0:T(8,128)(2,1)S(1)} %slice.19), channel_id=1, source_target_pairs={{0,4},{8,0},{16,8},{24,16},{28,24},{20,28},{12,20},{4,12},{1,5},{9... | collective-permute-start | bytes 3145736 | tf_op jit(solution)/shard_map/ppermute | solution.py:70
  236.3 121.5 %all-to-all-start = ((bf16[8,2,16,2048]{3,2,1,0:T(8,128)(2,1)}), bf16[8,2,16,2048]{3,2,1,0:T(8,128)(2,1)S(1)}, u32[]{:S(2)}, u32[]{:S(2)}) async-start(bf16[8,2,16,2048]{3,2,1,0:T(8,128)(2,1)} %bitcast.9), calls=%async_computation | async-start | bytes 2097152 | tf_op jit(solution)/shard_map/all_to_all | solution.py:78
  241.4 106.1 %copy-start.8 = (s32[16,8]{0,1:T(8,128)S(1)}, s32[16,8]{0,1:T(8,128)}, u32[]{:S(2)}) copy-start(s32[16,8]{0,1:T(8,128)} %param.20) | copy-start | bytes 1540
  241.4 106.3 %copy-start.9 = (s32[16]{0:T(128)S(1)}, s32[16]{0:T(128)}, u32[]{:S(2)}) copy-start(s32[16]{0:T(128)} %param.21) | copy-start | bytes 196
  241.4 36.6 %collective-permute-start.2 = (bf16[512,1024]{1,0:T(8,128)(2,1)}, bf16[512,1024]{1,0:T(8,128)(2,1)S(1)}, u32[]{:S(2)}, u32[]{:S(2)}) collective-permute-start(bf16[512,1024]{1,0:T(8,128)(2,1)} %get-tuple-element.498), channel_id=1, source_target_pairs={{0,8},{8,16},{16,24},{24,28},{28,20},{20,12},{12,4},{4,0},{1,9},{9... | collective-permute-start | bytes 3145736 | tf_op jit(solution)/shard_map/while/body/eval_jaxpr/ppermute | solution.py:60
  243.5 36.1 %collective-permute-start.3 = (bf16[512,1024]{1,0:T(8,128)(2,1)}, bf16[512,1024]{1,0:T(8,128)(2,1)S(1)}, u32[]{:S(2)}, u32[]{:S(2)}) collective-permute-start(bf16[512,1024]{1,0:T(8,128)(2,1)} %get-tuple-element.499), channel_id=1, source_target_pairs={{0,4},{8,0},{16,8},{24,16},{28,24},{20,28},{12,20},{4,12},{1,5},{9... | collective-permute-start | bytes 3145736 | tf_op jit(solution)/shard_map/while/body/eval_jaxpr/ppermute | solution.py:61
  282.7 27.6 %collective-permute-start.2 = (bf16[512,1024]{1,0:T(8,128)(2,1)}, bf16[512,1024]{1,0:T(8,128)(2,1)S(1)}, u32[]{:S(2)}, u32[]{:S(2)}) collective-permute-start(bf16[512,1024]{1,0:T(8,128)(2,1)} %get-tuple-element.498), channel_id=1, source_target_pairs={{0,8},{8,16},{16,24},{24,28},{28,20},{20,12},{12,4},{4,0},{1,9},{9... | collective-permute-start | bytes 3145736 | tf_op jit(solution)/shard_map/while/body/eval_jaxpr/ppermute | solution.py:60
  290.0 23.0 %collective-permute-start.3 = (bf16[512,1024]{1,0:T(8,128)(2,1)}, bf16[512,1024]{1,0:T(8,128)(2,1)S(1)}, u32[]{:S(2)}, u32[]{:S(2)}) collective-permute-start(bf16[512,1024]{1,0:T(8,128)(2,1)} %get-tuple-element.499), channel_id=1, source_target_pairs={{0,4},{8,0},{16,8},{24,16},{28,24},{20,28},{12,20},{4,12},{1,5},{9... | collective-permute-start | bytes 3145736 | tf_op jit(solution)/shard_map/while/body/eval_jaxpr/ppermute | solution.py:61
  316.1 22.0 %collective-permute-start.2 = (bf16[512,1024]{1,0:T(8,128)(2,1)}, bf16[512,1024]{1,0:T(8,128)(2,1)S(1)}, u32[]{:S(2)}, u32[]{:S(2)}) collective-permute-start(bf16[512,1024]{1,0:T(8,128)(2,1)} %get-tuple-element.498), channel_id=1, source_target_pairs={{0,8},{8,16},{16,24},{24,28},{28,20},{20,12},{12,4},{4,0},{1,9},{9... | collective-permute-start | bytes 3145736 | tf_op jit(solution)/shard_map/while/body/eval_jaxpr/ppermute | solution.py:60
  317.8 22.1 %collective-permute-start.3 = (bf16[512,1024]{1,0:T(8,128)(2,1)}, bf16[512,1024]{1,0:T(8,128)(2,1)S(1)}, u32[]{:S(2)}, u32[]{:S(2)}) collective-permute-start(bf16[512,1024]{1,0:T(8,128)(2,1)} %get-tuple-element.499), channel_id=1, source_target_pairs={{0,4},{8,0},{16,8},{24,16},{28,24},{20,28},{12,20},{4,12},{1,5},{9... | collective-permute-start | bytes 3145736 | tf_op jit(solution)/shard_map/while/body/eval_jaxpr/ppermute | solution.py:61
  344.1 9.8 %collective-permute-start.6 = (bf16[256,1024]{1,0:T(8,128)(2,1)S(1)}, bf16[256,1024]{1,0:T(8,128)(2,1)S(1)}, u32[]{:S(2)}, u32[]{:S(2)}) collective-permute-start(bf16[256,1024]{1,0:T(8,128)(2,1)S(1)} %slice.21), channel_id=1, source_target_pairs={{0,8},{8,16},{16,24},{24,28},{28,20},{20,12},{12,4},{4,0},{1,9},{9... | collective-permute-start | bytes 1572872 | tf_op jit(solution)/shard_map/ppermute | solution.py:69
  346.9 10.0 %collective-permute-start.7 = (bf16[256,1024]{1,0:T(8,128)(2,1)S(1)}, bf16[256,1024]{1,0:T(8,128)(2,1)S(1)}, u32[]{:S(2)}, u32[]{:S(2)}) collective-permute-start(bf16[256,1024]{1,0:T(8,128)(2,1)S(1)} %slice.22), channel_id=1, source_target_pairs={{0,4},{8,0},{16,8},{24,16},{28,24},{20,28},{12,20},{4,12},{1,5},{9... | collective-permute-start | bytes 1572872 | tf_op jit(solution)/shard_map/ppermute | solution.py:70
  396.5 1.3 copy-start.5
  399.0 11.9 %copy-start.1 = (bf16[1024,1024]{1,0:T(8,128)(2,1)S(1)}, bf16[1024,1024]{1,0:T(8,128)(2,1)}, u32[]{:S(2)}) copy-start(bf16[1024,1024]{1,0:T(8,128)(2,1)} %param.15) | copy-start | bytes 6291460
  (2 other events, 2.6 us)
Sparse Core Ops, SparseCore 0:
  11.4 25.2 all-gather.2
  202.0 35.6 all-gather.4

commit v3 on v2

--- a/solution.py
+++ b/solution.py
@@ -55,15 +55,13 @@
         buf = jnp.zeros((ncrop,) + piece.shape, piece.dtype)
         buf = lax.dynamic_update_slice(buf, piece[None], (me, 0, 0))
 
-        def ring_step(k, carry):
-            fwd, bwd, buf = carry
+        fwd = piece
+        bwd = piece
+        for k in range(1, steps_bwd + 1):
             fwd = lax.ppermute(fwd, "crop", fwd_perm)
             bwd = lax.ppermute(bwd, "crop", bwd_perm)
             buf = lax.dynamic_update_slice(buf, fwd[None], (ring_arr[(pos - k) % ncrop], 0, 0))
             buf = lax.dynamic_update_slice(buf, bwd[None], (ring_arr[(pos + k) % ncrop], 0, 0))
-            return fwd, bwd, buf
-
-        fwd, bwd, buf = lax.fori_loop(1, steps_bwd + 1, ring_step, (piece, piece, buf))
         if steps_fwd > steps_bwd:
             src = ring_arr[(pos - steps_fwd) % ncrop]
             top = lax.ppermute(fwd[:split], "crop", fwd_perm)

time: 419 us -> 349 us (0.83)
  local copies, waits for them, and re-layouts: 112 us -> 80.6 us
  loops' own time: 30.8 us -> 0 us
  waiting for transfers between devices: 194 us -> 175 us
  between operations: 16.2 us -> 32.2 us
  starting transfers between devices: 28.1 us -> 23.2 us
    ppermute x12, waiting for transfers between devices: 178 us -> 139 us  [the longest x6 139 us: ring_gather(): fwd = lax.ppermute(fwd, 'crop', fwd_perm)]
    another operation x2 -> x0, loops' own time: 30.8 us -> none  [ring_gather(): lax.fori_loop(1, steps_bwd + 1, ring_step, (piece, piece, buf))]
    while x24 -> x0, local copies, waits for them, and re-layouts: 23.3 us -> none
    ppermute x2, waiting for transfers between devices: 12.4 us -> 26.6 us  [ring_gather(): top = lax.ppermute(fwd[:split], 'crop', fwd_perm)]
    unnamed x24 -> x19, local copies, waits for them, and re-layouts: 15.3 us -> 4.8 us
    all_to_all x1, waiting for transfers between devices: 0.01 us -> 9.42 us  [body(): lax.all_to_all(packed, 'crop', split_axis=0, concat_axis=0, tiled=True)]
    ppermute x12, starting transfers between devices: 18.5 us -> 13.4 us  [the longest x6 12.9 us: ring_gather(): fwd = lax.ppermute(fwd, 'crop', fwd_perm)]
  transfers between devices with their start and end apart: 19 -> 19, of which waited for: 15 -> 7; matrix products, arithmetic and copies ran while one was open for 25% -> 21% of each run, Pallas kernels for 0% -> 0%
where the time goes in v3:
time: 349 us; the launch traced here: 348 us
  waiting for transfers between devices  175 us (50%)
  local copies, waits for them, and re-layouts  80.6 us (23%)
  matrix products  34.6 us (10%)
  between operations  32.2 us (9%)
  starting transfers between devices  23.2 us (7%)
    ppermute x6, waiting for transfers between devices, ring_gather(): fwd = lax.ppermute(fwd, 'crop', fwd_perm)  139 us
    ppermute x2, waiting for transfers between devices, ring_gather(): top = lax.ppermute(fwd[:split], 'crop', fwd_perm)  26.6 us
    ppermute x6, starting transfers between devices, ring_gather(): fwd = lax.ppermute(fwd, 'crop', fwd_perm)  12.9 us
    slice x2, local copies, waits for them, and re-layouts, body(): keys_row = listed[:, :, :width].reshape(rows_here, NB * CT, heads_here, HD)  12.5 us
    dynamic_update_slice x6, local copies, waits for them, and re-layouts, ring_gather(): lax.dynamic_update_slice(buf, fwd[None], (ring_arr[(pos - k) % ncrop], 0,...  12.3 us
    dynamic_update_slice x6, local copies, waits for them, and re-layouts, ring_gather(): lax.dynamic_update_slice(buf, bwd[None], (ring_arr[(pos + k) % ncrop], 0,...  12.3 us
    dot_general x1, matrix products, body(): jnp.dot(tokens_in, kv_weight, preferred_element_type=jnp.float32)  11.9 us
    broadcast_in_dim x2, local copies, waits for them, and re-layouts, ring_gather(): buf = jnp.zeros((ncrop,) + piece.shape, piece.dtype)  10.3 us
  transfers between devices with their start and end apart: 19, of which 7 were waited for; matrix products, arithmetic and copies ran while one was open for 21% of the time, Pallas kernels for 0%

profile of v3, /device:TPU:0, one launch (start us, length us, event | category | flops | bytes accessed | tf_op | source)
XLA Modules:
  0.0 347.5 jit_solution(2588097705934309809)
XLA Ops:
  12.2 3.1 collective-permute-start
  15.3 2.0 collective-permute-start.8
  17.4 4.3 %broadcast_in_dim.93 = bf16[8,512,1024]{2,1,0:T(8,128)(2,1)} broadcast(bf16[]{:T(256)} %constant.98.clone.1), dimensions={} | broadcast | bytes 8388610 | tf_op jit(solution)/shard_map/broadcast_in_dim | solution.py:55
  22.9 39.0 %collective-permute-done = bf16[512,2048]{1,0:T(8,128)(2,1)} collective-permute-done((bf16[512,2048]{1,0:T(8,128)(2,1)S(1)}, bf16[512,2048]{1,0:T(8,128)(2,1)}, u32[]{:S(2)}, u32[]{:S(2)}) %collective-permute-start) | collective-permute-done | bytes 2097184 | tf_op jit(solution)/shard_map/ppermute | solution.py:61
  61.8 2.1 collective-permute-start.2
  84.3 2.1 collective-permute-start.10
  86.4 6.0 %broadcast_in_dim.81 = bf16[8,512,2048]{2,1,0:T(8,128)(2,1)} broadcast(bf16[]{:T(256)} %constant.98.clone.1), dimensions={} | broadcast | bytes 16777218 | tf_op jit(solution)/shard_map/broadcast_in_dim | solution.py:55
  94.0 2.3 bitcast_dynamic-update-slice_fusion.12
  96.3 2.3 bitcast_dynamic-update-slice_fusion.11
  98.6 52.2 %collective-permute-done.10 = bf16[512,1024]{1,0:T(8,128)(2,1)S(1)} collective-permute-done((bf16[512,1024]{1,0:T(8,128)(2,1)}, bf16[512,1024]{1,0:T(8,128)(2,1)S(1)}, u32[]{:S(2)}, u32[]{:S(2)}) %collective-permute-start.10) | collective-permute-done | bytes 1048608 | tf_op jit(solution)/shard_map/ppermute | solution.py:61
  152.8 3.1 bitcast_dynamic-update-slice_fusion.5
  157.0 1.8 collective-permute-start.4
  160.1 3.2 bitcast_dynamic-update-slice_fusion.4
  163.3 13.6 %collective-permute-done.12 = bf16[512,1024]{1,0:T(8,128)(2,1)S(1)} collective-permute-done((bf16[512,1024]{1,0:T(8,128)(2,1)S(1)}, bf16[512,1024]{1,0:T(8,128)(2,1)S(1)}, u32[]{:S(2)}, u32[]{:S(2)}) %collective-permute-start.12) | collective-permute-done | bytes 1048608 | tf_op jit(solution)/shard_map/ppermute | solution.py:61
  177.7 1.8 collective-permute-start.14
  181.6 3.2 bitcast_dynamic-update-slice_fusion.3
  184.8 3.2 bitcast_dynamic-update-slice_fusion.2
  188.1 33.7 %collective-permute-done.4 = bf16[512,2048]{1,0:T(8,128)(2,1)S(1)} collective-permute-done((bf16[512,2048]{1,0:T(8,128)(2,1)}, bf16[512,2048]{1,0:T(8,128)(2,1)S(1)}, u32[]{:S(2)}, u32[]{:S(2)}) %collective-permute-start.4) | collective-permute-done | bytes 2097184 | tf_op jit(solution)/shard_map/ppermute | solution.py:61
  221.9 1.8 collective-permute-start.6
  227.2 26.6 %collective-permute-done.6 = bf16[256,2048]{1,0:T(8,128)(2,1)S(1)} collective-permute-done((bf16[256,2048]{1,0:T(8,128)(2,1)S(1)}, bf16[256,2048]{1,0:T(8,128)(2,1)S(1)}, u32[]{:S(2)}, u32[]{:S(2)}) %collective-permute-start.6) | collective-permute-done | bytes 1048608 | tf_op jit(solution)/shard_map/ppermute | solution.py:67
  256.0 11.9 %convolution_convert_fusion = bf16[256,2048]{1,0:T(8,128)(2,1)} fusion(bf16[256,4096]{1,0:T(8,128)(2,1)} %all-gather.3.cloned.1.call-done, bf16[4096,2048]{1,0:T(8,128)(2,1)} %bitcast.26), kind=kOutput, calls=%fused_computation.3 | convolution fusion | flops 4295491584 | bytes 19922944 | tf_op jit(solution)/shard_map/dot_general | solution.py:74
  267.9 5.6 %all-to-all-start = ((bf16[8,2,16,2048]{3,2,1,0:T(8,128)(2,1)}), bf16[8,2,16,2048]{3,2,1,0:T(8,128)(2,1)S(1)}, u32[]{:S(2)}, u32[]{:S(2)}) async-start(bf16[8,2,16,2048]{3,2,1,0:T(8,128)(2,1)} %bitcast.27), calls=%async_computation | async-start | bytes 2097152 | tf_op jit(solution)/shard_map/all_to_all | solution.py:76
  274.5 1.9 bitcast_dynamic-update-slice_fusion.17
  276.4 1.9 bitcast_dynamic-update-slice_fusion.16
  278.3 9.1 %fusion.3 = bf16[512,1024]{0,1:T(8,128)(2,1)S(1)} fusion(bf16[4096,1024]{1,0:T(8,128)(2,1)} %bitcast.40, bf16[512,4096]{1,0:T(8,128)(2,1)} %all-gather.5.cloned.1.call-done), kind=kOutput, calls=%fused_computation.18 | convolution fusion | flops 4295491584 | bytes 13631488 | tf_op jit(solution)/shard_map/dot_general | solution.py:78
  288.2 9.4 %all-to-all-done = bf16[8,2,16,2048]{3,2,1,0:T(8,128)(2,1)S(1)} async-done(((bf16[8,2,16,2048]{3,2,1,0:T(8,128)(2,1)}), bf16[8,2,16,2048]{3,2,1,0:T(8,128)(2,1)S(1)}, u32[]{:S(2)}, u32[]{:S(2)}) %all-to-all-start) | async-done | bytes 1048608 | tf_op jit(solution)/shard_map/all_to_all | solution.py:76
  297.7 6.3 %gather_fusion.1 = bf16[128,16,2048]{2,1,0:T(8,128)(2,1)} fusion(bf16[16,16,2048]{2,1,0:T(8,128)(2,1)S(1)} %bitcast.82, s32[1024]{0:T(1024)S(1)} %pad_clamp_fusion), kind=kCustom, calls=%fused_computation.1 | custom fusion | bytes 16777728 | tf_op jit(solution)/shard_map/gather | solution.py:80
  303.9 6.1 %fusion.17 = (bf16[16,128,1024]{2,1,0:T(8,128)(2,1)}, bf16[16,128,1024]{2,1,0:T(8,128)(2,1)}) fusion(bf16[16,128,2048]{2,1,0:T(8,128)(2,1)} %bitcast.83), kind=kLoop, calls=%fused_computation.53 | loop fusion | bytes 16777216 | tf_op jit(solution)/shard_map/slice | solution.py:81
  310.0 6.5 %copy.25 = bf16[16,128,1024]{1,2,0:T(8,128)(2,1)} copy(bf16[16,128,1024]{2,1,0:T(8,128)(2,1)} %get-tuple-element.5) | data formatting | bytes 8388608 | tf_op jit(solution)/shard_map/slice | solution.py:81
  316.5 6.4 %copy.23 = bf16[16,128,1024]{1,2,0:T(8,128)(2,1)} copy(bf16[16,128,1024]{2,1,0:T(8,128)(2,1)} %get-tuple-element.6) | data formatting | bytes 8388608 | tf_op jit(solution)/shard_map/slice | solution.py:82
  322.8 3.4 fusion.4
  328.7 10.2 %fusion.2 = bf16[16,32,8,128]{3,1,2,0:T(8,128)(2,1)S(1)} fusion(bf16[16,128,8,128]{1,3,2,0:T(8,128)(2,1)} %bitcast.86, f32[16,8,32]{2,1,0:T(8,128)S(1)} %fusion.19, f32[16,8,32,128]{3,2,1,0:T(8,128)} %copy-done.2, pred[16,128]{1,0:T(8,128)(4,1)S(1)} %broadcast_compare_fusion), kind=kOutput, calls=%fused_computation.17 | convolution fusion | flops 137367680 | bytes 7358464 | tf_op jit(solution)/shard_map/rhgk,rkhe->rghe/dot_general | solution.py:94
  (76 shorter events, 29.2 us)
Async XLA Ops:
  6.5 1.6 copy-start
  6.5 8.8 %copy-start.3 = (bf16[512,1024]{1,0:T(8,128)(2,1)S(1)}, bf16[512,1024]{1,0:T(8,128)(2,1)}, u32[]{:S(2)}) copy-start(bf16[512,1024]{1,0:T(8,128)(2,1)} %param.12) | copy-start | bytes 3145732
  6.5 10.8 %copy-start.5 = (s32[16,8]{0,1:T(8,128)S(1)}, s32[16,8]{0,1:T(8,128)}, u32[]{:S(2)}) copy-start(s32[16,8]{0,1:T(8,128)} %param.16) | copy-start | bytes 1540
  6.5 249.5 %all-gather.3.cloned.1.call-start = ((), (), s32[]{:S(2)}) async-start(), calls=%async_computation.1 | async-start | bytes 2621440 | tf_op jit(solution)/shard_map/all_gather | solution.py:48
  9.5 268.8 %all-gather.5.cloned.1.call-start = ((), (), s32[]{:S(2)}) async-start(), calls=%async_computation.2 | async-start | bytes 5242880 | tf_op jit(solution)/shard_map/all_gather | solution.py:44
  12.2 49.6 %collective-permute-start = (bf16[512,2048]{1,0:T(8,128)(2,1)S(1)}, bf16[512,2048]{1,0:T(8,128)(2,1)}, u32[]{:S(2)}, u32[]{:S(2)}) collective-permute-start(bf16[512,2048]{1,0:T(8,128)(2,1)S(1)} %constant_dynamic-update-slice_fusion), channel_id=1, source_target_pairs={{0,8},{8,16},{16,24},{24,28},{28,20},{20,12},{12,4},{4,0},{1,9},{9... | collective-permute-start | bytes 6291464 | tf_op jit(solution)/shard_map/ppermute | solution.py:61
  15.3 48.7 %collective-permute-start.1 = (bf16[512,2048]{1,0:T(8,128)(2,1)S(1)}, bf16[512,2048]{1,0:T(8,128)(2,1)}, u32[]{:S(2)}, u32[]{:S(2)}) collective-permute-start(bf16[512,2048]{1,0:T(8,128)(2,1)S(1)} %constant_dynamic-update-slice_fusion), channel_id=1, source_target_pairs={{0,4},{8,0},{16,8},{24,16},{28,24},{20,28},{12,20},{4,12},{1,5},{9... | collective-permute-start | bytes 6291464 | tf_op jit(solution)/shard_map/ppermute | solution.py:62
  15.3 69.0 %collective-permute-start.8 = (bf16[512,1024]{1,0:T(8,128)(2,1)S(1)}, bf16[512,1024]{1,0:T(8,128)(2,1)}, u32[]{:S(2)}, u32[]{:S(2)}) collective-permute-start(bf16[512,1024]{1,0:T(8,128)(2,1)S(1)} %copy-done.3), channel_id=1, source_target_pairs={{0,8},{8,16},{16,24},{24,28},{28,20},{20,12},{12,4},{4,0},{1,9},{9... | collective-permute-start | bytes 3145736 | tf_op jit(solution)/shard_map/ppermute | solution.py:61
  17.3 69.1 %collective-permute-start.9 = (bf16[512,1024]{1,0:T(8,128)(2,1)S(1)}, bf16[512,1024]{1,0:T(8,128)(2,1)}, u32[]{:S(2)}, u32[]{:S(2)}) collective-permute-start(bf16[512,1024]{1,0:T(8,128)(2,1)S(1)} %copy-done.3), channel_id=1, source_target_pairs={{0,4},{8,0},{16,8},{24,16},{28,24},{20,28},{12,20},{4,12},{1,5},{9... | collective-permute-start | bytes 3145736 | tf_op jit(solution)/shard_map/ppermute | solution.py:62
  17.4 46.6 %copy-start.6 = (s32[16]{0:T(128)S(1)}, s32[16]{0:T(128)}, u32[]{:S(2)}) copy-start(s32[16]{0:T(128)} %param.17) | copy-start | bytes 196
  17.4 46.6 %copy-start.7 = (s32[8]{0:T(128)S(1)}, s32[8]{0:T(128)}, u32[]{:S(2)}) copy-start(s32[8]{0:T(128)} %constant.120.clone) | copy-start | bytes 100
  17.4 52.2 %copy-start.4 = (s32[8]{0:T(128)S(1)}, s32[8]{0:T(128)}, u32[]{:S(2)}) copy-start(s32[8]{0:T(128)} %constant.121.clone) | copy-start | bytes 100
  61.8 95.2 %collective-permute-start.2 = (bf16[512,2048]{1,0:T(8,128)(2,1)}, bf16[512,2048]{1,0:T(8,128)(2,1)}, u32[]{:S(2)}, u32[]{:S(2)}) collective-permute-start(bf16[512,2048]{1,0:T(8,128)(2,1)} %collective-permute-done), channel_id=1, source_target_pairs={{0,8},{8,16},{16,24},{24,28},{28,20},{20,12},{12,4},{4,0},{1,9},{9... | collective-permute-start | bytes 6291464 | tf_op jit(solution)/shard_map/ppermute | solution.py:61
  64.0 94.8 %collective-permute-start.3 = (bf16[512,2048]{1,0:T(8,128)(2,1)}, bf16[512,2048]{1,0:T(8,128)(2,1)}, u32[]{:S(2)}, u32[]{:S(2)}) collective-permute-start(bf16[512,2048]{1,0:T(8,128)(2,1)} %collective-permute-done.1), channel_id=1, source_target_pairs={{0,4},{8,0},{16,8},{24,16},{28,24},{20,28},{12,20},{4,12},{1,5},{9... | collective-permute-start | bytes 6291464 | tf_op jit(solution)/shard_map/ppermute | solution.py:62
  84.3 66.5 %collective-permute-start.10 = (bf16[512,1024]{1,0:T(8,128)(2,1)}, bf16[512,1024]{1,0:T(8,128)(2,1)S(1)}, u32[]{:S(2)}, u32[]{:S(2)}) collective-permute-start(bf16[512,1024]{1,0:T(8,128)(2,1)} %collective-permute-done.8), channel_id=1, source_target_pairs={{0,8},{8,16},{16,24},{24,28},{28,20},{20,12},{12,4},{4,0},{1,9},{9... | collective-permute-start | bytes 3145736 | tf_op jit(solution)/shard_map/ppermute | solution.py:61
  86.4 66.1 %collective-permute-start.11 = (bf16[512,1024]{1,0:T(8,128)(2,1)}, bf16[512,1024]{1,0:T(8,128)(2,1)S(1)}, u32[]{:S(2)}, u32[]{:S(2)}) collective-permute-start(bf16[512,1024]{1,0:T(8,128)(2,1)} %collective-permute-done.9), channel_id=1, source_target_pairs={{0,4},{8,0},{16,8},{24,16},{28,24},{20,28},{12,20},{4,12},{1,5},{9... | collective-permute-start | bytes 3145736 | tf_op jit(solution)/shard_map/ppermute | solution.py:62
  150.8 26.1 %collective-permute-start.12 = (bf16[512,1024]{1,0:T(8,128)(2,1)S(1)}, bf16[512,1024]{1,0:T(8,128)(2,1)S(1)}, u32[]{:S(2)}, u32[]{:S(2)}) collective-permute-start(bf16[512,1024]{1,0:T(8,128)(2,1)S(1)} %collective-permute-done.10), channel_id=1, source_target_pairs={{0,8},{8,16},{16,24},{24,28},{28,20},{20,12},{12,4},{4,0},{1,9},{9... | collective-permute-start | bytes 3145736 | tf_op jit(solution)/shard_map/ppermute | solution.py:61
  152.6 26.9 %collective-permute-start.13 = (bf16[512,1024]{1,0:T(8,128)(2,1)S(1)}, bf16[512,1024]{1,0:T(8,128)(2,1)S(1)}, u32[]{:S(2)}, u32[]{:S(2)}) collective-permute-start(bf16[512,1024]{1,0:T(8,128)(2,1)S(1)} %collective-permute-done.11), channel_id=1, source_target_pairs={{0,4},{8,0},{16,8},{24,16},{28,24},{20,28},{12,20},{4,12},{1,5},{9... | collective-permute-start | bytes 3145736 | tf_op jit(solution)/shard_map/ppermute | solution.py:62
  157.0 64.8 %collective-permute-start.4 = (bf16[512,2048]{1,0:T(8,128)(2,1)}, bf16[512,2048]{1,0:T(8,128)(2,1)S(1)}, u32[]{:S(2)}, u32[]{:S(2)}) collective-permute-start(bf16[512,2048]{1,0:T(8,128)(2,1)} %collective-permute-done.2), channel_id=1, source_target_pairs={{0,8},{8,16},{16,24},{24,28},{28,20},{20,12},{12,4},{4,0},{1,9},{9... | collective-permute-start | bytes 6291464 | tf_op jit(solution)/shard_map/ppermute | solution.py:61
  158.8 64.9 %collective-permute-start.5 = (bf16[512,2048]{1,0:T(8,128)(2,1)}, bf16[512,2048]{1,0:T(8,128)(2,1)S(1)}, u32[]{:S(2)}, u32[]{:S(2)}) collective-permute-start(bf16[512,2048]{1,0:T(8,128)(2,1)} %collective-permute-done.3), channel_id=1, source_target_pairs={{0,4},{8,0},{16,8},{24,16},{28,24},{20,28},{12,20},{4,12},{1,5},{9... | collective-permute-start | bytes 6291464 | tf_op jit(solution)/shard_map/ppermute | solution.py:62
  177.7 96.8 %collective-permute-start.14 = (bf16[256,1024]{1,0:T(8,128)(2,1)}, bf16[256,1024]{1,0:T(8,128)(2,1)}, u32[]{:S(2)}, u32[]{:S(2)}) collective-permute-start(bf16[256,1024]{1,0:T(8,128)(2,1)} %slice.31), channel_id=1, source_target_pairs={{0,8},{8,16},{16,24},{24,28},{28,20},{20,12},{12,4},{4,0},{1,9},{9... | collective-permute-start | bytes 1572872 | tf_op jit(solution)/shard_map/ppermute | solution.py:67
  180.3 96.0 %collective-permute-start.15 = (bf16[256,1024]{1,0:T(8,128)(2,1)}, bf16[256,1024]{1,0:T(8,128)(2,1)}, u32[]{:S(2)}, u32[]{:S(2)}) collective-permute-start(bf16[256,1024]{1,0:T(8,128)(2,1)} %slice.32), channel_id=1, source_target_pairs={{0,4},{8,0},{16,8},{24,16},{28,24},{20,28},{12,20},{4,12},{1,5},{9... | collective-permute-start | bytes 1572872 | tf_op jit(solution)/shard_map/ppermute | solution.py:68
  221.9 31.9 %collective-permute-start.6 = (bf16[256,2048]{1,0:T(8,128)(2,1)S(1)}, bf16[256,2048]{1,0:T(8,128)(2,1)S(1)}, u32[]{:S(2)}, u32[]{:S(2)}) collective-permute-start(bf16[256,2048]{1,0:T(8,128)(2,1)S(1)} %slice.28), channel_id=1, source_target_pairs={{0,8},{8,16},{16,24},{24,28},{28,20},{20,12},{12,4},{4,0},{1,9},{9... | collective-permute-start | bytes 3145736 | tf_op jit(solution)/shard_map/ppermute | solution.py:67
  223.8 31.1 %collective-permute-start.7 = (bf16[256,2048]{1,0:T(8,128)(2,1)S(1)}, bf16[256,2048]{1,0:T(8,128)(2,1)S(1)}, u32[]{:S(2)}, u32[]{:S(2)}) collective-permute-start(bf16[256,2048]{1,0:T(8,128)(2,1)S(1)} %slice.29), channel_id=1, source_target_pairs={{0,4},{8,0},{16,8},{24,16},{28,24},{20,28},{12,20},{4,12},{1,5},{9... | collective-permute-start | bytes 3145736 | tf_op jit(solution)/shard_map/ppermute | solution.py:68
  267.9 29.8 %all-to-all-start = ((bf16[8,2,16,2048]{3,2,1,0:T(8,128)(2,1)}), bf16[8,2,16,2048]{3,2,1,0:T(8,128)(2,1)S(1)}, u32[]{:S(2)}, u32[]{:S(2)}) async-start(bf16[8,2,16,2048]{3,2,1,0:T(8,128)(2,1)} %bitcast.27), calls=%async_computation | async-start | bytes 2097152 | tf_op jit(solution)/shard_map/all_to_all | solution.py:76
  326.2 1.4 copy-start.2
  328.7 11.9 %copy-start.1 = (bf16[1024,1024]{1,0:T(8,128)(2,1)S(1)}, bf16[1024,1024]{1,0:T(8,128)(2,1)}, u32[]{:S(2)}) copy-start(bf16[1024,1024]{1,0:T(8,128)(2,1)} %param.11) | copy-start | bytes 6291460
Sparse Core Ops, SparseCore 0:
  9.7 25.2 all-gather.2
  36.5 34.4 all-gather.4

commit v4 on v3

--- a/solution.py
+++ b/solution.py
@@ -76,22 +76,24 @@
     incoming = lax.all_to_all(packed, "crop", split_axis=0, concat_axis=0, tiled=True)
     q_weight = ring_gather(query_weight)
     query = jnp.dot(queries_in, q_weight, preferred_element_type=jnp.float32).astype(jnp.bfloat16)
-    slotted = incoming.reshape(ncrop * CAP, CT, 2 * width)
-    listed = slotted[region_slots].reshape(rows_here, NB * CT, 2 * width)
-    keys_row = listed[:, :, :width].reshape(rows_here, NB * CT, heads_here, HD)
-    vals_row = listed[:, :, width:].reshape(rows_here, NB * CT, heads_here, HD)
+    nslots = ncrop * CAP
+    keys_all = incoming[..., :width].reshape(nslots * CT, heads_here, HD)
+    vals_all = incoming[..., width:].reshape(nslots * CT, heads_here, HD)
     query_row = query.reshape(rows_here, GR, heads_here, HD)
+    in_use = (jnp.arange(NB, dtype=jnp.int32)[None, :] < region_len[:, None])[:, :, None]
+    hits = region_slots[:, :, None] == jnp.arange(nslots, dtype=jnp.int32)[None, None, :]
+    member = jnp.any(hits & in_use, axis=1)
+    member = jnp.repeat(member, CT, axis=1)
     scale = 1.0 / HD**0.5
     scores = (
-        jnp.einsum("rghe,rkhe->rhgk", query_row, keys_row, preferred_element_type=jnp.float32)
+        jnp.einsum("rghe,khe->rhgk", query_row, keys_all, preferred_element_type=jnp.float32)
         * scale
     )
-    used = (jnp.arange(NB * CT, dtype=jnp.int32) // CT)[None, :] < region_len[:, None]
-    scores = jnp.where(used[:, None, None, :], scores, jnp.float32(-1e30))
+    scores = jnp.where(member[:, None, None, :], scores, jnp.float32(-1e30))
     top = jnp.max(scores, axis=-1, keepdims=True)
     expo = jnp.exp(scores - top)
     weights = (expo / jnp.sum(expo, axis=-1, keepdims=True)).astype(jnp.bfloat16)
-    result = jnp.einsum("rhgk,rkhe->rghe", weights, vals_row, preferred_element_type=jnp.float32)
+    result = jnp.einsum("rhgk,khe->rghe", weights, vals_all, preferred_element_type=jnp.float32)
     return result.astype(jnp.bfloat16).reshape(rows_here * GR, width)
 
 

time: 349 us -> 313 us (0.90)
  local copies, waits for them, and re-layouts: 80.6 us -> 45.4 us
  matrix products: 34.6 us -> 22.7 us
  waiting for transfers between devices: 175 us -> 185 us
    slice x3 -> x1, local copies, waits for them, and re-layouts: 18.9 us -> 0.09 us  [body(): vals_all = incoming[..., width:].reshape(nslots * CT, heads_here, HD)]
    dot_general x2 -> x1, matrix products: 13.6 us -> 1.01 us  [body(): jnp.einsum('rhgk,khe->rghe', weights, vals_all, preferred_element_type=jn...]
    ppermute x6, waiting for transfers between devices: 139 us -> 148 us  [ring_gather(): fwd = lax.ppermute(fwd, 'crop', fwd_perm)]
    gather x1 -> x0, local copies, waits for them, and re-layouts: 6.27 us -> none  [body(): listed = slotted[region_slots].reshape(rows_here, NB * CT, 2 * width)]
    dynamic_update_slice x6, local copies, waits for them, and re-layouts: 12.3 us -> 7.87 us  [ring_gather(): lax.dynamic_update_slice(buf, fwd[None], (ring_arr[(pos - k) % ncrop], 0,...]
  transfers between devices with their start and end apart: 19 -> 19, of which waited for: 7 -> 8; matrix products, arithmetic and copies ran while one was open for 21% -> 20% of each run, Pallas kernels for 0% -> 0%
where the time goes in v4:
time: 313 us; the launch traced here: 312 us
  waiting for transfers between devices  185 us (59%)
  local copies, waits for them, and re-layouts  45.4 us (15%)
  between operations  30.9 us (10%)
  starting transfers between devices  23.3 us (7%)
  matrix products  22.7 us (7%)
  other arithmetic  5.15 us (2%)
    ppermute x6, waiting for transfers between devices, ring_gather(): fwd = lax.ppermute(fwd, 'crop', fwd_perm)  148 us
    ppermute x2, waiting for transfers between devices, ring_gather(): top = lax.ppermute(fwd[:split], 'crop', fwd_perm)  26.6 us
    ppermute x6, starting transfers between devices, ring_gather(): fwd = lax.ppermute(fwd, 'crop', fwd_perm)  13 us
    dot_general x1, matrix products, body(): jnp.dot(tokens_in, kv_weight, preferred_element_type=jnp.float32)  11.9 us
    dynamic_update_slice x6, local copies, waits for them, and re-layouts, ring_gather(): lax.dynamic_update_slice(buf, bwd[None], (ring_arr[(pos + k) % ncrop], 0,...  9.29 us
    all_to_all x1, waiting for transfers between devices, body(): lax.all_to_all(packed, 'crop', split_axis=0, concat_axis=0, tiled=True)  9.24 us
    dot_general x1, matrix products, body(): jnp.dot(queries_in, q_weight, preferred_element_type=jnp.float32)  9.11 us
    dynamic_update_slice x6, local copies, waits for them, and re-layouts, ring_gather(): lax.dynamic_update_slice(buf, fwd[None], (ring_arr[(pos - k) % ncrop], 0,...  7.87 us
  transfers between devices with their start and end apart: 19, of which 8 were waited for; matrix products, arithmetic and copies ran while one was open for 20% of the time, Pallas kernels for 0%

profile of v4, /device:TPU:0, one launch (start us, length us, event | category | flops | bytes accessed | tf_op | source)
XLA Modules:
  0.0 312.0 jit_solution(4413806784989268191)
XLA Ops:
  8.1 1.4 gather_fusion
  12.2 3.1 collective-permute-start
  15.3 2.0 collective-permute-start.8
  22.7 1.6 fusion.17
  39.3 22.5 %collective-permute-done = bf16[512,2048]{1,0:T(8,128)(2,1)} collective-permute-done((bf16[512,2048]{1,0:T(8,128)(2,1)S(1)}, bf16[512,2048]{1,0:T(8,128)(2,1)}, u32[]{:S(2)}, u32[]{:S(2)}) %collective-permute-start) | collective-permute-done | bytes 2097184 | tf_op jit(solution)/shard_map/ppermute | solution.py:61
  61.8 2.1 collective-permute-start.2
  65.2 19.1 %collective-permute-done.8 = bf16[512,1024]{1,0:T(8,128)(2,1)} collective-permute-done((bf16[512,1024]{1,0:T(8,128)(2,1)}, bf16[512,1024]{1,0:T(8,128)(2,1)}, u32[]{:S(2)}, u32[]{:S(2)}) %collective-permute-start.8) | collective-permute-done | bytes 1048608 | tf_op jit(solution)/shard_map/ppermute | solution.py:61
  84.3 2.1 collective-permute-start.10
  86.4 6.0 %broadcast_in_dim.85 = bf16[8,512,2048]{2,1,0:T(8,128)(2,1)} broadcast(bf16[]{:T(256)} %constant.84.clone.1), dimensions={} | broadcast | bytes 16777218 | tf_op jit(solution)/shard_map/broadcast_in_dim | solution.py:55
  92.4 1.6 bitcast_dynamic-update-slice_fusion.6
  95.3 1.3 bitcast_dynamic-update-slice_fusion.11
  96.7 54.1 %collective-permute-done.10 = bf16[512,1024]{1,0:T(8,128)(2,1)S(1)} collective-permute-done((bf16[512,1024]{1,0:T(8,128)(2,1)}, bf16[512,1024]{1,0:T(8,128)(2,1)S(1)}, u32[]{:S(2)}, u32[]{:S(2)}) %collective-permute-start.10) | collective-permute-done | bytes 1048608 | tf_op jit(solution)/shard_map/ppermute | solution.py:61
  150.8 1.8 collective-permute-start.12
  152.8 3.1 %bitcast_dynamic-update-slice_fusion.5 = bf16[8,512,2048]{2,1,0:T(8,128)(2,1)} fusion(bf16[8,512,2048]{2,1,0:T(8,128)(2,1)} %bitcast_dynamic-update-slice_fusion.6, s32[]{:T(128)S(6)} %select_n.126, bf16[512,2048]{1,0:T(8,128)(2,1)} %collective-permute-done), kind=kLoop, calls=%fused_computation.12 | loop fusion | bytes 4194308 | tf_op jit(solution)/shard_map/dynamic_update_slice | solution.py:63
  156.1 1.9 collective-permute-start.4
  158.3 3.2 %bitcast_dynamic-update-slice_fusion.4 = bf16[8,512,2048]{2,1,0:T(8,128)(2,1)} fusion(bf16[8,512,2048]{2,1,0:T(8,128)(2,1)} %bitcast_dynamic-update-slice_fusion.5, s32[]{:T(128)S(6)} %select_n.129, bf16[512,2048]{1,0:T(8,128)(2,1)} %collective-permute-done.1), kind=kLoop, calls=%fused_computation.11 | loop fusion | bytes 4194308 | tf_op jit(solution)/shard_map/dynamic_update_slice | solution.py:64
  161.4 15.4 %collective-permute-done.12 = bf16[512,1024]{1,0:T(8,128)(2,1)S(1)} collective-permute-done((bf16[512,1024]{1,0:T(8,128)(2,1)S(1)}, bf16[512,1024]{1,0:T(8,128)(2,1)S(1)}, u32[]{:S(2)}, u32[]{:S(2)}) %collective-permute-start.12) | collective-permute-done | bytes 1048608 | tf_op jit(solution)/shard_map/ppermute | solution.py:61
  177.7 1.8 collective-permute-start.14
  180.7 1.6 bitcast_dynamic-update-slice_fusion.3
  182.3 2.2 bitcast_dynamic-update-slice_fusion.2
  184.5 37.3 %collective-permute-done.4 = bf16[512,2048]{1,0:T(8,128)(2,1)S(1)} collective-permute-done((bf16[512,2048]{1,0:T(8,128)(2,1)S(1)}, bf16[512,2048]{1,0:T(8,128)(2,1)S(1)}, u32[]{:S(2)}, u32[]{:S(2)}) %collective-permute-start.4) | collective-permute-done | bytes 2097184 | tf_op jit(solution)/shard_map/ppermute | solution.py:61
  221.9 1.8 collective-permute-start.6
  224.1 1.6 bitcast_dynamic-update-slice_fusion.1
  225.7 1.5 bitcast_dynamic-update-slice_fusion
  227.2 26.6 %collective-permute-done.6 = bf16[256,2048]{1,0:T(8,128)(2,1)S(1)} collective-permute-done((bf16[256,2048]{1,0:T(8,128)(2,1)S(1)}, bf16[256,2048]{1,0:T(8,128)(2,1)S(1)}, u32[]{:S(2)}, u32[]{:S(2)}) %collective-permute-start.6) | collective-permute-done | bytes 1048608 | tf_op jit(solution)/shard_map/ppermute | solution.py:67
  256.0 11.9 %convolution_convert_fusion = bf16[256,2048]{1,0:T(8,128)(2,1)} fusion(bf16[256,4096]{1,0:T(8,128)(2,1)} %all-gather.3.cloned.1.call-done, bf16[4096,2048]{1,0:T(8,128)(2,1)} %bitcast.26), kind=kOutput, calls=%fused_computation.6 | convolution fusion | flops 4295491584 | bytes 19922944 | tf_op jit(solution)/shard_map/dot_general | solution.py:74
  267.9 5.6 %all-to-all-start = ((bf16[8,2,16,2048]{3,2,1,0:T(8,128)(2,1)}), bf16[8,2,16,2048]{3,2,1,0:T(8,128)(2,1)S(1)}, u32[]{:S(2)}, u32[]{:S(2)}) async-start(bf16[8,2,16,2048]{3,2,1,0:T(8,128)(2,1)} %bitcast.27), calls=%async_computation | async-start | bytes 2097152 | tf_op jit(solution)/shard_map/all_to_all | solution.py:76
  274.5 1.9 bitcast_dynamic-update-slice_fusion.17
  276.4 1.9 bitcast_dynamic-update-slice_fusion.16
  278.3 9.1 %fusion.8 = bf16[512,1024]{0,1:T(8,128)(2,1)S(1)} fusion(bf16[4096,1024]{1,0:T(8,128)(2,1)} %bitcast.102, bf16[512,4096]{1,0:T(8,128)(2,1)} %all-gather.5.cloned.1.call-done), kind=kOutput, calls=%fused_computation.21 | convolution fusion | flops 4295491584 | bytes 13631488 | tf_op jit(solution)/shard_map/dot_general | solution.py:78
  288.4 9.2 %all-to-all-done = bf16[8,2,16,2048]{3,2,1,0:T(8,128)(2,1)S(1)} async-done(((bf16[8,2,16,2048]{3,2,1,0:T(8,128)(2,1)}), bf16[8,2,16,2048]{3,2,1,0:T(8,128)(2,1)S(1)}, u32[]{:S(2)}, u32[]{:S(2)}) %all-to-all-start) | async-done | bytes 1048608 | tf_op jit(solution)/shard_map/all_to_all | solution.py:76
  298.7 3.5 %fusion.18 = (f32[16,8,32]{2,0,1:T(8,128)S(1)}, f32[16,8,32,256]{3,2,0,1:T(8,128)S(1)}) fusion(f32[8,256,16,32]{1,3,2,0:T(8,128)S(1)} %bitcast.103, pred[16,256]{1,0:T(8,128)(4,1)S(1)} %broadcast_in_dim.96), kind=kOutput, calls=%fused_computation.49 | output fusion | flops 6291711 | bytes 8409088 | tf_op jit(solution)/shard_map/sub | solution.py:94
  (67 shorter events, 21.3 us)
Async XLA Ops:
  6.5 1.6 copy-start
  6.5 58.5 %copy-start.3 = (bf16[512,1024]{1,0:T(8,128)(2,1)S(1)}, bf16[512,1024]{1,0:T(8,128)(2,1)}, u32[]{:S(2)}) copy-start(bf16[512,1024]{1,0:T(8,128)(2,1)} %param.12) | copy-start | bytes 3145732
  6.5 249.5 %all-gather.3.cloned.1.call-start = ((), (), s32[]{:S(2)}) async-start(), calls=%async_computation.1 | async-start | bytes 2621440 | tf_op jit(solution)/shard_map/all_gather | solution.py:48
  9.5 268.8 %all-gather.5.cloned.1.call-start = ((), (), s32[]{:S(2)}) async-start(), calls=%async_computation.2 | async-start | bytes 5242880 | tf_op jit(solution)/shard_map/all_gather | solution.py:44
  12.2 49.6 %collective-permute-start = (bf16[512,2048]{1,0:T(8,128)(2,1)S(1)}, bf16[512,2048]{1,0:T(8,128)(2,1)}, u32[]{:S(2)}, u32[]{:S(2)}) collective-permute-start(bf16[512,2048]{1,0:T(8,128)(2,1)S(1)} %constant_dynamic-update-slice_fusion), channel_id=1, source_target_pairs={{0,8},{8,16},{16,24},{24,28},{28,20},{20,12},{12,4},{4,0},{1,9},{9... | collective-permute-start | bytes 6291464 | tf_op jit(solution)/shard_map/ppermute | solution.py:61
  15.3 48.7 %collective-permute-start.1 = (bf16[512,2048]{1,0:T(8,128)(2,1)S(1)}, bf16[512,2048]{1,0:T(8,128)(2,1)}, u32[]{:S(2)}, u32[]{:S(2)}) collective-permute-start(bf16[512,2048]{1,0:T(8,128)(2,1)S(1)} %constant_dynamic-update-slice_fusion), channel_id=1, source_target_pairs={{0,4},{8,0},{16,8},{24,16},{28,24},{20,28},{12,20},{4,12},{1,5},{9... | collective-permute-start | bytes 6291464 | tf_op jit(solution)/shard_map/ppermute | solution.py:62
  15.3 69.0 %collective-permute-start.8 = (bf16[512,1024]{1,0:T(8,128)(2,1)}, bf16[512,1024]{1,0:T(8,128)(2,1)}, u32[]{:S(2)}, u32[]{:S(2)}) collective-permute-start(bf16[512,1024]{1,0:T(8,128)(2,1)} %param.12), channel_id=1, source_target_pairs={{0,8},{8,16},{16,24},{24,28},{28,20},{20,12},{12,4},{4,0},{1,9},{9... | collective-permute-start | bytes 3145736 | tf_op jit(solution)/shard_map/ppermute | solution.py:61
  17.3 69.1 %collective-permute-start.9 = (bf16[512,1024]{1,0:T(8,128)(2,1)}, bf16[512,1024]{1,0:T(8,128)(2,1)}, u32[]{:S(2)}, u32[]{:S(2)}) collective-permute-start(bf16[512,1024]{1,0:T(8,128)(2,1)} %param.12), channel_id=1, source_target_pairs={{0,4},{8,0},{16,8},{24,16},{28,24},{20,28},{12,20},{4,12},{1,5},{9... | collective-permute-start | bytes 3145736 | tf_op jit(solution)/shard_map/ppermute | solution.py:62
  61.8 94.2 %collective-permute-start.2 = (bf16[512,2048]{1,0:T(8,128)(2,1)}, bf16[512,2048]{1,0:T(8,128)(2,1)S(1)}, u32[]{:S(2)}, u32[]{:S(2)}) collective-permute-start(bf16[512,2048]{1,0:T(8,128)(2,1)} %collective-permute-done), channel_id=1, source_target_pairs={{0,8},{8,16},{16,24},{24,28},{28,20},{20,12},{12,4},{4,0},{1,9},{9... | collective-permute-start | bytes 6291464 | tf_op jit(solution)/shard_map/ppermute | solution.py:61
  64.0 94.0 %collective-permute-start.3 = (bf16[512,2048]{1,0:T(8,128)(2,1)}, bf16[512,2048]{1,0:T(8,128)(2,1)S(1)}, u32[]{:S(2)}, u32[]{:S(2)}) collective-permute-start(bf16[512,2048]{1,0:T(8,128)(2,1)} %collective-permute-done.1), channel_id=1, source_target_pairs={{0,4},{8,0},{16,8},{24,16},{28,24},{20,28},{12,20},{4,12},{1,5},{9... | collective-permute-start | bytes 6291464 | tf_op jit(solution)/shard_map/ppermute | solution.py:62
  84.3 66.5 %collective-permute-start.10 = (bf16[512,1024]{1,0:T(8,128)(2,1)}, bf16[512,1024]{1,0:T(8,128)(2,1)S(1)}, u32[]{:S(2)}, u32[]{:S(2)}) collective-permute-start(bf16[512,1024]{1,0:T(8,128)(2,1)} %collective-permute-done.8), channel_id=1, source_target_pairs={{0,8},{8,16},{16,24},{24,28},{28,20},{20,12},{12,4},{4,0},{1,9},{9... | collective-permute-start | bytes 3145736 | tf_op jit(solution)/shard_map/ppermute | solution.py:61
  86.4 66.1 %collective-permute-start.11 = (bf16[512,1024]{1,0:T(8,128)(2,1)}, bf16[512,1024]{1,0:T(8,128)(2,1)S(1)}, u32[]{:S(2)}, u32[]{:S(2)}) collective-permute-start(bf16[512,1024]{1,0:T(8,128)(2,1)} %collective-permute-done.9), channel_id=1, source_target_pairs={{0,4},{8,0},{16,8},{24,16},{28,24},{20,28},{12,20},{4,12},{1,5},{9... | collective-permute-start | bytes 3145736 | tf_op jit(solution)/shard_map/ppermute | solution.py:62
  150.8 26.1 %collective-permute-start.12 = (bf16[512,1024]{1,0:T(8,128)(2,1)S(1)}, bf16[512,1024]{1,0:T(8,128)(2,1)S(1)}, u32[]{:S(2)}, u32[]{:S(2)}) collective-permute-start(bf16[512,1024]{1,0:T(8,128)(2,1)S(1)} %collective-permute-done.10), channel_id=1, source_target_pairs={{0,8},{8,16},{16,24},{24,28},{28,20},{20,12},{12,4},{4,0},{1,9},{9... | collective-permute-start | bytes 3145736 | tf_op jit(solution)/shard_map/ppermute | solution.py:61
  152.6 26.9 %collective-permute-start.13 = (bf16[512,1024]{1,0:T(8,128)(2,1)S(1)}, bf16[512,1024]{1,0:T(8,128)(2,1)S(1)}, u32[]{:S(2)}, u32[]{:S(2)}) collective-permute-start(bf16[512,1024]{1,0:T(8,128)(2,1)S(1)} %collective-permute-done.11), channel_id=1, source_target_pairs={{0,4},{8,0},{16,8},{24,16},{28,24},{20,28},{12,20},{4,12},{1,5},{9... | collective-permute-start | bytes 3145736 | tf_op jit(solution)/shard_map/ppermute | solution.py:62
  156.1 65.7 %collective-permute-start.4 = (bf16[512,2048]{1,0:T(8,128)(2,1)S(1)}, bf16[512,2048]{1,0:T(8,128)(2,1)S(1)}, u32[]{:S(2)}, u32[]{:S(2)}) collective-permute-start(bf16[512,2048]{1,0:T(8,128)(2,1)S(1)} %collective-permute-done.2), channel_id=1, source_target_pairs={{0,8},{8,16},{16,24},{24,28},{28,20},{20,12},{12,4},{4,0},{1,9},{9... | collective-permute-start | bytes 6291464 | tf_op jit(solution)/shard_map/ppermute | solution.py:61
  157.9 65.8 %collective-permute-start.5 = (bf16[512,2048]{1,0:T(8,128)(2,1)S(1)}, bf16[512,2048]{1,0:T(8,128)(2,1)S(1)}, u32[]{:S(2)}, u32[]{:S(2)}) collective-permute-start(bf16[512,2048]{1,0:T(8,128)(2,1)S(1)} %collective-permute-done.3), channel_id=1, source_target_pairs={{0,4},{8,0},{16,8},{24,16},{28,24},{20,28},{12,20},{4,12},{1,5},{9... | collective-permute-start | bytes 6291464 | tf_op jit(solution)/shard_map/ppermute | solution.py:62
  177.7 96.8 %collective-permute-start.14 = (bf16[256,1024]{1,0:T(8,128)(2,1)}, bf16[256,1024]{1,0:T(8,128)(2,1)}, u32[]{:S(2)}, u32[]{:S(2)}) collective-permute-start(bf16[256,1024]{1,0:T(8,128)(2,1)} %slice.30), channel_id=1, source_target_pairs={{0,8},{8,16},{16,24},{24,28},{28,20},{20,12},{12,4},{4,0},{1,9},{9... | collective-permute-start | bytes 1572872 | tf_op jit(solution)/shard_map/ppermute | solution.py:67
  180.4 96.0 %collective-permute-start.15 = (bf16[256,1024]{1,0:T(8,128)(2,1)}, bf16[256,1024]{1,0:T(8,128)(2,1)}, u32[]{:S(2)}, u32[]{:S(2)}) collective-permute-start(bf16[256,1024]{1,0:T(8,128)(2,1)} %slice.31), channel_id=1, source_target_pairs={{0,4},{8,0},{16,8},{24,16},{28,24},{20,28},{12,20},{4,12},{1,5},{9... | collective-permute-start | bytes 1572872 | tf_op jit(solution)/shard_map/ppermute | solution.py:68
  180.7 45.0 %copy-start.2 = (bf16[8,512,1024]{2,1,0:T(8,128)(2,1)}, bf16[8,512,1024]{2,1,0:T(8,128)(2,1)S(1)}, u32[]{:S(2)}) copy-start(bf16[8,512,1024]{2,1,0:T(8,128)(2,1)S(1)} %bitcast_dynamic-update-slice_fusion.8) | copy-start | bytes 25165828
  221.9 31.9 %collective-permute-start.6 = (bf16[256,2048]{1,0:T(8,128)(2,1)S(1)}, bf16[256,2048]{1,0:T(8,128)(2,1)S(1)}, u32[]{:S(2)}, u32[]{:S(2)}) collective-permute-start(bf16[256,2048]{1,0:T(8,128)(2,1)S(1)} %slice.26), channel_id=1, source_target_pairs={{0,8},{8,16},{16,24},{24,28},{28,20},{20,12},{12,4},{4,0},{1,9},{9... | collective-permute-start | bytes 3145736 | tf_op jit(solution)/shard_map/ppermute | solution.py:67
  223.8 31.1 %collective-permute-start.7 = (bf16[256,2048]{1,0:T(8,128)(2,1)S(1)}, bf16[256,2048]{1,0:T(8,128)(2,1)S(1)}, u32[]{:S(2)}, u32[]{:S(2)}) collective-permute-start(bf16[256,2048]{1,0:T(8,128)(2,1)S(1)} %slice.27), channel_id=1, source_target_pairs={{0,4},{8,0},{16,8},{24,16},{28,24},{20,28},{12,20},{4,12},{1,5},{9... | collective-permute-start | bytes 3145736 | tf_op jit(solution)/shard_map/ppermute | solution.py:68
  267.9 29.8 %all-to-all-start = ((bf16[8,2,16,2048]{3,2,1,0:T(8,128)(2,1)}), bf16[8,2,16,2048]{3,2,1,0:T(8,128)(2,1)S(1)}, u32[]{:S(2)}, u32[]{:S(2)}) async-start(bf16[8,2,16,2048]{3,2,1,0:T(8,128)(2,1)} %bitcast.27), calls=%async_computation | async-start | bytes 2097152 | tf_op jit(solution)/shard_map/all_to_all | solution.py:76
  302.1 3.0 copy-start.1
Sparse Core Ops, SparseCore 0:
  9.7 25.3 all-gather.2
  36.6 34.4 all-gather.4

commit v5 on v4

--- a/solution.py
+++ b/solution.py
@@ -74,8 +74,25 @@
     kv = jnp.dot(tokens_in, kv_weight, preferred_element_type=jnp.float32).astype(jnp.bfloat16)
     packed = kv.reshape(ncrop, CAP, CT, 2 * width)
     incoming = lax.all_to_all(packed, "crop", split_axis=0, concat_axis=0, tiled=True)
-    q_weight = ring_gather(query_weight)
-    query = jnp.dot(queries_in, q_weight, preferred_element_type=jnp.float32).astype(jnp.bfloat16)
+    q_piece, kv_weight = lax.optimization_barrier((query_weight, kv_weight))
+
+    def q_part(acc, piece, src, lo, n):
+        cols = lax.dynamic_slice_in_dim(queries_in, src * wrows + lo, n, 1)
+        return acc + jnp.dot(cols, piece, preferred_element_type=jnp.float32)
+
+    acc = q_part(jnp.zeros((queries_in.shape[0], width), jnp.float32), q_piece, me, 0, wrows)
+    fwd = q_piece
+    bwd = q_piece
+    for k in range(1, steps_bwd + 1):
+        fwd = lax.ppermute(fwd, "crop", fwd_perm)
+        bwd = lax.ppermute(bwd, "crop", bwd_perm)
+        acc = q_part(acc, fwd, ring_arr[(pos - k) % ncrop], 0, wrows)
+        acc = q_part(acc, bwd, ring_arr[(pos + k) % ncrop], 0, wrows)
+    if steps_fwd > steps_bwd:
+        src = ring_arr[(pos - steps_fwd) % ncrop]
+        acc = q_part(acc, lax.ppermute(fwd[:split], "crop", fwd_perm), src, 0, split)
+        acc = q_part(acc, lax.ppermute(bwd[split:], "crop", bwd_perm), src, split, wrows - split)
+    query = acc.astype(jnp.bfloat16)
     nslots = ncrop * CAP
     keys_all = incoming[..., :width].reshape(nslots * CT, heads_here, HD)
     vals_all = incoming[..., width:].reshape(nslots * CT, heads_here, HD)

time: 313 us -> 301 us (0.962)
  waiting for transfers between devices: 185 us -> 156 us
  matrix products: 22.7 us -> 32 us
  starting transfers between devices: 23.3 us -> 32.2 us
  between operations: 30.9 us -> 36.3 us
  local copies, waits for them, and re-layouts: 45.4 us -> 40.1 us
    ppermute x6 -> x3, waiting for transfers between devices: 148 us -> 93.7 us  [ring_gather(): fwd = lax.ppermute(fwd, 'crop', fwd_perm)]
    ppermute x0 -> x8, waiting for transfers between devices: none -> 44.9 us  [the longest x3 37.8 us: body(): fwd = lax.ppermute(fwd, 'crop', fwd_perm)]
    ppermute x0 -> x8, starting transfers between devices: none -> 17.7 us  [the longest x3 10.9 us: body(): fwd = lax.ppermute(fwd, 'crop', fwd_perm)]
    dot_general x1 -> x9, matrix products: 9.11 us -> 18.4 us  [q_part(): return acc + jnp.dot(cols, piece, preferred_element_type=jnp.float32)]
    all_to_all x1, waiting for transfers between devices: 9.24 us -> 0.01 us  [body(): lax.all_to_all(packed, 'crop', split_axis=0, concat_axis=0, tiled=True)]
    ppermute x2 -> x1, waiting for transfers between devices: 26.6 us -> 17.4 us  [ring_gather(): top = lax.ppermute(fwd[:split], 'crop', fwd_perm)]
    ppermute x6 -> x3, starting transfers between devices: 13 us -> 6.31 us  [ring_gather(): fwd = lax.ppermute(fwd, 'crop', fwd_perm)]
    dynamic_update_slice x6 -> x3, local copies, waits for them, and re-layouts: 9.29 us -> 6.14 us  [ring_gather(): lax.dynamic_update_slice(buf, bwd[None], (ring_arr[(pos + k) % ncrop], 0,...]
  transfers between devices with their start and end apart: 19 -> 19, of which waited for: 8 -> 9; matrix products, arithmetic and copies ran while one was open for 20% -> 19% of each run, Pallas kernels for 0% -> 0%
where the time goes in v5:
time: 301 us; the launch traced here: 300 us
  waiting for transfers between devices  156 us (52%)
  local copies, waits for them, and re-layouts  40.1 us (13%)
  between operations  36.3 us (12%)
  starting transfers between devices  32.2 us (11%)
  matrix products  32 us (11%)
  other arithmetic  3.67 us (1%)
    ppermute x3, waiting for transfers between devices, ring_gather(): fwd = lax.ppermute(fwd, 'crop', fwd_perm)  93.7 us
    ppermute x3, waiting for transfers between devices, body(): fwd = lax.ppermute(fwd, 'crop', fwd_perm)  37.8 us
    dot_general x9, matrix products, q_part(): return acc + jnp.dot(cols, piece, preferred_element_type=jnp.float32)  18.4 us
    ppermute x1, waiting for transfers between devices, ring_gather(): top = lax.ppermute(fwd[:split], 'crop', fwd_perm)  17.4 us
    dot_general x1, matrix products, body(): jnp.dot(tokens_in, kv_weight, preferred_element_type=jnp.float32)  11.9 us
    ppermute x3, starting transfers between devices, body(): fwd = lax.ppermute(fwd, 'crop', fwd_perm)  10.9 us
    dynamic_update_slice x3, local copies, waits for them, and re-layouts, ring_gather(): lax.dynamic_update_slice(buf, fwd[None], (ring_arr[(pos - k) % ncrop], 0,...  7.86 us
    ppermute x3, starting transfers between devices, ring_gather(): fwd = lax.ppermute(fwd, 'crop', fwd_perm)  6.31 us
  transfers between devices with their start and end apart: 19, of which 9 were waited for; matrix products, arithmetic and copies ran while one was open for 19% of the time, Pallas kernels for 0%

profile of v5, /device:TPU:0, one launch (start us, length us, event | category | flops | bytes accessed | tf_op | source)
XLA Modules:
  0.0 300.4 jit_solution(15329586403219766784)
XLA Ops:
  6.6 2.4 constant_dynamic-update-slice_fusion.1
  9.0 2.3 constant_dynamic-update-slice_fusion
  11.3 3.0 %collective-permute-start = (bf16[512,2048]{1,0:T(8,128)(2,1)}, bf16[512,2048]{1,0:T(8,128)(2,1)}, u32[]{:S(2)}, u32[]{:S(2)}) collective-permute-start(bf16[512,2048]{1,0:T(8,128)(2,1)} %constant_dynamic-update-slice_fusion), channel_id=1, source_target_pairs={{0,8},{8,16},{16,24},{24,28},{28,20},{20,12},{12,4},{4,0},{1,9},{9... | collective-permute-start | bytes 6291464 | tf_op jit(solution)/shard_map/ppermute | solution.py:61
  16.0 44.2 %collective-permute-done = bf16[512,2048]{1,0:T(8,128)(2,1)} collective-permute-done((bf16[512,2048]{1,0:T(8,128)(2,1)}, bf16[512,2048]{1,0:T(8,128)(2,1)}, u32[]{:S(2)}, u32[]{:S(2)}) %collective-permute-start) | collective-permute-done | bytes 2097184 | tf_op jit(solution)/shard_map/ppermute | solution.py:61
  60.2 1.8 collective-permute-start.2
  81.6 6.0 %broadcast_in_dim.55 = bf16[8,512,2048]{2,1,0:T(8,128)(2,1)} broadcast(bf16[]{:T(256)} %constant.86.clone.1), dimensions={} | broadcast | bytes 16777218 | tf_op jit(solution)/shard_map/broadcast_in_dim | solution.py:55
  87.7 3.2 %bitcast_dynamic-update-slice_fusion.6 = bf16[8,512,2048]{2,1,0:T(8,128)(2,1)} fusion(bf16[8,512,2048]{2,1,0:T(8,128)(2,1)} %broadcast_in_dim.55, s32[]{:T(128)S(6)} %select_n.141, bf16[512,2048]{1,0:T(8,128)(2,1)} %constant_dynamic-update-slice_fusion), kind=kLoop, calls=%fused_computation.13 | loop fusion | bytes 4194308 | tf_op jit(solution)/shard_map/dynamic_update_slice | solution.py:56
  90.8 16.5 %collective-permute-done.2 = bf16[512,2048]{1,0:T(8,128)(2,1)} collective-permute-done((bf16[512,2048]{1,0:T(8,128)(2,1)}, bf16[512,2048]{1,0:T(8,128)(2,1)}, u32[]{:S(2)}, u32[]{:S(2)}) %collective-permute-start.2) | collective-permute-done | bytes 2097184 | tf_op jit(solution)/shard_map/ppermute | solution.py:61
  109.4 3.1 %bitcast_dynamic-update-slice_fusion.5 = bf16[8,512,2048]{2,1,0:T(8,128)(2,1)} fusion(bf16[8,512,2048]{2,1,0:T(8,128)(2,1)} %bitcast_dynamic-update-slice_fusion.6, s32[]{:T(128)S(6)} %select_n.144, bf16[512,2048]{1,0:T(8,128)(2,1)} %collective-permute-done), kind=kLoop, calls=%fused_computation.12 | loop fusion | bytes 4194308 | tf_op jit(solution)/shard_map/dynamic_update_slice | solution.py:63
  112.5 3.2 %bitcast_dynamic-update-slice_fusion.4 = bf16[8,512,2048]{2,1,0:T(8,128)(2,1)} fusion(bf16[8,512,2048]{2,1,0:T(8,128)(2,1)} %bitcast_dynamic-update-slice_fusion.5, s32[]{:T(128)S(6)} %select_n.147, bf16[512,2048]{1,0:T(8,128)(2,1)} %collective-permute-done.1), kind=kLoop, calls=%fused_computation.11 | loop fusion | bytes 4194308 | tf_op jit(solution)/shard_map/dynamic_update_slice | solution.py:64
  115.7 3.2 %bitcast_dynamic-update-slice_fusion.3 = bf16[8,512,2048]{2,1,0:T(8,128)(2,1)} fusion(bf16[8,512,2048]{2,1,0:T(8,128)(2,1)} %bitcast_dynamic-update-slice_fusion.4, s32[]{:T(128)S(6)} %select_n.150, bf16[512,2048]{1,0:T(8,128)(2,1)} %collective-permute-done.2), kind=kLoop, calls=%fused_computation.10 | loop fusion | bytes 4194308 | tf_op jit(solution)/shard_map/dynamic_update_slice | solution.py:63
  119.0 1.5 bitcast_dynamic-update-slice_fusion.2
  120.5 33.0 %collective-permute-done.4 = bf16[512,2048]{1,0:T(8,128)(2,1)S(1)} collective-permute-done((bf16[512,2048]{1,0:T(8,128)(2,1)}, bf16[512,2048]{1,0:T(8,128)(2,1)S(1)}, u32[]{:S(2)}, u32[]{:S(2)}) %collective-permute-start.4) | collective-permute-done | bytes 2097184 | tf_op jit(solution)/shard_map/ppermute | solution.py:61
  158.7 17.4 %collective-permute-done.6 = bf16[256,2048]{1,0:T(8,128)(2,1)S(1)} collective-permute-done((bf16[256,2048]{1,0:T(8,128)(2,1)S(1)}, bf16[256,2048]{1,0:T(8,128)(2,1)S(1)}, u32[]{:S(2)}, u32[]{:S(2)}) %collective-permute-start.6) | collective-permute-done | bytes 1048608 | tf_op jit(solution)/shard_map/ppermute | solution.py:67
  180.3 11.9 %convolution_convert_fusion = bf16[256,2048]{1,0:T(8,128)(2,1)} fusion(bf16[256,4096]{1,0:T(8,128)(2,1)} %all-gather.3.cloned.1.call-done, bf16[4096,2048]{1,0:T(8,128)(2,1)} %bitcast.26), kind=kOutput, calls=%fused_computation.6 | convolution fusion | flops 4295491584 | bytes 19922944 | tf_op jit(solution)/shard_map/dot_general | solution.py:74
  192.1 5.2 %all-to-all-start = ((bf16[8,2,16,2048]{3,2,1,0:T(8,128)(2,1)}), bf16[8,2,16,2048]{3,2,1,0:T(8,128)(2,1)S(1)}, u32[]{:S(2)}, u32[]{:S(2)}) async-start(bf16[8,2,16,2048]{3,2,1,0:T(8,128)(2,1)} %bitcast.27), calls=%async_computation | async-start | bytes 2097152 | tf_op jit(solution)/shard_map/all_to_all | solution.py:76
  197.3 10.4 %collective-permute-done.8 = bf16[512,1024]{1,0:T(8,128)(2,1)} collective-permute-done((bf16[512,1024]{1,0:T(8,128)(2,1)S(1)}, bf16[512,1024]{1,0:T(8,128)(2,1)}, u32[]{:S(2)}, u32[]{:S(2)}) %collective-permute-start.8) | collective-permute-done | bytes 1048608 | tf_op jit(solution)/shard_map/ppermute | solution.py:87
  207.7 2.0 collective-permute-start.10
  214.8 2.1 fusion.26
  217.0 21.6 %collective-permute-done.10 = bf16[512,1024]{1,0:T(8,128)(2,1)} collective-permute-done((bf16[512,1024]{1,0:T(8,128)(2,1)}, bf16[512,1024]{1,0:T(8,128)(2,1)}, u32[]{:S(2)}, u32[]{:S(2)}) %collective-permute-start.10) | collective-permute-done | bytes 1048608 | tf_op jit(solution)/shard_map/ppermute | solution.py:87
  238.6 7.8 %collective-permute-start.12 = (bf16[512,1024]{1,0:T(8,128)(2,1)}, bf16[512,1024]{1,0:T(8,128)(2,1)}, u32[]{:S(2)}, u32[]{:S(2)}) collective-permute-start(bf16[512,1024]{1,0:T(8,128)(2,1)} %collective-permute-done.10), channel_id=1, source_target_pairs={{0,8},{8,16},{16,24},{24,28},{28,20},{20,12},{12,4},{4,0},{1,9},{9... | collective-permute-start | bytes 3145736 | tf_op jit(solution)/shard_map/ppermute | solution.py:87
  246.4 3.4 %fusion.22 = f32[512,1024]{1,0:T(8,128)} fusion(bf16[512,1024]{1,0:T(8,128)(2,1)} %collective-permute-done.9, bf16[512,4096]{1,0:T(8,128)(2,1)} %all-gather.5.cloned.1.call-done, s32[]{:T(128)S(6)} %select_n.165), kind=kOutput, calls=%fused_computation.36 | convolution fusion | flops 536870912 | bytes 3670020 | tf_op jit(solution)/shard_map/dot_general | solution.py:81
  249.8 3.4 %fusion.24 = f32[512,1024]{1,0:T(8,128)} fusion(bf16[512,1024]{1,0:T(8,128)(2,1)} %collective-permute-done.8, bf16[512,4096]{1,0:T(8,128)(2,1)} %all-gather.5.cloned.1.call-done, s32[]{:T(128)S(6)} %select_n.164), kind=kOutput, calls=%fused_computation.38 | convolution fusion | flops 536870912 | bytes 3670020 | tf_op jit(solution)/shard_map/dot_general | solution.py:81
  253.5 1.9 copy-done.4
  255.4 1.9 fusion.20
  257.4 5.9 %collective-permute-done.12 = bf16[512,1024]{1,0:T(8,128)(2,1)} collective-permute-done((bf16[512,1024]{1,0:T(8,128)(2,1)}, bf16[512,1024]{1,0:T(8,128)(2,1)}, u32[]{:S(2)}, u32[]{:S(2)}) %collective-permute-start.12) | collective-permute-done | bytes 1048608 | tf_op jit(solution)/shard_map/ppermute | solution.py:87
  264.3 5.6 %collective-permute-start.14 = (bf16[256,1024]{1,0:T(8,128)(2,1)S(1)}, bf16[256,1024]{1,0:T(8,128)(2,1)S(1)}, u32[]{:S(2)}, u32[]{:S(2)}) collective-permute-start(bf16[256,1024]{1,0:T(8,128)(2,1)S(1)} %slice.30), channel_id=1, source_target_pairs={{0,8},{8,16},{16,24},{24,28},{28,20},{20,12},{12,4},{4,0},{1,9},{9... | collective-permute-start | bytes 1572872 | tf_op jit(solution)/shard_map/ppermute | solution.py:93
  269.9 1.9 fusion.18
  273.2 2.1 fusion.16
  277.1 5.8 %collective-permute-done.15 = bf16[256,1024]{1,0:T(8,128)(2,1)S(1)} collective-permute-done((bf16[256,1024]{1,0:T(8,128)(2,1)S(1)}, bf16[256,1024]{1,0:T(8,128)(2,1)S(1)}, u32[]{:S(2)}, u32[]{:S(2)}) %collective-permute-start.15) | collective-permute-done | bytes 524320 | tf_op jit(solution)/shard_map/ppermute | solution.py:94
  283.3 2.6 fusion.8
  287.1 3.5 %fusion.47 = (f32[16,8,32]{2,0,1:T(8,128)S(1)}, f32[16,8,32,256]{3,2,0,1:T(8,128)S(1)}) fusion(f32[8,256,16,32]{1,3,2,0:T(8,128)S(1)} %bitcast.89, pred[16,256]{1,0:T(8,128)(4,1)S(1)} %broadcast_in_dim.66), kind=kOutput, calls=%fused_computation.67 | output fusion | flops 6291711 | bytes 8409088 | tf_op jit(solution)/shard_map/sub | solution.py:111
  (78 shorter events, 24.1 us)
Async XLA Ops:
  6.5 8.0 %copy-start = (bf16[1024,1024]{1,0:T(8,128)(2,1)S(1)}, bf16[1024,1024]{1,0:T(8,128)(2,1)}, u32[]{:S(2)}) copy-start(bf16[1024,1024]{1,0:T(8,128)(2,1)} %param.11) | copy-start | bytes 6291460
  6.5 55.7 %copy-start.10 = (s32[8]{0:T(128)S(1)}, s32[8]{0:T(128)}, u32[]{:S(2)}) copy-start(s32[8]{0:T(128)} %constant.107.clone) | copy-start | bytes 100
  6.5 60.9 %copy-start.6 = (s32[8]{0:T(128)S(1)}, s32[8]{0:T(128)}, u32[]{:S(2)}) copy-start(s32[8]{0:T(128)} %constant.108.clone) | copy-start | bytes 100
  6.5 7.8 %copy-start.8 = (s32[1,8,2]{1,2,0:T(2,128)S(1)}, s32[1,8,2]{1,2,0:T(2,128)}, u32[]{:S(2)}) copy-start(s32[1,8,2]{1,2,0:T(2,128)} %param.15) | copy-start | bytes 196
  6.5 173.7 %all-gather.3.cloned.1.call-start = ((), (), s32[]{:S(2)}) async-start(), calls=%async_computation.1 | async-start | bytes 2621440 | tf_op jit(solution)/shard_map/all_gather | solution.py:48
  11.3 48.9 %collective-permute-start = (bf16[512,2048]{1,0:T(8,128)(2,1)}, bf16[512,2048]{1,0:T(8,128)(2,1)}, u32[]{:S(2)}, u32[]{:S(2)}) collective-permute-start(bf16[512,2048]{1,0:T(8,128)(2,1)} %constant_dynamic-update-slice_fusion), channel_id=1, source_target_pairs={{0,8},{8,16},{16,24},{24,28},{28,20},{20,12},{12,4},{4,0},{1,9},{9... | collective-permute-start | bytes 6291464 | tf_op jit(solution)/shard_map/ppermute | solution.py:61
  14.3 47.7 %collective-permute-start.1 = (bf16[512,2048]{1,0:T(8,128)(2,1)}, bf16[512,2048]{1,0:T(8,128)(2,1)}, u32[]{:S(2)}, u32[]{:S(2)}) collective-permute-start(bf16[512,2048]{1,0:T(8,128)(2,1)} %constant_dynamic-update-slice_fusion), channel_id=1, source_target_pairs={{0,4},{8,0},{16,8},{24,16},{28,24},{20,28},{12,20},{4,12},{1,5},{9... | collective-permute-start | bytes 6291464 | tf_op jit(solution)/shard_map/ppermute | solution.py:62
  15.9 198.9 %all-gather.5.cloned.1.call-start = ((), (), s32[]{:S(2)}) async-start(), calls=%async_computation.2 | async-start | bytes 5242880 | tf_op jit(solution)/shard_map/all_gather | solution.py:44
  60.2 47.1 %collective-permute-start.2 = (bf16[512,2048]{1,0:T(8,128)(2,1)}, bf16[512,2048]{1,0:T(8,128)(2,1)}, u32[]{:S(2)}, u32[]{:S(2)}) collective-permute-start(bf16[512,2048]{1,0:T(8,128)(2,1)} %collective-permute-done), channel_id=1, source_target_pairs={{0,8},{8,16},{16,24},{24,28},{28,20},{20,12},{12,4},{4,0},{1,9},{9... | collective-permute-start | bytes 6291464 | tf_op jit(solution)/shard_map/ppermute | solution.py:61
  62.0 46.8 %collective-permute-start.3 = (bf16[512,2048]{1,0:T(8,128)(2,1)}, bf16[512,2048]{1,0:T(8,128)(2,1)S(1)}, u32[]{:S(2)}, u32[]{:S(2)}) collective-permute-start(bf16[512,2048]{1,0:T(8,128)(2,1)} %collective-permute-done.1), channel_id=1, source_target_pairs={{0,4},{8,0},{16,8},{24,16},{28,24},{20,28},{12,20},{4,12},{1,5},{9... | collective-permute-start | bytes 6291464 | tf_op jit(solution)/shard_map/ppermute | solution.py:62
  107.3 46.1 %collective-permute-start.4 = (bf16[512,2048]{1,0:T(8,128)(2,1)}, bf16[512,2048]{1,0:T(8,128)(2,1)S(1)}, u32[]{:S(2)}, u32[]{:S(2)}) collective-permute-start(bf16[512,2048]{1,0:T(8,128)(2,1)} %collective-permute-done.2), channel_id=1, source_target_pairs={{0,8},{8,16},{16,24},{24,28},{28,20},{20,12},{12,4},{4,0},{1,9},{9... | collective-permute-start | bytes 6291464 | tf_op jit(solution)/shard_map/ppermute | solution.py:61
  108.8 46.0 %collective-permute-start.5 = (bf16[512,2048]{1,0:T(8,128)(2,1)S(1)}, bf16[512,2048]{1,0:T(8,128)(2,1)S(1)}, u32[]{:S(2)}, u32[]{:S(2)}) collective-permute-start(bf16[512,2048]{1,0:T(8,128)(2,1)S(1)} %collective-permute-done.3), channel_id=1, source_target_pairs={{0,4},{8,0},{16,8},{24,16},{28,24},{20,28},{12,20},{4,12},{1,5},{9... | collective-permute-start | bytes 6291464 | tf_op jit(solution)/shard_map/ppermute | solution.py:62
  153.6 22.6 %collective-permute-start.6 = (bf16[256,2048]{1,0:T(8,128)(2,1)S(1)}, bf16[256,2048]{1,0:T(8,128)(2,1)S(1)}, u32[]{:S(2)}, u32[]{:S(2)}) collective-permute-start(bf16[256,2048]{1,0:T(8,128)(2,1)S(1)} %slice.26), channel_id=1, source_target_pairs={{0,8},{8,16},{16,24},{24,28},{28,20},{20,12},{12,4},{4,0},{1,9},{9... | collective-permute-start | bytes 3145736 | tf_op jit(solution)/shard_map/ppermute | solution.py:67
  154.9 22.2 %collective-permute-start.7 = (bf16[256,2048]{1,0:T(8,128)(2,1)S(1)}, bf16[256,2048]{1,0:T(8,128)(2,1)S(1)}, u32[]{:S(2)}, u32[]{:S(2)}) collective-permute-start(bf16[256,2048]{1,0:T(8,128)(2,1)S(1)} %slice.27), channel_id=1, source_target_pairs={{0,4},{8,0},{16,8},{24,16},{28,24},{20,28},{12,20},{4,12},{1,5},{9... | collective-permute-start | bytes 3145736 | tf_op jit(solution)/shard_map/ppermute | solution.py:68
  157.3 21.0 %copy-start.5 = (bf16[512,1024]{1,0:T(8,128)(2,1)S(1)}, bf16[512,1024]{1,0:T(8,128)(2,1)}, u32[]{:S(2)}) copy-start(bf16[512,1024]{1,0:T(8,128)(2,1)} %param.12) | copy-start | bytes 3145732
  178.2 36.0 %copy-start.7 = (s32[16,8]{0,1:T(8,128)S(1)}, s32[16,8]{0,1:T(8,128)}, u32[]{:S(2)}) copy-start(s32[16,8]{0,1:T(8,128)} %param.16) | copy-start | bytes 1540
  178.2 36.1 %copy-start.9 = (s32[16]{0:T(128)S(1)}, s32[16]{0:T(128)}, u32[]{:S(2)}) copy-start(s32[16]{0:T(128)} %param.17) | copy-start | bytes 196
  178.2 31.5 %collective-permute-start.9 = (bf16[512,1024]{1,0:T(8,128)(2,1)S(1)}, bf16[512,1024]{1,0:T(8,128)(2,1)}, u32[]{:S(2)}, u32[]{:S(2)}) collective-permute-start(bf16[512,1024]{1,0:T(8,128)(2,1)S(1)} %copy-done.5), channel_id=1, source_target_pairs={{0,4},{8,0},{16,8},{24,16},{28,24},{20,28},{12,20},{4,12},{1,5},{9... | collective-permute-start | bytes 3145736 | tf_op jit(solution)/shard_map/ppermute | solution.py:88
  179.2 28.5 %collective-permute-start.8 = (bf16[512,1024]{1,0:T(8,128)(2,1)S(1)}, bf16[512,1024]{1,0:T(8,128)(2,1)}, u32[]{:S(2)}, u32[]{:S(2)}) collective-permute-start(bf16[512,1024]{1,0:T(8,128)(2,1)S(1)} %copy-done.5), channel_id=1, source_target_pairs={{0,8},{8,16},{16,24},{24,28},{28,20},{20,12},{12,4},{4,0},{1,9},{9... | collective-permute-start | bytes 3145736 | tf_op jit(solution)/shard_map/ppermute | solution.py:87
  192.1 61.1 %all-to-all-start = ((bf16[8,2,16,2048]{3,2,1,0:T(8,128)(2,1)}), bf16[8,2,16,2048]{3,2,1,0:T(8,128)(2,1)S(1)}, u32[]{:S(2)}, u32[]{:S(2)}) async-start(bf16[8,2,16,2048]{3,2,1,0:T(8,128)(2,1)} %bitcast.27), calls=%async_computation | async-start | bytes 2097152 | tf_op jit(solution)/shard_map/all_to_all | solution.py:76
  207.7 30.9 %collective-permute-start.10 = (bf16[512,1024]{1,0:T(8,128)(2,1)}, bf16[512,1024]{1,0:T(8,128)(2,1)}, u32[]{:S(2)}, u32[]{:S(2)}) collective-permute-start(bf16[512,1024]{1,0:T(8,128)(2,1)} %collective-permute-done.8), channel_id=1, source_target_pairs={{0,8},{8,16},{16,24},{24,28},{28,20},{20,12},{12,4},{4,0},{1,9},{9... | collective-permute-start | bytes 3145736 | tf_op jit(solution)/shard_map/ppermute | solution.py:87
  209.7 40.1 %collective-permute-start.11 = (bf16[512,1024]{1,0:T(8,128)(2,1)}, bf16[512,1024]{1,0:T(8,128)(2,1)}, u32[]{:S(2)}, u32[]{:S(2)}) collective-permute-start(bf16[512,1024]{1,0:T(8,128)(2,1)} %collective-permute-done.9), channel_id=1, source_target_pairs={{0,4},{8,0},{16,8},{24,16},{28,24},{20,28},{12,20},{4,12},{1,5},{9... | collective-permute-start | bytes 3145736 | tf_op jit(solution)/shard_map/ppermute | solution.py:88
  238.6 24.7 %collective-permute-start.12 = (bf16[512,1024]{1,0:T(8,128)(2,1)}, bf16[512,1024]{1,0:T(8,128)(2,1)}, u32[]{:S(2)}, u32[]{:S(2)}) collective-permute-start(bf16[512,1024]{1,0:T(8,128)(2,1)} %collective-permute-done.10), channel_id=1, source_target_pairs={{0,8},{8,16},{16,24},{24,28},{28,20},{20,12},{12,4},{4,0},{1,9},{9... | collective-permute-start | bytes 3145736 | tf_op jit(solution)/shard_map/ppermute | solution.py:87
  249.8 22.0 %collective-permute-start.13 = (bf16[512,1024]{1,0:T(8,128)(2,1)}, bf16[512,1024]{1,0:T(8,128)(2,1)}, u32[]{:S(2)}, u32[]{:S(2)}) collective-permute-start(bf16[512,1024]{1,0:T(8,128)(2,1)} %collective-permute-done.11), channel_id=1, source_target_pairs={{0,4},{8,0},{16,8},{24,16},{28,24},{20,28},{12,20},{4,12},{1,5},{9... | collective-permute-start | bytes 3145736 | tf_op jit(solution)/shard_map/ppermute | solution.py:88
  253.2 2.2 copy-start.4
  264.3 12.3 %collective-permute-start.14 = (bf16[256,1024]{1,0:T(8,128)(2,1)S(1)}, bf16[256,1024]{1,0:T(8,128)(2,1)S(1)}, u32[]{:S(2)}, u32[]{:S(2)}) collective-permute-start(bf16[256,1024]{1,0:T(8,128)(2,1)S(1)} %slice.30), channel_id=1, source_target_pairs={{0,8},{8,16},{16,24},{24,28},{28,20},{20,12},{12,4},{4,0},{1,9},{9... | collective-permute-start | bytes 1572872 | tf_op jit(solution)/shard_map/ppermute | solution.py:93
  272.9 10.3 %copy-start.2 = (f32[512,1024]{1,0:T(8,128)S(1)}, f32[512,1024]{1,0:T(8,128)}, u32[]{:S(2)}) copy-start(f32[512,1024]{1,0:T(8,128)} %fusion.22) | copy-start | bytes 6291460
  273.0 10.3 %copy-start.3 = (f32[512,1024]{1,0:T(8,128)S(1)}, f32[512,1024]{1,0:T(8,128)}, u32[]{:S(2)}) copy-start(f32[512,1024]{1,0:T(8,128)} %fusion.24) | copy-start | bytes 6291460
  273.0 9.9 %collective-permute-start.15 = (bf16[256,1024]{1,0:T(8,128)(2,1)S(1)}, bf16[256,1024]{1,0:T(8,128)(2,1)S(1)}, u32[]{:S(2)}, u32[]{:S(2)}) collective-permute-start(bf16[256,1024]{1,0:T(8,128)(2,1)S(1)} %slice.31), channel_id=1, source_target_pairs={{0,4},{8,0},{16,8},{24,16},{28,24},{20,28},{12,20},{4,12},{1,5},{9... | collective-permute-start | bytes 1572872 | tf_op jit(solution)/shard_map/ppermute | solution.py:94
  290.6 3.0 copy-start.1
Sparse Core Ops, SparseCore 0:
  16.0 24.2 all-gather.2
  62.4 35.9 all-gather.4

commit v6 on v5

--- a/solution.py
+++ b/solution.py
@@ -44,37 +44,43 @@
     queries_in = lax.all_gather(global_rows, "head", axis=1, tiled=True)
     picks = fetch_slots[0]
     blocks = crop_tokens.reshape(-1, CT, crop_tokens.shape[1])
-    chosen = blocks[picks].reshape(-1, crop_tokens.shape[1])
-    tokens_in = lax.all_gather(chosen, "head", axis=1, tiled=True)
+    chosen = blocks[picks]
+    delivered = lax.all_to_all(chosen, "crop", split_axis=0, concat_axis=0, tiled=True)
+    delivered = delivered.reshape(-1, crop_tokens.shape[1])
 
     steps_fwd = ncrop // 2
     steps_bwd = (ncrop - 1) // 2
     split = wrows // 2
 
-    def ring_gather(piece):
-        buf = jnp.zeros((ncrop,) + piece.shape, piece.dtype)
-        buf = lax.dynamic_update_slice(buf, piece[None], (me, 0, 0))
-
+    def ring_pieces(piece):
+        got = [(piece, me, 0, wrows)]
         fwd = piece
         bwd = piece
         for k in range(1, steps_bwd + 1):
             fwd = lax.ppermute(fwd, "crop", fwd_perm)
             bwd = lax.ppermute(bwd, "crop", bwd_perm)
-            buf = lax.dynamic_update_slice(buf, fwd[None], (ring_arr[(pos - k) % ncrop], 0, 0))
-            buf = lax.dynamic_update_slice(buf, bwd[None], (ring_arr[(pos + k) % ncrop], 0, 0))
+            got.append((fwd, ring_arr[(pos - k) % ncrop], 0, wrows))
+            got.append((bwd, ring_arr[(pos + k) % ncrop], 0, wrows))
         if steps_fwd > steps_bwd:
             src = ring_arr[(pos - steps_fwd) % ncrop]
-            top = lax.ppermute(fwd[:split], "crop", fwd_perm)
-            bottom = lax.ppermute(bwd[split:], "crop", bwd_perm)
-            buf = lax.dynamic_update_slice(buf, top[None], (src, 0, 0))
-            buf = lax.dynamic_update_slice(buf, bottom[None], (src, split, 0))
-        return buf.reshape(ncrop * wrows, piece.shape[1])
+            got.append((lax.ppermute(fwd[:split], "crop", fwd_perm), src, 0, split))
+            got.append((lax.ppermute(bwd[split:], "crop", bwd_perm), src, split, wrows - split))
+        return got
 
-    kv_weight = ring_gather(jnp.concatenate([key_weight, value_weight], axis=1))
-    kv = jnp.dot(tokens_in, kv_weight, preferred_element_type=jnp.float32).astype(jnp.bfloat16)
-    packed = kv.reshape(ncrop, CAP, CT, 2 * width)
-    incoming = lax.all_to_all(packed, "crop", split_axis=0, concat_axis=0, tiled=True)
-    q_piece, kv_weight = lax.optimization_barrier((query_weight, kv_weight))
+    kv_got = ring_pieces(jnp.concatenate([key_weight, value_weight], axis=1))
+    q_piece, last_a, last_b = lax.optimization_barrier(
+        (query_weight, kv_got[-1][0], kv_got[-2][0])
+    )
+    kv_got[-1] = (last_a,) + kv_got[-1][1:]
+    kv_got[-2] = (last_b,) + kv_got[-2][1:]
+    tokens_in = lax.all_gather(delivered, "head", axis=1, tiled=True)
+    kv_weight = jnp.concatenate([p for p, _, _, _ in kv_got], axis=0)
+    tokens_perm = jnp.concatenate(
+        [lax.dynamic_slice_in_dim(tokens_in, src * wrows + lo, n, 1) for _, src, lo, n in kv_got],
+        axis=1,
+    )
+    kv = jnp.dot(tokens_perm, kv_weight, preferred_element_type=jnp.float32).astype(jnp.bfloat16)
+    incoming = kv.reshape(ncrop, CAP, CT, 2 * width)
 
     def q_part(acc, piece, src, lo, n):
         cols = lax.dynamic_slice_in_dim(queries_in, src * wrows + lo, n, 1)

time: 301 us -> 296 us (0.983)
  waiting for transfers between devices: 156 us -> 183 us
  between operations: 36.3 us -> 23.2 us
  matrix products: 32 us -> 22.8 us
  starting transfers between devices: 32.2 us -> 25 us
  local copies, waits for them, and re-layouts: 40.1 us -> 35.9 us
    unnamed x28 -> x48, local copies, waits for them, and re-layouts: 6.15 us -> 29.3 us
    dynamic_update_slice x9 -> x0, local copies, waits for them, and re-layouts: 19.3 us -> none  [the longest x3 7.86 us: ring_gather(): lax.dynamic_update_slice(buf, fwd[None], (ring_arr[(pos - k) % ncrop], 0,...]
    ppermute x8, waiting for transfers between devices: 111 us -> 126 us  [the longest x3 107 us: ring_pieces(): bwd = lax.ppermute(bwd, 'crop', bwd_perm)]
    all_to_all x1, waiting for transfers between devices: 0.01 us -> 9.3 us  [body(): lax.all_to_all(chosen, 'crop', split_axis=0, concat_axis=0, tiled=True)]
    ppermute x3, starting transfers between devices: 10.9 us -> 1.69 us  [body(): fwd = lax.ppermute(fwd, 'crop', fwd_perm)]
    broadcast_in_dim x1 -> x0, local copies, waits for them, and re-layouts: 6.03 us -> none  [ring_gather(): buf = jnp.zeros((ncrop,) + piece.shape, piece.dtype)]
    dot_general x9, matrix products: 18.4 us -> 12.8 us  [q_part(): return acc + jnp.dot(cols, piece, preferred_element_type=jnp.float32)]
    ppermute x1, starting transfers between devices: 5.61 us -> 0.62 us  [body(): lax.ppermute(fwd[:split], 'crop', fwd_perm)]
  transfers between devices with their start and end apart: 19 -> 19, of which waited for: 9 -> 13; matrix products, arithmetic and copies ran while one was open for 19% -> 17% of each run, Pallas kernels for 0% -> 0%
where the time goes in v6:
time: 296 us; the launch traced here: 295 us
  waiting for transfers between devices  183 us (62%)
  local copies, waits for them, and re-layouts  35.9 us (12%)
  starting transfers between devices  25 us (8%)
  between operations  23.2 us (8%)
  matrix products  22.8 us (8%)
  other arithmetic  4.49 us (2%)
    ppermute x3, waiting for transfers between devices, ring_pieces(): bwd = lax.ppermute(bwd, 'crop', bwd_perm)  107 us
    ppermute x3, waiting for transfers between devices, body(): fwd = lax.ppermute(fwd, 'crop', fwd_perm)  41.4 us
    unnamed x48, local copies, waits for them, and re-layouts  29.3 us
    dot_general x9, matrix products, q_part(): return acc + jnp.dot(cols, piece, preferred_element_type=jnp.float32)  12.8 us
    ppermute x1, waiting for transfers between devices, ring_pieces(): lax.ppermute(bwd[split:], 'crop', bwd_perm)  11.6 us
    all_to_all x1, waiting for transfers between devices, body(): lax.all_to_all(chosen, 'crop', split_axis=0, concat_axis=0, tiled=True)  9.3 us
    dot_general x1, matrix products, body(): jnp.dot(tokens_perm, kv_weight, preferred_element_type=jnp.float32)  8.28 us
    all_to_all x1, starting transfers between devices, body(): lax.all_to_all(chosen, 'crop', split_axis=0, concat_axis=0, tiled=True)  7.41 us
  transfers between devices with their start and end apart: 19, of which 13 were waited for; matrix products, arithmetic and copies ran while one was open for 17% of the time, Pallas kernels for 0%

profile of v6, /device:TPU:0, one launch (start us, length us, event | category | flops | bytes accessed | tf_op | source)
XLA Modules:
  0.0 294.8 jit_solution(16594161271160027359)
XLA Ops:
  9.5 7.4 %all-to-all-start = ((bf16[8,2,16,1024]{3,2,1,0:T(8,128)(2,1)}), bf16[8,2,16,1024]{3,2,1,0:T(8,128)(2,1)S(1)}, u32[]{:S(2)}, u32[]{:S(2)}) async-start(bf16[8,2,16,1024]{3,2,1,0:T(8,128)(2,1)} %bitcast.2), calls=%async_computation | async-start | bytes 1048576 | tf_op jit(solution)/shard_map/all_to_all | solution.py:48
  17.0 2.9 constant_dynamic-update-slice_fusion.11
  19.9 1.7 constant_dynamic-update-slice_fusion.10
  21.6 2.0 collective-permute-start.1
  23.6 9.3 %all-to-all-done = bf16[8,2,16,1024]{3,2,1,0:T(8,128)(2,1)S(1)} async-done(((bf16[8,2,16,1024]{3,2,1,0:T(8,128)(2,1)}), bf16[8,2,16,1024]{3,2,1,0:T(8,128)(2,1)S(1)}, u32[]{:S(2)}, u32[]{:S(2)}) %all-to-all-start) | async-done | bytes 524320 | tf_op jit(solution)/shard_map/all_to_all | solution.py:48
  33.7 39.2 %collective-permute-done.1 = bf16[512,2048]{1,0:T(8,128)(2,1)S(1)} collective-permute-done((bf16[512,2048]{1,0:T(8,128)(2,1)}, bf16[512,2048]{1,0:T(8,128)(2,1)S(1)}, u32[]{:S(2)}, u32[]{:S(2)}) %collective-permute-start.1) | collective-permute-done | bytes 2097184 | tf_op jit(solution)/shard_map/ppermute | solution.py:61
  72.9 4.1 %collective-permute-start.2 = (bf16[512,2048]{1,0:T(8,128)(2,1)}, bf16[512,2048]{1,0:T(8,128)(2,1)}, u32[]{:S(2)}, u32[]{:S(2)}) collective-permute-start(bf16[512,2048]{1,0:T(8,128)(2,1)} %collective-permute-done), channel_id=1, source_target_pairs={{0,8},{8,16},{16,24},{24,28},{28,20},{20,12},{12,4},{4,0},{1,9},{9... | collective-permute-start | bytes 6291464 | tf_op jit(solution)/shard_map/ppermute | solution.py:60
  77.0 44.4 %collective-permute-done.3 = bf16[512,2048]{1,0:T(8,128)(2,1)} collective-permute-done((bf16[512,2048]{1,0:T(8,128)(2,1)S(1)}, bf16[512,2048]{1,0:T(8,128)(2,1)}, u32[]{:S(2)}, u32[]{:S(2)}) %collective-permute-start.3) | collective-permute-done | bytes 2097184 | tf_op jit(solution)/shard_map/ppermute | solution.py:61
  134.8 3.3 %constant_dynamic-update-slice_fusion.9 = bf16[4096,2048]{1,0:T(8,128)(2,1)} fusion(bf16[4096,2048]{1,0:T(8,128)(2,1)} %get-tuple-element.13, bf16[512,2048]{1,0:T(8,128)(2,1)} %collective-permute-done), kind=kLoop, calls=%fused_computation.58 | loop fusion | bytes 4194304
  138.1 1.5 constant_dynamic-update-slice_fusion.8
  143.6 23.7 %collective-permute-done.5 = bf16[512,2048]{1,0:T(8,128)(2,1)S(1)} collective-permute-done((bf16[512,2048]{1,0:T(8,128)(2,1)}, bf16[512,2048]{1,0:T(8,128)(2,1)S(1)}, u32[]{:S(2)}, u32[]{:S(2)}) %collective-permute-start.5) | collective-permute-done | bytes 2097184 | tf_op jit(solution)/shard_map/ppermute | solution.py:61
  167.3 1.7 collective-permute-start.6
  171.7 3.2 %constant_dynamic-update-slice_fusion.7 = bf16[4096,2048]{1,0:T(8,128)(2,1)} fusion(bf16[4096,2048]{1,0:T(8,128)(2,1)} %constant_dynamic-update-slice_fusion.8, bf16[512,2048]{1,0:T(8,128)(2,1)} %collective-permute-done.2), kind=kLoop, calls=%fused_computation.56 | loop fusion | bytes 4194304
  174.9 3.3 %constant_dynamic-update-slice_fusion.6 = bf16[4096,2048]{1,0:T(8,128)(2,1)} fusion(bf16[4096,2048]{1,0:T(8,128)(2,1)} %constant_dynamic-update-slice_fusion.7, bf16[512,2048]{1,0:T(8,128)(2,1)} %collective-permute-done.3), kind=kLoop, calls=%fused_computation.55 | loop fusion | bytes 4194304
  178.2 11.6 %collective-permute-done.6 = bf16[256,2048]{1,0:T(8,128)(2,1)S(1)} collective-permute-done((bf16[256,2048]{1,0:T(8,128)(2,1)S(1)}, bf16[256,2048]{1,0:T(8,128)(2,1)S(1)}, u32[]{:S(2)}, u32[]{:S(2)}) %collective-permute-start.6) | collective-permute-done | bytes 1048608 | tf_op jit(solution)/shard_map/ppermute | solution.py:67
  189.8 5.3 %collective-permute-done.7 = bf16[256,2048]{1,0:T(8,128)(2,1)S(1)} collective-permute-done((bf16[256,2048]{1,0:T(8,128)(2,1)S(1)}, bf16[256,2048]{1,0:T(8,128)(2,1)S(1)}, u32[]{:S(2)}, u32[]{:S(2)}) %collective-permute-start.7) | collective-permute-done | bytes 1048608 | tf_op jit(solution)/shard_map/ppermute | solution.py:66
  197.1 3.2 %constant_dynamic-update-slice_fusion.5 = bf16[4096,2048]{1,0:T(8,128)(2,1)} fusion(bf16[4096,2048]{1,0:T(8,128)(2,1)} %constant_dynamic-update-slice_fusion.6, bf16[512,2048]{1,0:T(8,128)(2,1)} %collective-permute-done.4), kind=kLoop, calls=%fused_computation.54 | loop fusion | bytes 4194304
  200.3 1.6 constant_dynamic-update-slice_fusion.4
  204.0 15.7 %collective-permute-done.8 = bf16[512,1024]{1,0:T(8,128)(2,1)} collective-permute-done((bf16[512,1024]{1,0:T(8,128)(2,1)S(1)}, bf16[512,1024]{1,0:T(8,128)(2,1)}, u32[]{:S(2)}, u32[]{:S(2)}) %collective-permute-start.8) | collective-permute-done | bytes 1048608 | tf_op jit(solution)/shard_map/ppermute | solution.py:93
  221.7 8.3 %convolution_convert_fusion = bf16[256,2048]{1,0:T(8,128)(2,1)S(1)} fusion(bf16[256,4096]{1,0:T(8,128)(2,1)S(1)} %dynamic-slice_dynamic-update-slice_fusion.7, bf16[4096,2048]{1,0:T(8,128)(2,1)} %constant_dynamic-update-slice_fusion.2), kind=kOutput, calls=%fused_computation.6 | convolution fusion | flops 4295491584 | bytes 19922944 | tf_op jit(solution)/shard_map/dot_general | solution.py:82
  230.0 2.1 fusion.26
  232.1 10.9 %collective-permute-done.10 = bf16[512,1024]{1,0:T(8,128)(2,1)} collective-permute-done((bf16[512,1024]{1,0:T(8,128)(2,1)}, bf16[512,1024]{1,0:T(8,128)(2,1)}, u32[]{:S(2)}, u32[]{:S(2)}) %collective-permute-start.10) | collective-permute-done | bytes 1048608 | tf_op jit(solution)/shard_map/ppermute | solution.py:93
  243.8 1.5 collective-permute-start.13
  245.7 1.9 fusion.22
  247.7 1.9 fusion.24
  249.6 1.9 fusion.20
  251.6 14.9 %collective-permute-done.12 = bf16[512,1024]{1,0:T(8,128)(2,1)S(1)} collective-permute-done((bf16[512,1024]{1,0:T(8,128)(2,1)}, bf16[512,1024]{1,0:T(8,128)(2,1)S(1)}, u32[]{:S(2)}, u32[]{:S(2)}) %collective-permute-start.12) | collective-permute-done | bytes 1048608 | tf_op jit(solution)/shard_map/ppermute | solution.py:93
  267.1 1.9 fusion.18
  269.1 1.7 collective-permute-start.15
  271.5 4.2 %collective-permute-done.14 = bf16[256,1024]{1,0:T(8,128)(2,1)S(1)} collective-permute-done((bf16[256,1024]{1,0:T(8,128)(2,1)S(1)}, bf16[256,1024]{1,0:T(8,128)(2,1)S(1)}, u32[]{:S(2)}, u32[]{:S(2)}) %collective-permute-start.14) | collective-permute-done | bytes 524320 | tf_op jit(solution)/shard_map/ppermute | solution.py:99
  276.1 2.4 collective-permute-done.15
  281.5 3.5 %fusion.47 = (f32[16,8,32]{2,0,1:T(8,128)S(1)}, f32[16,8,32,256]{3,2,0,1:T(8,128)S(1)}) fusion(f32[8,256,16,32]{1,3,2,0:T(8,128)S(1)} %bitcast.71, pred[16,256]{1,0:T(8,128)(4,1)S(1)} %broadcast_in_dim.26), kind=kOutput, calls=%fused_computation.77 | output fusion | flops 6291711 | bytes 8409088 | tf_op jit(solution)/shard_map/sub | solution.py:117
  (89 shorter events, 29.6 us)
Async XLA Ops:
  6.5 1.6 copy-start
  9.5 10.3 %copy-start.7 = (bf16[512,1024]{1,0:T(8,128)(2,1)S(1)}, bf16[512,1024]{1,0:T(8,128)(2,1)}, u32[]{:S(2)}) copy-start(bf16[512,1024]{1,0:T(8,128)(2,1)} %param.14) | copy-start | bytes 3145732
  9.5 23.4 %all-to-all-start = ((bf16[8,2,16,1024]{3,2,1,0:T(8,128)(2,1)}), bf16[8,2,16,1024]{3,2,1,0:T(8,128)(2,1)S(1)}, u32[]{:S(2)}, u32[]{:S(2)}) async-start(bf16[8,2,16,1024]{3,2,1,0:T(8,128)(2,1)} %bitcast.2), calls=%async_computation | async-start | bytes 1048576 | tf_op jit(solution)/shard_map/all_to_all | solution.py:48
  16.9 122.7 %all-gather.3.cloned.1.call-start = ((), (), s32[]{:S(2)}) async-start(), calls=%async_computation.1 | async-start | bytes 2621440 | tf_op jit(solution)/shard_map/all_gather | solution.py:76
  19.9 103.6 %copy-start.12 = (s32[8]{0:T(128)S(1)}, s32[8]{0:T(128)}, u32[]{:S(2)}) copy-start(s32[8]{0:T(128)} %constant.113.clone) | copy-start | bytes 100
  19.9 109.2 %copy-start.9 = (s32[8]{0:T(128)S(1)}, s32[8]{0:T(128)}, u32[]{:S(2)}) copy-start(s32[8]{0:T(128)} %constant.114.clone) | copy-start | bytes 100
  19.9 114.3 %copy-start.10 = (s32[16,8]{0,1:T(8,128)S(1)}, s32[16,8]{0,1:T(8,128)}, u32[]{:S(2)}) copy-start(s32[16,8]{0,1:T(8,128)} %param.16) | copy-start | bytes 1540
  19.9 114.4 %copy-start.11 = (s32[16]{0:T(128)S(1)}, s32[16]{0:T(128)}, u32[]{:S(2)}) copy-start(s32[16]{0:T(128)} %param.17) | copy-start | bytes 196
  21.6 51.4 %collective-permute-start.1 = (bf16[512,2048]{1,0:T(8,128)(2,1)}, bf16[512,2048]{1,0:T(8,128)(2,1)S(1)}, u32[]{:S(2)}, u32[]{:S(2)}) collective-permute-start(bf16[512,2048]{1,0:T(8,128)(2,1)} %get-tuple-element.14), channel_id=1, source_target_pairs={{0,4},{8,0},{16,8},{24,16},{28,24},{20,28},{12,20},{4,12},{1,5},{9... | collective-permute-start | bytes 6291464 | tf_op jit(solution)/shard_map/ppermute | solution.py:61
  23.5 49.4 %collective-permute-start = (bf16[512,2048]{1,0:T(8,128)(2,1)}, bf16[512,2048]{1,0:T(8,128)(2,1)}, u32[]{:S(2)}, u32[]{:S(2)}) collective-permute-start(bf16[512,2048]{1,0:T(8,128)(2,1)} %get-tuple-element.14), channel_id=1, source_target_pairs={{0,8},{8,16},{16,24},{24,28},{28,20},{20,12},{12,4},{4,0},{1,9},{9... | collective-permute-start | bytes 6291464 | tf_op jit(solution)/shard_map/ppermute | solution.py:60
  32.9 0.8 copy-start.6
  33.7 196.3 %all-gather.5.cloned.1.call-start = ((), (), s32[]{:S(2)}) async-start(), calls=%async_computation.2 | async-start | bytes 5242880 | tf_op jit(solution)/shard_map/all_gather | solution.py:44
  72.9 4.1 %copy-start.4 = (bf16[512,2048]{1,0:T(8,128)(2,1)}, bf16[512,2048]{1,0:T(8,128)(2,1)S(1)}, u32[]{:S(2)}) copy-start(bf16[512,2048]{1,0:T(8,128)(2,1)S(1)} %collective-permute-done.1) | copy-start | bytes 6291460
  72.9 48.6 %collective-permute-start.3 = (bf16[512,2048]{1,0:T(8,128)(2,1)S(1)}, bf16[512,2048]{1,0:T(8,128)(2,1)}, u32[]{:S(2)}, u32[]{:S(2)}) collective-permute-start(bf16[512,2048]{1,0:T(8,128)(2,1)S(1)} %collective-permute-done.1), channel_id=1, source_target_pairs={{0,4},{8,0},{16,8},{24,16},{28,24},{20,28},{12,20},{4,12},{1,5},{9... | collective-permute-start | bytes 6291464 | tf_op jit(solution)/shard_map/ppermute | solution.py:61
  72.9 49.6 %collective-permute-start.2 = (bf16[512,2048]{1,0:T(8,128)(2,1)}, bf16[512,2048]{1,0:T(8,128)(2,1)}, u32[]{:S(2)}, u32[]{:S(2)}) collective-permute-start(bf16[512,2048]{1,0:T(8,128)(2,1)} %collective-permute-done), channel_id=1, source_target_pairs={{0,8},{8,16},{16,24},{24,28},{28,20},{20,12},{12,4},{4,0},{1,9},{9... | collective-permute-start | bytes 6291464 | tf_op jit(solution)/shard_map/ppermute | solution.py:60
  121.5 45.7 %collective-permute-start.5 = (bf16[512,2048]{1,0:T(8,128)(2,1)}, bf16[512,2048]{1,0:T(8,128)(2,1)S(1)}, u32[]{:S(2)}, u32[]{:S(2)}) collective-permute-start(bf16[512,2048]{1,0:T(8,128)(2,1)} %collective-permute-done.3), channel_id=1, source_target_pairs={{0,4},{8,0},{16,8},{24,16},{28,24},{20,28},{12,20},{4,12},{1,5},{9... | collective-permute-start | bytes 6291464 | tf_op jit(solution)/shard_map/ppermute | solution.py:61
  122.5 47.7 %collective-permute-start.4 = (bf16[512,2048]{1,0:T(8,128)(2,1)}, bf16[512,2048]{1,0:T(8,128)(2,1)}, u32[]{:S(2)}, u32[]{:S(2)}) collective-permute-start(bf16[512,2048]{1,0:T(8,128)(2,1)} %collective-permute-done.2), channel_id=1, source_target_pairs={{0,8},{8,16},{16,24},{24,28},{28,20},{20,12},{12,4},{4,0},{1,9},{9... | collective-permute-start | bytes 6291464 | tf_op jit(solution)/shard_map/ppermute | solution.py:60
  134.8 3.3 %copy-start.5 = (bf16[512,2048]{1,0:T(8,128)(2,1)S(1)}, bf16[512,2048]{1,0:T(8,128)(2,1)}, u32[]{:S(2)}) copy-start(bf16[512,2048]{1,0:T(8,128)(2,1)} %copy-done.4) | copy-start | bytes 6291460
  143.5 27.9 %copy-start.3 = (bf16[256,4096]{1,0:T(8,128)(2,1)S(1)}, bf16[256,4096]{1,0:T(8,128)(2,1)}, u32[]{:S(2)}) copy-start(bf16[256,4096]{1,0:T(8,128)(2,1)} %all-gather.3.cloned.1.call-done) | copy-start | bytes 6291460
  167.3 22.5 %collective-permute-start.6 = (bf16[256,2048]{1,0:T(8,128)(2,1)S(1)}, bf16[256,2048]{1,0:T(8,128)(2,1)S(1)}, u32[]{:S(2)}, u32[]{:S(2)}) collective-permute-start(bf16[256,2048]{1,0:T(8,128)(2,1)S(1)} %slice.26), channel_id=1, source_target_pairs={{0,4},{8,0},{16,8},{24,16},{28,24},{20,28},{12,20},{4,12},{1,5},{9... | collective-permute-start | bytes 3145736 | tf_op jit(solution)/shard_map/ppermute | solution.py:67
  171.4 23.6 %collective-permute-start.7 = (bf16[256,2048]{1,0:T(8,128)(2,1)S(1)}, bf16[256,2048]{1,0:T(8,128)(2,1)S(1)}, u32[]{:S(2)}, u32[]{:S(2)}) collective-permute-start(bf16[256,2048]{1,0:T(8,128)(2,1)S(1)} %slice.27), channel_id=1, source_target_pairs={{0,8},{8,16},{16,24},{24,28},{28,20},{20,12},{12,4},{4,0},{1,9},{9... | collective-permute-start | bytes 3145736 | tf_op jit(solution)/shard_map/ppermute | solution.py:66
  174.9 20.2 %copy-start.8 = (bf16[512,1024]{1,0:T(8,128)(2,1)S(1)}, bf16[512,1024]{1,0:T(8,128)(2,1)}, u32[]{:S(2)}) copy-start(bf16[512,1024]{1,0:T(8,128)(2,1)} %param.12) | copy-start | bytes 3145732
  195.1 25.1 %collective-permute-start.9 = (bf16[512,1024]{1,0:T(8,128)(2,1)S(1)}, bf16[512,1024]{1,0:T(8,128)(2,1)}, u32[]{:S(2)}, u32[]{:S(2)}) collective-permute-start(bf16[512,1024]{1,0:T(8,128)(2,1)S(1)} %copy-done.8), channel_id=1, source_target_pairs={{0,4},{8,0},{16,8},{24,16},{28,24},{20,28},{12,20},{4,12},{1,5},{9... | collective-permute-start | bytes 3145736 | tf_op jit(solution)/shard_map/ppermute | solution.py:94
  196.5 23.1 %collective-permute-start.8 = (bf16[512,1024]{1,0:T(8,128)(2,1)S(1)}, bf16[512,1024]{1,0:T(8,128)(2,1)}, u32[]{:S(2)}, u32[]{:S(2)}) collective-permute-start(bf16[512,1024]{1,0:T(8,128)(2,1)S(1)} %copy-done.8), channel_id=1, source_target_pairs={{0,8},{8,16},{16,24},{24,28},{28,20},{20,12},{12,4},{4,0},{1,9},{9... | collective-permute-start | bytes 3145736 | tf_op jit(solution)/shard_map/ppermute | solution.py:93
  219.6 23.3 %collective-permute-start.10 = (bf16[512,1024]{1,0:T(8,128)(2,1)}, bf16[512,1024]{1,0:T(8,128)(2,1)}, u32[]{:S(2)}, u32[]{:S(2)}) collective-permute-start(bf16[512,1024]{1,0:T(8,128)(2,1)} %collective-permute-done.8), channel_id=1, source_target_pairs={{0,8},{8,16},{16,24},{24,28},{28,20},{20,12},{12,4},{4,0},{1,9},{9... | collective-permute-start | bytes 3145736 | tf_op jit(solution)/shard_map/ppermute | solution.py:93
  220.2 23.6 %collective-permute-start.11 = (bf16[512,1024]{1,0:T(8,128)(2,1)}, bf16[512,1024]{1,0:T(8,128)(2,1)}, u32[]{:S(2)}, u32[]{:S(2)}) collective-permute-start(bf16[512,1024]{1,0:T(8,128)(2,1)} %collective-permute-done.9), channel_id=1, source_target_pairs={{0,4},{8,0},{16,8},{24,16},{28,24},{20,28},{12,20},{4,12},{1,5},{9... | collective-permute-start | bytes 3145736 | tf_op jit(solution)/shard_map/ppermute | solution.py:94
  243.0 23.4 %collective-permute-start.12 = (bf16[512,1024]{1,0:T(8,128)(2,1)}, bf16[512,1024]{1,0:T(8,128)(2,1)S(1)}, u32[]{:S(2)}, u32[]{:S(2)}) collective-permute-start(bf16[512,1024]{1,0:T(8,128)(2,1)} %collective-permute-done.10), channel_id=1, source_target_pairs={{0,8},{8,16},{16,24},{24,28},{28,20},{20,12},{12,4},{4,0},{1,9},{9... | collective-permute-start | bytes 3145736 | tf_op jit(solution)/shard_map/ppermute | solution.py:93
  243.5 2.2 copy-start.2
  243.8 25.2 %collective-permute-start.13 = (bf16[512,1024]{1,0:T(8,128)(2,1)}, bf16[512,1024]{1,0:T(8,128)(2,1)S(1)}, u32[]{:S(2)}, u32[]{:S(2)}) collective-permute-start(bf16[512,1024]{1,0:T(8,128)(2,1)} %collective-permute-done.11), channel_id=1, source_target_pairs={{0,4},{8,0},{16,8},{24,16},{28,24},{20,28},{12,20},{4,12},{1,5},{9... | collective-permute-start | bytes 3145736 | tf_op jit(solution)/shard_map/ppermute | solution.py:94
  266.5 9.2 %collective-permute-start.14 = (bf16[256,1024]{1,0:T(8,128)(2,1)S(1)}, bf16[256,1024]{1,0:T(8,128)(2,1)S(1)}, u32[]{:S(2)}, u32[]{:S(2)}) collective-permute-start(bf16[256,1024]{1,0:T(8,128)(2,1)S(1)} %slice.30), channel_id=1, source_target_pairs={{0,8},{8,16},{16,24},{24,28},{28,20},{20,12},{12,4},{4,0},{1,9},{9... | collective-permute-start | bytes 1572872 | tf_op jit(solution)/shard_map/ppermute | solution.py:99
  269.1 9.4 %collective-permute-start.15 = (bf16[256,1024]{1,0:T(8,128)(2,1)S(1)}, bf16[256,1024]{1,0:T(8,128)(2,1)S(1)}, u32[]{:S(2)}, u32[]{:S(2)}) collective-permute-start(bf16[256,1024]{1,0:T(8,128)(2,1)S(1)} %slice.31), channel_id=1, source_target_pairs={{0,4},{8,0},{16,8},{24,16},{28,24},{20,28},{12,20},{4,12},{1,5},{9... | collective-permute-start | bytes 1572872 | tf_op jit(solution)/shard_map/ppermute | solution.py:100
  284.9 3.0 %copy-start.1 = (bf16[1024,1024]{1,0:T(8,128)(2,1)S(1)}, bf16[1024,1024]{1,0:T(8,128)(2,1)}, u32[]{:S(2)}) copy-start(bf16[1024,1024]{1,0:T(8,128)(2,1)} %param.11) | copy-start | bytes 6291460
Sparse Core Ops, SparseCore 0:
  33.8 20.3 all-gather.2
  77.1 34.0 all-gather.4

commit v7 on v6

--- a/solution.py
+++ b/solution.py
@@ -41,46 +41,65 @@
     fwd_perm = [(ring[i], ring[(i + 1) % ncrop]) for i in range(ncrop)]
     bwd_perm = [(ring[i], ring[(i - 1) % ncrop]) for i in range(ncrop)]
 
-    queries_in = lax.all_gather(global_rows, "head", axis=1, tiled=True)
+    nhead = lax.axis_size("head")
+    hme = lax.axis_index("head")
+
+    def head_gather(x):
+        full = jnp.zeros((x.shape[0], nhead * x.shape[1]), x.dtype)
+        full = lax.dynamic_update_slice(full, x, (0, hme * x.shape[1]))
+        for k in range(1, nhead):
+            part = lax.ppermute(x, "head", [(j, (j + k) % nhead) for j in range(nhead)])
+            full = lax.dynamic_update_slice(full, part, (0, ((hme - k) % nhead) * x.shape[1]))
+        return full
+
+    queries_in = head_gather(global_rows)
     picks = fetch_slots[0]
     blocks = crop_tokens.reshape(-1, CT, crop_tokens.shape[1])
-    chosen = blocks[picks]
-    delivered = lax.all_to_all(chosen, "crop", split_axis=0, concat_axis=0, tiled=True)
-    delivered = delivered.reshape(-1, crop_tokens.shape[1])
 
     steps_fwd = ncrop // 2
     steps_bwd = (ncrop - 1) // 2
     split = wrows // 2
 
-    def ring_pieces(piece):
-        got = [(piece, me, 0, wrows)]
-        fwd = piece
-        bwd = piece
+    def ring_pieces(pieces):
+        got = [[(p, me, 0, wrows)] for p in pieces]
+        fwd = list(pieces)
+        bwd = list(pieces)
         for k in range(1, steps_bwd + 1):
-            fwd = lax.ppermute(fwd, "crop", fwd_perm)
-            bwd = lax.ppermute(bwd, "crop", bwd_perm)
-            got.append((fwd, ring_arr[(pos - k) % ncrop], 0, wrows))
-            got.append((bwd, ring_arr[(pos + k) % ncrop], 0, wrows))
+            for i in range(len(pieces)):
+                fwd[i] = lax.ppermute(fwd[i], "crop", fwd_perm)
+                bwd[i] = lax.ppermute(bwd[i], "crop", bwd_perm)
+                got[i].append((fwd[i], ring_arr[(pos - k) % ncrop], 0, wrows))
+                got[i].append((bwd[i], ring_arr[(pos + k) % ncrop], 0, wrows))
         if steps_fwd > steps_bwd:
             src = ring_arr[(pos - steps_fwd) % ncrop]
-            got.append((lax.ppermute(fwd[:split], "crop", fwd_perm), src, 0, split))
-            got.append((lax.ppermute(bwd[split:], "crop", bwd_perm), src, split, wrows - split))
+            for i in range(len(pieces)):
+                top = lax.ppermute(fwd[i][:split], "crop", fwd_perm)
+                bottom = lax.ppermute(bwd[i][split:], "crop", bwd_perm)
+                got[i].append((top, src, 0, split))
+                got[i].append((bottom, src, split, wrows - split))
         return got
 
-    kv_got = ring_pieces(jnp.concatenate([key_weight, value_weight], axis=1))
-    q_piece, last_a, last_b = lax.optimization_barrier(
-        (query_weight, kv_got[-1][0], kv_got[-2][0])
-    )
-    kv_got[-1] = (last_a,) + kv_got[-1][1:]
-    kv_got[-2] = (last_b,) + kv_got[-2][1:]
-    tokens_in = lax.all_gather(delivered, "head", axis=1, tiled=True)
-    kv_weight = jnp.concatenate([p for p, _, _, _ in kv_got], axis=0)
+    k_got, v_got = ring_pieces([key_weight, value_weight])
+    chosen, k_first, v_first = lax.optimization_barrier((blocks[picks], k_got[1][0], v_got[1][0]))
+    k_got[1] = (k_first,) + k_got[1][1:]
+    v_got[1] = (v_first,) + v_got[1][1:]
+    delivered = lax.all_to_all(chosen, "crop", split_axis=0, concat_axis=0, tiled=True)
+    tokens_in = head_gather(delivered.reshape(-1, crop_tokens.shape[1]))
+    q_piece, k_last, v_last = lax.optimization_barrier((query_weight, k_got[-1][0], v_got[-1][0]))
+    k_got[-1] = (k_last,) + k_got[-1][1:]
+    v_got[-1] = (v_last,) + v_got[-1][1:]
     tokens_perm = jnp.concatenate(
-        [lax.dynamic_slice_in_dim(tokens_in, src * wrows + lo, n, 1) for _, src, lo, n in kv_got],
+        [lax.dynamic_slice_in_dim(tokens_in, src * wrows + lo, n, 1) for _, src, lo, n in k_got],
         axis=1,
     )
-    kv = jnp.dot(tokens_perm, kv_weight, preferred_element_type=jnp.float32).astype(jnp.bfloat16)
-    incoming = kv.reshape(ncrop, CAP, CT, 2 * width)
+
+    def project(got):
+        weight = jnp.concatenate([p for p, _, _, _ in got], axis=0)
+        out = jnp.dot(tokens_perm, weight, preferred_element_type=jnp.float32)
+        return out.astype(jnp.bfloat16)
+
+    keys_all = project(k_got)
+    vals_all = project(v_got)
 
     def q_part(acc, piece, src, lo, n):
         cols = lax.dynamic_slice_in_dim(queries_in, src * wrows + lo, n, 1)
@@ -100,8 +119,8 @@
         acc = q_part(acc, lax.ppermute(bwd[split:], "crop", bwd_perm), src, split, wrows - split)
     query = acc.astype(jnp.bfloat16)
     nslots = ncrop * CAP
-    keys_all = incoming[..., :width].reshape(nslots * CT, heads_here, HD)
-    vals_all = incoming[..., width:].reshape(nslots * CT, heads_here, HD)
+    keys_all = keys_all.reshape(nslots * CT, heads_here, HD)
+    vals_all = vals_all.reshape(nslots * CT, heads_here, HD)
     query_row = query.reshape(rows_here, GR, heads_here, HD)
     in_use = (jnp.arange(NB, dtype=jnp.int32)[None, :] < region_len[:, None])[:, :, None]
     hits = region_slots[:, :, None] == jnp.arange(nslots, dtype=jnp.int32)[None, None, :]

time: 296 us -> 309 us (1.044)
  starting transfers between devices: 25 us -> 42.6 us
  between operations: 23.2 us -> 9.51 us
  local copies, waits for them, and re-layouts: 35.9 us -> 44.2 us
    ppermute x8 -> x22, waiting for transfers between devices: 126 us -> 149 us  [the longest x6 50.2 us: ring_pieces(): bwd[i] = lax.ppermute(bwd[i], 'crop', bwd_perm)]
    ppermute x8 -> x22, starting transfers between devices: 9.06 us -> 26.1 us  [the longest x6 13 us: ring_pieces(): fwd[i] = lax.ppermute(fwd[i], 'crop', fwd_perm)]
    ppermute x3, waiting for transfers between devices: 41.4 us -> 29.5 us  [body(): fwd = lax.ppermute(fwd, 'crop', fwd_perm)]
    all_to_all x1, waiting for transfers between devices: 9.3 us -> 0.01 us  [body(): lax.all_to_all(chosen, 'crop', split_axis=0, concat_axis=0, tiled=True)]
    dynamic_update_slice x0 -> x8, local copies, waits for them, and re-layouts: none -> 7.06 us  [the longest x6 5.86 us: head_gather(): lax.dynamic_update_slice(full, part, (0, (hme - k) % nhead * x.shape[1]))]
    dot_general x1 -> x2, matrix products: 8.28 us -> 4.79 us  [project(): out = jnp.dot(tokens_perm, weight, preferred_element_type=jnp.float32)]
    ppermute x3, starting transfers between devices: 1.69 us -> 5.06 us  [body(): fwd = lax.ppermute(fwd, 'crop', fwd_perm)]
    unnamed x48 -> x40, local copies, waits for them, and re-layouts: 29.3 us -> 27.9 us
  transfers between devices with their start and end apart: 19 -> 31, of which waited for: 13 -> 15; matrix products, arithmetic and copies ran while one was open for 17% -> 19% of each run, Pallas kernels for 0% -> 0%
where the time goes in v7:
time: 309 us; the launch traced here: 308 us
  waiting for transfers between devices  185 us (60%)
  local copies, waits for them, and re-layouts  44.2 us (14%)
  starting transfers between devices  42.6 us (14%)
  matrix products  22.1 us (7%)
  between operations  9.51 us (3%)
  other arithmetic  5 us (2%)
    ppermute x6, waiting for transfers between devices, ring_pieces(): bwd[i] = lax.ppermute(bwd[i], 'crop', bwd_perm)  50.2 us
    ppermute x2, waiting for transfers between devices, ring_pieces(): top = lax.ppermute(fwd[i][:split], 'crop', fwd_perm)  39.8 us
    ppermute x6, waiting for transfers between devices, ring_pieces(): fwd[i] = lax.ppermute(fwd[i], 'crop', fwd_perm)  36.4 us
    ppermute x3, waiting for transfers between devices, body(): fwd = lax.ppermute(fwd, 'crop', fwd_perm)  29.5 us
    unnamed x40, local copies, waits for them, and re-layouts  27.9 us
    ppermute x2, waiting for transfers between devices, ring_pieces(): bottom = lax.ppermute(bwd[i][split:], 'crop', bwd_perm)  22.6 us
    dot_general x9, matrix products, q_part(): return acc + jnp.dot(cols, piece, preferred_element_type=jnp.float32)  15.6 us
    ppermute x6, starting transfers between devices, ring_pieces(): fwd[i] = lax.ppermute(fwd[i], 'crop', fwd_perm)  13 us
  transfers between devices with their start and end apart: 31, of which 15 were waited for; matrix products, arithmetic and copies ran while one was open for 19% of the time, Pallas kernels for 0%

profile of v7, /device:TPU:0, one launch (start us, length us, event | category | flops | bytes accessed | tf_op | source)
XLA Modules:
  0.0 308.2 jit_solution(832060816154196835)
XLA Ops:
  0.0 3.0 collective-permute-start
  18.6 8.7 %collective-permute-done = bf16[512,1024]{1,0:T(8,128)(2,1)} collective-permute-done((bf16[512,1024]{1,0:T(8,128)(2,1)}, bf16[512,1024]{1,0:T(8,128)(2,1)}, u32[]{:S(2)}, u32[]{:S(2)}) %collective-permute-start) | collective-permute-done | bytes 1048608 | tf_op jit(solution)/shard_map/ppermute | solution.py:69
  31.8 2.4 constant_dynamic-update-slice_fusion.8
  34.1 14.8 %collective-permute-done.1 = bf16[512,1024]{1,0:T(8,128)(2,1)} collective-permute-done((bf16[512,1024]{1,0:T(8,128)(2,1)}, bf16[512,1024]{1,0:T(8,128)(2,1)}, u32[]{:S(2)}, u32[]{:S(2)}) %collective-permute-start.1) | collective-permute-done | bytes 1048608 | tf_op jit(solution)/shard_map/ppermute | solution.py:69
  49.2 2.3 constant_dynamic-update-slice_fusion.17
  51.5 2.5 broadcast_in_dim.35
  55.1 5.9 %all-to-all-start = ((bf16[8,2,16,1024]{3,2,1,0:T(8,128)(2,1)}), bf16[8,2,16,1024]{3,2,1,0:T(8,128)(2,1)S(1)}, u32[]{:S(2)}, u32[]{:S(2)}) async-start(bf16[8,2,16,1024]{3,2,1,0:T(8,128)(2,1)} %bitcast.2), calls=%async_computation | async-start | bytes 1048576 | tf_op jit(solution)/shard_map/all_to_all | solution.py:86
  65.1 2.3 constant_dynamic-update-slice_fusion.7
  67.3 2.3 constant_dynamic-update-slice_fusion.16
  69.7 2.3 constant_dynamic-update-slice_fusion.6
  72.0 2.3 constant_dynamic-update-slice_fusion.15
  75.4 2.3 constant_dynamic-update-slice_fusion.19
  77.7 2.3 constant_dynamic-update-slice_fusion.18
  80.3 13.0 %collective-permute-done.6 = bf16[512,1024]{1,0:T(8,128)(2,1)S(1)} collective-permute-done((bf16[512,1024]{1,0:T(8,128)(2,1)}, bf16[512,1024]{1,0:T(8,128)(2,1)S(1)}, u32[]{:S(2)}, u32[]{:S(2)}) %collective-permute-start.6) | collective-permute-done | bytes 1048608 | tf_op jit(solution)/shard_map/ppermute | solution.py:69
  95.8 2.7 collective-permute-start.9
  98.4 19.8 %collective-permute-done.12 = bf16[512,1024]{1,0:T(8,128)(2,1)} collective-permute-done((bf16[512,1024]{1,0:T(8,128)(2,1)}, bf16[512,1024]{1,0:T(8,128)(2,1)}, u32[]{:S(2)}, u32[]{:S(2)}) %collective-permute-start.12) | collective-permute-done | bytes 1048608 | tf_op jit(solution)/shard_map/ppermute | solution.py:70
  119.3 2.3 constant_dynamic-update-slice_fusion.4
  121.6 2.3 constant_dynamic-update-slice_fusion.14
  123.9 2.3 constant_dynamic-update-slice_fusion.13
  126.2 4.3 %collective-permute-start.8 = (bf16[512,1024]{1,0:T(8,128)(2,1)S(1)}, bf16[512,1024]{1,0:T(8,128)(2,1)S(1)}, u32[]{:S(2)}, u32[]{:S(2)}) collective-permute-start(bf16[512,1024]{1,0:T(8,128)(2,1)S(1)} %collective-permute-done.6), channel_id=1, source_target_pairs={{0,8},{8,16},{16,24},{24,28},{28,20},{20,12},{12,4},{4,0},{1,9},{9... | collective-permute-start | bytes 3145736 | tf_op jit(solution)/shard_map/ppermute | solution.py:69
  132.8 29.4 %collective-permute-done.13 = bf16[512,1024]{1,0:T(8,128)(2,1)S(1)} collective-permute-done((bf16[512,1024]{1,0:T(8,128)(2,1)}, bf16[512,1024]{1,0:T(8,128)(2,1)S(1)}, u32[]{:S(2)}, u32[]{:S(2)}) %collective-permute-start.13) | collective-permute-done | bytes 1048608 | tf_op jit(solution)/shard_map/ppermute | solution.py:70
  162.4 4.0 %collective-permute-start.15 = (bf16[256,1024]{1,0:T(8,128)(2,1)S(1)}, bf16[256,1024]{1,0:T(8,128)(2,1)S(1)}, u32[]{:S(2)}, u32[]{:S(2)}) collective-permute-start(bf16[256,1024]{1,0:T(8,128)(2,1)S(1)} %slice.28), channel_id=1, source_target_pairs={{0,4},{8,0},{16,8},{24,16},{28,24},{20,28},{12,20},{4,12},{1,5},{9... | collective-permute-start | bytes 1572872 | tf_op jit(solution)/shard_map/ppermute | solution.py:77
  166.5 12.9 %collective-permute-done.14 = bf16[256,1024]{1,0:T(8,128)(2,1)S(1)} collective-permute-done((bf16[256,1024]{1,0:T(8,128)(2,1)S(1)}, bf16[256,1024]{1,0:T(8,128)(2,1)S(1)}, u32[]{:S(2)}, u32[]{:S(2)}) %collective-permute-start.14) | collective-permute-done | bytes 524320 | tf_op jit(solution)/shard_map/ppermute | solution.py:77
  179.4 9.7 %collective-permute-done.15 = bf16[256,1024]{1,0:T(8,128)(2,1)S(1)} collective-permute-done((bf16[256,1024]{1,0:T(8,128)(2,1)S(1)}, bf16[256,1024]{1,0:T(8,128)(2,1)S(1)}, u32[]{:S(2)}, u32[]{:S(2)}) %collective-permute-start.15) | collective-permute-done | bytes 524320 | tf_op jit(solution)/shard_map/ppermute | solution.py:77
  195.4 31.0 %collective-permute-done.10 = bf16[256,1024]{1,0:T(8,128)(2,1)S(1)} collective-permute-done((bf16[256,1024]{1,0:T(8,128)(2,1)S(1)}, bf16[256,1024]{1,0:T(8,128)(2,1)S(1)}, u32[]{:S(2)}, u32[]{:S(2)}) %collective-permute-start.10) | collective-permute-done | bytes 524320 | tf_op jit(solution)/shard_map/ppermute | solution.py:76
  226.5 8.8 %collective-permute-done.18 = bf16[256,1024]{1,0:T(8,128)(2,1)S(1)} collective-permute-done((bf16[256,1024]{1,0:T(8,128)(2,1)S(1)}, bf16[256,1024]{1,0:T(8,128)(2,1)S(1)}, u32[]{:S(2)}, u32[]{:S(2)}) %collective-permute-start.18) | collective-permute-done | bytes 524320 | tf_op jit(solution)/shard_map/ppermute | solution.py:76
  238.4 2.4 fusion.8
  241.8 2.4 fusion.9
  244.2 15.6 %collective-permute-done.24 = bf16[512,1024]{1,0:T(8,128)(2,1)S(1)} collective-permute-done((bf16[512,1024]{1,0:T(8,128)(2,1)S(1)}, bf16[512,1024]{1,0:T(8,128)(2,1)S(1)}, u32[]{:S(2)}, u32[]{:S(2)}) %collective-permute-start.24) | collective-permute-done | bytes 1048608 | tf_op jit(solution)/shard_map/ppermute | solution.py:112
  269.7 13.8 %collective-permute-done.26 = bf16[512,1024]{1,0:T(8,128)(2,1)S(1)} collective-permute-done((bf16[512,1024]{1,0:T(8,128)(2,1)S(1)}, bf16[512,1024]{1,0:T(8,128)(2,1)S(1)}, u32[]{:S(2)}, u32[]{:S(2)}) %collective-permute-start.26) | collective-permute-done | bytes 1048608 | tf_op jit(solution)/shard_map/ppermute | solution.py:112
  289.4 5.3 %collective-permute-done.28 = bf16[256,1024]{1,0:T(8,128)(2,1)S(1)} collective-permute-done((bf16[256,1024]{1,0:T(8,128)(2,1)S(1)}, bf16[256,1024]{1,0:T(8,128)(2,1)S(1)}, u32[]{:S(2)}, u32[]{:S(2)}) %collective-permute-start.28) | collective-permute-done | bytes 524320 | tf_op jit(solution)/shard_map/ppermute | solution.py:118
  301.8 3.5 %fusion.49 = (f32[16,8,32]{2,0,1:T(8,128)S(1)}, f32[16,8,32,256]{3,2,0,1:T(8,128)S(1)}) fusion(f32[8,256,16,32]{1,3,2,0:T(8,128)S(1)} %bitcast.72, pred[16,256]{1,0:T(8,128)(4,1)S(1)} %broadcast_in_dim.33), kind=kOutput, calls=%fused_computation.94 | output fusion | flops 6291711 | bytes 8409088 | tf_op jit(solution)/shard_map/sub | solution.py:136
  (115 shorter events, 60.2 us)
Async XLA Ops:
  0.0 27.3 %collective-permute-start = (bf16[512,1024]{1,0:T(8,128)(2,1)}, bf16[512,1024]{1,0:T(8,128)(2,1)}, u32[]{:S(2)}, u32[]{:S(2)}) collective-permute-start(bf16[512,1024]{1,0:T(8,128)(2,1)} %param.13), channel_id=1, source_target_pairs={{0,8},{8,16},{16,24},{24,28},{28,20},{20,12},{12,4},{4,0},{1,9},{9... | collective-permute-start | bytes 3145736 | tf_op jit(solution)/shard_map/ppermute | solution.py:69
  3.0 45.9 %collective-permute-start.1 = (bf16[512,1024]{1,0:T(8,128)(2,1)}, bf16[512,1024]{1,0:T(8,128)(2,1)}, u32[]{:S(2)}, u32[]{:S(2)}) collective-permute-start(bf16[512,1024]{1,0:T(8,128)(2,1)} %param.14), channel_id=1, source_target_pairs={{0,8},{8,16},{16,24},{24,28},{28,20},{20,12},{12,4},{4,0},{1,9},{9... | collective-permute-start | bytes 3145736 | tf_op jit(solution)/shard_map/ppermute | solution.py:69
  4.6 56.4 %collective-permute-start.5 = (bf16[512,1024]{1,0:T(8,128)(2,1)}, bf16[512,1024]{1,0:T(8,128)(2,1)}, u32[]{:S(2)}, u32[]{:S(2)}) collective-permute-start(bf16[512,1024]{1,0:T(8,128)(2,1)} %param.14), channel_id=1, source_target_pairs={{0,4},{8,0},{16,8},{24,16},{28,24},{20,28},{12,20},{4,12},{1,5},{9... | collective-permute-start | bytes 3145736 | tf_op jit(solution)/shard_map/ppermute | solution.py:70
  5.1 58.0 %collective-permute-start.11 = (bf16[512,1024]{1,0:T(8,128)(2,1)}, bf16[512,1024]{1,0:T(8,128)(2,1)}, u32[]{:S(2)}, u32[]{:S(2)}) collective-permute-start(bf16[512,1024]{1,0:T(8,128)(2,1)} %param.13), channel_id=1, source_target_pairs={{0,4},{8,0},{16,8},{24,16},{28,24},{20,28},{12,20},{4,12},{1,5},{9... | collective-permute-start | bytes 3145736 | tf_op jit(solution)/shard_map/ppermute | solution.py:70
  5.1 58.0 %collective-permute-start.19 = (bf16[512,1024]{1,0:T(8,128)(2,1)}, bf16[512,1024]{1,0:T(8,128)(2,1)S(1)}, u32[]{:S(2)}, u32[]{:S(2)}) collective-permute-start(bf16[512,1024]{1,0:T(8,128)(2,1)} %param.10), channel_id=1, source_target_pairs={{0,1},{1,2},{2,3},{3,0},{4,5},{5,6},{6,7},{7,4},{8,9},{9,10},{10,1... | collective-permute-start | bytes 3145736 | tf_op jit(solution)/shard_map/ppermute | solution.py:51
  27.3 42.4 %collective-permute-start.20 = (bf16[512,1024]{1,0:T(8,128)(2,1)}, bf16[512,1024]{1,0:T(8,128)(2,1)}, u32[]{:S(2)}, u32[]{:S(2)}) collective-permute-start(bf16[512,1024]{1,0:T(8,128)(2,1)} %param.10), channel_id=1, source_target_pairs={{0,2},{1,3},{2,0},{3,1},{4,6},{5,7},{6,4},{7,5},{8,10},{9,11},{10,... | collective-permute-start | bytes 3145736 | tf_op jit(solution)/shard_map/ppermute | solution.py:51
  48.9 28.8 %collective-permute-start.21 = (bf16[512,1024]{1,0:T(8,128)(2,1)}, bf16[512,1024]{1,0:T(8,128)(2,1)}, u32[]{:S(2)}, u32[]{:S(2)}) collective-permute-start(bf16[512,1024]{1,0:T(8,128)(2,1)} %param.10), channel_id=1, source_target_pairs={{0,3},{1,0},{2,1},{3,2},{4,7},{5,4},{6,5},{7,6},{8,11},{9,8},{10,9... | collective-permute-start | bytes 3145736 | tf_op jit(solution)/shard_map/ppermute | solution.py:51
  55.1 24.8 %all-to-all-start = ((bf16[8,2,16,1024]{3,2,1,0:T(8,128)(2,1)}), bf16[8,2,16,1024]{3,2,1,0:T(8,128)(2,1)S(1)}, u32[]{:S(2)}, u32[]{:S(2)}) async-start(bf16[8,2,16,1024]{3,2,1,0:T(8,128)(2,1)} %bitcast.2), calls=%async_computation | async-start | bytes 1048576 | tf_op jit(solution)/shard_map/all_to_all | solution.py:86
  61.0 32.2 %collective-permute-start.6 = (bf16[512,1024]{1,0:T(8,128)(2,1)}, bf16[512,1024]{1,0:T(8,128)(2,1)S(1)}, u32[]{:S(2)}, u32[]{:S(2)}) collective-permute-start(bf16[512,1024]{1,0:T(8,128)(2,1)} %collective-permute-done.1), channel_id=1, source_target_pairs={{0,8},{8,16},{16,24},{24,28},{28,20},{20,12},{12,4},{4,0},{1,9},{9... | collective-permute-start | bytes 3145736 | tf_op jit(solution)/shard_map/ppermute | solution.py:69
  63.0 32.7 %collective-permute-start.7 = (bf16[512,1024]{1,0:T(8,128)(2,1)}, bf16[512,1024]{1,0:T(8,128)(2,1)}, u32[]{:S(2)}, u32[]{:S(2)}) collective-permute-start(bf16[512,1024]{1,0:T(8,128)(2,1)} %collective-permute-done.5), channel_id=1, source_target_pairs={{0,4},{8,0},{16,8},{24,16},{28,24},{20,28},{12,20},{4,12},{1,5},{9... | collective-permute-start | bytes 3145736 | tf_op jit(solution)/shard_map/ppermute | solution.py:70
  63.1 55.1 %collective-permute-start.12 = (bf16[512,1024]{1,0:T(8,128)(2,1)}, bf16[512,1024]{1,0:T(8,128)(2,1)}, u32[]{:S(2)}, u32[]{:S(2)}) collective-permute-start(bf16[512,1024]{1,0:T(8,128)(2,1)} %collective-permute-done.11), channel_id=1, source_target_pairs={{0,4},{8,0},{16,8},{24,16},{28,24},{20,28},{12,20},{4,12},{1,5},{9... | collective-permute-start | bytes 3145736 | tf_op jit(solution)/shard_map/ppermute | solution.py:70
  69.6 52.0 %collective-permute-start.16 = (bf16[512,1024]{1,0:T(8,128)(2,1)}, bf16[512,1024]{1,0:T(8,128)(2,1)}, u32[]{:S(2)}, u32[]{:S(2)}) collective-permute-start(bf16[512,1024]{1,0:T(8,128)(2,1)} %collective-permute-done), channel_id=1, source_target_pairs={{0,8},{8,16},{16,24},{24,28},{28,20},{20,12},{12,4},{4,0},{1,9},{9... | collective-permute-start | bytes 3145736 | tf_op jit(solution)/shard_map/ppermute | solution.py:69
  80.0 46.2 %collective-permute-start.2 = (bf16[256,1024]{1,0:T(8,128)(2,1)S(1)}, bf16[256,1024]{1,0:T(8,128)(2,1)S(1)}, u32[]{:S(2)}, u32[]{:S(2)}) collective-permute-start(bf16[256,1024]{1,0:T(8,128)(2,1)S(1)} %bitcast.76), channel_id=1, source_target_pairs={{0,1},{1,2},{2,3},{3,0},{4,5},{5,6},{6,7},{7,4},{8,9},{9,10},{10,1... | collective-permute-start | bytes 1572872 | tf_op jit(solution)/shard_map/ppermute | solution.py:51
  93.2 37.3 %collective-permute-start.3 = (bf16[256,1024]{1,0:T(8,128)(2,1)S(1)}, bf16[256,1024]{1,0:T(8,128)(2,1)S(1)}, u32[]{:S(2)}, u32[]{:S(2)}) collective-permute-start(bf16[256,1024]{1,0:T(8,128)(2,1)S(1)} %bitcast.78), channel_id=1, source_target_pairs={{0,2},{1,3},{2,0},{3,1},{4,6},{5,7},{6,4},{7,5},{8,10},{9,11},{10,... | collective-permute-start | bytes 1572872 | tf_op jit(solution)/shard_map/ppermute | solution.py:51
  95.8 66.5 %collective-permute-start.9 = (bf16[512,1024]{1,0:T(8,128)(2,1)}, bf16[512,1024]{1,0:T(8,128)(2,1)S(1)}, u32[]{:S(2)}, u32[]{:S(2)}) collective-permute-start(bf16[512,1024]{1,0:T(8,128)(2,1)} %collective-permute-done.7), channel_id=1, source_target_pairs={{0,4},{8,0},{16,8},{24,16},{28,24},{20,28},{12,20},{4,12},{1,5},{9... | collective-permute-start | bytes 3145736 | tf_op jit(solution)/shard_map/ppermute | solution.py:70
  118.2 44.0 %collective-permute-start.13 = (bf16[512,1024]{1,0:T(8,128)(2,1)}, bf16[512,1024]{1,0:T(8,128)(2,1)S(1)}, u32[]{:S(2)}, u32[]{:S(2)}) collective-permute-start(bf16[512,1024]{1,0:T(8,128)(2,1)} %collective-permute-done.12), channel_id=1, source_target_pairs={{0,4},{8,0},{16,8},{24,16},{28,24},{20,28},{12,20},{4,12},{1,5},{9... | collective-permute-start | bytes 3145736 | tf_op jit(solution)/shard_map/ppermute | solution.py:70
  121.6 11.1 %collective-permute-start.4 = (bf16[256,1024]{1,0:T(8,128)(2,1)S(1)}, bf16[256,1024]{1,0:T(8,128)(2,1)S(1)}, u32[]{:S(2)}, u32[]{:S(2)}) collective-permute-start(bf16[256,1024]{1,0:T(8,128)(2,1)S(1)} %bitcast.79), channel_id=1, source_target_pairs={{0,3},{1,0},{2,1},{3,2},{4,7},{5,4},{6,5},{7,6},{8,11},{9,8},{10,9... | collective-permute-start | bytes 1572872 | tf_op jit(solution)/shard_map/ppermute | solution.py:51
  126.2 64.7 %collective-permute-start.8 = (bf16[512,1024]{1,0:T(8,128)(2,1)S(1)}, bf16[512,1024]{1,0:T(8,128)(2,1)S(1)}, u32[]{:S(2)}, u32[]{:S(2)}) collective-permute-start(bf16[512,1024]{1,0:T(8,128)(2,1)S(1)} %collective-permute-done.6), channel_id=1, source_target_pairs={{0,8},{8,16},{16,24},{24,28},{28,20},{20,12},{12,4},{4,0},{1,9},{9... | collective-permute-start | bytes 3145736 | tf_op jit(solution)/shard_map/ppermute | solution.py:69
  130.5 58.6 %copy-start.3 = (bf16[512,1024]{1,0:T(8,128)(2,1)S(1)}, bf16[512,1024]{1,0:T(8,128)(2,1)}, u32[]{:S(2)}) copy-start(bf16[512,1024]{1,0:T(8,128)(2,1)} %param.12) | copy-start | bytes 3145732
  130.5 60.5 %collective-permute-start.17 = (bf16[512,1024]{1,0:T(8,128)(2,1)}, bf16[512,1024]{1,0:T(8,128)(2,1)S(1)}, u32[]{:S(2)}, u32[]{:S(2)}) collective-permute-start(bf16[512,1024]{1,0:T(8,128)(2,1)} %collective-permute-done.16), channel_id=1, source_target_pairs={{0,8},{8,16},{16,24},{24,28},{28,20},{20,12},{12,4},{4,0},{1,9},{9... | collective-permute-start | bytes 3145736 | tf_op jit(solution)/shard_map/ppermute | solution.py:69
  162.2 17.2 %collective-permute-start.14 = (bf16[256,1024]{1,0:T(8,128)(2,1)S(1)}, bf16[256,1024]{1,0:T(8,128)(2,1)S(1)}, u32[]{:S(2)}, u32[]{:S(2)}) collective-permute-start(bf16[256,1024]{1,0:T(8,128)(2,1)S(1)} %slice.27), channel_id=1, source_target_pairs={{0,4},{8,0},{16,8},{24,16},{28,24},{20,28},{12,20},{4,12},{1,5},{9... | collective-permute-start | bytes 1572872 | tf_op jit(solution)/shard_map/ppermute | solution.py:77
  162.4 26.8 %collective-permute-start.15 = (bf16[256,1024]{1,0:T(8,128)(2,1)S(1)}, bf16[256,1024]{1,0:T(8,128)(2,1)S(1)}, u32[]{:S(2)}, u32[]{:S(2)}) collective-permute-start(bf16[256,1024]{1,0:T(8,128)(2,1)S(1)} %slice.28), channel_id=1, source_target_pairs={{0,4},{8,0},{16,8},{24,16},{28,24},{20,28},{12,20},{4,12},{1,5},{9... | collective-permute-start | bytes 1572872 | tf_op jit(solution)/shard_map/ppermute | solution.py:77
  189.1 47.8 %collective-permute-start.22 = (bf16[512,1024]{1,0:T(8,128)(2,1)S(1)}, bf16[512,1024]{1,0:T(8,128)(2,1)S(1)}, u32[]{:S(2)}, u32[]{:S(2)}) collective-permute-start(bf16[512,1024]{1,0:T(8,128)(2,1)S(1)} %copy-done.3), channel_id=1, source_target_pairs={{0,8},{8,16},{16,24},{24,28},{28,20},{20,12},{12,4},{4,0},{1,9},{9... | collective-permute-start | bytes 3145736 | tf_op jit(solution)/shard_map/ppermute | solution.py:112
  190.9 35.5 %collective-permute-start.10 = (bf16[256,1024]{1,0:T(8,128)(2,1)S(1)}, bf16[256,1024]{1,0:T(8,128)(2,1)S(1)}, u32[]{:S(2)}, u32[]{:S(2)}) collective-permute-start(bf16[256,1024]{1,0:T(8,128)(2,1)S(1)} %slice.26), channel_id=1, source_target_pairs={{0,8},{8,16},{16,24},{24,28},{28,20},{20,12},{12,4},{4,0},{1,9},{9... | collective-permute-start | bytes 1572872 | tf_op jit(solution)/shard_map/ppermute | solution.py:76
  191.1 44.2 %collective-permute-start.18 = (bf16[256,1024]{1,0:T(8,128)(2,1)S(1)}, bf16[256,1024]{1,0:T(8,128)(2,1)S(1)}, u32[]{:S(2)}, u32[]{:S(2)}) collective-permute-start(bf16[256,1024]{1,0:T(8,128)(2,1)S(1)} %slice.29), channel_id=1, source_target_pairs={{0,8},{8,16},{16,24},{24,28},{28,20},{20,12},{12,4},{4,0},{1,9},{9... | collective-permute-start | bytes 1572872 | tf_op jit(solution)/shard_map/ppermute | solution.py:76
  193.4 47.4 %collective-permute-start.23 = (bf16[512,1024]{1,0:T(8,128)(2,1)S(1)}, bf16[512,1024]{1,0:T(8,128)(2,1)S(1)}, u32[]{:S(2)}, u32[]{:S(2)}) collective-permute-start(bf16[512,1024]{1,0:T(8,128)(2,1)S(1)} %copy-done.3), channel_id=1, source_target_pairs={{0,4},{8,0},{16,8},{24,16},{28,24},{20,28},{12,20},{4,12},{1,5},{9... | collective-permute-start | bytes 3145736 | tf_op jit(solution)/shard_map/ppermute | solution.py:113
  237.0 22.9 %collective-permute-start.24 = (bf16[512,1024]{1,0:T(8,128)(2,1)S(1)}, bf16[512,1024]{1,0:T(8,128)(2,1)S(1)}, u32[]{:S(2)}, u32[]{:S(2)}) collective-permute-start(bf16[512,1024]{1,0:T(8,128)(2,1)S(1)} %collective-permute-done.22), channel_id=1, source_target_pairs={{0,8},{8,16},{16,24},{24,28},{28,20},{20,12},{12,4},{4,0},{1,9},{9... | collective-permute-start | bytes 3145736 | tf_op jit(solution)/shard_map/ppermute | solution.py:112
  240.8 22.8 %collective-permute-start.25 = (bf16[512,1024]{1,0:T(8,128)(2,1)S(1)}, bf16[512,1024]{1,0:T(8,128)(2,1)S(1)}, u32[]{:S(2)}, u32[]{:S(2)}) collective-permute-start(bf16[512,1024]{1,0:T(8,128)(2,1)S(1)} %collective-permute-done.23), channel_id=1, source_target_pairs={{0,4},{8,0},{16,8},{24,16},{28,24},{20,28},{12,20},{4,12},{1,5},{9... | collective-permute-start | bytes 3145736 | tf_op jit(solution)/shard_map/ppermute | solution.py:113
  259.9 23.6 %collective-permute-start.26 = (bf16[512,1024]{1,0:T(8,128)(2,1)S(1)}, bf16[512,1024]{1,0:T(8,128)(2,1)S(1)}, u32[]{:S(2)}, u32[]{:S(2)}) collective-permute-start(bf16[512,1024]{1,0:T(8,128)(2,1)S(1)} %collective-permute-done.24), channel_id=1, source_target_pairs={{0,8},{8,16},{16,24},{24,28},{28,20},{20,12},{12,4},{4,0},{1,9},{9... | collective-permute-start | bytes 3145736 | tf_op jit(solution)/shard_map/ppermute | solution.py:112
  263.6 21.9 %collective-permute-start.27 = (bf16[512,1024]{1,0:T(8,128)(2,1)S(1)}, bf16[512,1024]{1,0:T(8,128)(2,1)S(1)}, u32[]{:S(2)}, u32[]{:S(2)}) collective-permute-start(bf16[512,1024]{1,0:T(8,128)(2,1)S(1)} %collective-permute-done.25), channel_id=1, source_target_pairs={{0,4},{8,0},{16,8},{24,16},{28,24},{20,28},{12,20},{4,12},{1,5},{9... | collective-permute-start | bytes 3145736 | tf_op jit(solution)/shard_map/ppermute | solution.py:113
  283.5 11.2 %collective-permute-start.28 = (bf16[256,1024]{1,0:T(8,128)(2,1)S(1)}, bf16[256,1024]{1,0:T(8,128)(2,1)S(1)}, u32[]{:S(2)}, u32[]{:S(2)}) collective-permute-start(bf16[256,1024]{1,0:T(8,128)(2,1)S(1)} %slice.30), channel_id=1, source_target_pairs={{0,8},{8,16},{16,24},{24,28},{28,20},{20,12},{12,4},{4,0},{1,9},{9... | collective-permute-start | bytes 1572872 | tf_op jit(solution)/shard_map/ppermute | solution.py:118
  285.5 11.4 %collective-permute-start.29 = (bf16[256,1024]{1,0:T(8,128)(2,1)S(1)}, bf16[256,1024]{1,0:T(8,128)(2,1)S(1)}, u32[]{:S(2)}, u32[]{:S(2)}) collective-permute-start(bf16[256,1024]{1,0:T(8,128)(2,1)S(1)} %slice.31), channel_id=1, source_target_pairs={{0,4},{8,0},{16,8},{24,16},{28,24},{20,28},{12,20},{4,12},{1,5},{9... | collective-permute-start | bytes 1572872 | tf_op jit(solution)/shard_map/ppermute | solution.py:119
  (5 other events, 117.4 us)

commit v8 on v6

--- a/solution.py
+++ b/solution.py
@@ -44,9 +44,6 @@
     queries_in = lax.all_gather(global_rows, "head", axis=1, tiled=True)
     picks = fetch_slots[0]
     blocks = crop_tokens.reshape(-1, CT, crop_tokens.shape[1])
-    chosen = blocks[picks]
-    delivered = lax.all_to_all(chosen, "crop", split_axis=0, concat_axis=0, tiled=True)
-    delivered = delivered.reshape(-1, crop_tokens.shape[1])
 
     steps_fwd = ncrop // 2
     steps_bwd = (ncrop - 1) // 2
@@ -73,6 +70,10 @@
     )
     kv_got[-1] = (last_a,) + kv_got[-1][1:]
     kv_got[-2] = (last_b,) + kv_got[-2][1:]
+    chosen, first = lax.optimization_barrier((blocks[picks], kv_got[1][0]))
+    kv_got[1] = (first,) + kv_got[1][1:]
+    delivered = lax.all_to_all(chosen, "crop", split_axis=0, concat_axis=0, tiled=True)
+    delivered = delivered.reshape(-1, crop_tokens.shape[1])
     tokens_in = lax.all_gather(delivered, "head", axis=1, tiled=True)
     kv_weight = jnp.concatenate([p for p, _, _, _ in kv_got], axis=0)
     tokens_perm = jnp.concatenate(

time: 296 us -> 343 us (1.16)
  waiting for transfers between devices: 183 us -> 227 us
    ppermute x3, waiting for transfers between devices: 1.96 us -> 45.1 us  [ring_pieces(): fwd = lax.ppermute(fwd, 'crop', fwd_perm)]
    all_to_all x1, waiting for transfers between devices: 9.3 us -> 13.4 us  [body(): lax.all_to_all(chosen, 'crop', split_axis=0, concat_axis=0, tiled=True)]
    ppermute x3, starting transfers between devices: 5.14 us -> 8.9 us  [ring_pieces(): fwd = lax.ppermute(fwd, 'crop', fwd_perm)]
    unnamed x48 -> x50, local copies, waits for them, and re-layouts: 29.3 us -> 29.9 us
  transfers between devices with their start and end apart: 19 -> 19, of which waited for: 13 -> 14; matrix products, arithmetic and copies ran while one was open for 17% -> 15% of each run, Pallas kernels for 0% -> 0%
where the time goes in v8:
time: 343 us
  waiting for transfers between devices  227 us (66%)
  local copies, waits for them, and re-layouts  38.3 us (11%)
  starting transfers between devices  27.6 us (8%)
  matrix products  22.8 us (7%)
  between operations  22.7 us (7%)
  other arithmetic  3.67 us (1%)
    ppermute x3, waiting for transfers between devices, ring_pieces(): bwd = lax.ppermute(bwd, 'crop', bwd_perm)  104 us
    ppermute x3, waiting for transfers between devices, ring_pieces(): fwd = lax.ppermute(fwd, 'crop', fwd_perm)  45.1 us
    ppermute x3, waiting for transfers between devices, body(): fwd = lax.ppermute(fwd, 'crop', fwd_perm)  41.1 us
    unnamed x50, local copies, waits for them, and re-layouts  29.9 us
    ppermute x1, waiting for transfers between devices, ring_pieces(): lax.ppermute(bwd[split:], 'crop', bwd_perm)  13.6 us
    all_to_all x1, waiting for transfers between devices, body(): lax.all_to_all(chosen, 'crop', split_axis=0, concat_axis=0, tiled=True)  13.4 us
    dot_general x9, matrix products, q_part(): return acc + jnp.dot(cols, piece, preferred_element_type=jnp.float32)  12.8 us
    ppermute x3, starting transfers between devices, ring_pieces(): fwd = lax.ppermute(fwd, 'crop', fwd_perm)  8.9 us
  transfers between devices with their start and end apart: 19, of which 14 were waited for; matrix products, arithmetic and copies ran while one was open for 15% of the time, Pallas kernels for 0%

profile of v8, /device:TPU:0, one launch (start us, length us, event | category | flops | bytes accessed | tf_op | source)
XLA Modules:
  0.0 342.5 jit_solution(2126134226643883827)
XLA Ops:
  6.5 3.1 constant_dynamic-update-slice_fusion.11
  11.3 3.1 collective-permute-start
  15.9 44.3 %collective-permute-done = bf16[512,2048]{1,0:T(8,128)(2,1)} collective-permute-done((bf16[512,2048]{1,0:T(8,128)(2,1)}, bf16[512,2048]{1,0:T(8,128)(2,1)}, u32[]{:S(2)}, u32[]{:S(2)}) %collective-permute-start) | collective-permute-done | bytes 2097184 | tf_op jit(solution)/shard_map/ppermute | solution.py:57
  60.3 6.1 %all-to-all-start = ((bf16[8,2,16,1024]{3,2,1,0:T(8,128)(2,1)}), bf16[8,2,16,1024]{3,2,1,0:T(8,128)(2,1)S(1)}, u32[]{:S(2)}, u32[]{:S(2)}) async-start(bf16[8,2,16,1024]{3,2,1,0:T(8,128)(2,1)} %bitcast.2), calls=%async_computation | async-start | bytes 1048576 | tf_op jit(solution)/shard_map/all_to_all | solution.py:75
  66.4 2.0 collective-permute-start.1
  68.3 13.4 %all-to-all-done = bf16[8,2,16,1024]{3,2,1,0:T(8,128)(2,1)S(1)} async-done(((bf16[8,2,16,1024]{3,2,1,0:T(8,128)(2,1)}), bf16[8,2,16,1024]{3,2,1,0:T(8,128)(2,1)S(1)}, u32[]{:S(2)}, u32[]{:S(2)}) %all-to-all-start) | async-done | bytes 524320 | tf_op jit(solution)/shard_map/all_to_all | solution.py:75
  82.6 38.5 %collective-permute-done.1 = bf16[512,2048]{1,0:T(8,128)(2,1)S(1)} collective-permute-done((bf16[512,2048]{1,0:T(8,128)(2,1)}, bf16[512,2048]{1,0:T(8,128)(2,1)S(1)}, u32[]{:S(2)}, u32[]{:S(2)}) %collective-permute-start.1) | collective-permute-done | bytes 2097184 | tf_op jit(solution)/shard_map/ppermute | solution.py:58
  121.2 4.3 %collective-permute-start.2 = (bf16[512,2048]{1,0:T(8,128)(2,1)}, bf16[512,2048]{1,0:T(8,128)(2,1)}, u32[]{:S(2)}, u32[]{:S(2)}) collective-permute-start(bf16[512,2048]{1,0:T(8,128)(2,1)} %collective-permute-done), channel_id=1, source_target_pairs={{0,8},{8,16},{16,24},{24,28},{28,20},{20,12},{12,4},{4,0},{1,9},{9... | collective-permute-start | bytes 6291464 | tf_op jit(solution)/shard_map/ppermute | solution.py:57
  125.5 44.2 %collective-permute-done.3 = bf16[512,2048]{1,0:T(8,128)(2,1)} collective-permute-done((bf16[512,2048]{1,0:T(8,128)(2,1)S(1)}, bf16[512,2048]{1,0:T(8,128)(2,1)}, u32[]{:S(2)}, u32[]{:S(2)}) %collective-permute-start.3) | collective-permute-done | bytes 2097184 | tf_op jit(solution)/shard_map/ppermute | solution.py:58
  182.5 3.3 constant_dynamic-update-slice_fusion.9
  187.3 3.2 constant_dynamic-update-slice_fusion.7
  190.6 3.2 constant_dynamic-update-slice_fusion.6
  193.8 21.4 %collective-permute-done.5 = bf16[512,2048]{1,0:T(8,128)(2,1)S(1)} collective-permute-done((bf16[512,2048]{1,0:T(8,128)(2,1)}, bf16[512,2048]{1,0:T(8,128)(2,1)S(1)}, u32[]{:S(2)}, u32[]{:S(2)}) %collective-permute-start.5) | collective-permute-done | bytes 2097184 | tf_op jit(solution)/shard_map/ppermute | solution.py:58
  217.1 2.3 slice.27
  224.9 13.6 %collective-permute-done.6 = bf16[256,2048]{1,0:T(8,128)(2,1)S(1)} collective-permute-done((bf16[256,2048]{1,0:T(8,128)(2,1)}, bf16[256,2048]{1,0:T(8,128)(2,1)S(1)}, u32[]{:S(2)}, u32[]{:S(2)}) %collective-permute-start.6) | collective-permute-done | bytes 1048608 | tf_op jit(solution)/shard_map/ppermute | solution.py:64
  238.4 4.1 %collective-permute-done.7 = bf16[256,2048]{1,0:T(8,128)(2,1)} collective-permute-done((bf16[256,2048]{1,0:T(8,128)(2,1)}, bf16[256,2048]{1,0:T(8,128)(2,1)}, u32[]{:S(2)}, u32[]{:S(2)}) %collective-permute-start.7) | collective-permute-done | bytes 1048608 | tf_op jit(solution)/shard_map/ppermute | solution.py:63
  242.5 2.3 collective-permute-start.9
  244.9 3.2 constant_dynamic-update-slice_fusion.5
  249.6 2.3 constant_dynamic-update-slice_fusion.3
  253.0 15.0 %collective-permute-done.8 = bf16[512,1024]{1,0:T(8,128)(2,1)} collective-permute-done((bf16[512,1024]{1,0:T(8,128)(2,1)S(1)}, bf16[512,1024]{1,0:T(8,128)(2,1)}, u32[]{:S(2)}, u32[]{:S(2)}) %collective-permute-start.8) | collective-permute-done | bytes 1048608 | tf_op jit(solution)/shard_map/ppermute | solution.py:94
  268.0 2.0 collective-permute-start.11
  270.0 8.3 %convolution_convert_fusion = bf16[256,2048]{1,0:T(8,128)(2,1)S(1)} fusion(bf16[256,4096]{1,0:T(8,128)(2,1)S(1)} %dynamic-slice_dynamic-update-slice_fusion.7, bf16[4096,2048]{1,0:T(8,128)(2,1)} %constant_dynamic-update-slice_fusion.2), kind=kOutput, calls=%fused_computation.6 | convolution fusion | flops 4295491584 | bytes 19922944 | tf_op jit(solution)/shard_map/dot_general | solution.py:83
  278.3 2.1 fusion.26
  280.4 10.9 %collective-permute-done.10 = bf16[512,1024]{1,0:T(8,128)(2,1)} collective-permute-done((bf16[512,1024]{1,0:T(8,128)(2,1)}, bf16[512,1024]{1,0:T(8,128)(2,1)}, u32[]{:S(2)}, u32[]{:S(2)}) %collective-permute-start.10) | collective-permute-done | bytes 1048608 | tf_op jit(solution)/shard_map/ppermute | solution.py:94
  291.6 2.1 collective-permute-start.13
  293.7 1.9 fusion.22
  295.6 1.9 fusion.24
  299.5 15.2 %collective-permute-done.12 = bf16[512,1024]{1,0:T(8,128)(2,1)S(1)} collective-permute-done((bf16[512,1024]{1,0:T(8,128)(2,1)}, bf16[512,1024]{1,0:T(8,128)(2,1)S(1)}, u32[]{:S(2)}, u32[]{:S(2)}) %collective-permute-start.12) | collective-permute-done | bytes 1048608 | tf_op jit(solution)/shard_map/ppermute | solution.py:94
  314.9 2.0 fusion.18
  316.9 2.2 collective-permute-start.15
  319.8 4.2 %collective-permute-done.14 = bf16[256,1024]{1,0:T(8,128)(2,1)S(1)} collective-permute-done((bf16[256,1024]{1,0:T(8,128)(2,1)S(1)}, bf16[256,1024]{1,0:T(8,128)(2,1)S(1)}, u32[]{:S(2)}, u32[]{:S(2)}) %collective-permute-start.14) | collective-permute-done | bytes 524320 | tf_op jit(solution)/shard_map/ppermute | solution.py:100
  329.3 3.5 %fusion.47 = (f32[16,8,32]{2,0,1:T(8,128)S(1)}, f32[16,8,32,256]{3,2,0,1:T(8,128)S(1)}) fusion(f32[8,256,16,32]{1,3,2,0:T(8,128)S(1)} %bitcast.71, pred[16,256]{1,0:T(8,128)(4,1)S(1)} %broadcast_in_dim.26), kind=kOutput, calls=%fused_computation.77 | output fusion | flops 6291711 | bytes 8409088 | tf_op jit(solution)/shard_map/sub | solution.py:118
  (91 shorter events, 30.5 us)
Async XLA Ops:
  6.5 8.0 %copy-start = (bf16[1024,1024]{1,0:T(8,128)(2,1)S(1)}, bf16[1024,1024]{1,0:T(8,128)(2,1)}, u32[]{:S(2)}) copy-start(bf16[1024,1024]{1,0:T(8,128)(2,1)} %param.11) | copy-start | bytes 6291460
  6.5 3.1 copy-start.7
  9.6 4.7 %copy-start.11 = (s32[1,8,2]{1,2,0:T(2,128)S(1)}, s32[1,8,2]{1,2,0:T(2,128)}, u32[]{:S(2)}) copy-start(s32[1,8,2]{1,2,0:T(2,128)} %param.15) | copy-start | bytes 196
  11.3 160.5 %copy-start.13 = (s32[8]{0:T(128)S(1)}, s32[8]{0:T(128)}, u32[]{:S(2)}) copy-start(s32[8]{0:T(128)} %constant.113.clone) | copy-start | bytes 100
  11.3 165.7 %copy-start.9 = (s32[8]{0:T(128)S(1)}, s32[8]{0:T(128)}, u32[]{:S(2)}) copy-start(s32[8]{0:T(128)} %constant.114.clone) | copy-start | bytes 100
  11.3 170.6 %copy-start.10 = (s32[16,8]{0,1:T(8,128)S(1)}, s32[16,8]{0,1:T(8,128)}, u32[]{:S(2)}) copy-start(s32[16,8]{0,1:T(8,128)} %param.16) | copy-start | bytes 1540
  11.3 170.7 %copy-start.12 = (s32[16]{0:T(128)S(1)}, s32[16]{0:T(128)}, u32[]{:S(2)}) copy-start(s32[16]{0:T(128)} %param.17) | copy-start | bytes 196
  11.3 49.0 %collective-permute-start = (bf16[512,2048]{1,0:T(8,128)(2,1)}, bf16[512,2048]{1,0:T(8,128)(2,1)}, u32[]{:S(2)}, u32[]{:S(2)}) collective-permute-start(bf16[512,2048]{1,0:T(8,128)(2,1)} %get-tuple-element.18), channel_id=1, source_target_pairs={{0,8},{8,16},{16,24},{24,28},{28,20},{20,12},{12,4},{4,0},{1,9},{9... | collective-permute-start | bytes 6291464 | tf_op jit(solution)/shard_map/ppermute | solution.py:57
  60.3 21.5 %all-to-all-start = ((bf16[8,2,16,1024]{3,2,1,0:T(8,128)(2,1)}), bf16[8,2,16,1024]{3,2,1,0:T(8,128)(2,1)S(1)}, u32[]{:S(2)}, u32[]{:S(2)}) async-start(bf16[8,2,16,1024]{3,2,1,0:T(8,128)(2,1)} %bitcast.2), calls=%async_computation | async-start | bytes 1048576 | tf_op jit(solution)/shard_map/all_to_all | solution.py:75
  66.3 154.3 %all-gather.3.cloned.1.call-start = ((), (), s32[]{:S(2)}) async-start(), calls=%async_computation.1 | async-start | bytes 2621440 | tf_op jit(solution)/shard_map/all_gather | solution.py:77
  66.4 54.8 %collective-permute-start.1 = (bf16[512,2048]{1,0:T(8,128)(2,1)}, bf16[512,2048]{1,0:T(8,128)(2,1)S(1)}, u32[]{:S(2)}, u32[]{:S(2)}) collective-permute-start(bf16[512,2048]{1,0:T(8,128)(2,1)} %get-tuple-element.18), channel_id=1, source_target_pairs={{0,4},{8,0},{16,8},{24,16},{28,24},{20,28},{12,20},{4,12},{1,5},{9... | collective-permute-start | bytes 6291464 | tf_op jit(solution)/shard_map/ppermute | solution.py:58
  82.6 195.7 %all-gather.5.cloned.1.call-start = ((), (), s32[]{:S(2)}) async-start(), calls=%async_computation.2 | async-start | bytes 5242880 | tf_op jit(solution)/shard_map/all_gather | solution.py:44
  121.2 4.4 %copy-start.4 = (bf16[512,2048]{1,0:T(8,128)(2,1)}, bf16[512,2048]{1,0:T(8,128)(2,1)S(1)}, u32[]{:S(2)}) copy-start(bf16[512,2048]{1,0:T(8,128)(2,1)S(1)} %collective-permute-done.1) | copy-start | bytes 6291460
  121.2 48.6 %collective-permute-start.3 = (bf16[512,2048]{1,0:T(8,128)(2,1)S(1)}, bf16[512,2048]{1,0:T(8,128)(2,1)}, u32[]{:S(2)}, u32[]{:S(2)}) collective-permute-start(bf16[512,2048]{1,0:T(8,128)(2,1)S(1)} %collective-permute-done.1), channel_id=1, source_target_pairs={{0,4},{8,0},{16,8},{24,16},{28,24},{20,28},{12,20},{4,12},{1,5},{9... | collective-permute-start | bytes 6291464 | tf_op jit(solution)/shard_map/ppermute | solution.py:58
  121.2 49.1 %collective-permute-start.2 = (bf16[512,2048]{1,0:T(8,128)(2,1)}, bf16[512,2048]{1,0:T(8,128)(2,1)}, u32[]{:S(2)}, u32[]{:S(2)}) collective-permute-start(bf16[512,2048]{1,0:T(8,128)(2,1)} %collective-permute-done), channel_id=1, source_target_pairs={{0,8},{8,16},{16,24},{24,28},{28,20},{20,12},{12,4},{4,0},{1,9},{9... | collective-permute-start | bytes 6291464 | tf_op jit(solution)/shard_map/ppermute | solution.py:57
  169.7 45.4 %collective-permute-start.5 = (bf16[512,2048]{1,0:T(8,128)(2,1)}, bf16[512,2048]{1,0:T(8,128)(2,1)S(1)}, u32[]{:S(2)}, u32[]{:S(2)}) collective-permute-start(bf16[512,2048]{1,0:T(8,128)(2,1)} %collective-permute-done.3), channel_id=1, source_target_pairs={{0,4},{8,0},{16,8},{24,16},{28,24},{20,28},{12,20},{4,12},{1,5},{9... | collective-permute-start | bytes 6291464 | tf_op jit(solution)/shard_map/ppermute | solution.py:58
  170.3 46.9 %collective-permute-start.4 = (bf16[512,2048]{1,0:T(8,128)(2,1)}, bf16[512,2048]{1,0:T(8,128)(2,1)}, u32[]{:S(2)}, u32[]{:S(2)}) collective-permute-start(bf16[512,2048]{1,0:T(8,128)(2,1)} %collective-permute-done.2), channel_id=1, source_target_pairs={{0,8},{8,16},{16,24},{24,28},{28,20},{20,12},{12,4},{4,0},{1,9},{9... | collective-permute-start | bytes 6291464 | tf_op jit(solution)/shard_map/ppermute | solution.py:57
  182.5 3.3 copy-start.5
  216.3 22.2 %collective-permute-start.6 = (bf16[256,2048]{1,0:T(8,128)(2,1)}, bf16[256,2048]{1,0:T(8,128)(2,1)S(1)}, u32[]{:S(2)}, u32[]{:S(2)}) collective-permute-start(bf16[256,2048]{1,0:T(8,128)(2,1)} %slice.26), channel_id=1, source_target_pairs={{0,4},{8,0},{16,8},{24,16},{28,24},{20,28},{12,20},{4,12},{1,5},{9... | collective-permute-start | bytes 3145736 | tf_op jit(solution)/shard_map/ppermute | solution.py:64
  219.4 23.1 %collective-permute-start.7 = (bf16[256,2048]{1,0:T(8,128)(2,1)}, bf16[256,2048]{1,0:T(8,128)(2,1)}, u32[]{:S(2)}, u32[]{:S(2)}) collective-permute-start(bf16[256,2048]{1,0:T(8,128)(2,1)} %slice.27), channel_id=1, source_target_pairs={{0,8},{8,16},{16,24},{24,28},{28,20},{20,12},{12,4},{4,0},{1,9},{9... | collective-permute-start | bytes 3145736 | tf_op jit(solution)/shard_map/ppermute | solution.py:63
  220.6 4.1 %copy-start.3 = (bf16[256,4096]{1,0:T(8,128)(2,1)S(1)}, bf16[256,4096]{1,0:T(8,128)(2,1)}, u32[]{:S(2)}) copy-start(bf16[256,4096]{1,0:T(8,128)(2,1)} %all-gather.3.cloned.1.call-done) | copy-start | bytes 6291460
  220.6 21.9 %copy-start.8 = (bf16[512,1024]{1,0:T(8,128)(2,1)S(1)}, bf16[512,1024]{1,0:T(8,128)(2,1)}, u32[]{:S(2)}) copy-start(bf16[512,1024]{1,0:T(8,128)(2,1)} %param.12) | copy-start | bytes 3145732
  242.5 25.5 %collective-permute-start.9 = (bf16[512,1024]{1,0:T(8,128)(2,1)S(1)}, bf16[512,1024]{1,0:T(8,128)(2,1)}, u32[]{:S(2)}, u32[]{:S(2)}) collective-permute-start(bf16[512,1024]{1,0:T(8,128)(2,1)S(1)} %copy-done.8), channel_id=1, source_target_pairs={{0,4},{8,0},{16,8},{24,16},{28,24},{20,28},{12,20},{4,12},{1,5},{9... | collective-permute-start | bytes 3145736 | tf_op jit(solution)/shard_map/ppermute | solution.py:95
  244.9 23.1 %collective-permute-start.8 = (bf16[512,1024]{1,0:T(8,128)(2,1)S(1)}, bf16[512,1024]{1,0:T(8,128)(2,1)}, u32[]{:S(2)}, u32[]{:S(2)}) collective-permute-start(bf16[512,1024]{1,0:T(8,128)(2,1)S(1)} %copy-done.8), channel_id=1, source_target_pairs={{0,8},{8,16},{16,24},{24,28},{28,20},{20,12},{12,4},{4,0},{1,9},{9... | collective-permute-start | bytes 3145736 | tf_op jit(solution)/shard_map/ppermute | solution.py:94
  268.0 23.3 %collective-permute-start.10 = (bf16[512,1024]{1,0:T(8,128)(2,1)}, bf16[512,1024]{1,0:T(8,128)(2,1)}, u32[]{:S(2)}, u32[]{:S(2)}) collective-permute-start(bf16[512,1024]{1,0:T(8,128)(2,1)} %collective-permute-done.8), channel_id=1, source_target_pairs={{0,8},{8,16},{16,24},{24,28},{28,20},{20,12},{12,4},{4,0},{1,9},{9... | collective-permute-start | bytes 3145736 | tf_op jit(solution)/shard_map/ppermute | solution.py:94
  268.0 23.6 %collective-permute-start.11 = (bf16[512,1024]{1,0:T(8,128)(2,1)}, bf16[512,1024]{1,0:T(8,128)(2,1)}, u32[]{:S(2)}, u32[]{:S(2)}) collective-permute-start(bf16[512,1024]{1,0:T(8,128)(2,1)} %collective-permute-done.9), channel_id=1, source_target_pairs={{0,4},{8,0},{16,8},{24,16},{28,24},{20,28},{12,20},{4,12},{1,5},{9... | collective-permute-start | bytes 3145736 | tf_op jit(solution)/shard_map/ppermute | solution.py:95
  291.3 23.4 %collective-permute-start.12 = (bf16[512,1024]{1,0:T(8,128)(2,1)}, bf16[512,1024]{1,0:T(8,128)(2,1)S(1)}, u32[]{:S(2)}, u32[]{:S(2)}) collective-permute-start(bf16[512,1024]{1,0:T(8,128)(2,1)} %collective-permute-done.10), channel_id=1, source_target_pairs={{0,8},{8,16},{16,24},{24,28},{28,20},{20,12},{12,4},{4,0},{1,9},{9... | collective-permute-start | bytes 3145736 | tf_op jit(solution)/shard_map/ppermute | solution.py:94
  291.3 2.4 copy-start.2
  291.6 25.2 %collective-permute-start.13 = (bf16[512,1024]{1,0:T(8,128)(2,1)}, bf16[512,1024]{1,0:T(8,128)(2,1)S(1)}, u32[]{:S(2)}, u32[]{:S(2)}) collective-permute-start(bf16[512,1024]{1,0:T(8,128)(2,1)} %collective-permute-done.11), channel_id=1, source_target_pairs={{0,4},{8,0},{16,8},{24,16},{28,24},{20,28},{12,20},{4,12},{1,5},{9... | collective-permute-start | bytes 3145736 | tf_op jit(solution)/shard_map/ppermute | solution.py:95
  314.8 9.2 %collective-permute-start.14 = (bf16[256,1024]{1,0:T(8,128)(2,1)S(1)}, bf16[256,1024]{1,0:T(8,128)(2,1)S(1)}, u32[]{:S(2)}, u32[]{:S(2)}) collective-permute-start(bf16[256,1024]{1,0:T(8,128)(2,1)S(1)} %slice.30), channel_id=1, source_target_pairs={{0,8},{8,16},{16,24},{24,28},{28,20},{20,12},{12,4},{4,0},{1,9},{9... | collective-permute-start | bytes 1572872 | tf_op jit(solution)/shard_map/ppermute | solution.py:100
  316.9 9.4 %collective-permute-start.15 = (bf16[256,1024]{1,0:T(8,128)(2,1)S(1)}, bf16[256,1024]{1,0:T(8,128)(2,1)S(1)}, u32[]{:S(2)}, u32[]{:S(2)}) collective-permute-start(bf16[256,1024]{1,0:T(8,128)(2,1)S(1)} %slice.31), channel_id=1, source_target_pairs={{0,4},{8,0},{16,8},{24,16},{28,24},{20,28},{12,20},{4,12},{1,5},{9... | collective-permute-start | bytes 1572872 | tf_op jit(solution)/shard_map/ppermute | solution.py:101
  332.7 3.0 copy-start.1
  (1 other events, 0.8 us)
Sparse Core Ops, SparseCore 0:
  82.7 20.6 all-gather.2
  125.6 34.0 all-gather.4

commit v9 on v6

--- a/solution.py
+++ b/solution.py
@@ -41,7 +41,18 @@
     fwd_perm = [(ring[i], ring[(i + 1) % ncrop]) for i in range(ncrop)]
     bwd_perm = [(ring[i], ring[(i - 1) % ncrop]) for i in range(ncrop)]
 
-    queries_in = lax.all_gather(global_rows, "head", axis=1, tiled=True)
+    nhead = lax.axis_size("head")
+    hme = lax.axis_index("head")
+
+    def head_gather(x):
+        full = jnp.zeros((x.shape[0], nhead * x.shape[1]), x.dtype)
+        full = lax.dynamic_update_slice(full, x, (0, hme * x.shape[1]))
+        for k in range(1, nhead):
+            part = lax.ppermute(x, "head", [(j, (j + k) % nhead) for j in range(nhead)])
+            full = lax.dynamic_update_slice(full, part, (0, ((hme - k) % nhead) * x.shape[1]))
+        return full
+
+    queries_in = head_gather(global_rows)
     picks = fetch_slots[0]
     blocks = crop_tokens.reshape(-1, CT, crop_tokens.shape[1])
     chosen = blocks[picks]
@@ -73,7 +84,7 @@
     )
     kv_got[-1] = (last_a,) + kv_got[-1][1:]
     kv_got[-2] = (last_b,) + kv_got[-2][1:]
-    tokens_in = lax.all_gather(delivered, "head", axis=1, tiled=True)
+    tokens_in = head_gather(delivered)
     kv_weight = jnp.concatenate([p for p, _, _, _ in kv_got], axis=0)
     tokens_perm = jnp.concatenate(
         [lax.dynamic_slice_in_dim(tokens_in, src * wrows + lo, n, 1) for _, src, lo, n in kv_got],

time: 296 us -> 277 us (0.936)
  waiting for transfers between devices: 183 us -> 162 us
  between operations: 23.2 us -> 9.3 us
  starting transfers between devices: 25 us -> 32.4 us
  local copies, waits for them, and re-layouts: 35.9 us -> 43 us
    ppermute x3, waiting for transfers between devices: 107 us -> 0.01 us  [ring_pieces(): bwd = lax.ppermute(bwd, 'crop', bwd_perm)]
    ppermute x3, waiting for transfers between devices: 1.96 us -> 83.9 us  [ring_pieces(): fwd = lax.ppermute(fwd, 'crop', fwd_perm)]
    ppermute x0 -> x6, waiting for transfers between devices: none -> 14.1 us  [head_gather(): part = lax.ppermute(x, 'head', [(j, (j + k) % nhead) for j in range(nhead)])]
    dynamic_update_slice x0 -> x8, local copies, waits for them, and re-layouts: none -> 9.48 us  [the longest x6 7.13 us: head_gather(): lax.dynamic_update_slice(full, part, (0, (hme - k) % nhead * x.shape[1]))]
    ppermute x1, waiting for transfers between devices: 11.6 us -> 4.4 us  [ring_pieces(): lax.ppermute(bwd[split:], 'crop', bwd_perm)]
    ppermute x0 -> x6, starting transfers between devices: none -> 5.87 us  [head_gather(): part = lax.ppermute(x, 'head', [(j, (j + k) % nhead) for j in range(nhead)])]
    unnamed x48 -> x40, local copies, waits for them, and re-layouts: 29.3 us -> 24.3 us
    ppermute x1, starting transfers between devices: 0.06 us -> 4.44 us  [ring_pieces(): got.append((lax.ppermute(fwd[:split], 'crop', fwd_perm), src, 0, split))]
  transfers between devices with their start and end apart: 19 -> 23, of which waited for: 13 -> 14; matrix products, arithmetic and copies ran while one was open for 17% -> 21% of each run, Pallas kernels for 0% -> 0%
where the time goes in v9:
time: 277 us; the launch traced here: 276 us
  waiting for transfers between devices  162 us (58%)
  local copies, waits for them, and re-layouts  43 us (16%)
  starting transfers between devices  32.4 us (12%)
  matrix products  25.6 us (9%)
  between operations  9.3 us (3%)
  other arithmetic  3.67 us (1%)
    ppermute x3, waiting for transfers between devices, ring_pieces(): fwd = lax.ppermute(fwd, 'crop', fwd_perm)  83.9 us
    ppermute x3, waiting for transfers between devices, body(): fwd = lax.ppermute(fwd, 'crop', fwd_perm)  41.4 us
    unnamed x40, local copies, waits for them, and re-layouts  24.3 us
    dot_general x9, matrix products, q_part(): return acc + jnp.dot(cols, piece, preferred_element_type=jnp.float32)  15.6 us
    ppermute x6, waiting for transfers between devices, head_gather(): part = lax.ppermute(x, 'head', [(j, (j + k) % nhead) for j in range(nhead)])  14.1 us
    dot_general x1, matrix products, body(): jnp.dot(tokens_perm, kv_weight, preferred_element_type=jnp.float32)  8.27 us
    ppermute x3, starting transfers between devices, ring_pieces(): fwd = lax.ppermute(fwd, 'crop', fwd_perm)  7.5 us
    dynamic_update_slice x6, local copies, waits for them, and re-layouts, head_gather(): lax.dynamic_update_slice(full, part, (0, (hme - k) % nhead * x.shape[1]))  7.13 us
  transfers between devices with their start and end apart: 23, of which 14 were waited for; matrix products, arithmetic and copies ran while one was open for 21% of the time, Pallas kernels for 0%

profile of v9, /device:TPU:0, one launch (start us, length us, event | category | flops | bytes accessed | tf_op | source)
XLA Modules:
  0.0 276.0 jit_solution(8082816630583124154)
XLA Ops:
  0.0 2.5 constant_dynamic-update-slice_fusion.11
  3.7 3.0 %collective-permute-start.3 = (bf16[512,2048]{1,0:T(8,128)(2,1)S(1)}, bf16[512,2048]{1,0:T(8,128)(2,1)}, u32[]{:S(2)}, u32[]{:S(2)}) collective-permute-start(bf16[512,2048]{1,0:T(8,128)(2,1)S(1)} %get-tuple-element.14), channel_id=1, source_target_pairs={{0,8},{8,16},{16,24},{24,28},{28,20},{20,12},{12,4},{4,0},{1,9},{9... | collective-permute-start | bytes 6291464 | tf_op jit(solution)/shard_map/ppermute | solution.py:71
  6.8 45.7 %collective-permute-done.3 = bf16[512,2048]{1,0:T(8,128)(2,1)} collective-permute-done((bf16[512,2048]{1,0:T(8,128)(2,1)S(1)}, bf16[512,2048]{1,0:T(8,128)(2,1)}, u32[]{:S(2)}, u32[]{:S(2)}) %collective-permute-start.3) | collective-permute-done | bytes 2097184 | tf_op jit(solution)/shard_map/ppermute | solution.py:71
  57.8 5.8 %all-to-all-start = ((bf16[8,2,16,1024]{3,2,1,0:T(8,128)(2,1)}), bf16[8,2,16,1024]{3,2,1,0:T(8,128)(2,1)S(1)}, u32[]{:S(2)}, u32[]{:S(2)}) async-start(bf16[8,2,16,1024]{3,2,1,0:T(8,128)(2,1)} %bitcast.2), calls=%async_computation | async-start | bytes 1048576 | tf_op jit(solution)/shard_map/all_to_all | solution.py:59
  75.5 26.4 %collective-permute-done.5 = bf16[512,2048]{1,0:T(8,128)(2,1)} collective-permute-done((bf16[512,2048]{1,0:T(8,128)(2,1)}, bf16[512,2048]{1,0:T(8,128)(2,1)}, u32[]{:S(2)}, u32[]{:S(2)}) %collective-permute-start.5) | collective-permute-done | bytes 2097184 | tf_op jit(solution)/shard_map/ppermute | solution.py:71
  101.9 2.7 collective-permute-start.7
  104.6 2.5 broadcast_in_dim.35
  107.0 2.3 constant_dynamic-update-slice_fusion.15
  109.3 5.9 %all-to-all-done = bf16[8,2,16,1024]{3,2,1,0:T(8,128)(2,1)S(1)} async-done(((bf16[8,2,16,1024]{3,2,1,0:T(8,128)(2,1)}), bf16[8,2,16,1024]{3,2,1,0:T(8,128)(2,1)S(1)}, u32[]{:S(2)}, u32[]{:S(2)}) %all-to-all-start) | async-done | bytes 524320 | tf_op jit(solution)/shard_map/all_to_all | solution.py:59
  117.1 2.4 constant_dynamic-update-slice_fusion.14
  120.9 2.3 constant_dynamic-update-slice_fusion.13
  123.3 2.3 constant_dynamic-update-slice_fusion.12
  125.5 3.0 %collective-permute-done = bf16[256,1024]{1,0:T(8,128)(2,1)S(1)} collective-permute-done((bf16[256,1024]{1,0:T(8,128)(2,1)S(1)}, bf16[256,1024]{1,0:T(8,128)(2,1)S(1)}, u32[]{:S(2)}, u32[]{:S(2)}) %collective-permute-start) | collective-permute-done | bytes 524320 | tf_op jit(solution)/shard_map/ppermute | solution.py:51
  130.5 9.3 %collective-permute-done.2 = bf16[256,1024]{1,0:T(8,128)(2,1)S(1)} collective-permute-done((bf16[256,1024]{1,0:T(8,128)(2,1)S(1)}, bf16[256,1024]{1,0:T(8,128)(2,1)S(1)}, u32[]{:S(2)}, u32[]{:S(2)}) %collective-permute-start.2) | collective-permute-done | bytes 524320 | tf_op jit(solution)/shard_map/ppermute | solution.py:51
  140.1 11.8 %collective-permute-done.7 = bf16[512,2048]{1,0:T(8,128)(2,1)S(1)} collective-permute-done((bf16[512,2048]{1,0:T(8,128)(2,1)}, bf16[512,2048]{1,0:T(8,128)(2,1)S(1)}, u32[]{:S(2)}, u32[]{:S(2)}) %collective-permute-start.7) | collective-permute-done | bytes 2097184 | tf_op jit(solution)/shard_map/ppermute | solution.py:71
  152.0 4.4 %collective-permute-start.10 = (bf16[256,2048]{1,0:T(8,128)(2,1)S(1)}, bf16[256,2048]{1,0:T(8,128)(2,1)S(1)}, u32[]{:S(2)}, u32[]{:S(2)}) collective-permute-start(bf16[256,2048]{1,0:T(8,128)(2,1)S(1)} %slice.27), channel_id=1, source_target_pairs={{0,8},{8,16},{16,24},{24,28},{28,20},{20,12},{12,4},{4,0},{1,9},{9... | collective-permute-start | bytes 3145736 | tf_op jit(solution)/shard_map/ppermute | solution.py:77
  157.8 3.1 %constant_dynamic-update-slice_fusion.9 = bf16[4096,2048]{1,0:T(8,128)(2,1)} fusion(bf16[4096,2048]{1,0:T(8,128)(2,1)} %get-tuple-element.13, bf16[512,2048]{1,0:T(8,128)(2,1)} %collective-permute-done.3), kind=kLoop, calls=%fused_computation.58 | loop fusion | bytes 4194304
  161.0 3.2 %constant_dynamic-update-slice_fusion.8 = bf16[4096,2048]{1,0:T(8,128)(2,1)} fusion(bf16[4096,2048]{1,0:T(8,128)(2,1)} %constant_dynamic-update-slice_fusion.9, bf16[512,2048]{1,0:T(8,128)(2,1)} %collective-permute-done.4), kind=kLoop, calls=%fused_computation.57 | loop fusion | bytes 4194304
  164.2 3.2 %constant_dynamic-update-slice_fusion.7 = bf16[4096,2048]{1,0:T(8,128)(2,1)} fusion(bf16[4096,2048]{1,0:T(8,128)(2,1)} %constant_dynamic-update-slice_fusion.8, bf16[512,2048]{1,0:T(8,128)(2,1)} %collective-permute-done.5), kind=kLoop, calls=%fused_computation.56 | loop fusion | bytes 4194304
  167.4 3.3 %constant_dynamic-update-slice_fusion.6 = bf16[4096,2048]{1,0:T(8,128)(2,1)} fusion(bf16[4096,2048]{1,0:T(8,128)(2,1)} %constant_dynamic-update-slice_fusion.7, bf16[512,2048]{1,0:T(8,128)(2,1)} %collective-permute-done.6), kind=kLoop, calls=%fused_computation.55 | loop fusion | bytes 4194304
  170.7 6.4 %collective-permute-done.10 = bf16[256,2048]{1,0:T(8,128)(2,1)S(1)} collective-permute-done((bf16[256,2048]{1,0:T(8,128)(2,1)S(1)}, bf16[256,2048]{1,0:T(8,128)(2,1)S(1)}, u32[]{:S(2)}, u32[]{:S(2)}) %collective-permute-start.10) | collective-permute-done | bytes 1048608 | tf_op jit(solution)/shard_map/ppermute | solution.py:77
  177.1 4.4 %collective-permute-done.9 = bf16[256,2048]{1,0:T(8,128)(2,1)S(1)} collective-permute-done((bf16[256,2048]{1,0:T(8,128)(2,1)S(1)}, bf16[256,2048]{1,0:T(8,128)(2,1)S(1)}, u32[]{:S(2)}, u32[]{:S(2)}) %collective-permute-start.9) | collective-permute-done | bytes 1048608 | tf_op jit(solution)/shard_map/ppermute | solution.py:78
  185.0 3.1 %constant_dynamic-update-slice_fusion.4 = bf16[4096,2048]{1,0:T(8,128)(2,1)} fusion(bf16[4096,2048]{1,0:T(8,128)(2,1)} %constant_dynamic-update-slice_fusion.5, bf16[512,2048]{1,0:T(8,128)(2,1)} %collective-permute-done.8), kind=kLoop, calls=%fused_computation.53 | loop fusion | bytes 4194304
  190.2 14.6 %collective-permute-done.14 = bf16[512,1024]{1,0:T(8,128)(2,1)S(1)} collective-permute-done((bf16[512,1024]{1,0:T(8,128)(2,1)S(1)}, bf16[512,1024]{1,0:T(8,128)(2,1)S(1)}, u32[]{:S(2)}, u32[]{:S(2)}) %collective-permute-start.14) | collective-permute-done | bytes 1048608 | tf_op jit(solution)/shard_map/ppermute | solution.py:104
  206.8 8.3 %convolution_convert_fusion = bf16[256,2048]{1,0:T(8,128)(2,1)S(1)} fusion(bf16[256,4096]{1,0:T(8,128)(2,1)S(1)} %dynamic-slice_dynamic-update-slice_fusion.7, bf16[4096,2048]{1,0:T(8,128)(2,1)} %constant_dynamic-update-slice_fusion.2), kind=kOutput, calls=%fused_computation.6 | convolution fusion | flops 4295491584 | bytes 19922944 | tf_op jit(solution)/shard_map/dot_general | solution.py:93
  216.9 11.2 %collective-permute-done.16 = bf16[512,1024]{1,0:T(8,128)(2,1)S(1)} collective-permute-done((bf16[512,1024]{1,0:T(8,128)(2,1)S(1)}, bf16[512,1024]{1,0:T(8,128)(2,1)S(1)}, u32[]{:S(2)}, u32[]{:S(2)}) %collective-permute-start.16) | collective-permute-done | bytes 1048608 | tf_op jit(solution)/shard_map/ppermute | solution.py:104
  235.8 15.6 %collective-permute-done.18 = bf16[512,1024]{1,0:T(8,128)(2,1)S(1)} collective-permute-done((bf16[512,1024]{1,0:T(8,128)(2,1)S(1)}, bf16[512,1024]{1,0:T(8,128)(2,1)S(1)}, u32[]{:S(2)}, u32[]{:S(2)}) %collective-permute-start.18) | collective-permute-done | bytes 1048608 | tf_op jit(solution)/shard_map/ppermute | solution.py:104
  251.4 2.1 collective-permute-start.20
  257.3 3.3 %collective-permute-done.20 = bf16[256,1024]{1,0:T(8,128)(2,1)S(1)} collective-permute-done((bf16[256,1024]{1,0:T(8,128)(2,1)S(1)}, bf16[256,1024]{1,0:T(8,128)(2,1)S(1)}, u32[]{:S(2)}, u32[]{:S(2)}) %collective-permute-start.20) | collective-permute-done | bytes 524320 | tf_op jit(solution)/shard_map/ppermute | solution.py:110
  262.0 2.7 collective-permute-done.21
  266.1 2.2 fusion.8
  269.5 3.5 %fusion.47 = (f32[16,8,32]{2,0,1:T(8,128)S(1)}, f32[16,8,32,256]{3,2,0,1:T(8,128)S(1)}) fusion(f32[8,256,16,32]{1,3,2,0:T(8,128)S(1)} %bitcast.71, pred[16,256]{1,0:T(8,128)(4,1)S(1)} %broadcast_in_dim.33), kind=kOutput, calls=%fused_computation.85 | output fusion | flops 6291711 | bytes 8409088 | tf_op jit(solution)/shard_map/sub | solution.py:128
  (97 shorter events, 44.2 us)
Async XLA Ops:
  0.0 56.4 %copy-start = (bf16[1024,1024]{1,0:T(8,128)(2,1)S(1)}, bf16[1024,1024]{1,0:T(8,128)(2,1)}, u32[]{:S(2)}) copy-start(bf16[1024,1024]{1,0:T(8,128)(2,1)} %param.11) | copy-start | bytes 6291460
  0.0 2.5 copy-start.2
  2.5 53.7 %copy-start.6 = (s32[1,8,2]{1,2,0:T(2,128)S(1)}, s32[1,8,2]{1,2,0:T(2,128)}, u32[]{:S(2)}) copy-start(s32[1,8,2]{1,2,0:T(2,128)} %param.15) | copy-start | bytes 196
  2.5 62.2 %copy-start.8 = (s32[8]{0:T(128)S(1)}, s32[8]{0:T(128)}, u32[]{:S(2)}) copy-start(s32[8]{0:T(128)} %constant.150.clone) | copy-start | bytes 100
  2.5 67.3 %copy-start.4 = (s32[8]{0:T(128)S(1)}, s32[8]{0:T(128)}, u32[]{:S(2)}) copy-start(s32[8]{0:T(128)} %constant.151.clone) | copy-start | bytes 100
  2.5 72.4 %copy-start.5 = (s32[16,8]{0,1:T(8,128)S(1)}, s32[16,8]{0,1:T(8,128)}, u32[]{:S(2)}) copy-start(s32[16,8]{0,1:T(8,128)} %param.16) | copy-start | bytes 1540
  2.5 72.5 %copy-start.7 = (s32[16]{0:T(128)S(1)}, s32[16]{0:T(128)}, u32[]{:S(2)}) copy-start(s32[16]{0:T(128)} %param.17) | copy-start | bytes 196
  3.7 48.7 %collective-permute-start.3 = (bf16[512,2048]{1,0:T(8,128)(2,1)S(1)}, bf16[512,2048]{1,0:T(8,128)(2,1)}, u32[]{:S(2)}, u32[]{:S(2)}) collective-permute-start(bf16[512,2048]{1,0:T(8,128)(2,1)S(1)} %get-tuple-element.14), channel_id=1, source_target_pairs={{0,8},{8,16},{16,24},{24,28},{28,20},{20,12},{12,4},{4,0},{1,9},{9... | collective-permute-start | bytes 6291464 | tf_op jit(solution)/shard_map/ppermute | solution.py:71
  6.8 47.5 %collective-permute-start.4 = (bf16[512,2048]{1,0:T(8,128)(2,1)S(1)}, bf16[512,2048]{1,0:T(8,128)(2,1)}, u32[]{:S(2)}, u32[]{:S(2)}) collective-permute-start(bf16[512,2048]{1,0:T(8,128)(2,1)S(1)} %get-tuple-element.14), channel_id=1, source_target_pairs={{0,4},{8,0},{16,8},{24,16},{28,24},{20,28},{12,20},{4,12},{1,5},{9... | collective-permute-start | bytes 6291464 | tf_op jit(solution)/shard_map/ppermute | solution.py:72
  52.4 49.4 %collective-permute-start.5 = (bf16[512,2048]{1,0:T(8,128)(2,1)}, bf16[512,2048]{1,0:T(8,128)(2,1)}, u32[]{:S(2)}, u32[]{:S(2)}) collective-permute-start(bf16[512,2048]{1,0:T(8,128)(2,1)} %collective-permute-done.3), channel_id=1, source_target_pairs={{0,8},{8,16},{16,24},{24,28},{28,20},{20,12},{12,4},{4,0},{1,9},{9... | collective-permute-start | bytes 6291464 | tf_op jit(solution)/shard_map/ppermute | solution.py:71
  54.2 50.3 %collective-permute-start.6 = (bf16[512,2048]{1,0:T(8,128)(2,1)}, bf16[512,2048]{1,0:T(8,128)(2,1)}, u32[]{:S(2)}, u32[]{:S(2)}) collective-permute-start(bf16[512,2048]{1,0:T(8,128)(2,1)} %collective-permute-done.4), channel_id=1, source_target_pairs={{0,4},{8,0},{16,8},{24,16},{28,24},{20,28},{12,20},{4,12},{1,5},{9... | collective-permute-start | bytes 6291464 | tf_op jit(solution)/shard_map/ppermute | solution.py:72
  54.5 60.8 %collective-permute-start.11 = (bf16[512,1024]{1,0:T(8,128)(2,1)}, bf16[512,1024]{1,0:T(8,128)(2,1)}, u32[]{:S(2)}, u32[]{:S(2)}) collective-permute-start(bf16[512,1024]{1,0:T(8,128)(2,1)} %param.10), channel_id=1, source_target_pairs={{0,1},{1,2},{2,3},{3,0},{4,5},{5,6},{6,7},{7,4},{8,9},{9,10},{10,1... | collective-permute-start | bytes 3145736 | tf_op jit(solution)/shard_map/ppermute | solution.py:51
  54.5 61.1 %collective-permute-start.12 = (bf16[512,1024]{1,0:T(8,128)(2,1)}, bf16[512,1024]{1,0:T(8,128)(2,1)}, u32[]{:S(2)}, u32[]{:S(2)}) collective-permute-start(bf16[512,1024]{1,0:T(8,128)(2,1)} %param.10), channel_id=1, source_target_pairs={{0,2},{1,3},{2,0},{3,1},{4,6},{5,7},{6,4},{7,5},{8,10},{9,11},{10,... | collective-permute-start | bytes 3145736 | tf_op jit(solution)/shard_map/ppermute | solution.py:51
  57.8 57.5 %all-to-all-start = ((bf16[8,2,16,1024]{3,2,1,0:T(8,128)(2,1)}), bf16[8,2,16,1024]{3,2,1,0:T(8,128)(2,1)S(1)}, u32[]{:S(2)}, u32[]{:S(2)}) async-start(bf16[8,2,16,1024]{3,2,1,0:T(8,128)(2,1)} %bitcast.2), calls=%async_computation | async-start | bytes 1048576 | tf_op jit(solution)/shard_map/all_to_all | solution.py:59
  63.6 55.9 %collective-permute-start.13 = (bf16[512,1024]{1,0:T(8,128)(2,1)}, bf16[512,1024]{1,0:T(8,128)(2,1)}, u32[]{:S(2)}, u32[]{:S(2)}) collective-permute-start(bf16[512,1024]{1,0:T(8,128)(2,1)} %param.10), channel_id=1, source_target_pairs={{0,3},{1,0},{2,1},{3,2},{4,7},{5,4},{6,5},{7,6},{8,11},{9,8},{10,9... | collective-permute-start | bytes 3145736 | tf_op jit(solution)/shard_map/ppermute | solution.py:51
  101.9 50.1 %collective-permute-start.7 = (bf16[512,2048]{1,0:T(8,128)(2,1)}, bf16[512,2048]{1,0:T(8,128)(2,1)S(1)}, u32[]{:S(2)}, u32[]{:S(2)}) collective-permute-start(bf16[512,2048]{1,0:T(8,128)(2,1)} %collective-permute-done.5), channel_id=1, source_target_pairs={{0,8},{8,16},{16,24},{24,28},{28,20},{20,12},{12,4},{4,0},{1,9},{9... | collective-permute-start | bytes 6291464 | tf_op jit(solution)/shard_map/ppermute | solution.py:71
  104.6 51.9 %collective-permute-start.8 = (bf16[512,2048]{1,0:T(8,128)(2,1)}, bf16[512,2048]{1,0:T(8,128)(2,1)}, u32[]{:S(2)}, u32[]{:S(2)}) collective-permute-start(bf16[512,2048]{1,0:T(8,128)(2,1)} %collective-permute-done.6), channel_id=1, source_target_pairs={{0,4},{8,0},{16,8},{24,16},{28,24},{20,28},{12,20},{4,12},{1,5},{9... | collective-permute-start | bytes 6291464 | tf_op jit(solution)/shard_map/ppermute | solution.py:72
  115.3 13.3 %collective-permute-start = (bf16[256,1024]{1,0:T(8,128)(2,1)S(1)}, bf16[256,1024]{1,0:T(8,128)(2,1)S(1)}, u32[]{:S(2)}, u32[]{:S(2)}) collective-permute-start(bf16[256,1024]{1,0:T(8,128)(2,1)S(1)} %bitcast.75), channel_id=1, source_target_pairs={{0,1},{1,2},{2,3},{3,0},{4,5},{5,6},{6,7},{7,4},{8,9},{9,10},{10,1... | collective-permute-start | bytes 1572872 | tf_op jit(solution)/shard_map/ppermute | solution.py:51
  115.6 14.9 %collective-permute-start.1 = (bf16[256,1024]{1,0:T(8,128)(2,1)S(1)}, bf16[256,1024]{1,0:T(8,128)(2,1)S(1)}, u32[]{:S(2)}, u32[]{:S(2)}) collective-permute-start(bf16[256,1024]{1,0:T(8,128)(2,1)S(1)} %bitcast.77), channel_id=1, source_target_pairs={{0,2},{1,3},{2,0},{3,1},{4,6},{5,7},{6,4},{7,5},{8,10},{9,11},{10,... | collective-permute-start | bytes 1572872 | tf_op jit(solution)/shard_map/ppermute | solution.py:51
  119.5 20.2 %collective-permute-start.2 = (bf16[256,1024]{1,0:T(8,128)(2,1)S(1)}, bf16[256,1024]{1,0:T(8,128)(2,1)S(1)}, u32[]{:S(2)}, u32[]{:S(2)}) collective-permute-start(bf16[256,1024]{1,0:T(8,128)(2,1)S(1)} %bitcast.78), channel_id=1, source_target_pairs={{0,3},{1,0},{2,1},{3,2},{4,7},{5,4},{6,5},{7,6},{8,11},{9,8},{10,9... | collective-permute-start | bytes 1572872 | tf_op jit(solution)/shard_map/ppermute | solution.py:51
  152.0 25.1 %collective-permute-start.10 = (bf16[256,2048]{1,0:T(8,128)(2,1)S(1)}, bf16[256,2048]{1,0:T(8,128)(2,1)S(1)}, u32[]{:S(2)}, u32[]{:S(2)}) collective-permute-start(bf16[256,2048]{1,0:T(8,128)(2,1)S(1)} %slice.27), channel_id=1, source_target_pairs={{0,8},{8,16},{16,24},{24,28},{28,20},{20,12},{12,4},{4,0},{1,9},{9... | collective-permute-start | bytes 3145736 | tf_op jit(solution)/shard_map/ppermute | solution.py:77
  157.7 23.7 %collective-permute-start.9 = (bf16[256,2048]{1,0:T(8,128)(2,1)S(1)}, bf16[256,2048]{1,0:T(8,128)(2,1)S(1)}, u32[]{:S(2)}, u32[]{:S(2)}) collective-permute-start(bf16[256,2048]{1,0:T(8,128)(2,1)S(1)} %slice.26), channel_id=1, source_target_pairs={{0,4},{8,0},{16,8},{24,16},{28,24},{20,28},{12,20},{4,12},{1,5},{9... | collective-permute-start | bytes 3145736 | tf_op jit(solution)/shard_map/ppermute | solution.py:78
  167.4 14.1 %copy-start.3 = (bf16[512,1024]{1,0:T(8,128)(2,1)S(1)}, bf16[512,1024]{1,0:T(8,128)(2,1)}, u32[]{:S(2)}) copy-start(bf16[512,1024]{1,0:T(8,128)(2,1)} %param.12) | copy-start | bytes 3145732
  181.5 25.4 %collective-permute-start.15 = (bf16[512,1024]{1,0:T(8,128)(2,1)S(1)}, bf16[512,1024]{1,0:T(8,128)(2,1)S(1)}, u32[]{:S(2)}, u32[]{:S(2)}) collective-permute-start(bf16[512,1024]{1,0:T(8,128)(2,1)S(1)} %copy-done.3), channel_id=1, source_target_pairs={{0,4},{8,0},{16,8},{24,16},{28,24},{20,28},{12,20},{4,12},{1,5},{9... | collective-permute-start | bytes 3145736 | tf_op jit(solution)/shard_map/ppermute | solution.py:105
  181.5 23.3 %collective-permute-start.14 = (bf16[512,1024]{1,0:T(8,128)(2,1)S(1)}, bf16[512,1024]{1,0:T(8,128)(2,1)S(1)}, u32[]{:S(2)}, u32[]{:S(2)}) collective-permute-start(bf16[512,1024]{1,0:T(8,128)(2,1)S(1)} %copy-done.3), channel_id=1, source_target_pairs={{0,8},{8,16},{16,24},{24,28},{28,20},{20,12},{12,4},{4,0},{1,9},{9... | collective-permute-start | bytes 3145736 | tf_op jit(solution)/shard_map/ppermute | solution.py:104
  204.8 23.3 %collective-permute-start.16 = (bf16[512,1024]{1,0:T(8,128)(2,1)S(1)}, bf16[512,1024]{1,0:T(8,128)(2,1)S(1)}, u32[]{:S(2)}, u32[]{:S(2)}) collective-permute-start(bf16[512,1024]{1,0:T(8,128)(2,1)S(1)} %collective-permute-done.14), channel_id=1, source_target_pairs={{0,8},{8,16},{16,24},{24,28},{28,20},{20,12},{12,4},{4,0},{1,9},{9... | collective-permute-start | bytes 3145736 | tf_op jit(solution)/shard_map/ppermute | solution.py:104
  206.8 23.6 %collective-permute-start.17 = (bf16[512,1024]{1,0:T(8,128)(2,1)S(1)}, bf16[512,1024]{1,0:T(8,128)(2,1)S(1)}, u32[]{:S(2)}, u32[]{:S(2)}) collective-permute-start(bf16[512,1024]{1,0:T(8,128)(2,1)S(1)} %collective-permute-done.15), channel_id=1, source_target_pairs={{0,4},{8,0},{16,8},{24,16},{28,24},{20,28},{12,20},{4,12},{1,5},{9... | collective-permute-start | bytes 3145736 | tf_op jit(solution)/shard_map/ppermute | solution.py:105
  228.1 23.2 %collective-permute-start.18 = (bf16[512,1024]{1,0:T(8,128)(2,1)S(1)}, bf16[512,1024]{1,0:T(8,128)(2,1)S(1)}, u32[]{:S(2)}, u32[]{:S(2)}) collective-permute-start(bf16[512,1024]{1,0:T(8,128)(2,1)S(1)} %collective-permute-done.16), channel_id=1, source_target_pairs={{0,8},{8,16},{16,24},{24,28},{28,20},{20,12},{12,4},{4,0},{1,9},{9... | collective-permute-start | bytes 3145736 | tf_op jit(solution)/shard_map/ppermute | solution.py:104
  230.5 24.8 %collective-permute-start.19 = (bf16[512,1024]{1,0:T(8,128)(2,1)S(1)}, bf16[512,1024]{1,0:T(8,128)(2,1)S(1)}, u32[]{:S(2)}, u32[]{:S(2)}) collective-permute-start(bf16[512,1024]{1,0:T(8,128)(2,1)S(1)} %collective-permute-done.17), channel_id=1, source_target_pairs={{0,4},{8,0},{16,8},{24,16},{28,24},{20,28},{12,20},{4,12},{1,5},{9... | collective-permute-start | bytes 3145736 | tf_op jit(solution)/shard_map/ppermute | solution.py:105
  251.4 9.2 %collective-permute-start.20 = (bf16[256,1024]{1,0:T(8,128)(2,1)S(1)}, bf16[256,1024]{1,0:T(8,128)(2,1)S(1)}, u32[]{:S(2)}, u32[]{:S(2)}) collective-permute-start(bf16[256,1024]{1,0:T(8,128)(2,1)S(1)} %slice.30), channel_id=1, source_target_pairs={{0,8},{8,16},{16,24},{24,28},{28,20},{20,12},{12,4},{4,0},{1,9},{9... | collective-permute-start | bytes 1572872 | tf_op jit(solution)/shard_map/ppermute | solution.py:110
  255.3 9.4 %collective-permute-start.21 = (bf16[256,1024]{1,0:T(8,128)(2,1)S(1)}, bf16[256,1024]{1,0:T(8,128)(2,1)S(1)}, u32[]{:S(2)}, u32[]{:S(2)}) collective-permute-start(bf16[256,1024]{1,0:T(8,128)(2,1)S(1)} %slice.31), channel_id=1, source_target_pairs={{0,4},{8,0},{16,8},{24,16},{28,24},{20,28},{12,20},{4,12},{1,5},{9... | collective-permute-start | bytes 1572872 | tf_op jit(solution)/shard_map/ppermute | solution.py:111
  273.0 3.0 %copy-start.1 = (bf16[1024,1024]{1,0:T(8,128)(2,1)S(1)}, bf16[1024,1024]{1,0:T(8,128)(2,1)}, u32[]{:S(2)}) copy-start(bf16[1024,1024]{1,0:T(8,128)(2,1)} %param.11) | copy-start | bytes 6291460

commit v10 on v9

--- a/solution.py
+++ b/solution.py
@@ -55,51 +55,19 @@
     queries_in = head_gather(global_rows)
     picks = fetch_slots[0]
     blocks = crop_tokens.reshape(-1, CT, crop_tokens.shape[1])
-    chosen = blocks[picks]
-    delivered = lax.all_to_all(chosen, "crop", split_axis=0, concat_axis=0, tiled=True)
-    delivered = delivered.reshape(-1, crop_tokens.shape[1])
+    nslots = ncrop * CAP
 
     steps_fwd = ncrop // 2
     steps_bwd = (ncrop - 1) // 2
     split = wrows // 2
 
-    def ring_pieces(piece):
-        got = [(piece, me, 0, wrows)]
-        fwd = piece
-        bwd = piece
-        for k in range(1, steps_bwd + 1):
-            fwd = lax.ppermute(fwd, "crop", fwd_perm)
-            bwd = lax.ppermute(bwd, "crop", bwd_perm)
-            got.append((fwd, ring_arr[(pos - k) % ncrop], 0, wrows))
-            got.append((bwd, ring_arr[(pos + k) % ncrop], 0, wrows))
-        if steps_fwd > steps_bwd:
-            src = ring_arr[(pos - steps_fwd) % ncrop]
-            got.append((lax.ppermute(fwd[:split], "crop", fwd_perm), src, 0, split))
-            got.append((lax.ppermute(bwd[split:], "crop", bwd_perm), src, split, wrows - split))
-        return got
-
-    kv_got = ring_pieces(jnp.concatenate([key_weight, value_weight], axis=1))
-    q_piece, last_a, last_b = lax.optimization_barrier(
-        (query_weight, kv_got[-1][0], kv_got[-2][0])
-    )
-    kv_got[-1] = (last_a,) + kv_got[-1][1:]
-    kv_got[-2] = (last_b,) + kv_got[-2][1:]
-    tokens_in = head_gather(delivered)
-    kv_weight = jnp.concatenate([p for p, _, _, _ in kv_got], axis=0)
-    tokens_perm = jnp.concatenate(
-        [lax.dynamic_slice_in_dim(tokens_in, src * wrows + lo, n, 1) for _, src, lo, n in kv_got],
-        axis=1,
-    )
-    kv = jnp.dot(tokens_perm, kv_weight, preferred_element_type=jnp.float32).astype(jnp.bfloat16)
-    incoming = kv.reshape(ncrop, CAP, CT, 2 * width)
-
     def q_part(acc, piece, src, lo, n):
         cols = lax.dynamic_slice_in_dim(queries_in, src * wrows + lo, n, 1)
         return acc + jnp.dot(cols, piece, preferred_element_type=jnp.float32)
 
-    acc = q_part(jnp.zeros((queries_in.shape[0], width), jnp.float32), q_piece, me, 0, wrows)
-    fwd = q_piece
-    bwd = q_piece
+    acc = q_part(jnp.zeros((queries_in.shape[0], width), jnp.float32), query_weight, me, 0, wrows)
+    fwd = query_weight
+    bwd = query_weight
     for k in range(1, steps_bwd + 1):
         fwd = lax.ppermute(fwd, "crop", fwd_perm)
         bwd = lax.ppermute(bwd, "crop", bwd_perm)
@@ -109,10 +77,36 @@
         src = ring_arr[(pos - steps_fwd) % ncrop]
         acc = q_part(acc, lax.ppermute(fwd[:split], "crop", fwd_perm), src, 0, split)
         acc = q_part(acc, lax.ppermute(bwd[split:], "crop", bwd_perm), src, split, wrows - split)
+
+    chosen = blocks[picks].reshape(-1, crop_tokens.shape[1])
+    chosen_full = head_gather(chosen)
+    sent = chosen_full.reshape(chosen_full.shape[0], ncrop, wrows).transpose(1, 0, 2)
+    got = lax.all_to_all(sent, "crop", split_axis=0, concat_axis=0, tiled=True)
+    got = got.reshape(ncrop, ncrop, CAP * CT, wrows).transpose(1, 0, 2, 3)
+    own_cols = got.reshape(ncrop, nslots * CT, wrows)
+
+    def partial(dest, weight):
+        rows = lax.dynamic_index_in_dim(own_cols, dest, 0, keepdims=False)
+        return jnp.dot(rows, weight, preferred_element_type=jnp.float32)
+
+    def reduce_ring(weight, perm, step):
+        if ncrop == 1:
+            return partial(me, weight).astype(jnp.bfloat16)
+        send = partial(ring_arr[(pos + step) % ncrop], weight).astype(jnp.bfloat16)
+        for k in range(1, ncrop):
+            recv = lax.ppermute(send, "crop", perm).astype(jnp.float32)
+            if k < ncrop - 1:
+                nxt = ring_arr[(pos + step * (k + 1)) % ncrop]
+                send = (recv + partial(nxt, weight)).astype(jnp.bfloat16)
+            else:
+                return (recv + partial(me, weight)).astype(jnp.bfloat16)
+
+    keys_all = reduce_ring(key_weight, fwd_perm, -1)
+    vals_all = reduce_ring(value_weight, bwd_perm, 1)
     query = acc.astype(jnp.bfloat16)
     nslots = ncrop * CAP
-    keys_all = incoming[..., :width].reshape(nslots * CT, heads_here, HD)
-    vals_all = incoming[..., width:].reshape(nslots * CT, heads_here, HD)
+    keys_all = keys_all.reshape(nslots * CT, heads_here, HD)
+    vals_all = vals_all.reshape(nslots * CT, heads_here, HD)
     query_row = query.reshape(rows_here, GR, heads_here, HD)
     in_use = (jnp.arange(NB, dtype=jnp.int32)[None, :] < region_len[:, None])[:, :, None]
     hits = region_slots[:, :, None] == jnp.arange(nslots, dtype=jnp.int32)[None, None, :]

time: 277 us -> 256 us (0.924)
  waiting for transfers between devices: 162 us -> 110 us
  between operations: 9.3 us -> 39.8 us
  local copies, waits for them, and re-layouts: 43 us -> 27.1 us
  starting transfers between devices: 32.4 us -> 45.2 us
  other arithmetic: 3.67 us -> 6.67 us
    ppermute x3, waiting for transfers between devices: 41.4 us -> 0.01 us  [body(): fwd = lax.ppermute(fwd, 'crop', fwd_perm)]
    ppermute x8 -> x14, waiting for transfers between devices: 94.6 us -> 66.1 us  [reduce_ring(): recv = lax.ppermute(send, 'crop', perm).astype(jnp.float32)]
    ppermute x3, waiting for transfers between devices: 0.01 us -> 23.9 us  [body(): bwd = lax.ppermute(bwd, 'crop', bwd_perm)]
    unnamed x40 -> x30, local copies, waits for them, and re-layouts: 24.3 us -> 3.14 us
    ppermute x8 -> x14, starting transfers between devices: 12.2 us -> 20.2 us  [reduce_ring(): recv = lax.ppermute(send, 'crop', perm).astype(jnp.float32)]
    ppermute x3, starting transfers between devices: 0.07 us -> 6.62 us  [body(): bwd = lax.ppermute(bwd, 'crop', bwd_perm)]
    all_to_all x1, waiting for transfers between devices: 5.93 us -> 0.01 us  [body(): got = lax.all_to_all(sent, 'crop', split_axis=0, concat_axis=0, tiled=True)]
    ppermute x3, starting transfers between devices: 6.06 us -> 1.35 us  [body(): fwd = lax.ppermute(fwd, 'crop', fwd_perm)]
  transfers between devices with their start and end apart: 23 -> 29, of which waited for: 14 -> 17; matrix products, arithmetic and copies ran while one was open for 21% -> 17% of each run, Pallas kernels for 0% -> 0%
where the time goes in v10:
time: 256 us; the launch traced here: 254 us
  waiting for transfers between devices  110 us (43%)
  starting transfers between devices  45.2 us (18%)
  between operations  39.8 us (16%)
  local copies, waits for them, and re-layouts  27.1 us (11%)
  matrix products  25.7 us (10%)
  other arithmetic  6.67 us (3%)
    ppermute x14, waiting for transfers between devices, reduce_ring(): recv = lax.ppermute(send, 'crop', perm).astype(jnp.float32)  66.1 us
    ppermute x3, waiting for transfers between devices, body(): bwd = lax.ppermute(bwd, 'crop', bwd_perm)  23.9 us
    ppermute x14, starting transfers between devices, reduce_ring(): recv = lax.ppermute(send, 'crop', perm).astype(jnp.float32)  20.2 us
    dot_general x9, matrix products, q_part(): return acc + jnp.dot(cols, piece, preferred_element_type=jnp.float32)  16.9 us
    ppermute x6, waiting for transfers between devices, head_gather(): part = lax.ppermute(x, 'head', [(j, (j + k) % nhead) for j in range(nhead)])  13.4 us
    dynamic_update_slice x6, local copies, waits for them, and re-layouts, head_gather(): lax.dynamic_update_slice(full, part, (0, (hme - k) % nhead * x.shape[1]))  8.2 us
    dot_general x16, matrix products, partial(): return jnp.dot(rows, weight, preferred_element_type=jnp.float32)  6.98 us
    ppermute x3, starting transfers between devices, body(): bwd = lax.ppermute(bwd, 'crop', bwd_perm)  6.62 us
  transfers between devices with their start and end apart: 29, of which 17 were waited for; matrix products, arithmetic and copies ran while one was open for 17% of the time, Pallas kernels for 0%

profile of v10, /device:TPU:0, one launch (start us, length us, event | category | flops | bytes accessed | tf_op | source)
XLA Modules:
  0.0 254.5 jit_solution(10461441973713090703)
XLA Ops:
  0.0 3.0 %collective-permute-start.21 = (bf16[512,1024]{1,0:T(8,128)(2,1)}, bf16[512,1024]{1,0:T(8,128)(2,1)}, u32[]{:S(2)}, u32[]{:S(2)}) collective-permute-start(bf16[512,1024]{1,0:T(8,128)(2,1)} %param.12), channel_id=1, source_target_pairs={{0,4},{8,0},{16,8},{24,16},{28,24},{20,28},{12,20},{4,12},{1,5},{9... | collective-permute-start | bytes 3145736 | tf_op jit(solution)/shard_map/ppermute | solution.py:73
  7.9 10.2 %collective-permute-done = bf16[256,1024]{1,0:T(8,128)(2,1)S(1)} collective-permute-done((bf16[256,1024]{1,0:T(8,128)(2,1)S(1)}, bf16[256,1024]{1,0:T(8,128)(2,1)S(1)}, u32[]{:S(2)}, u32[]{:S(2)}) %collective-permute-start) | collective-permute-done | bytes 524320 | tf_op jit(solution)/shard_map/ppermute | solution.py:51
  26.3 3.3 %collective-permute-done.2 = bf16[256,1024]{1,0:T(8,128)(2,1)S(1)} collective-permute-done((bf16[256,1024]{1,0:T(8,128)(2,1)S(1)}, bf16[256,1024]{1,0:T(8,128)(2,1)S(1)}, u32[]{:S(2)}, u32[]{:S(2)}) %collective-permute-start.2) | collective-permute-done | bytes 524320 | tf_op jit(solution)/shard_map/ppermute | solution.py:51
  29.6 2.3 collective-permute-start.19
  35.3 2.5 broadcast_in_dim.35
  45.5 5.2 %all-to-all-start = ((bf16[8,256,512]{1,2,0:T(8,128)(2,1)}), bf16[8,256,512]{1,2,0:T(8,128)(2,1)S(1)}, u32[]{:S(2)}, u32[]{:S(2)}) async-start(bf16[8,256,512]{1,2,0:T(8,128)(2,1)} %bitcast.173), calls=%async_computation | async-start | bytes 4194304 | tf_op jit(solution)/shard_map/all_to_all | solution.py:84
  85.1 2.3 constant_dynamic-update-slice_fusion.2
  87.4 2.4 constant_dynamic-update-slice_fusion.1
  89.8 2.3 constant_dynamic-update-slice_fusion
  96.0 2.1 fusion.25
  98.1 2.1 fusion.27
  100.2 2.1 fusion.21
  102.3 23.9 %collective-permute-done.25 = bf16[512,1024]{1,0:T(8,128)(2,1)S(1)} collective-permute-done((bf16[512,1024]{1,0:T(8,128)(2,1)}, bf16[512,1024]{1,0:T(8,128)(2,1)S(1)}, u32[]{:S(2)}, u32[]{:S(2)}) %collective-permute-start.25) | collective-permute-done | bytes 1048608 | tf_op jit(solution)/shard_map/ppermute | solution.py:73
  126.3 2.1 fusion.23
  128.5 5.2 %collective-permute-start.26 = (bf16[256,1024]{1,0:T(8,128)(2,1)S(1)}, bf16[256,1024]{1,0:T(8,128)(2,1)S(1)}, u32[]{:S(2)}, u32[]{:S(2)}) collective-permute-start(bf16[256,1024]{1,0:T(8,128)(2,1)S(1)} %slice.10), channel_id=1, source_target_pairs={{0,8},{8,16},{16,24},{24,28},{28,20},{20,12},{12,4},{4,0},{1,9},{9... | collective-permute-start | bytes 1572872 | tf_op jit(solution)/shard_map/ppermute | solution.py:78
  135.4 4.7 %collective-permute-done.27 = bf16[256,1024]{1,0:T(8,128)(2,1)S(1)} collective-permute-done((bf16[256,1024]{1,0:T(8,128)(2,1)S(1)}, bf16[256,1024]{1,0:T(8,128)(2,1)S(1)}, u32[]{:S(2)}, u32[]{:S(2)}) %collective-permute-start.27) | collective-permute-done | bytes 524320 | tf_op jit(solution)/shard_map/ppermute | solution.py:79
  144.9 2.2 fusion.8
  147.6 2.4 copy.54
  154.2 2.7 %collective-permute-start.10 = (bf16[256,1024]{1,0:T(8,128)(2,1)S(1)}, bf16[256,1024]{1,0:T(8,128)(2,1)S(1)}, u32[]{:S(2)}, u32[]{:S(2)}) collective-permute-start(bf16[256,1024]{1,0:T(8,128)(2,1)S(1)} %convolution_convert_fusion), channel_id=1, source_target_pairs={{0,8},{8,16},{16,24},{24,28},{28,20},{20,12},{12,4},{4,0},{1,9},{9... | collective-permute-start | bytes 1572872 | tf_op jit(solution)/shard_map/ppermute | solution.py:97
  157.3 2.7 %collective-permute-start.3 = (bf16[256,1024]{1,0:T(8,128)(2,1)S(1)}, bf16[256,1024]{1,0:T(8,128)(2,1)S(1)}, u32[]{:S(2)}, u32[]{:S(2)}) collective-permute-start(bf16[256,1024]{1,0:T(8,128)(2,1)S(1)} %convolution_convert_fusion.1), channel_id=1, source_target_pairs={{0,4},{8,0},{16,8},{24,16},{28,24},{20,28},{12,20},{4,12},{1,5},{9... | collective-permute-start | bytes 1572872 | tf_op jit(solution)/shard_map/ppermute | solution.py:97
  161.0 8.3 %collective-permute-done.3 = bf16[256,1024]{1,0:T(8,128)(2,1)S(1)} collective-permute-done((bf16[256,1024]{1,0:T(8,128)(2,1)S(1)}, bf16[256,1024]{1,0:T(8,128)(2,1)S(1)}, u32[]{:S(2)}, u32[]{:S(2)}) %collective-permute-start.3) | collective-permute-done | bytes 524320 | tf_op jit(solution)/shard_map/ppermute | solution.py:97
  169.8 2.5 collective-permute-start.4
  173.3 8.4 %collective-permute-done.4 = bf16[256,1024]{1,0:T(8,128)(2,1)S(1)} collective-permute-done((bf16[256,1024]{1,0:T(8,128)(2,1)S(1)}, bf16[256,1024]{1,0:T(8,128)(2,1)S(1)}, u32[]{:S(2)}, u32[]{:S(2)}) %collective-permute-start.4) | collective-permute-done | bytes 524320 | tf_op jit(solution)/shard_map/ppermute | solution.py:97
  181.9 2.5 collective-permute-start.5
  185.3 8.4 %collective-permute-done.5 = bf16[256,1024]{1,0:T(8,128)(2,1)S(1)} collective-permute-done((bf16[256,1024]{1,0:T(8,128)(2,1)S(1)}, bf16[256,1024]{1,0:T(8,128)(2,1)S(1)}, u32[]{:S(2)}, u32[]{:S(2)}) %collective-permute-start.5) | collective-permute-done | bytes 524320 | tf_op jit(solution)/shard_map/ppermute | solution.py:97
  193.9 2.5 collective-permute-start.6
  197.4 8.8 %collective-permute-done.6 = bf16[256,1024]{1,0:T(8,128)(2,1)S(1)} collective-permute-done((bf16[256,1024]{1,0:T(8,128)(2,1)S(1)}, bf16[256,1024]{1,0:T(8,128)(2,1)S(1)}, u32[]{:S(2)}, u32[]{:S(2)}) %collective-permute-start.6) | collective-permute-done | bytes 524320 | tf_op jit(solution)/shard_map/ppermute | solution.py:97
  206.4 2.5 collective-permute-start.7
  209.8 10.6 %collective-permute-done.7 = bf16[256,1024]{1,0:T(8,128)(2,1)S(1)} collective-permute-done((bf16[256,1024]{1,0:T(8,128)(2,1)S(1)}, bf16[256,1024]{1,0:T(8,128)(2,1)S(1)}, u32[]{:S(2)}, u32[]{:S(2)}) %collective-permute-start.7) | collective-permute-done | bytes 524320 | tf_op jit(solution)/shard_map/ppermute | solution.py:97
  223.7 12.0 %collective-permute-done.8 = bf16[256,1024]{1,0:T(8,128)(2,1)S(1)} collective-permute-done((bf16[256,1024]{1,0:T(8,128)(2,1)S(1)}, bf16[256,1024]{1,0:T(8,128)(2,1)S(1)}, u32[]{:S(2)}, u32[]{:S(2)}) %collective-permute-start.8) | collective-permute-done | bytes 524320 | tf_op jit(solution)/shard_map/ppermute | solution.py:97
  238.6 6.5 %collective-permute-done.9 = bf16[256,1024]{1,0:T(8,128)(2,1)S(1)} collective-permute-done((bf16[256,1024]{1,0:T(8,128)(2,1)S(1)}, bf16[256,1024]{1,0:T(8,128)(2,1)S(1)}, u32[]{:S(2)}, u32[]{:S(2)}) %collective-permute-start.9) | collective-permute-done | bytes 524320 | tf_op jit(solution)/shard_map/ppermute | solution.py:97
  248.0 3.5 %fusion.115 = (f32[16,8,32]{2,0,1:T(8,128)S(1)}, f32[16,8,32,256]{3,2,0,1:T(8,128)S(1)}) fusion(f32[8,256,16,32]{1,3,2,0:T(8,128)S(1)} %bitcast.177, pred[16,256]{1,0:T(8,128)(4,1)S(1)} %broadcast_in_dim.33), kind=kOutput, calls=%fused_computation.143 | output fusion | flops 6291711 | bytes 8409088 | tf_op jit(solution)/shard_map/sub | solution.py:122
  (126 shorter events, 52.3 us)
Async XLA Ops:
  0.0 33.2 %copy-start.12 = (s32[16,8]{0,1:T(8,128)S(1)}, s32[16,8]{0,1:T(8,128)}, u32[]{:S(2)}) copy-start(s32[16,8]{0,1:T(8,128)} %param.16) | copy-start | bytes 1540
  0.0 33.5 %collective-permute-start.21 = (bf16[512,1024]{1,0:T(8,128)(2,1)}, bf16[512,1024]{1,0:T(8,128)(2,1)}, u32[]{:S(2)}, u32[]{:S(2)}) collective-permute-start(bf16[512,1024]{1,0:T(8,128)(2,1)} %param.12), channel_id=1, source_target_pairs={{0,4},{8,0},{16,8},{24,16},{28,24},{20,28},{12,20},{4,12},{1,5},{9... | collective-permute-start | bytes 3145736 | tf_op jit(solution)/shard_map/ppermute | solution.py:73
  4.4 13.7 %collective-permute-start = (bf16[256,1024]{1,0:T(8,128)(2,1)S(1)}, bf16[256,1024]{1,0:T(8,128)(2,1)S(1)}, u32[]{:S(2)}, u32[]{:S(2)}) collective-permute-start(bf16[256,1024]{1,0:T(8,128)(2,1)S(1)} %bitcast.179), channel_id=1, source_target_pairs={{0,1},{1,2},{2,3},{3,0},{4,5},{5,6},{6,7},{7,4},{8,9},{9,10},{10,1... | collective-permute-start | bytes 1572872 | tf_op jit(solution)/shard_map/ppermute | solution.py:51
  4.5 19.5 %collective-permute-start.1 = (bf16[256,1024]{1,0:T(8,128)(2,1)S(1)}, bf16[256,1024]{1,0:T(8,128)(2,1)S(1)}, u32[]{:S(2)}, u32[]{:S(2)}) collective-permute-start(bf16[256,1024]{1,0:T(8,128)(2,1)S(1)} %bitcast.180), channel_id=1, source_target_pairs={{0,2},{1,3},{2,0},{3,1},{4,6},{5,7},{6,4},{7,5},{8,10},{9,11},{10,... | collective-permute-start | bytes 1572872 | tf_op jit(solution)/shard_map/ppermute | solution.py:51
  6.0 36.4 %collective-permute-start.20 = (bf16[512,1024]{1,0:T(8,128)(2,1)}, bf16[512,1024]{1,0:T(8,128)(2,1)}, u32[]{:S(2)}, u32[]{:S(2)}) collective-permute-start(bf16[512,1024]{1,0:T(8,128)(2,1)} %param.12), channel_id=1, source_target_pairs={{0,8},{8,16},{16,24},{24,28},{28,20},{20,12},{12,4},{4,0},{1,9},{9... | collective-permute-start | bytes 3145736 | tf_op jit(solution)/shard_map/ppermute | solution.py:72
  6.8 22.7 %collective-permute-start.2 = (bf16[256,1024]{1,0:T(8,128)(2,1)S(1)}, bf16[256,1024]{1,0:T(8,128)(2,1)S(1)}, u32[]{:S(2)}, u32[]{:S(2)}) collective-permute-start(bf16[256,1024]{1,0:T(8,128)(2,1)S(1)} %bitcast.181), channel_id=1, source_target_pairs={{0,3},{1,0},{2,1},{3,2},{4,7},{5,4},{6,5},{7,6},{8,11},{9,8},{10,9... | collective-permute-start | bytes 1572872 | tf_op jit(solution)/shard_map/ppermute | solution.py:51
  18.1 15.2 %copy-start.7 = (bf16[256,1024]{1,0:T(8,128)(2,1)}, bf16[256,1024]{1,0:T(8,128)(2,1)S(1)}, u32[]{:S(2)}) copy-start(bf16[256,1024]{1,0:T(8,128)(2,1)S(1)} %collective-permute-done) | copy-start | bytes 1572868
  18.1 67.0 %collective-permute-start.17 = (bf16[512,1024]{1,0:T(8,128)(2,1)}, bf16[512,1024]{1,0:T(8,128)(2,1)}, u32[]{:S(2)}, u32[]{:S(2)}) collective-permute-start(bf16[512,1024]{1,0:T(8,128)(2,1)} %param.10), channel_id=1, source_target_pairs={{0,1},{1,2},{2,3},{3,0},{4,5},{5,6},{6,7},{7,4},{8,9},{9,10},{10,1... | collective-permute-start | bytes 3145736 | tf_op jit(solution)/shard_map/ppermute | solution.py:51
  24.0 9.3 %copy-start.9 = (bf16[256,1024]{1,0:T(8,128)(2,1)}, bf16[256,1024]{1,0:T(8,128)(2,1)S(1)}, u32[]{:S(2)}) copy-start(bf16[256,1024]{1,0:T(8,128)(2,1)S(1)} %collective-permute-done.1) | copy-start | bytes 1572868
  24.0 63.4 %collective-permute-start.18 = (bf16[512,1024]{1,0:T(8,128)(2,1)}, bf16[512,1024]{1,0:T(8,128)(2,1)}, u32[]{:S(2)}, u32[]{:S(2)}) collective-permute-start(bf16[512,1024]{1,0:T(8,128)(2,1)} %param.10), channel_id=1, source_target_pairs={{0,2},{1,3},{2,0},{3,1},{4,6},{5,7},{6,4},{7,5},{8,10},{9,11},{10,... | collective-permute-start | bytes 3145736 | tf_op jit(solution)/shard_map/ppermute | solution.py:51
  29.6 60.3 %collective-permute-start.19 = (bf16[512,1024]{1,0:T(8,128)(2,1)}, bf16[512,1024]{1,0:T(8,128)(2,1)}, u32[]{:S(2)}, u32[]{:S(2)}) collective-permute-start(bf16[512,1024]{1,0:T(8,128)(2,1)} %param.10), channel_id=1, source_target_pairs={{0,3},{1,0},{2,1},{3,2},{4,7},{5,4},{6,5},{7,6},{8,11},{9,8},{10,9... | collective-permute-start | bytes 3145736 | tf_op jit(solution)/shard_map/ppermute | solution.py:51
  33.5 58.6 %collective-permute-start.23 = (bf16[512,1024]{1,0:T(8,128)(2,1)}, bf16[512,1024]{1,0:T(8,128)(2,1)}, u32[]{:S(2)}, u32[]{:S(2)}) collective-permute-start(bf16[512,1024]{1,0:T(8,128)(2,1)} %collective-permute-done.21), channel_id=1, source_target_pairs={{0,4},{8,0},{16,8},{24,16},{28,24},{20,28},{12,20},{4,12},{1,5},{9... | collective-permute-start | bytes 3145736 | tf_op jit(solution)/shard_map/ppermute | solution.py:73
  42.5 53.5 %collective-permute-start.22 = (bf16[512,1024]{1,0:T(8,128)(2,1)}, bf16[512,1024]{1,0:T(8,128)(2,1)}, u32[]{:S(2)}, u32[]{:S(2)}) collective-permute-start(bf16[512,1024]{1,0:T(8,128)(2,1)} %collective-permute-done.20), channel_id=1, source_target_pairs={{0,8},{8,16},{16,24},{24,28},{28,20},{20,12},{12,4},{4,0},{1,9},{9... | collective-permute-start | bytes 3145736 | tf_op jit(solution)/shard_map/ppermute | solution.py:72
  45.5 102.1 %all-to-all-start = ((bf16[8,256,512]{1,2,0:T(8,128)(2,1)}), bf16[8,256,512]{1,2,0:T(8,128)(2,1)S(1)}, u32[]{:S(2)}, u32[]{:S(2)}) async-start(bf16[8,256,512]{1,2,0:T(8,128)(2,1)} %bitcast.173), calls=%async_computation | async-start | bytes 4194304 | tf_op jit(solution)/shard_map/all_to_all | solution.py:84
  92.1 34.1 %collective-permute-start.25 = (bf16[512,1024]{1,0:T(8,128)(2,1)}, bf16[512,1024]{1,0:T(8,128)(2,1)S(1)}, u32[]{:S(2)}, u32[]{:S(2)}) collective-permute-start(bf16[512,1024]{1,0:T(8,128)(2,1)} %collective-permute-done.23), channel_id=1, source_target_pairs={{0,4},{8,0},{16,8},{24,16},{28,24},{20,28},{12,20},{4,12},{1,5},{9... | collective-permute-start | bytes 3145736 | tf_op jit(solution)/shard_map/ppermute | solution.py:73
  95.9 32.5 %collective-permute-start.24 = (bf16[512,1024]{1,0:T(8,128)(2,1)}, bf16[512,1024]{1,0:T(8,128)(2,1)S(1)}, u32[]{:S(2)}, u32[]{:S(2)}) collective-permute-start(bf16[512,1024]{1,0:T(8,128)(2,1)} %collective-permute-done.22), channel_id=1, source_target_pairs={{0,8},{8,16},{16,24},{24,28},{28,20},{20,12},{12,4},{4,0},{1,9},{9... | collective-permute-start | bytes 3145736 | tf_op jit(solution)/shard_map/ppermute | solution.py:72
  126.2 13.9 %collective-permute-start.27 = (bf16[256,1024]{1,0:T(8,128)(2,1)S(1)}, bf16[256,1024]{1,0:T(8,128)(2,1)S(1)}, u32[]{:S(2)}, u32[]{:S(2)}) collective-permute-start(bf16[256,1024]{1,0:T(8,128)(2,1)S(1)} %slice.11), channel_id=1, source_target_pairs={{0,4},{8,0},{16,8},{24,16},{28,24},{20,28},{12,20},{4,12},{1,5},{9... | collective-permute-start | bytes 1572872 | tf_op jit(solution)/shard_map/ppermute | solution.py:79
  128.5 15.0 %collective-permute-start.26 = (bf16[256,1024]{1,0:T(8,128)(2,1)S(1)}, bf16[256,1024]{1,0:T(8,128)(2,1)S(1)}, u32[]{:S(2)}, u32[]{:S(2)}) collective-permute-start(bf16[256,1024]{1,0:T(8,128)(2,1)S(1)} %slice.10), channel_id=1, source_target_pairs={{0,8},{8,16},{16,24},{24,28},{28,20},{20,12},{12,4},{4,0},{1,9},{9... | collective-permute-start | bytes 1572872 | tf_op jit(solution)/shard_map/ppermute | solution.py:78
  154.2 18.1 %collective-permute-start.10 = (bf16[256,1024]{1,0:T(8,128)(2,1)S(1)}, bf16[256,1024]{1,0:T(8,128)(2,1)S(1)}, u32[]{:S(2)}, u32[]{:S(2)}) collective-permute-start(bf16[256,1024]{1,0:T(8,128)(2,1)S(1)} %convolution_convert_fusion), channel_id=1, source_target_pairs={{0,8},{8,16},{16,24},{24,28},{28,20},{20,12},{12,4},{4,0},{1,9},{9... | collective-permute-start | bytes 1572872 | tf_op jit(solution)/shard_map/ppermute | solution.py:97
  157.3 12.0 %collective-permute-start.3 = (bf16[256,1024]{1,0:T(8,128)(2,1)S(1)}, bf16[256,1024]{1,0:T(8,128)(2,1)S(1)}, u32[]{:S(2)}, u32[]{:S(2)}) collective-permute-start(bf16[256,1024]{1,0:T(8,128)(2,1)S(1)} %convolution_convert_fusion.1), channel_id=1, source_target_pairs={{0,4},{8,0},{16,8},{24,16},{28,24},{20,28},{12,20},{4,12},{1,5},{9... | collective-permute-start | bytes 1572872 | tf_op jit(solution)/shard_map/ppermute | solution.py:97
  169.8 11.9 %collective-permute-start.4 = (bf16[256,1024]{1,0:T(8,128)(2,1)S(1)}, bf16[256,1024]{1,0:T(8,128)(2,1)S(1)}, u32[]{:S(2)}, u32[]{:S(2)}) collective-permute-start(bf16[256,1024]{1,0:T(8,128)(2,1)S(1)} %add_convert_fusion.14), channel_id=1, source_target_pairs={{0,4},{8,0},{16,8},{24,16},{28,24},{20,28},{12,20},{4,12},{1,5},{9... | collective-permute-start | bytes 1572872 | tf_op jit(solution)/shard_map/ppermute | solution.py:97
  172.8 11.9 %collective-permute-start.11 = (bf16[256,1024]{1,0:T(8,128)(2,1)S(1)}, bf16[256,1024]{1,0:T(8,128)(2,1)S(1)}, u32[]{:S(2)}, u32[]{:S(2)}) collective-permute-start(bf16[256,1024]{1,0:T(8,128)(2,1)S(1)} %add_convert_fusion.7), channel_id=1, source_target_pairs={{0,8},{8,16},{16,24},{24,28},{28,20},{20,12},{12,4},{4,0},{1,9},{9... | collective-permute-start | bytes 1572872 | tf_op jit(solution)/shard_map/ppermute | solution.py:97
  181.9 11.9 %collective-permute-start.5 = (bf16[256,1024]{1,0:T(8,128)(2,1)S(1)}, bf16[256,1024]{1,0:T(8,128)(2,1)S(1)}, u32[]{:S(2)}, u32[]{:S(2)}) collective-permute-start(bf16[256,1024]{1,0:T(8,128)(2,1)S(1)} %add_convert_fusion.13), channel_id=1, source_target_pairs={{0,4},{8,0},{16,8},{24,16},{28,24},{20,28},{12,20},{4,12},{1,5},{9... | collective-permute-start | bytes 1572872 | tf_op jit(solution)/shard_map/ppermute | solution.py:97
  184.8 11.9 %collective-permute-start.12 = (bf16[256,1024]{1,0:T(8,128)(2,1)S(1)}, bf16[256,1024]{1,0:T(8,128)(2,1)S(1)}, u32[]{:S(2)}, u32[]{:S(2)}) collective-permute-start(bf16[256,1024]{1,0:T(8,128)(2,1)S(1)} %add_convert_fusion.6), channel_id=1, source_target_pairs={{0,8},{8,16},{16,24},{24,28},{28,20},{20,12},{12,4},{4,0},{1,9},{9... | collective-permute-start | bytes 1572872 | tf_op jit(solution)/shard_map/ppermute | solution.py:97
  193.9 12.3 %collective-permute-start.6 = (bf16[256,1024]{1,0:T(8,128)(2,1)S(1)}, bf16[256,1024]{1,0:T(8,128)(2,1)S(1)}, u32[]{:S(2)}, u32[]{:S(2)}) collective-permute-start(bf16[256,1024]{1,0:T(8,128)(2,1)S(1)} %add_convert_fusion.12), channel_id=1, source_target_pairs={{0,4},{8,0},{16,8},{24,16},{28,24},{20,28},{12,20},{4,12},{1,5},{9... | collective-permute-start | bytes 1572872 | tf_op jit(solution)/shard_map/ppermute | solution.py:97
  196.9 12.3 %collective-permute-start.13 = (bf16[256,1024]{1,0:T(8,128)(2,1)S(1)}, bf16[256,1024]{1,0:T(8,128)(2,1)S(1)}, u32[]{:S(2)}, u32[]{:S(2)}) collective-permute-start(bf16[256,1024]{1,0:T(8,128)(2,1)S(1)} %add_convert_fusion.5), channel_id=1, source_target_pairs={{0,8},{8,16},{16,24},{24,28},{28,20},{20,12},{12,4},{4,0},{1,9},{9... | collective-permute-start | bytes 1572872 | tf_op jit(solution)/shard_map/ppermute | solution.py:97
  206.4 14.1 %collective-permute-start.7 = (bf16[256,1024]{1,0:T(8,128)(2,1)S(1)}, bf16[256,1024]{1,0:T(8,128)(2,1)S(1)}, u32[]{:S(2)}, u32[]{:S(2)}) collective-permute-start(bf16[256,1024]{1,0:T(8,128)(2,1)S(1)} %add_convert_fusion.11), channel_id=1, source_target_pairs={{0,4},{8,0},{16,8},{24,16},{28,24},{20,28},{12,20},{4,12},{1,5},{9... | collective-permute-start | bytes 1572872 | tf_op jit(solution)/shard_map/ppermute | solution.py:97
  209.3 13.1 %collective-permute-start.14 = (bf16[256,1024]{1,0:T(8,128)(2,1)S(1)}, bf16[256,1024]{1,0:T(8,128)(2,1)S(1)}, u32[]{:S(2)}, u32[]{:S(2)}) collective-permute-start(bf16[256,1024]{1,0:T(8,128)(2,1)S(1)} %add_convert_fusion.4), channel_id=1, source_target_pairs={{0,8},{8,16},{16,24},{24,28},{28,20},{20,12},{12,4},{4,0},{1,9},{9... | collective-permute-start | bytes 1572872 | tf_op jit(solution)/shard_map/ppermute | solution.py:97
  220.6 15.1 %collective-permute-start.8 = (bf16[256,1024]{1,0:T(8,128)(2,1)S(1)}, bf16[256,1024]{1,0:T(8,128)(2,1)S(1)}, u32[]{:S(2)}, u32[]{:S(2)}) collective-permute-start(bf16[256,1024]{1,0:T(8,128)(2,1)S(1)} %add_convert_fusion.10), channel_id=1, source_target_pairs={{0,4},{8,0},{16,8},{24,16},{28,24},{20,28},{12,20},{4,12},{1,5},{9... | collective-permute-start | bytes 1572872 | tf_op jit(solution)/shard_map/ppermute | solution.py:97
  222.6 14.5 %collective-permute-start.15 = (bf16[256,1024]{1,0:T(8,128)(2,1)S(1)}, bf16[256,1024]{1,0:T(8,128)(2,1)S(1)}, u32[]{:S(2)}, u32[]{:S(2)}) collective-permute-start(bf16[256,1024]{1,0:T(8,128)(2,1)S(1)} %add_convert_fusion.3), channel_id=1, source_target_pairs={{0,8},{8,16},{16,24},{24,28},{28,20},{20,12},{12,4},{4,0},{1,9},{9... | collective-permute-start | bytes 1572872 | tf_op jit(solution)/shard_map/ppermute | solution.py:97
  235.9 9.2 %collective-permute-start.9 = (bf16[256,1024]{1,0:T(8,128)(2,1)S(1)}, bf16[256,1024]{1,0:T(8,128)(2,1)S(1)}, u32[]{:S(2)}, u32[]{:S(2)}) collective-permute-start(bf16[256,1024]{1,0:T(8,128)(2,1)S(1)} %add_convert_fusion.9), channel_id=1, source_target_pairs={{0,4},{8,0},{16,8},{24,16},{28,24},{20,28},{12,20},{4,12},{1,5},{9... | collective-permute-start | bytes 1572872 | tf_op jit(solution)/shard_map/ppermute | solution.py:97
  237.2 10.1 %collective-permute-start.16 = (bf16[256,1024]{1,0:T(8,128)(2,1)S(1)}, bf16[256,1024]{1,0:T(8,128)(2,1)S(1)}, u32[]{:S(2)}, u32[]{:S(2)}) collective-permute-start(bf16[256,1024]{1,0:T(8,128)(2,1)S(1)} %add_convert_fusion.2), channel_id=1, source_target_pairs={{0,8},{8,16},{16,24},{24,28},{28,20},{20,12},{12,4},{4,0},{1,9},{9... | collective-permute-start | bytes 1572872 | tf_op jit(solution)/shard_map/ppermute | solution.py:97
  (10 other events, 35.5 us)

commit v11 on v10

--- a/solution.py
+++ b/solution.py
@@ -61,13 +61,21 @@
     steps_bwd = (ncrop - 1) // 2
     split = wrows // 2
 
+    chosen = blocks[picks].reshape(-1, crop_tokens.shape[1])
+    chosen_full = head_gather(chosen)
+    sent = chosen_full.reshape(chosen_full.shape[0], ncrop, wrows).transpose(1, 0, 2)
+    got = lax.all_to_all(sent, "crop", split_axis=0, concat_axis=0, tiled=True)
+    got = got.reshape(ncrop, ncrop, CAP * CT, wrows).transpose(1, 0, 2, 3)
+    own_cols = got.reshape(ncrop, nslots * CT, wrows)
+
     def q_part(acc, piece, src, lo, n):
         cols = lax.dynamic_slice_in_dim(queries_in, src * wrows + lo, n, 1)
         return acc + jnp.dot(cols, piece, preferred_element_type=jnp.float32)
 
-    acc = q_part(jnp.zeros((queries_in.shape[0], width), jnp.float32), query_weight, me, 0, wrows)
-    fwd = query_weight
-    bwd = query_weight
+    q_piece, own_cols = lax.optimization_barrier((query_weight, own_cols))
+    acc = q_part(jnp.zeros((queries_in.shape[0], width), jnp.float32), q_piece, me, 0, wrows)
+    fwd = q_piece
+    bwd = q_piece
     for k in range(1, steps_bwd + 1):
         fwd = lax.ppermute(fwd, "crop", fwd_perm)
         bwd = lax.ppermute(bwd, "crop", bwd_perm)
@@ -77,13 +85,6 @@
         src = ring_arr[(pos - steps_fwd) % ncrop]
         acc = q_part(acc, lax.ppermute(fwd[:split], "crop", fwd_perm), src, 0, split)
         acc = q_part(acc, lax.ppermute(bwd[split:], "crop", bwd_perm), src, split, wrows - split)
-
-    chosen = blocks[picks].reshape(-1, crop_tokens.shape[1])
-    chosen_full = head_gather(chosen)
-    sent = chosen_full.reshape(chosen_full.shape[0], ncrop, wrows).transpose(1, 0, 2)
-    got = lax.all_to_all(sent, "crop", split_axis=0, concat_axis=0, tiled=True)
-    got = got.reshape(ncrop, ncrop, CAP * CT, wrows).transpose(1, 0, 2, 3)
-    own_cols = got.reshape(ncrop, nslots * CT, wrows)
 
     def partial(dest, weight):
         rows = lax.dynamic_index_in_dim(own_cols, dest, 0, keepdims=False)

time: 256 us -> 274 us (1.070)
  waiting for transfers between devices: 110 us -> 138 us
  starting transfers between devices: 45.2 us -> 36.4 us
    ppermute x14, waiting for transfers between devices: 66.1 us -> 113 us  [reduce_ring(): recv = lax.ppermute(send, 'crop', perm).astype(jnp.float32)]
    ppermute x3, waiting for transfers between devices: 23.9 us -> 0.01 us  [body(): bwd = lax.ppermute(bwd, 'crop', bwd_perm)]
    ppermute x14, starting transfers between devices: 20.2 us -> 14.5 us  [reduce_ring(): recv = lax.ppermute(send, 'crop', perm).astype(jnp.float32)]
    ppermute x6, waiting for transfers between devices: 13.4 us -> 19 us  [head_gather(): part = lax.ppermute(x, 'head', [(j, (j + k) % nhead) for j in range(nhead)])]
    ppermute x1, starting transfers between devices: 5.16 us -> 0.42 us  [body(): lax.ppermute(fwd[:split], 'crop', fwd_perm)]
  transfers between devices with their start and end apart: 29 -> 29, of which waited for: 17 -> 14; matrix products, arithmetic and copies ran while one was open for 17% -> 15% of each run, Pallas kernels for 0% -> 0%
where the time goes in v11:
time: 274 us; the launch traced here: 273 us
  waiting for transfers between devices  138 us (50%)
  between operations  40.2 us (15%)
  starting transfers between devices  36.4 us (13%)
  local copies, waits for them, and re-layouts  27.8 us (10%)
  matrix products  24.2 us (9%)
  other arithmetic  6.09 us (2%)
    ppermute x14, waiting for transfers between devices, reduce_ring(): recv = lax.ppermute(send, 'crop', perm).astype(jnp.float32)  113 us
    ppermute x6, waiting for transfers between devices, head_gather(): part = lax.ppermute(x, 'head', [(j, (j + k) % nhead) for j in range(nhead)])  19 us
    dot_general x9, matrix products, q_part(): return acc + jnp.dot(cols, piece, preferred_element_type=jnp.float32)  15.5 us
    ppermute x14, starting transfers between devices, reduce_ring(): recv = lax.ppermute(send, 'crop', perm).astype(jnp.float32)  14.5 us
    dynamic_update_slice x6, local copies, waits for them, and re-layouts, head_gather(): lax.dynamic_update_slice(full, part, (0, (hme - k) % nhead * x.shape[1]))  8.2 us
    ppermute x6, starting transfers between devices, head_gather(): part = lax.ppermute(x, 'head', [(j, (j + k) % nhead) for j in range(nhead)])  7.75 us
    dot_general x16, matrix products, partial(): return jnp.dot(rows, weight, preferred_element_type=jnp.float32)  6.98 us
    all_to_all x1, starting transfers between devices, body(): got = lax.all_to_all(sent, 'crop', split_axis=0, concat_axis=0, tiled=True)  5.91 us
  transfers between devices with their start and end apart: 29, of which 14 were waited for; matrix products, arithmetic and copies ran while one was open for 15% of the time, Pallas kernels for 0%

profile of v11, /device:TPU:0, one launch (start us, length us, event | category | flops | bytes accessed | tf_op | source)
XLA Modules:
  0.0 272.7 jit_solution(9808384590662758454)
XLA Ops:
  2.2 3.0 %collective-permute-start.1 = (bf16[256,1024]{1,0:T(8,128)(2,1)S(1)}, bf16[256,1024]{1,0:T(8,128)(2,1)}, u32[]{:S(2)}, u32[]{:S(2)}) collective-permute-start(bf16[256,1024]{1,0:T(8,128)(2,1)S(1)} %bitcast.179), channel_id=1, source_target_pairs={{0,2},{1,3},{2,0},{3,1},{4,6},{5,7},{6,4},{7,5},{8,10},{9,11},{10,... | collective-permute-start | bytes 1572872 | tf_op jit(solution)/shard_map/ppermute | solution.py:51
  5.2 1.7 collective-permute-start.2
  7.4 10.7 %collective-permute-done.1 = bf16[256,1024]{1,0:T(8,128)(2,1)} collective-permute-done((bf16[256,1024]{1,0:T(8,128)(2,1)S(1)}, bf16[256,1024]{1,0:T(8,128)(2,1)}, u32[]{:S(2)}, u32[]{:S(2)}) %collective-permute-start.1) | collective-permute-done | bytes 524320 | tf_op jit(solution)/shard_map/ppermute | solution.py:51
  19.3 8.3 %collective-permute-done = bf16[256,1024]{1,0:T(8,128)(2,1)} collective-permute-done((bf16[256,1024]{1,0:T(8,128)(2,1)S(1)}, bf16[256,1024]{1,0:T(8,128)(2,1)}, u32[]{:S(2)}, u32[]{:S(2)}) %collective-permute-start) | collective-permute-done | bytes 524320 | tf_op jit(solution)/shard_map/ppermute | solution.py:51
  27.6 2.0 copy.51
  33.5 5.9 %all-to-all-start = ((bf16[8,256,512]{1,2,0:T(8,128)(2,1)}), bf16[8,256,512]{1,2,0:T(8,128)(2,1)S(1)}, u32[]{:S(2)}, u32[]{:S(2)}) async-start(bf16[8,256,512]{1,2,0:T(8,128)(2,1)} %bitcast.173), calls=%async_computation | async-start | bytes 4194304 | tf_op jit(solution)/shard_map/all_to_all | solution.py:67
  83.9 2.5 broadcast_in_dim.35
  87.5 2.3 constant_dynamic-update-slice_fusion.2
  89.8 2.4 constant_dynamic-update-slice_fusion.1
  92.2 2.3 constant_dynamic-update-slice_fusion
  94.5 2.4 copy.54
  96.9 1.9 copy.55
  98.8 2.0 collective-permute-start.21
  102.7 2.0 collective-permute-start.3
  107.9 1.8 fusion.29
  110.6 24.0 %collective-permute-done.3 = bf16[256,1024]{1,0:T(8,128)(2,1)S(1)} collective-permute-done((bf16[256,1024]{1,0:T(8,128)(2,1)S(1)}, bf16[256,1024]{1,0:T(8,128)(2,1)S(1)}, u32[]{:S(2)}, u32[]{:S(2)}) %collective-permute-start.3) | collective-permute-done | bytes 524320 | tf_op jit(solution)/shard_map/ppermute | solution.py:98
  135.0 1.8 collective-permute-start.4
  138.0 9.3 %collective-permute-done.4 = bf16[256,1024]{1,0:T(8,128)(2,1)S(1)} collective-permute-done((bf16[256,1024]{1,0:T(8,128)(2,1)S(1)}, bf16[256,1024]{1,0:T(8,128)(2,1)S(1)}, u32[]{:S(2)}, u32[]{:S(2)}) %collective-permute-start.4) | collective-permute-done | bytes 524320 | tf_op jit(solution)/shard_map/ppermute | solution.py:98
  151.8 1.7 fusion.25
  153.5 8.8 %collective-permute-done.5 = bf16[256,1024]{1,0:T(8,128)(2,1)S(1)} collective-permute-done((bf16[256,1024]{1,0:T(8,128)(2,1)S(1)}, bf16[256,1024]{1,0:T(8,128)(2,1)S(1)}, u32[]{:S(2)}, u32[]{:S(2)}) %collective-permute-start.5) | collective-permute-done | bytes 524320 | tf_op jit(solution)/shard_map/ppermute | solution.py:98
  162.5 1.7 collective-permute-start.6
  165.0 1.8 fusion.27
  166.7 26.4 %collective-permute-done.6 = bf16[256,1024]{1,0:T(8,128)(2,1)S(1)} collective-permute-done((bf16[256,1024]{1,0:T(8,128)(2,1)S(1)}, bf16[256,1024]{1,0:T(8,128)(2,1)S(1)}, u32[]{:S(2)}, u32[]{:S(2)}) %collective-permute-start.6) | collective-permute-done | bytes 524320 | tf_op jit(solution)/shard_map/ppermute | solution.py:98
  197.6 1.8 fusion.21
  199.3 8.8 %collective-permute-done.7 = bf16[256,1024]{1,0:T(8,128)(2,1)S(1)} collective-permute-done((bf16[256,1024]{1,0:T(8,128)(2,1)S(1)}, bf16[256,1024]{1,0:T(8,128)(2,1)S(1)}, u32[]{:S(2)}, u32[]{:S(2)}) %collective-permute-start.7) | collective-permute-done | bytes 524320 | tf_op jit(solution)/shard_map/ppermute | solution.py:98
  210.6 1.8 fusion.23
  212.3 26.5 %collective-permute-done.8 = bf16[256,1024]{1,0:T(8,128)(2,1)S(1)} collective-permute-done((bf16[256,1024]{1,0:T(8,128)(2,1)S(1)}, bf16[256,1024]{1,0:T(8,128)(2,1)S(1)}, u32[]{:S(2)}, u32[]{:S(2)}) %collective-permute-start.8) | collective-permute-done | bytes 524320 | tf_op jit(solution)/shard_map/ppermute | solution.py:98
  243.5 1.7 fusion.19
  245.3 8.7 %collective-permute-done.9 = bf16[256,1024]{1,0:T(8,128)(2,1)S(1)} collective-permute-done((bf16[256,1024]{1,0:T(8,128)(2,1)S(1)}, bf16[256,1024]{1,0:T(8,128)(2,1)S(1)}, u32[]{:S(2)}, u32[]{:S(2)}) %collective-permute-start.9) | collective-permute-done | bytes 524320 | tf_op jit(solution)/shard_map/ppermute | solution.py:98
  254.2 5.7 %collective-permute-done.27 = bf16[256,1024]{1,0:T(8,128)(2,1)S(1)} collective-permute-done((bf16[256,1024]{1,0:T(8,128)(2,1)S(1)}, bf16[256,1024]{1,0:T(8,128)(2,1)S(1)}, u32[]{:S(2)}, u32[]{:S(2)}) %collective-permute-start.27) | collective-permute-done | bytes 524320 | tf_op jit(solution)/shard_map/ppermute | solution.py:87
  262.8 2.2 fusion.8
  266.2 3.5 %fusion.115 = (f32[16,8,32]{2,0,1:T(8,128)S(1)}, f32[16,8,32,256]{3,2,0,1:T(8,128)S(1)}) fusion(f32[8,256,16,32]{1,3,2,0:T(8,128)S(1)} %bitcast.177, pred[16,256]{1,0:T(8,128)(4,1)S(1)} %broadcast_in_dim.33), kind=kOutput, calls=%fused_computation.143 | output fusion | flops 6291711 | bytes 8409088 | tf_op jit(solution)/shard_map/sub | solution.py:123
  (122 shorter events, 44.9 us)
Async XLA Ops:
  2.2 15.9 %collective-permute-start.1 = (bf16[256,1024]{1,0:T(8,128)(2,1)S(1)}, bf16[256,1024]{1,0:T(8,128)(2,1)}, u32[]{:S(2)}, u32[]{:S(2)}) collective-permute-start(bf16[256,1024]{1,0:T(8,128)(2,1)S(1)} %bitcast.179), channel_id=1, source_target_pairs={{0,2},{1,3},{2,0},{3,1},{4,6},{5,7},{6,4},{7,5},{8,10},{9,11},{10,... | collective-permute-start | bytes 1572872 | tf_op jit(solution)/shard_map/ppermute | solution.py:51
  5.2 22.4 %collective-permute-start = (bf16[256,1024]{1,0:T(8,128)(2,1)S(1)}, bf16[256,1024]{1,0:T(8,128)(2,1)}, u32[]{:S(2)}, u32[]{:S(2)}) collective-permute-start(bf16[256,1024]{1,0:T(8,128)(2,1)S(1)} %bitcast.180), channel_id=1, source_target_pairs={{0,1},{1,2},{2,3},{3,0},{4,5},{5,6},{6,7},{7,4},{8,9},{9,10},{10,1... | collective-permute-start | bytes 1572872 | tf_op jit(solution)/shard_map/ppermute | solution.py:51
  5.2 25.6 %collective-permute-start.2 = (bf16[256,1024]{1,0:T(8,128)(2,1)S(1)}, bf16[256,1024]{1,0:T(8,128)(2,1)}, u32[]{:S(2)}, u32[]{:S(2)}) collective-permute-start(bf16[256,1024]{1,0:T(8,128)(2,1)S(1)} %bitcast.181), channel_id=1, source_target_pairs={{0,3},{1,0},{2,1},{3,2},{4,7},{5,4},{6,5},{7,6},{8,11},{9,8},{10,9... | collective-permute-start | bytes 1572872 | tf_op jit(solution)/shard_map/ppermute | solution.py:51
  33.5 18.9 %copy-start.7 = (s32[8]{0:T(128)S(1)}, s32[8]{0:T(128)}, u32[]{:S(2)}) copy-start(s32[8]{0:T(128)} %constant.229.clone) | copy-start | bytes 100
  33.5 41.2 %copy-start.8 = (s32[16,8]{0,1:T(8,128)S(1)}, s32[16,8]{0,1:T(8,128)}, u32[]{:S(2)}) copy-start(s32[16,8]{0,1:T(8,128)} %param.16) | copy-start | bytes 1540
  33.5 41.3 %copy-start.9 = (s32[16]{0:T(128)S(1)}, s32[16]{0:T(128)}, u32[]{:S(2)}) copy-start(s32[16]{0:T(128)} %param.17) | copy-start | bytes 196
  33.5 61.0 %all-to-all-start = ((bf16[8,256,512]{1,2,0:T(8,128)(2,1)}), bf16[8,256,512]{1,2,0:T(8,128)(2,1)S(1)}, u32[]{:S(2)}, u32[]{:S(2)}) async-start(bf16[8,256,512]{1,2,0:T(8,128)(2,1)} %bitcast.173), calls=%async_computation | async-start | bytes 4194304 | tf_op jit(solution)/shard_map/all_to_all | solution.py:67
  39.4 48.1 %collective-permute-start.17 = (bf16[512,1024]{1,0:T(8,128)(2,1)S(1)}, bf16[512,1024]{1,0:T(8,128)(2,1)}, u32[]{:S(2)}, u32[]{:S(2)}) collective-permute-start(bf16[512,1024]{1,0:T(8,128)(2,1)S(1)} %copy-done.5), channel_id=1, source_target_pairs={{0,1},{1,2},{2,3},{3,0},{4,5},{5,6},{6,7},{7,4},{8,9},{9,10},{10,1... | collective-permute-start | bytes 3145736 | tf_op jit(solution)/shard_map/ppermute | solution.py:51
  39.5 50.3 %collective-permute-start.18 = (bf16[512,1024]{1,0:T(8,128)(2,1)S(1)}, bf16[512,1024]{1,0:T(8,128)(2,1)}, u32[]{:S(2)}, u32[]{:S(2)}) collective-permute-start(bf16[512,1024]{1,0:T(8,128)(2,1)S(1)} %copy-done.5), channel_id=1, source_target_pairs={{0,2},{1,3},{2,0},{3,1},{4,6},{5,7},{6,4},{7,5},{8,10},{9,11},{10,... | collective-permute-start | bytes 3145736 | tf_op jit(solution)/shard_map/ppermute | solution.py:51
  41.0 51.2 %collective-permute-start.19 = (bf16[512,1024]{1,0:T(8,128)(2,1)S(1)}, bf16[512,1024]{1,0:T(8,128)(2,1)}, u32[]{:S(2)}, u32[]{:S(2)}) collective-permute-start(bf16[512,1024]{1,0:T(8,128)(2,1)S(1)} %copy-done.5), channel_id=1, source_target_pairs={{0,3},{1,0},{2,1},{3,2},{4,7},{5,4},{6,5},{7,6},{8,11},{9,8},{10,9... | collective-permute-start | bytes 3145736 | tf_op jit(solution)/shard_map/ppermute | solution.py:51
  98.8 50.9 %collective-permute-start.21 = (bf16[512,1024]{1,0:T(8,128)(2,1)S(1)}, bf16[512,1024]{1,0:T(8,128)(2,1)S(1)}, u32[]{:S(2)}, u32[]{:S(2)}) collective-permute-start(bf16[512,1024]{1,0:T(8,128)(2,1)S(1)} %copy-done.6), channel_id=1, source_target_pairs={{0,4},{8,0},{16,8},{24,16},{28,24},{20,28},{12,20},{4,12},{1,5},{9... | collective-permute-start | bytes 3145736 | tf_op jit(solution)/shard_map/ppermute | solution.py:81
  100.9 50.5 %collective-permute-start.20 = (bf16[512,1024]{1,0:T(8,128)(2,1)S(1)}, bf16[512,1024]{1,0:T(8,128)(2,1)S(1)}, u32[]{:S(2)}, u32[]{:S(2)}) collective-permute-start(bf16[512,1024]{1,0:T(8,128)(2,1)S(1)} %copy-done.6), channel_id=1, source_target_pairs={{0,8},{8,16},{16,24},{24,28},{28,20},{20,12},{12,4},{4,0},{1,9},{9... | collective-permute-start | bytes 3145736 | tf_op jit(solution)/shard_map/ppermute | solution.py:80
  102.7 31.8 %collective-permute-start.3 = (bf16[256,1024]{1,0:T(8,128)(2,1)S(1)}, bf16[256,1024]{1,0:T(8,128)(2,1)S(1)}, u32[]{:S(2)}, u32[]{:S(2)}) collective-permute-start(bf16[256,1024]{1,0:T(8,128)(2,1)S(1)} %convolution_convert_fusion.1), channel_id=1, source_target_pairs={{0,4},{8,0},{16,8},{24,16},{28,24},{20,28},{12,20},{4,12},{1,5},{9... | collective-permute-start | bytes 1572872 | tf_op jit(solution)/shard_map/ppermute | solution.py:98
  104.7 32.0 %collective-permute-start.10 = (bf16[256,1024]{1,0:T(8,128)(2,1)S(1)}, bf16[256,1024]{1,0:T(8,128)(2,1)S(1)}, u32[]{:S(2)}, u32[]{:S(2)}) collective-permute-start(bf16[256,1024]{1,0:T(8,128)(2,1)S(1)} %convolution_convert_fusion), channel_id=1, source_target_pairs={{0,8},{8,16},{16,24},{24,28},{28,20},{20,12},{12,4},{4,0},{1,9},{9... | collective-permute-start | bytes 1572872 | tf_op jit(solution)/shard_map/ppermute | solution.py:98
  135.0 12.3 %collective-permute-start.4 = (bf16[256,1024]{1,0:T(8,128)(2,1)S(1)}, bf16[256,1024]{1,0:T(8,128)(2,1)S(1)}, u32[]{:S(2)}, u32[]{:S(2)}) collective-permute-start(bf16[256,1024]{1,0:T(8,128)(2,1)S(1)} %add_convert_fusion.14), channel_id=1, source_target_pairs={{0,4},{8,0},{16,8},{24,16},{28,24},{20,28},{12,20},{4,12},{1,5},{9... | collective-permute-start | bytes 1572872 | tf_op jit(solution)/shard_map/ppermute | solution.py:98
  137.2 11.9 %collective-permute-start.11 = (bf16[256,1024]{1,0:T(8,128)(2,1)S(1)}, bf16[256,1024]{1,0:T(8,128)(2,1)S(1)}, u32[]{:S(2)}, u32[]{:S(2)}) collective-permute-start(bf16[256,1024]{1,0:T(8,128)(2,1)S(1)} %add_convert_fusion.7), channel_id=1, source_target_pairs={{0,8},{8,16},{16,24},{24,28},{28,20},{20,12},{12,4},{4,0},{1,9},{9... | collective-permute-start | bytes 1572872 | tf_op jit(solution)/shard_map/ppermute | solution.py:98
  147.5 14.9 %collective-permute-start.5 = (bf16[256,1024]{1,0:T(8,128)(2,1)S(1)}, bf16[256,1024]{1,0:T(8,128)(2,1)S(1)}, u32[]{:S(2)}, u32[]{:S(2)}) collective-permute-start(bf16[256,1024]{1,0:T(8,128)(2,1)S(1)} %add_convert_fusion.13), channel_id=1, source_target_pairs={{0,4},{8,0},{16,8},{24,16},{28,24},{20,28},{12,20},{4,12},{1,5},{9... | collective-permute-start | bytes 1572872 | tf_op jit(solution)/shard_map/ppermute | solution.py:98
  149.3 14.9 %collective-permute-start.12 = (bf16[256,1024]{1,0:T(8,128)(2,1)S(1)}, bf16[256,1024]{1,0:T(8,128)(2,1)S(1)}, u32[]{:S(2)}, u32[]{:S(2)}) collective-permute-start(bf16[256,1024]{1,0:T(8,128)(2,1)S(1)} %add_convert_fusion.6), channel_id=1, source_target_pairs={{0,8},{8,16},{16,24},{24,28},{28,20},{20,12},{12,4},{4,0},{1,9},{9... | collective-permute-start | bytes 1572872 | tf_op jit(solution)/shard_map/ppermute | solution.py:98
  149.8 45.8 %collective-permute-start.23 = (bf16[512,1024]{1,0:T(8,128)(2,1)S(1)}, bf16[512,1024]{1,0:T(8,128)(2,1)S(1)}, u32[]{:S(2)}, u32[]{:S(2)}) collective-permute-start(bf16[512,1024]{1,0:T(8,128)(2,1)S(1)} %collective-permute-done.21), channel_id=1, source_target_pairs={{0,4},{8,0},{16,8},{24,16},{28,24},{20,28},{12,20},{4,12},{1,5},{9... | collective-permute-start | bytes 3145736 | tf_op jit(solution)/shard_map/ppermute | solution.py:81
  151.4 45.8 %collective-permute-start.22 = (bf16[512,1024]{1,0:T(8,128)(2,1)S(1)}, bf16[512,1024]{1,0:T(8,128)(2,1)S(1)}, u32[]{:S(2)}, u32[]{:S(2)}) collective-permute-start(bf16[512,1024]{1,0:T(8,128)(2,1)S(1)} %collective-permute-done.20), channel_id=1, source_target_pairs={{0,8},{8,16},{16,24},{24,28},{28,20},{20,12},{12,4},{4,0},{1,9},{9... | collective-permute-start | bytes 3145736 | tf_op jit(solution)/shard_map/ppermute | solution.py:80
  162.5 30.6 %collective-permute-start.6 = (bf16[256,1024]{1,0:T(8,128)(2,1)S(1)}, bf16[256,1024]{1,0:T(8,128)(2,1)S(1)}, u32[]{:S(2)}, u32[]{:S(2)}) collective-permute-start(bf16[256,1024]{1,0:T(8,128)(2,1)S(1)} %add_convert_fusion.12), channel_id=1, source_target_pairs={{0,4},{8,0},{16,8},{24,16},{28,24},{20,28},{12,20},{4,12},{1,5},{9... | collective-permute-start | bytes 1572872 | tf_op jit(solution)/shard_map/ppermute | solution.py:98
  164.4 30.5 %collective-permute-start.13 = (bf16[256,1024]{1,0:T(8,128)(2,1)S(1)}, bf16[256,1024]{1,0:T(8,128)(2,1)S(1)}, u32[]{:S(2)}, u32[]{:S(2)}) collective-permute-start(bf16[256,1024]{1,0:T(8,128)(2,1)S(1)} %add_convert_fusion.5), channel_id=1, source_target_pairs={{0,8},{8,16},{16,24},{24,28},{28,20},{20,12},{12,4},{4,0},{1,9},{9... | collective-permute-start | bytes 1572872 | tf_op jit(solution)/shard_map/ppermute | solution.py:98
  193.2 14.9 %collective-permute-start.7 = (bf16[256,1024]{1,0:T(8,128)(2,1)S(1)}, bf16[256,1024]{1,0:T(8,128)(2,1)S(1)}, u32[]{:S(2)}, u32[]{:S(2)}) collective-permute-start(bf16[256,1024]{1,0:T(8,128)(2,1)S(1)} %add_convert_fusion.11), channel_id=1, source_target_pairs={{0,4},{8,0},{16,8},{24,16},{28,24},{20,28},{12,20},{4,12},{1,5},{9... | collective-permute-start | bytes 1572872 | tf_op jit(solution)/shard_map/ppermute | solution.py:98
  195.1 14.9 %collective-permute-start.14 = (bf16[256,1024]{1,0:T(8,128)(2,1)S(1)}, bf16[256,1024]{1,0:T(8,128)(2,1)S(1)}, u32[]{:S(2)}, u32[]{:S(2)}) collective-permute-start(bf16[256,1024]{1,0:T(8,128)(2,1)S(1)} %add_convert_fusion.4), channel_id=1, source_target_pairs={{0,8},{8,16},{16,24},{24,28},{28,20},{20,12},{12,4},{4,0},{1,9},{9... | collective-permute-start | bytes 1572872 | tf_op jit(solution)/shard_map/ppermute | solution.py:98
  195.5 45.8 %collective-permute-start.25 = (bf16[512,1024]{1,0:T(8,128)(2,1)S(1)}, bf16[512,1024]{1,0:T(8,128)(2,1)S(1)}, u32[]{:S(2)}, u32[]{:S(2)}) collective-permute-start(bf16[512,1024]{1,0:T(8,128)(2,1)S(1)} %collective-permute-done.23), channel_id=1, source_target_pairs={{0,4},{8,0},{16,8},{24,16},{28,24},{20,28},{12,20},{4,12},{1,5},{9... | collective-permute-start | bytes 3145736 | tf_op jit(solution)/shard_map/ppermute | solution.py:81
  197.2 45.9 %collective-permute-start.24 = (bf16[512,1024]{1,0:T(8,128)(2,1)S(1)}, bf16[512,1024]{1,0:T(8,128)(2,1)S(1)}, u32[]{:S(2)}, u32[]{:S(2)}) collective-permute-start(bf16[512,1024]{1,0:T(8,128)(2,1)S(1)} %collective-permute-done.22), channel_id=1, source_target_pairs={{0,8},{8,16},{16,24},{24,28},{28,20},{20,12},{12,4},{4,0},{1,9},{9... | collective-permute-start | bytes 3145736 | tf_op jit(solution)/shard_map/ppermute | solution.py:80
  208.3 30.6 %collective-permute-start.8 = (bf16[256,1024]{1,0:T(8,128)(2,1)S(1)}, bf16[256,1024]{1,0:T(8,128)(2,1)S(1)}, u32[]{:S(2)}, u32[]{:S(2)}) collective-permute-start(bf16[256,1024]{1,0:T(8,128)(2,1)S(1)} %add_convert_fusion.10), channel_id=1, source_target_pairs={{0,4},{8,0},{16,8},{24,16},{28,24},{20,28},{12,20},{4,12},{1,5},{9... | collective-permute-start | bytes 1572872 | tf_op jit(solution)/shard_map/ppermute | solution.py:98
  210.2 30.6 %collective-permute-start.15 = (bf16[256,1024]{1,0:T(8,128)(2,1)S(1)}, bf16[256,1024]{1,0:T(8,128)(2,1)S(1)}, u32[]{:S(2)}, u32[]{:S(2)}) collective-permute-start(bf16[256,1024]{1,0:T(8,128)(2,1)S(1)} %add_convert_fusion.3), channel_id=1, source_target_pairs={{0,8},{8,16},{16,24},{24,28},{28,20},{20,12},{12,4},{4,0},{1,9},{9... | collective-permute-start | bytes 1572872 | tf_op jit(solution)/shard_map/ppermute | solution.py:98
  239.0 14.9 %collective-permute-start.9 = (bf16[256,1024]{1,0:T(8,128)(2,1)S(1)}, bf16[256,1024]{1,0:T(8,128)(2,1)S(1)}, u32[]{:S(2)}, u32[]{:S(2)}) collective-permute-start(bf16[256,1024]{1,0:T(8,128)(2,1)S(1)} %add_convert_fusion.9), channel_id=1, source_target_pairs={{0,4},{8,0},{16,8},{24,16},{28,24},{20,28},{12,20},{4,12},{1,5},{9... | collective-permute-start | bytes 1572872 | tf_op jit(solution)/shard_map/ppermute | solution.py:98
  240.9 24.6 %collective-permute-start.16 = (bf16[256,1024]{1,0:T(8,128)(2,1)S(1)}, bf16[256,1024]{1,0:T(8,128)(2,1)S(1)}, u32[]{:S(2)}, u32[]{:S(2)}) collective-permute-start(bf16[256,1024]{1,0:T(8,128)(2,1)S(1)} %add_convert_fusion.2), channel_id=1, source_target_pairs={{0,8},{8,16},{16,24},{24,28},{28,20},{20,12},{12,4},{4,0},{1,9},{9... | collective-permute-start | bytes 1572872 | tf_op jit(solution)/shard_map/ppermute | solution.py:98
  241.4 18.6 %collective-permute-start.27 = (bf16[256,1024]{1,0:T(8,128)(2,1)S(1)}, bf16[256,1024]{1,0:T(8,128)(2,1)S(1)}, u32[]{:S(2)}, u32[]{:S(2)}) collective-permute-start(bf16[256,1024]{1,0:T(8,128)(2,1)S(1)} %slice.11), channel_id=1, source_target_pairs={{0,4},{8,0},{16,8},{24,16},{28,24},{20,28},{12,20},{4,12},{1,5},{9... | collective-permute-start | bytes 1572872 | tf_op jit(solution)/shard_map/ppermute | solution.py:87
  243.1 18.3 %collective-permute-start.26 = (bf16[256,1024]{1,0:T(8,128)(2,1)S(1)}, bf16[256,1024]{1,0:T(8,128)(2,1)S(1)}, u32[]{:S(2)}, u32[]{:S(2)}) collective-permute-start(bf16[256,1024]{1,0:T(8,128)(2,1)S(1)} %slice.10), channel_id=1, source_target_pairs={{0,8},{8,16},{16,24},{24,28},{28,20},{20,12},{12,4},{4,0},{1,9},{9... | collective-permute-start | bytes 1572872 | tf_op jit(solution)/shard_map/ppermute | solution.py:86
  (8 other events, 29.7 us)

commit v12 on v9

--- a/solution.py
+++ b/solution.py
@@ -67,6 +67,7 @@
         got = [(piece, me, 0, wrows)]
         fwd = piece
         bwd = piece
+        half = lambda x, sl: jax.tree.map(lambda a: a[sl], x)
         for k in range(1, steps_bwd + 1):
             fwd = lax.ppermute(fwd, "crop", fwd_perm)
             bwd = lax.ppermute(bwd, "crop", bwd_perm)
@@ -74,24 +75,29 @@
             got.append((bwd, ring_arr[(pos + k) % ncrop], 0, wrows))
         if steps_fwd > steps_bwd:
             src = ring_arr[(pos - steps_fwd) % ncrop]
-            got.append((lax.ppermute(fwd[:split], "crop", fwd_perm), src, 0, split))
-            got.append((lax.ppermute(bwd[split:], "crop", bwd_perm), src, split, wrows - split))
+            top = lax.ppermute(half(fwd, slice(None, split)), "crop", fwd_perm)
+            bottom = lax.ppermute(half(bwd, slice(split, None)), "crop", bwd_perm)
+            got.append((top, src, 0, split))
+            got.append((bottom, src, split, wrows - split))
         return got
 
-    kv_got = ring_pieces(jnp.concatenate([key_weight, value_weight], axis=1))
+    kv_got = ring_pieces((key_weight, value_weight))
     q_piece, last_a, last_b = lax.optimization_barrier(
         (query_weight, kv_got[-1][0], kv_got[-2][0])
     )
     kv_got[-1] = (last_a,) + kv_got[-1][1:]
     kv_got[-2] = (last_b,) + kv_got[-2][1:]
     tokens_in = head_gather(delivered)
-    kv_weight = jnp.concatenate([p for p, _, _, _ in kv_got], axis=0)
+    k_weight = jnp.concatenate([p[0] for p, _, _, _ in kv_got], axis=0)
+    v_weight = jnp.concatenate([p[1] for p, _, _, _ in kv_got], axis=0)
     tokens_perm = jnp.concatenate(
         [lax.dynamic_slice_in_dim(tokens_in, src * wrows + lo, n, 1) for _, src, lo, n in kv_got],
         axis=1,
     )
-    kv = jnp.dot(tokens_perm, kv_weight, preferred_element_type=jnp.float32).astype(jnp.bfloat16)
-    incoming = kv.reshape(ncrop, CAP, CT, 2 * width)
+    keys_all = jnp.dot(tokens_perm, k_weight, preferred_element_type=jnp.float32)
+    vals_all = jnp.dot(tokens_perm, v_weight, preferred_element_type=jnp.float32)
+    keys_all = keys_all.astype(jnp.bfloat16)
+    vals_all = vals_all.astype(jnp.bfloat16)
 
     def q_part(acc, piece, src, lo, n):
         cols = lax.dynamic_slice_in_dim(queries_in, src * wrows + lo, n, 1)
@@ -111,8 +117,8 @@
         acc = q_part(acc, lax.ppermute(bwd[split:], "crop", bwd_perm), src, split, wrows - split)
     query = acc.astype(jnp.bfloat16)
     nslots = ncrop * CAP
-    keys_all = incoming[..., :width].reshape(nslots * CT, heads_here, HD)
-    vals_all = incoming[..., width:].reshape(nslots * CT, heads_here, HD)
+    keys_all = keys_all.reshape(nslots * CT, heads_here, HD)
+    vals_all = vals_all.reshape(nslots * CT, heads_here, HD)
     query_row = query.reshape(rows_here, GR, heads_here, HD)
     in_use = (jnp.arange(NB, dtype=jnp.int32)[None, :] < region_len[:, None])[:, :, None]
     hits = region_slots[:, :, None] == jnp.arange(nslots, dtype=jnp.int32)[None, None, :]

time: 277 us -> 289 us (1.043)
  waiting for transfers between devices: 162 us -> 192 us
  local copies, waits for them, and re-layouts: 43 us -> 22.9 us
  matrix products: 25.6 us -> 13 us
  starting transfers between devices: 32.4 us -> 43.3 us
    ppermute x3 -> x6, waiting for transfers between devices: 0.01 us -> 107 us  [ring_pieces(): bwd = lax.ppermute(bwd, 'crop', bwd_perm)]
    ppermute x3 -> x6, waiting for transfers between devices: 83.9 us -> 0.44 us  [ring_pieces(): fwd = lax.ppermute(fwd, 'crop', fwd_perm)]
    ppermute x3, waiting for transfers between devices: 41.4 us -> 53.4 us  [body(): fwd = lax.ppermute(fwd, 'crop', fwd_perm)]
    ppermute x3 -> x6, starting transfers between devices: 0.23 us -> 11.9 us  [ring_pieces(): bwd = lax.ppermute(bwd, 'crop', bwd_perm)]
    unnamed x40 -> x42, local copies, waits for them, and re-layouts: 24.3 us -> 13.3 us
    ppermute x6, waiting for transfers between devices: 14.1 us -> 3.5 us  [head_gather(): part = lax.ppermute(x, 'head', [(j, (j + k) % nhead) for j in range(nhead)])]
    ppermute x2 -> x4, waiting for transfers between devices: 10.8 us -> 20.5 us  [the longest x2 16.3 us: ring_pieces(): bottom = lax.ppermute(half(bwd, slice(split, None)), 'crop', bwd_perm)]
    dot_general x9, matrix products: 15.6 us -> 6.54 us  [q_part(): return acc + jnp.dot(cols, piece, preferred_element_type=jnp.float32)]
  transfers between devices with their start and end apart: 23 -> 31, of which waited for: 14 -> 18; matrix products, arithmetic and copies ran while one was open for 21% -> 10% of each run, Pallas kernels for 0% -> 0%
where the time goes in v12:
time: 289 us; the launch traced here: 286 us
  waiting for transfers between devices  192 us (66%)
  starting transfers between devices  43.3 us (15%)
  local copies, waits for them, and re-layouts  22.9 us (8%)
  matrix products  13 us (4%)
  between operations  9.54 us (3%)
  other arithmetic  5 us (2%)
    ppermute x6, waiting for transfers between devices, ring_pieces(): bwd = lax.ppermute(bwd, 'crop', bwd_perm)  107 us
    ppermute x3, waiting for transfers between devices, body(): fwd = lax.ppermute(fwd, 'crop', fwd_perm)  53.4 us
    ppermute x2, waiting for transfers between devices, ring_pieces(): bottom = lax.ppermute(half(bwd, slice(split, None)), 'crop', bwd_perm)  16.3 us
    unnamed x42, local copies, waits for them, and re-layouts  13.3 us
    ppermute x6, starting transfers between devices, ring_pieces(): bwd = lax.ppermute(bwd, 'crop', bwd_perm)  11.9 us
    ppermute x3, starting transfers between devices, body(): bwd = lax.ppermute(bwd, 'crop', bwd_perm)  7.58 us
    ppermute x6, starting transfers between devices, ring_pieces(): fwd = lax.ppermute(fwd, 'crop', fwd_perm)  6.71 us
    dot_general x9, matrix products, q_part(): return acc + jnp.dot(cols, piece, preferred_element_type=jnp.float32)  6.54 us
  transfers between devices with their start and end apart: 31, of which 18 were waited for; matrix products, arithmetic and copies ran while one was open for 10% of the time, Pallas kernels for 0%

profile of v12, /device:TPU:0, one launch (start us, length us, event | category | flops | bytes accessed | tf_op | source)
XLA Modules:
  0.0 285.9 jit_solution(15082927449348280908)
XLA Ops:
  0.0 3.0 %collective-permute-start.9 = (bf16[512,1024]{1,0:T(8,128)(2,1)}, bf16[512,1024]{1,0:T(8,128)(2,1)}, u32[]{:S(2)}, u32[]{:S(2)}) collective-permute-start(bf16[512,1024]{1,0:T(8,128)(2,1)} %param.13), channel_id=1, source_target_pairs={{0,4},{8,0},{16,8},{24,16},{28,24},{20,28},{12,20},{4,12},{1,5},{9... | collective-permute-start | bytes 3145736 | tf_op jit(solution)/shard_map/ppermute | solution.py:73
  7.2 4.9 %all-to-all-start = ((bf16[8,2,16,1024]{3,2,1,0:T(8,128)(2,1)}), bf16[8,2,16,1024]{3,2,1,0:T(8,128)(2,1)S(1)}, u32[]{:S(2)}, u32[]{:S(2)}) async-start(bf16[8,2,16,1024]{3,2,1,0:T(8,128)(2,1)} %bitcast.2), calls=%async_computation | async-start | bytes 1048576 | tf_op jit(solution)/shard_map/all_to_all | solution.py:59
  12.1 2.0 collective-permute-start.14
  14.1 13.2 %collective-permute-done.9 = bf16[512,1024]{1,0:T(8,128)(2,1)} collective-permute-done((bf16[512,1024]{1,0:T(8,128)(2,1)}, bf16[512,1024]{1,0:T(8,128)(2,1)}, u32[]{:S(2)}, u32[]{:S(2)}) %collective-permute-start.9) | collective-permute-done | bytes 1048608 | tf_op jit(solution)/shard_map/ppermute | solution.py:73
  27.3 2.0 collective-permute-start.20
  29.3 20.9 %collective-permute-done.4 = bf16[512,1024]{1,0:T(8,128)(2,1)S(1)} collective-permute-done((bf16[512,1024]{1,0:T(8,128)(2,1)}, bf16[512,1024]{1,0:T(8,128)(2,1)S(1)}, u32[]{:S(2)}, u32[]{:S(2)}) %collective-permute-start.4) | collective-permute-done | bytes 1048608 | tf_op jit(solution)/shard_map/ppermute | solution.py:73
  64.0 2.4 constant_dynamic-update-slice_fusion.8
  69.1 2.4 copy-done.6
  76.5 3.6 %collective-permute-start.6 = (bf16[512,1024]{1,0:T(8,128)(2,1)S(1)}, bf16[512,1024]{1,0:T(8,128)(2,1)S(1)}, u32[]{:S(2)}, u32[]{:S(2)}) collective-permute-start(bf16[512,1024]{1,0:T(8,128)(2,1)S(1)} %copy-done.4), channel_id=1, source_target_pairs={{0,4},{8,0},{16,8},{24,16},{28,24},{20,28},{12,20},{4,12},{1,5},{9... | collective-permute-start | bytes 3145736 | tf_op jit(solution)/shard_map/ppermute | solution.py:73
  84.1 3.5 %collective-permute-done.1 = bf16[256,1024]{1,0:T(8,128)(2,1)S(1)} collective-permute-done((bf16[256,1024]{1,0:T(8,128)(2,1)S(1)}, bf16[256,1024]{1,0:T(8,128)(2,1)S(1)}, u32[]{:S(2)}, u32[]{:S(2)}) %collective-permute-start.1) | collective-permute-done | bytes 524320 | tf_op jit(solution)/shard_map/ppermute | solution.py:51
  89.1 13.1 %collective-permute-done.10 = bf16[512,1024]{1,0:T(8,128)(2,1)S(1)} collective-permute-done((bf16[512,1024]{1,0:T(8,128)(2,1)}, bf16[512,1024]{1,0:T(8,128)(2,1)S(1)}, u32[]{:S(2)}, u32[]{:S(2)}) %collective-permute-start.10) | collective-permute-done | bytes 1048608 | tf_op jit(solution)/shard_map/ppermute | solution.py:73
  102.3 1.7 collective-permute-start.11
  104.0 20.8 %collective-permute-done.6 = bf16[512,1024]{1,0:T(8,128)(2,1)S(1)} collective-permute-done((bf16[512,1024]{1,0:T(8,128)(2,1)S(1)}, bf16[512,1024]{1,0:T(8,128)(2,1)S(1)}, u32[]{:S(2)}, u32[]{:S(2)}) %collective-permute-start.6) | collective-permute-done | bytes 1048608 | tf_op jit(solution)/shard_map/ppermute | solution.py:73
  126.8 2.2 collective-permute-start.7
  129.3 17.9 %collective-permute-done.11 = bf16[512,1024]{1,0:T(8,128)(2,1)S(1)} collective-permute-done((bf16[512,1024]{1,0:T(8,128)(2,1)S(1)}, bf16[512,1024]{1,0:T(8,128)(2,1)S(1)}, u32[]{:S(2)}, u32[]{:S(2)}) %collective-permute-start.11) | collective-permute-done | bytes 1048608 | tf_op jit(solution)/shard_map/ppermute | solution.py:73
  148.9 20.8 %collective-permute-done.8 = bf16[512,1024]{1,0:T(8,128)(2,1)S(1)} collective-permute-done((bf16[512,1024]{1,0:T(8,128)(2,1)S(1)}, bf16[512,1024]{1,0:T(8,128)(2,1)S(1)}, u32[]{:S(2)}, u32[]{:S(2)}) %collective-permute-start.8) | collective-permute-done | bytes 1048608 | tf_op jit(solution)/shard_map/ppermute | solution.py:73
  169.7 1.6 collective-permute-start.13
  172.4 1.9 collective-permute-start.18
  174.5 6.4 %collective-permute-done.12 = bf16[256,1024]{1,0:T(8,128)(2,1)S(1)} collective-permute-done((bf16[256,1024]{1,0:T(8,128)(2,1)S(1)}, bf16[256,1024]{1,0:T(8,128)(2,1)S(1)}, u32[]{:S(2)}, u32[]{:S(2)}) %collective-permute-start.12) | collective-permute-done | bytes 524320 | tf_op jit(solution)/shard_map/ppermute | solution.py:79
  180.9 9.8 %collective-permute-done.13 = bf16[256,1024]{1,0:T(8,128)(2,1)S(1)} collective-permute-done((bf16[256,1024]{1,0:T(8,128)(2,1)S(1)}, bf16[256,1024]{1,0:T(8,128)(2,1)S(1)}, u32[]{:S(2)}, u32[]{:S(2)}) %collective-permute-start.13) | collective-permute-done | bytes 524320 | tf_op jit(solution)/shard_map/ppermute | solution.py:79
  190.8 4.2 %collective-permute-done.18 = bf16[256,1024]{1,0:T(8,128)(2,1)S(1)} collective-permute-done((bf16[256,1024]{1,0:T(8,128)(2,1)S(1)}, bf16[256,1024]{1,0:T(8,128)(2,1)S(1)}, u32[]{:S(2)}, u32[]{:S(2)}) %collective-permute-start.18) | collective-permute-done | bytes 524320 | tf_op jit(solution)/shard_map/ppermute | solution.py:78
  195.4 2.9 %collective-permute-start.23 = (bf16[512,1024]{1,0:T(8,128)(2,1)S(1)}, bf16[512,1024]{1,0:T(8,128)(2,1)S(1)}, u32[]{:S(2)}, u32[]{:S(2)}) collective-permute-start(bf16[512,1024]{1,0:T(8,128)(2,1)S(1)} %copy-done.5), channel_id=1, source_target_pairs={{0,4},{8,0},{16,8},{24,16},{28,24},{20,28},{12,20},{4,12},{1,5},{9... | collective-permute-start | bytes 3145736 | tf_op jit(solution)/shard_map/ppermute | solution.py:111
  198.4 20.2 %collective-permute-done.22 = bf16[512,1024]{1,0:T(8,128)(2,1)S(1)} collective-permute-done((bf16[512,1024]{1,0:T(8,128)(2,1)S(1)}, bf16[512,1024]{1,0:T(8,128)(2,1)S(1)}, u32[]{:S(2)}, u32[]{:S(2)}) %collective-permute-start.22) | collective-permute-done | bytes 1048608 | tf_op jit(solution)/shard_map/ppermute | solution.py:110
  218.6 2.4 fusion.8
  221.0 2.6 collective-permute-start.25
  223.6 2.4 fusion.9
  225.9 16.0 %collective-permute-done.24 = bf16[512,1024]{1,0:T(8,128)(2,1)S(1)} collective-permute-done((bf16[512,1024]{1,0:T(8,128)(2,1)S(1)}, bf16[512,1024]{1,0:T(8,128)(2,1)S(1)}, u32[]{:S(2)}, u32[]{:S(2)}) %collective-permute-start.24) | collective-permute-done | bytes 1048608 | tf_op jit(solution)/shard_map/ppermute | solution.py:110
  243.6 2.1 collective-permute-start.27
  247.9 17.2 %collective-permute-done.26 = bf16[512,1024]{1,0:T(8,128)(2,1)S(1)} collective-permute-done((bf16[512,1024]{1,0:T(8,128)(2,1)S(1)}, bf16[512,1024]{1,0:T(8,128)(2,1)S(1)}, u32[]{:S(2)}, u32[]{:S(2)}) %collective-permute-start.26) | collective-permute-done | bytes 1048608 | tf_op jit(solution)/shard_map/ppermute | solution.py:110
  266.5 2.5 collective-permute-start.29
  269.8 5.2 %collective-permute-done.28 = bf16[256,1024]{1,0:T(8,128)(2,1)S(1)} collective-permute-done((bf16[256,1024]{1,0:T(8,128)(2,1)S(1)}, bf16[256,1024]{1,0:T(8,128)(2,1)S(1)}, u32[]{:S(2)}, u32[]{:S(2)}) %collective-permute-start.28) | collective-permute-done | bytes 524320 | tf_op jit(solution)/shard_map/ppermute | solution.py:116
  279.4 3.5 %fusion.49 = (f32[16,8,32]{2,0,1:T(8,128)S(1)}, f32[16,8,32,256]{3,2,0,1:T(8,128)S(1)}) fusion(f32[8,256,16,32]{1,3,2,0:T(8,128)S(1)} %bitcast.72, pred[16,256]{1,0:T(8,128)(4,1)S(1)} %broadcast_in_dim.33), kind=kOutput, calls=%fused_computation.94 | output fusion | flops 6291711 | bytes 8409088 | tf_op jit(solution)/shard_map/sub | solution.py:134
  (117 shorter events, 41.2 us)
Async XLA Ops:
  0.0 27.3 %collective-permute-start.9 = (bf16[512,1024]{1,0:T(8,128)(2,1)}, bf16[512,1024]{1,0:T(8,128)(2,1)}, u32[]{:S(2)}, u32[]{:S(2)}) collective-permute-start(bf16[512,1024]{1,0:T(8,128)(2,1)} %param.13), channel_id=1, source_target_pairs={{0,4},{8,0},{16,8},{24,16},{28,24},{20,28},{12,20},{4,12},{1,5},{9... | collective-permute-start | bytes 3145736 | tf_op jit(solution)/shard_map/ppermute | solution.py:73
  3.0 47.2 %collective-permute-start.4 = (bf16[512,1024]{1,0:T(8,128)(2,1)}, bf16[512,1024]{1,0:T(8,128)(2,1)S(1)}, u32[]{:S(2)}, u32[]{:S(2)}) collective-permute-start(bf16[512,1024]{1,0:T(8,128)(2,1)} %param.14), channel_id=1, source_target_pairs={{0,4},{8,0},{16,8},{24,16},{28,24},{20,28},{12,20},{4,12},{1,5},{9... | collective-permute-start | bytes 3145736 | tf_op jit(solution)/shard_map/ppermute | solution.py:73
  4.5 61.8 %collective-permute-start.3 = (bf16[512,1024]{1,0:T(8,128)(2,1)}, bf16[512,1024]{1,0:T(8,128)(2,1)}, u32[]{:S(2)}, u32[]{:S(2)}) collective-permute-start(bf16[512,1024]{1,0:T(8,128)(2,1)} %param.14), channel_id=1, source_target_pairs={{0,8},{8,16},{16,24},{24,28},{28,20},{20,12},{12,4},{4,0},{1,9},{9... | collective-permute-start | bytes 3145736 | tf_op jit(solution)/shard_map/ppermute | solution.py:72
  7.2 59.2 %all-to-all-start = ((bf16[8,2,16,1024]{3,2,1,0:T(8,128)(2,1)}), bf16[8,2,16,1024]{3,2,1,0:T(8,128)(2,1)S(1)}, u32[]{:S(2)}, u32[]{:S(2)}) async-start(bf16[8,2,16,1024]{3,2,1,0:T(8,128)(2,1)} %bitcast.2), calls=%async_computation | async-start | bytes 1048576 | tf_op jit(solution)/shard_map/all_to_all | solution.py:59
  12.1 60.7 %collective-permute-start.14 = (bf16[512,1024]{1,0:T(8,128)(2,1)}, bf16[512,1024]{1,0:T(8,128)(2,1)}, u32[]{:S(2)}, u32[]{:S(2)}) collective-permute-start(bf16[512,1024]{1,0:T(8,128)(2,1)} %param.13), channel_id=1, source_target_pairs={{0,8},{8,16},{16,24},{24,28},{28,20},{20,12},{12,4},{4,0},{1,9},{9... | collective-permute-start | bytes 3145736 | tf_op jit(solution)/shard_map/ppermute | solution.py:72
  14.1 60.3 %collective-permute-start.19 = (bf16[512,1024]{1,0:T(8,128)(2,1)}, bf16[512,1024]{1,0:T(8,128)(2,1)}, u32[]{:S(2)}, u32[]{:S(2)}) collective-permute-start(bf16[512,1024]{1,0:T(8,128)(2,1)} %param.10), channel_id=1, source_target_pairs={{0,1},{1,2},{2,3},{3,0},{4,5},{5,6},{6,7},{7,4},{8,9},{9,10},{10,1... | collective-permute-start | bytes 3145736 | tf_op jit(solution)/shard_map/ppermute | solution.py:51
  27.3 48.7 %collective-permute-start.20 = (bf16[512,1024]{1,0:T(8,128)(2,1)}, bf16[512,1024]{1,0:T(8,128)(2,1)S(1)}, u32[]{:S(2)}, u32[]{:S(2)}) collective-permute-start(bf16[512,1024]{1,0:T(8,128)(2,1)} %param.10), channel_id=1, source_target_pairs={{0,2},{1,3},{2,0},{3,1},{4,6},{5,7},{6,4},{7,5},{8,10},{9,11},{10,... | collective-permute-start | bytes 3145736 | tf_op jit(solution)/shard_map/ppermute | solution.py:51
  50.2 26.3 %collective-permute-start.21 = (bf16[512,1024]{1,0:T(8,128)(2,1)}, bf16[512,1024]{1,0:T(8,128)(2,1)}, u32[]{:S(2)}, u32[]{:S(2)}) collective-permute-start(bf16[512,1024]{1,0:T(8,128)(2,1)} %param.10), channel_id=1, source_target_pairs={{0,3},{1,0},{2,1},{3,2},{4,7},{5,4},{6,5},{7,6},{8,11},{9,8},{10,9... | collective-permute-start | bytes 3145736 | tf_op jit(solution)/shard_map/ppermute | solution.py:51
  66.4 13.7 %collective-permute-start = (bf16[256,1024]{1,0:T(8,128)(2,1)S(1)}, bf16[256,1024]{1,0:T(8,128)(2,1)S(1)}, u32[]{:S(2)}, u32[]{:S(2)}) collective-permute-start(bf16[256,1024]{1,0:T(8,128)(2,1)S(1)} %bitcast.76), channel_id=1, source_target_pairs={{0,1},{1,2},{2,3},{3,0},{4,5},{5,6},{6,7},{7,4},{8,9},{9,10},{10,1... | collective-permute-start | bytes 1572872 | tf_op jit(solution)/shard_map/ppermute | solution.py:51
  72.9 14.7 %collective-permute-start.1 = (bf16[256,1024]{1,0:T(8,128)(2,1)S(1)}, bf16[256,1024]{1,0:T(8,128)(2,1)S(1)}, u32[]{:S(2)}, u32[]{:S(2)}) collective-permute-start(bf16[256,1024]{1,0:T(8,128)(2,1)S(1)} %bitcast.78), channel_id=1, source_target_pairs={{0,2},{1,3},{2,0},{3,1},{4,6},{5,7},{6,4},{7,5},{8,10},{9,11},{10,... | collective-permute-start | bytes 1572872 | tf_op jit(solution)/shard_map/ppermute | solution.py:51
  74.4 52.4 %collective-permute-start.5 = (bf16[512,1024]{1,0:T(8,128)(2,1)}, bf16[512,1024]{1,0:T(8,128)(2,1)S(1)}, u32[]{:S(2)}, u32[]{:S(2)}) collective-permute-start(bf16[512,1024]{1,0:T(8,128)(2,1)} %collective-permute-done.3), channel_id=1, source_target_pairs={{0,8},{8,16},{16,24},{24,28},{28,20},{20,12},{12,4},{4,0},{1,9},{9... | collective-permute-start | bytes 3145736 | tf_op jit(solution)/shard_map/ppermute | solution.py:72
  76.0 26.3 %collective-permute-start.10 = (bf16[512,1024]{1,0:T(8,128)(2,1)}, bf16[512,1024]{1,0:T(8,128)(2,1)S(1)}, u32[]{:S(2)}, u32[]{:S(2)}) collective-permute-start(bf16[512,1024]{1,0:T(8,128)(2,1)} %collective-permute-done.9), channel_id=1, source_target_pairs={{0,4},{8,0},{16,8},{24,16},{28,24},{20,28},{12,20},{4,12},{1,5},{9... | collective-permute-start | bytes 3145736 | tf_op jit(solution)/shard_map/ppermute | solution.py:73
  76.5 48.2 %collective-permute-start.6 = (bf16[512,1024]{1,0:T(8,128)(2,1)S(1)}, bf16[512,1024]{1,0:T(8,128)(2,1)S(1)}, u32[]{:S(2)}, u32[]{:S(2)}) collective-permute-start(bf16[512,1024]{1,0:T(8,128)(2,1)S(1)} %copy-done.4), channel_id=1, source_target_pairs={{0,4},{8,0},{16,8},{24,16},{28,24},{20,28},{12,20},{4,12},{1,5},{9... | collective-permute-start | bytes 3145736 | tf_op jit(solution)/shard_map/ppermute | solution.py:73
  80.1 46.2 %collective-permute-start.15 = (bf16[512,1024]{1,0:T(8,128)(2,1)}, bf16[512,1024]{1,0:T(8,128)(2,1)S(1)}, u32[]{:S(2)}, u32[]{:S(2)}) collective-permute-start(bf16[512,1024]{1,0:T(8,128)(2,1)} %collective-permute-done.14), channel_id=1, source_target_pairs={{0,8},{8,16},{16,24},{24,28},{28,20},{20,12},{12,4},{4,0},{1,9},{9... | collective-permute-start | bytes 3145736 | tf_op jit(solution)/shard_map/ppermute | solution.py:72
  87.6 41.4 %collective-permute-start.2 = (bf16[256,1024]{1,0:T(8,128)(2,1)S(1)}, bf16[256,1024]{1,0:T(8,128)(2,1)S(1)}, u32[]{:S(2)}, u32[]{:S(2)}) collective-permute-start(bf16[256,1024]{1,0:T(8,128)(2,1)S(1)} %bitcast.79), channel_id=1, source_target_pairs={{0,3},{1,0},{2,1},{3,2},{4,7},{5,4},{6,5},{7,6},{8,11},{9,8},{10,9... | collective-permute-start | bytes 1572872 | tf_op jit(solution)/shard_map/ppermute | solution.py:51
  102.3 44.9 %collective-permute-start.11 = (bf16[512,1024]{1,0:T(8,128)(2,1)S(1)}, bf16[512,1024]{1,0:T(8,128)(2,1)S(1)}, u32[]{:S(2)}, u32[]{:S(2)}) collective-permute-start(bf16[512,1024]{1,0:T(8,128)(2,1)S(1)} %collective-permute-done.10), channel_id=1, source_target_pairs={{0,4},{8,0},{16,8},{24,16},{28,24},{20,28},{12,20},{4,12},{1,5},{9... | collective-permute-start | bytes 3145736 | tf_op jit(solution)/shard_map/ppermute | solution.py:73
  124.7 44.9 %collective-permute-start.8 = (bf16[512,1024]{1,0:T(8,128)(2,1)S(1)}, bf16[512,1024]{1,0:T(8,128)(2,1)S(1)}, u32[]{:S(2)}, u32[]{:S(2)}) collective-permute-start(bf16[512,1024]{1,0:T(8,128)(2,1)S(1)} %collective-permute-done.6), channel_id=1, source_target_pairs={{0,4},{8,0},{16,8},{24,16},{28,24},{20,28},{12,20},{4,12},{1,5},{9... | collective-permute-start | bytes 3145736 | tf_op jit(solution)/shard_map/ppermute | solution.py:73
  126.3 45.0 %collective-permute-start.16 = (bf16[512,1024]{1,0:T(8,128)(2,1)S(1)}, bf16[512,1024]{1,0:T(8,128)(2,1)S(1)}, u32[]{:S(2)}, u32[]{:S(2)}) collective-permute-start(bf16[512,1024]{1,0:T(8,128)(2,1)S(1)} %collective-permute-done.15), channel_id=1, source_target_pairs={{0,8},{8,16},{16,24},{24,28},{28,20},{20,12},{12,4},{4,0},{1,9},{9... | collective-permute-start | bytes 3145736 | tf_op jit(solution)/shard_map/ppermute | solution.py:72
  126.8 45.6 %collective-permute-start.7 = (bf16[512,1024]{1,0:T(8,128)(2,1)S(1)}, bf16[512,1024]{1,0:T(8,128)(2,1)S(1)}, u32[]{:S(2)}, u32[]{:S(2)}) collective-permute-start(bf16[512,1024]{1,0:T(8,128)(2,1)S(1)} %collective-permute-done.5), channel_id=1, source_target_pairs={{0,8},{8,16},{16,24},{24,28},{28,20},{20,12},{12,4},{4,0},{1,9},{9... | collective-permute-start | bytes 3145736 | tf_op jit(solution)/shard_map/ppermute | solution.py:72
  147.3 33.7 %collective-permute-start.12 = (bf16[256,1024]{1,0:T(8,128)(2,1)S(1)}, bf16[256,1024]{1,0:T(8,128)(2,1)S(1)}, u32[]{:S(2)}, u32[]{:S(2)}) collective-permute-start(bf16[256,1024]{1,0:T(8,128)(2,1)S(1)} %slice.26), channel_id=1, source_target_pairs={{0,4},{8,0},{16,8},{24,16},{28,24},{20,28},{12,20},{4,12},{1,5},{9... | collective-permute-start | bytes 1572872 | tf_op jit(solution)/shard_map/ppermute | solution.py:79
  169.7 25.3 %copy-start.5 = (bf16[512,1024]{1,0:T(8,128)(2,1)S(1)}, bf16[512,1024]{1,0:T(8,128)(2,1)}, u32[]{:S(2)}) copy-start(bf16[512,1024]{1,0:T(8,128)(2,1)} %param.12) | copy-start | bytes 3145732
  169.7 21.0 %collective-permute-start.13 = (bf16[256,1024]{1,0:T(8,128)(2,1)S(1)}, bf16[256,1024]{1,0:T(8,128)(2,1)S(1)}, u32[]{:S(2)}, u32[]{:S(2)}) collective-permute-start(bf16[256,1024]{1,0:T(8,128)(2,1)S(1)} %slice.27), channel_id=1, source_target_pairs={{0,4},{8,0},{16,8},{24,16},{28,24},{20,28},{12,20},{4,12},{1,5},{9... | collective-permute-start | bytes 1572872 | tf_op jit(solution)/shard_map/ppermute | solution.py:79
  171.4 19.3 %collective-permute-start.17 = (bf16[256,1024]{1,0:T(8,128)(2,1)S(1)}, bf16[256,1024]{1,0:T(8,128)(2,1)S(1)}, u32[]{:S(2)}, u32[]{:S(2)}) collective-permute-start(bf16[256,1024]{1,0:T(8,128)(2,1)S(1)} %slice.28), channel_id=1, source_target_pairs={{0,8},{8,16},{16,24},{24,28},{28,20},{20,12},{12,4},{4,0},{1,9},{9... | collective-permute-start | bytes 1572872 | tf_op jit(solution)/shard_map/ppermute | solution.py:78
  172.4 22.6 %collective-permute-start.18 = (bf16[256,1024]{1,0:T(8,128)(2,1)S(1)}, bf16[256,1024]{1,0:T(8,128)(2,1)S(1)}, u32[]{:S(2)}, u32[]{:S(2)}) collective-permute-start(bf16[256,1024]{1,0:T(8,128)(2,1)S(1)} %slice.29), channel_id=1, source_target_pairs={{0,8},{8,16},{16,24},{24,28},{28,20},{20,12},{12,4},{4,0},{1,9},{9... | collective-permute-start | bytes 1572872 | tf_op jit(solution)/shard_map/ppermute | solution.py:78
  195.0 23.6 %collective-permute-start.22 = (bf16[512,1024]{1,0:T(8,128)(2,1)S(1)}, bf16[512,1024]{1,0:T(8,128)(2,1)S(1)}, u32[]{:S(2)}, u32[]{:S(2)}) collective-permute-start(bf16[512,1024]{1,0:T(8,128)(2,1)S(1)} %copy-done.5), channel_id=1, source_target_pairs={{0,8},{8,16},{16,24},{24,28},{28,20},{20,12},{12,4},{4,0},{1,9},{9... | collective-permute-start | bytes 3145736 | tf_op jit(solution)/shard_map/ppermute | solution.py:110
  195.4 25.6 %collective-permute-start.23 = (bf16[512,1024]{1,0:T(8,128)(2,1)S(1)}, bf16[512,1024]{1,0:T(8,128)(2,1)S(1)}, u32[]{:S(2)}, u32[]{:S(2)}) collective-permute-start(bf16[512,1024]{1,0:T(8,128)(2,1)S(1)} %copy-done.5), channel_id=1, source_target_pairs={{0,4},{8,0},{16,8},{24,16},{28,24},{20,28},{12,20},{4,12},{1,5},{9... | collective-permute-start | bytes 3145736 | tf_op jit(solution)/shard_map/ppermute | solution.py:111
  218.6 23.3 %collective-permute-start.24 = (bf16[512,1024]{1,0:T(8,128)(2,1)S(1)}, bf16[512,1024]{1,0:T(8,128)(2,1)S(1)}, u32[]{:S(2)}, u32[]{:S(2)}) collective-permute-start(bf16[512,1024]{1,0:T(8,128)(2,1)S(1)} %collective-permute-done.22), channel_id=1, source_target_pairs={{0,8},{8,16},{16,24},{24,28},{28,20},{20,12},{12,4},{4,0},{1,9},{9... | collective-permute-start | bytes 3145736 | tf_op jit(solution)/shard_map/ppermute | solution.py:110
  221.0 22.6 %collective-permute-start.25 = (bf16[512,1024]{1,0:T(8,128)(2,1)S(1)}, bf16[512,1024]{1,0:T(8,128)(2,1)S(1)}, u32[]{:S(2)}, u32[]{:S(2)}) collective-permute-start(bf16[512,1024]{1,0:T(8,128)(2,1)S(1)} %collective-permute-done.23), channel_id=1, source_target_pairs={{0,4},{8,0},{16,8},{24,16},{28,24},{20,28},{12,20},{4,12},{1,5},{9... | collective-permute-start | bytes 3145736 | tf_op jit(solution)/shard_map/ppermute | solution.py:111
  241.9 23.2 %collective-permute-start.26 = (bf16[512,1024]{1,0:T(8,128)(2,1)S(1)}, bf16[512,1024]{1,0:T(8,128)(2,1)S(1)}, u32[]{:S(2)}, u32[]{:S(2)}) collective-permute-start(bf16[512,1024]{1,0:T(8,128)(2,1)S(1)} %collective-permute-done.24), channel_id=1, source_target_pairs={{0,8},{8,16},{16,24},{24,28},{28,20},{20,12},{12,4},{4,0},{1,9},{9... | collective-permute-start | bytes 3145736 | tf_op jit(solution)/shard_map/ppermute | solution.py:110
  243.6 22.9 %collective-permute-start.27 = (bf16[512,1024]{1,0:T(8,128)(2,1)S(1)}, bf16[512,1024]{1,0:T(8,128)(2,1)S(1)}, u32[]{:S(2)}, u32[]{:S(2)}) collective-permute-start(bf16[512,1024]{1,0:T(8,128)(2,1)S(1)} %collective-permute-done.25), channel_id=1, source_target_pairs={{0,4},{8,0},{16,8},{24,16},{28,24},{20,28},{12,20},{4,12},{1,5},{9... | collective-permute-start | bytes 3145736 | tf_op jit(solution)/shard_map/ppermute | solution.py:111
  265.2 9.8 %collective-permute-start.28 = (bf16[256,1024]{1,0:T(8,128)(2,1)S(1)}, bf16[256,1024]{1,0:T(8,128)(2,1)S(1)}, u32[]{:S(2)}, u32[]{:S(2)}) collective-permute-start(bf16[256,1024]{1,0:T(8,128)(2,1)S(1)} %slice.30), channel_id=1, source_target_pairs={{0,8},{8,16},{16,24},{24,28},{28,20},{20,12},{12,4},{4,0},{1,9},{9... | collective-permute-start | bytes 1572872 | tf_op jit(solution)/shard_map/ppermute | solution.py:116
  266.5 9.9 %collective-permute-start.29 = (bf16[256,1024]{1,0:T(8,128)(2,1)S(1)}, bf16[256,1024]{1,0:T(8,128)(2,1)S(1)}, u32[]{:S(2)}, u32[]{:S(2)}) collective-permute-start(bf16[256,1024]{1,0:T(8,128)(2,1)S(1)} %slice.31), channel_id=1, source_target_pairs={{0,4},{8,0},{16,8},{24,16},{28,24},{20,28},{12,20},{4,12},{1,5},{9... | collective-permute-start | bytes 1572872 | tf_op jit(solution)/shard_map/ppermute | solution.py:117
  (6 other events, 38.5 us)

commit v13 on v9

--- a/solution.py
+++ b/solution.py
@@ -95,7 +95,7 @@
 
     def q_part(acc, piece, src, lo, n):
         cols = lax.dynamic_slice_in_dim(queries_in, src * wrows + lo, n, 1)
-        return acc + jnp.dot(cols, piece, preferred_element_type=jnp.float32)
+        return lax.optimization_barrier(acc + jnp.dot(cols, piece, preferred_element_type=jnp.float32))
 
     acc = q_part(jnp.zeros((queries_in.shape[0], width), jnp.float32), q_piece, me, 0, wrows)
     fwd = q_piece

time: 277 us -> 275 us (level)
  local copies, waits for them, and re-layouts: 43 us -> 33.8 us
  waiting for transfers between devices: 162 us -> 170 us
  matrix products: 25.6 us -> 21.6 us
  other arithmetic: 3.67 us -> 6.93 us
    ppermute x3, waiting for transfers between devices: 0.01 us -> 19.1 us  [body(): bwd = lax.ppermute(bwd, 'crop', bwd_perm)]
    ppermute x3, waiting for transfers between devices: 41.4 us -> 26.7 us  [body(): fwd = lax.ppermute(fwd, 'crop', fwd_perm)]
    unnamed x40 -> x42, local copies, waits for them, and re-layouts: 24.3 us -> 15.2 us
    ppermute x1, waiting for transfers between devices: 6.37 us -> 11.8 us  [ring_pieces(): got.append((lax.ppermute(fwd[:split], 'crop', fwd_perm), src, 0, split))]
    dot_general x1, matrix products: 8.27 us -> 4.63 us  [body(): jnp.dot(tokens_perm, kv_weight, preferred_element_type=jnp.float32)]
    add x0 -> x6, other arithmetic: none -> 3.26 us  [q_part(): acc + jnp.dot(cols, piece, preferred_element_type=jnp.float32)]
  transfers between devices with their start and end apart: 23 -> 23, of which waited for: 14 -> 14; matrix products, arithmetic and copies ran while one was open for 21% -> 18% of each run, Pallas kernels for 0% -> 0%
where the time goes in v13:
time: 275 us; the launch traced here: 274 us
  waiting for transfers between devices  170 us (62%)
  local copies, waits for them, and re-layouts  33.8 us (12%)
  starting transfers between devices  32.5 us (12%)
  matrix products  21.6 us (8%)
  between operations  9.58 us (3%)
  other arithmetic  6.93 us (3%)
    ppermute x3, waiting for transfers between devices, ring_pieces(): fwd = lax.ppermute(fwd, 'crop', fwd_perm)  83.7 us
    ppermute x3, waiting for transfers between devices, body(): fwd = lax.ppermute(fwd, 'crop', fwd_perm)  26.7 us
    ppermute x3, waiting for transfers between devices, body(): bwd = lax.ppermute(bwd, 'crop', bwd_perm)  19.1 us
    dot_general x9, matrix products, q_part(): jnp.dot(cols, piece, preferred_element_type=jnp.float32)  15.2 us
    unnamed x42, local copies, waits for them, and re-layouts  15.2 us
    ppermute x6, waiting for transfers between devices, head_gather(): part = lax.ppermute(x, 'head', [(j, (j + k) % nhead) for j in range(nhead)])  13 us
    ppermute x1, waiting for transfers between devices, ring_pieces(): got.append((lax.ppermute(fwd[:split], 'crop', fwd_perm), src, 0, split))  11.8 us
    dynamic_update_slice x6, local copies, waits for them, and re-layouts, head_gather(): lax.dynamic_update_slice(full, part, (0, (hme - k) % nhead * x.shape[1]))  8.06 us
  transfers between devices with their start and end apart: 23, of which 14 were waited for; matrix products, arithmetic and copies ran while one was open for 18% of the time, Pallas kernels for 0%

profile of v13, /device:TPU:0, one launch (start us, length us, event | category | flops | bytes accessed | tf_op | source)
XLA Modules:
  0.0 274.1 jit_solution(4876469590475227627)
XLA Ops:
  0.0 2.5 constant_dynamic-update-slice_fusion.11
  3.7 3.0 %collective-permute-start.3 = (bf16[512,2048]{1,0:T(8,128)(2,1)S(1)}, bf16[512,2048]{1,0:T(8,128)(2,1)}, u32[]{:S(2)}, u32[]{:S(2)}) collective-permute-start(bf16[512,2048]{1,0:T(8,128)(2,1)S(1)} %get-tuple-element.14), channel_id=1, source_target_pairs={{0,8},{8,16},{16,24},{24,28},{28,20},{20,12},{12,4},{4,0},{1,9},{9... | collective-permute-start | bytes 6291464 | tf_op jit(solution)/shard_map/ppermute | solution.py:71
  6.8 45.7 %collective-permute-done.3 = bf16[512,2048]{1,0:T(8,128)(2,1)} collective-permute-done((bf16[512,2048]{1,0:T(8,128)(2,1)S(1)}, bf16[512,2048]{1,0:T(8,128)(2,1)}, u32[]{:S(2)}, u32[]{:S(2)}) %collective-permute-start.3) | collective-permute-done | bytes 2097184 | tf_op jit(solution)/shard_map/ppermute | solution.py:71
  57.8 5.8 %all-to-all-start = ((bf16[8,2,16,1024]{3,2,1,0:T(8,128)(2,1)}), bf16[8,2,16,1024]{3,2,1,0:T(8,128)(2,1)S(1)}, u32[]{:S(2)}, u32[]{:S(2)}) async-start(bf16[8,2,16,1024]{3,2,1,0:T(8,128)(2,1)} %bitcast.2), calls=%async_computation | async-start | bytes 1048576 | tf_op jit(solution)/shard_map/all_to_all | solution.py:59
  75.6 26.2 %collective-permute-done.5 = bf16[512,2048]{1,0:T(8,128)(2,1)} collective-permute-done((bf16[512,2048]{1,0:T(8,128)(2,1)}, bf16[512,2048]{1,0:T(8,128)(2,1)}, u32[]{:S(2)}, u32[]{:S(2)}) %collective-permute-start.5) | collective-permute-done | bytes 2097184 | tf_op jit(solution)/shard_map/ppermute | solution.py:71
  101.9 2.7 collective-permute-start.7
  104.6 2.5 broadcast_in_dim.35
  107.0 2.3 constant_dynamic-update-slice_fusion.15
  109.3 5.9 %all-to-all-done = bf16[8,2,16,1024]{3,2,1,0:T(8,128)(2,1)S(1)} async-done(((bf16[8,2,16,1024]{3,2,1,0:T(8,128)(2,1)}), bf16[8,2,16,1024]{3,2,1,0:T(8,128)(2,1)S(1)}, u32[]{:S(2)}, u32[]{:S(2)}) %all-to-all-start) | async-done | bytes 524320 | tf_op jit(solution)/shard_map/all_to_all | solution.py:59
  117.1 2.5 constant_dynamic-update-slice_fusion.14
  121.1 3.1 %constant_dynamic-update-slice_fusion.13 = bf16[512,4096]{1,0:T(8,128)(2,1)} fusion(bf16[512,4096]{1,0:T(8,128)(2,1)} %constant_dynamic-update-slice_fusion.14, bf16[512,1024]{1,0:T(8,128)(2,1)} %collective-permute-done.12, s32[]{:T(128)S(6)} %select_n.165), kind=kLoop, calls=%fused_computation.71 | loop fusion | bytes 2097156 | tf_op jit(solution)/shard_map/dynamic_update_slice | solution.py:52
  124.3 2.3 constant_dynamic-update-slice_fusion.12
  126.6 2.0 collective-permute-done
  130.5 9.3 %collective-permute-done.2 = bf16[256,1024]{1,0:T(8,128)(2,1)S(1)} collective-permute-done((bf16[256,1024]{1,0:T(8,128)(2,1)S(1)}, bf16[256,1024]{1,0:T(8,128)(2,1)S(1)}, u32[]{:S(2)}, u32[]{:S(2)}) %collective-permute-start.2) | collective-permute-done | bytes 524320 | tf_op jit(solution)/shard_map/ppermute | solution.py:51
  140.1 11.8 %collective-permute-done.7 = bf16[512,2048]{1,0:T(8,128)(2,1)S(1)} collective-permute-done((bf16[512,2048]{1,0:T(8,128)(2,1)}, bf16[512,2048]{1,0:T(8,128)(2,1)S(1)}, u32[]{:S(2)}, u32[]{:S(2)}) %collective-permute-start.7) | collective-permute-done | bytes 2097184 | tf_op jit(solution)/shard_map/ppermute | solution.py:71
  152.0 4.4 %collective-permute-start.10 = (bf16[256,2048]{1,0:T(8,128)(2,1)S(1)}, bf16[256,2048]{1,0:T(8,128)(2,1)S(1)}, u32[]{:S(2)}, u32[]{:S(2)}) collective-permute-start(bf16[256,2048]{1,0:T(8,128)(2,1)S(1)} %slice.27), channel_id=1, source_target_pairs={{0,8},{8,16},{16,24},{24,28},{28,20},{20,12},{12,4},{4,0},{1,9},{9... | collective-permute-start | bytes 3145736 | tf_op jit(solution)/shard_map/ppermute | solution.py:77
  159.7 1.8 constant_dynamic-update-slice_fusion.8
  161.5 1.8 constant_dynamic-update-slice_fusion.7
  163.3 1.9 constant_dynamic-update-slice_fusion.6
  165.3 11.8 %collective-permute-done.10 = bf16[256,2048]{1,0:T(8,128)(2,1)S(1)} collective-permute-done((bf16[256,2048]{1,0:T(8,128)(2,1)S(1)}, bf16[256,2048]{1,0:T(8,128)(2,1)S(1)}, u32[]{:S(2)}, u32[]{:S(2)}) %collective-permute-start.10) | collective-permute-done | bytes 1048608 | tf_op jit(solution)/shard_map/ppermute | solution.py:77
  177.1 4.4 %collective-permute-done.9 = bf16[256,2048]{1,0:T(8,128)(2,1)S(1)} collective-permute-done((bf16[256,2048]{1,0:T(8,128)(2,1)S(1)}, bf16[256,2048]{1,0:T(8,128)(2,1)S(1)}, u32[]{:S(2)}, u32[]{:S(2)}) %collective-permute-start.9) | collective-permute-done | bytes 1048608 | tf_op jit(solution)/shard_map/ppermute | solution.py:78
  181.5 2.0 collective-permute-start.14
  185.7 19.1 %collective-permute-done.15 = bf16[512,1024]{1,0:T(8,128)(2,1)S(1)} collective-permute-done((bf16[512,1024]{1,0:T(8,128)(2,1)S(1)}, bf16[512,1024]{1,0:T(8,128)(2,1)S(1)}, u32[]{:S(2)}, u32[]{:S(2)}) %collective-permute-start.15) | collective-permute-done | bytes 1048608 | tf_op jit(solution)/shard_map/ppermute | solution.py:105
  204.8 2.0 collective-permute-start.16
  206.8 4.6 %convolution_convert_fusion = bf16[256,2048]{1,0:T(8,128)(2,1)S(1)} fusion(bf16[256,4096]{1,0:T(8,128)(2,1)S(1)} %dynamic-slice_dynamic-update-slice_fusion.7, bf16[4096,2048]{1,0:T(8,128)(2,1)S(1)} %constant_dynamic-update-slice_fusion.2), kind=kOutput, calls=%fused_computation.6 | convolution fusion | flops 4295491584 | bytes 19922944 | tf_op jit(solution)/shard_map/dot_general | solution.py:93
  213.6 14.6 %collective-permute-done.16 = bf16[512,1024]{1,0:T(8,128)(2,1)S(1)} collective-permute-done((bf16[512,1024]{1,0:T(8,128)(2,1)S(1)}, bf16[512,1024]{1,0:T(8,128)(2,1)S(1)}, u32[]{:S(2)}, u32[]{:S(2)}) %collective-permute-start.16) | collective-permute-done | bytes 1048608 | tf_op jit(solution)/shard_map/ppermute | solution.py:104
  228.1 2.0 collective-permute-start.18
  239.2 12.1 %collective-permute-done.18 = bf16[512,1024]{1,0:T(8,128)(2,1)S(1)} collective-permute-done((bf16[512,1024]{1,0:T(8,128)(2,1)S(1)}, bf16[512,1024]{1,0:T(8,128)(2,1)S(1)}, u32[]{:S(2)}, u32[]{:S(2)}) %collective-permute-start.18) | collective-permute-done | bytes 1048608 | tf_op jit(solution)/shard_map/ppermute | solution.py:104
  251.4 2.1 collective-permute-start.20
  257.7 3.0 %collective-permute-done.20 = bf16[256,1024]{1,0:T(8,128)(2,1)S(1)} collective-permute-done((bf16[256,1024]{1,0:T(8,128)(2,1)S(1)}, bf16[256,1024]{1,0:T(8,128)(2,1)S(1)}, u32[]{:S(2)}, u32[]{:S(2)}) %collective-permute-start.20) | collective-permute-done | bytes 524320 | tf_op jit(solution)/shard_map/ppermute | solution.py:110
  262.6 1.9 collective-permute-done.21
  267.6 3.5 %fusion.42 = (f32[16,8,32]{2,0,1:T(8,128)S(1)}, f32[16,8,32,256]{3,2,0,1:T(8,128)S(1)}) fusion(f32[8,256,16,32]{1,3,2,0:T(8,128)S(1)} %bitcast.73, pred[16,256]{1,0:T(8,128)(4,1)S(1)} %broadcast_in_dim.33), kind=kOutput, calls=%fused_computation.84 | output fusion | flops 6291711 | bytes 8409088 | tf_op jit(solution)/shard_map/sub | solution.py:128
  (105 shorter events, 43.7 us)
Async XLA Ops:
  0.0 56.4 %copy-start = (bf16[1024,1024]{1,0:T(8,128)(2,1)S(1)}, bf16[1024,1024]{1,0:T(8,128)(2,1)}, u32[]{:S(2)}) copy-start(bf16[1024,1024]{1,0:T(8,128)(2,1)} %param.11) | copy-start | bytes 6291460
  2.5 53.7 %copy-start.7 = (s32[1,8,2]{1,2,0:T(2,128)S(1)}, s32[1,8,2]{1,2,0:T(2,128)}, u32[]{:S(2)}) copy-start(s32[1,8,2]{1,2,0:T(2,128)} %param.15) | copy-start | bytes 196
  2.5 62.2 %copy-start.9 = (s32[8]{0:T(128)S(1)}, s32[8]{0:T(128)}, u32[]{:S(2)}) copy-start(s32[8]{0:T(128)} %constant.150.clone) | copy-start | bytes 100
  2.5 67.3 %copy-start.5 = (s32[8]{0:T(128)S(1)}, s32[8]{0:T(128)}, u32[]{:S(2)}) copy-start(s32[8]{0:T(128)} %constant.151.clone) | copy-start | bytes 100
  2.5 72.5 %copy-start.6 = (s32[16,8]{0,1:T(8,128)S(1)}, s32[16,8]{0,1:T(8,128)}, u32[]{:S(2)}) copy-start(s32[16,8]{0,1:T(8,128)} %param.16) | copy-start | bytes 1540
  2.5 72.6 %copy-start.8 = (s32[16]{0:T(128)S(1)}, s32[16]{0:T(128)}, u32[]{:S(2)}) copy-start(s32[16]{0:T(128)} %param.17) | copy-start | bytes 196
  3.7 48.7 %collective-permute-start.3 = (bf16[512,2048]{1,0:T(8,128)(2,1)S(1)}, bf16[512,2048]{1,0:T(8,128)(2,1)}, u32[]{:S(2)}, u32[]{:S(2)}) collective-permute-start(bf16[512,2048]{1,0:T(8,128)(2,1)S(1)} %get-tuple-element.14), channel_id=1, source_target_pairs={{0,8},{8,16},{16,24},{24,28},{28,20},{20,12},{12,4},{4,0},{1,9},{9... | collective-permute-start | bytes 6291464 | tf_op jit(solution)/shard_map/ppermute | solution.py:71
  6.8 47.5 %collective-permute-start.4 = (bf16[512,2048]{1,0:T(8,128)(2,1)S(1)}, bf16[512,2048]{1,0:T(8,128)(2,1)}, u32[]{:S(2)}, u32[]{:S(2)}) collective-permute-start(bf16[512,2048]{1,0:T(8,128)(2,1)S(1)} %get-tuple-element.14), channel_id=1, source_target_pairs={{0,4},{8,0},{16,8},{24,16},{28,24},{20,28},{12,20},{4,12},{1,5},{9... | collective-permute-start | bytes 6291464 | tf_op jit(solution)/shard_map/ppermute | solution.py:72
  52.4 49.4 %collective-permute-start.5 = (bf16[512,2048]{1,0:T(8,128)(2,1)}, bf16[512,2048]{1,0:T(8,128)(2,1)}, u32[]{:S(2)}, u32[]{:S(2)}) collective-permute-start(bf16[512,2048]{1,0:T(8,128)(2,1)} %collective-permute-done.3), channel_id=1, source_target_pairs={{0,8},{8,16},{16,24},{24,28},{28,20},{20,12},{12,4},{4,0},{1,9},{9... | collective-permute-start | bytes 6291464 | tf_op jit(solution)/shard_map/ppermute | solution.py:71
  54.2 50.3 %collective-permute-start.6 = (bf16[512,2048]{1,0:T(8,128)(2,1)}, bf16[512,2048]{1,0:T(8,128)(2,1)}, u32[]{:S(2)}, u32[]{:S(2)}) collective-permute-start(bf16[512,2048]{1,0:T(8,128)(2,1)} %collective-permute-done.4), channel_id=1, source_target_pairs={{0,4},{8,0},{16,8},{24,16},{28,24},{20,28},{12,20},{4,12},{1,5},{9... | collective-permute-start | bytes 6291464 | tf_op jit(solution)/shard_map/ppermute | solution.py:72
  54.5 60.8 %collective-permute-start.11 = (bf16[512,1024]{1,0:T(8,128)(2,1)}, bf16[512,1024]{1,0:T(8,128)(2,1)}, u32[]{:S(2)}, u32[]{:S(2)}) collective-permute-start(bf16[512,1024]{1,0:T(8,128)(2,1)} %param.10), channel_id=1, source_target_pairs={{0,1},{1,2},{2,3},{3,0},{4,5},{5,6},{6,7},{7,4},{8,9},{9,10},{10,1... | collective-permute-start | bytes 3145736 | tf_op jit(solution)/shard_map/ppermute | solution.py:51
  54.5 61.1 %collective-permute-start.12 = (bf16[512,1024]{1,0:T(8,128)(2,1)}, bf16[512,1024]{1,0:T(8,128)(2,1)}, u32[]{:S(2)}, u32[]{:S(2)}) collective-permute-start(bf16[512,1024]{1,0:T(8,128)(2,1)} %param.10), channel_id=1, source_target_pairs={{0,2},{1,3},{2,0},{3,1},{4,6},{5,7},{6,4},{7,5},{8,10},{9,11},{10,... | collective-permute-start | bytes 3145736 | tf_op jit(solution)/shard_map/ppermute | solution.py:51
  57.8 57.5 %all-to-all-start = ((bf16[8,2,16,1024]{3,2,1,0:T(8,128)(2,1)}), bf16[8,2,16,1024]{3,2,1,0:T(8,128)(2,1)S(1)}, u32[]{:S(2)}, u32[]{:S(2)}) async-start(bf16[8,2,16,1024]{3,2,1,0:T(8,128)(2,1)} %bitcast.2), calls=%async_computation | async-start | bytes 1048576 | tf_op jit(solution)/shard_map/all_to_all | solution.py:59
  63.6 56.0 %collective-permute-start.13 = (bf16[512,1024]{1,0:T(8,128)(2,1)}, bf16[512,1024]{1,0:T(8,128)(2,1)}, u32[]{:S(2)}, u32[]{:S(2)}) collective-permute-start(bf16[512,1024]{1,0:T(8,128)(2,1)} %param.10), channel_id=1, source_target_pairs={{0,3},{1,0},{2,1},{3,2},{4,7},{5,4},{6,5},{7,6},{8,11},{9,8},{10,9... | collective-permute-start | bytes 3145736 | tf_op jit(solution)/shard_map/ppermute | solution.py:51
  101.9 50.1 %collective-permute-start.7 = (bf16[512,2048]{1,0:T(8,128)(2,1)}, bf16[512,2048]{1,0:T(8,128)(2,1)S(1)}, u32[]{:S(2)}, u32[]{:S(2)}) collective-permute-start(bf16[512,2048]{1,0:T(8,128)(2,1)} %collective-permute-done.5), channel_id=1, source_target_pairs={{0,8},{8,16},{16,24},{24,28},{28,20},{20,12},{12,4},{4,0},{1,9},{9... | collective-permute-start | bytes 6291464 | tf_op jit(solution)/shard_map/ppermute | solution.py:71
  104.6 51.9 %collective-permute-start.8 = (bf16[512,2048]{1,0:T(8,128)(2,1)}, bf16[512,2048]{1,0:T(8,128)(2,1)}, u32[]{:S(2)}, u32[]{:S(2)}) collective-permute-start(bf16[512,2048]{1,0:T(8,128)(2,1)} %collective-permute-done.6), channel_id=1, source_target_pairs={{0,4},{8,0},{16,8},{24,16},{28,24},{20,28},{12,20},{4,12},{1,5},{9... | collective-permute-start | bytes 6291464 | tf_op jit(solution)/shard_map/ppermute | solution.py:72
  115.3 13.3 %collective-permute-start = (bf16[256,1024]{1,0:T(8,128)(2,1)S(1)}, bf16[256,1024]{1,0:T(8,128)(2,1)S(1)}, u32[]{:S(2)}, u32[]{:S(2)}) collective-permute-start(bf16[256,1024]{1,0:T(8,128)(2,1)S(1)} %bitcast.77), channel_id=1, source_target_pairs={{0,1},{1,2},{2,3},{3,0},{4,5},{5,6},{6,7},{7,4},{8,9},{9,10},{10,1... | collective-permute-start | bytes 1572872 | tf_op jit(solution)/shard_map/ppermute | solution.py:51
  115.6 14.9 %collective-permute-start.1 = (bf16[256,1024]{1,0:T(8,128)(2,1)S(1)}, bf16[256,1024]{1,0:T(8,128)(2,1)S(1)}, u32[]{:S(2)}, u32[]{:S(2)}) collective-permute-start(bf16[256,1024]{1,0:T(8,128)(2,1)S(1)} %bitcast.79), channel_id=1, source_target_pairs={{0,2},{1,3},{2,0},{3,1},{4,6},{5,7},{6,4},{7,5},{8,10},{9,11},{10,... | collective-permute-start | bytes 1572872 | tf_op jit(solution)/shard_map/ppermute | solution.py:51
  117.1 40.7 %copy-start.4 = (bf16[4096,2048]{1,0:T(8,128)(2,1)S(1)}, bf16[4096,2048]{1,0:T(8,128)(2,1)}, u32[]{:S(2)}) copy-start(bf16[4096,2048]{1,0:T(8,128)(2,1)} %get-tuple-element.13) | copy-start | bytes 50331652
  119.6 20.1 %collective-permute-start.2 = (bf16[256,1024]{1,0:T(8,128)(2,1)S(1)}, bf16[256,1024]{1,0:T(8,128)(2,1)S(1)}, u32[]{:S(2)}, u32[]{:S(2)}) collective-permute-start(bf16[256,1024]{1,0:T(8,128)(2,1)S(1)} %bitcast.80), channel_id=1, source_target_pairs={{0,3},{1,0},{2,1},{3,2},{4,7},{5,4},{6,5},{7,6},{8,11},{9,8},{10,9... | collective-permute-start | bytes 1572872 | tf_op jit(solution)/shard_map/ppermute | solution.py:51
  152.0 25.1 %collective-permute-start.10 = (bf16[256,2048]{1,0:T(8,128)(2,1)S(1)}, bf16[256,2048]{1,0:T(8,128)(2,1)S(1)}, u32[]{:S(2)}, u32[]{:S(2)}) collective-permute-start(bf16[256,2048]{1,0:T(8,128)(2,1)S(1)} %slice.27), channel_id=1, source_target_pairs={{0,8},{8,16},{16,24},{24,28},{28,20},{20,12},{12,4},{4,0},{1,9},{9... | collective-permute-start | bytes 3145736 | tf_op jit(solution)/shard_map/ppermute | solution.py:77
  157.7 23.7 %collective-permute-start.9 = (bf16[256,2048]{1,0:T(8,128)(2,1)S(1)}, bf16[256,2048]{1,0:T(8,128)(2,1)S(1)}, u32[]{:S(2)}, u32[]{:S(2)}) collective-permute-start(bf16[256,2048]{1,0:T(8,128)(2,1)S(1)} %slice.26), channel_id=1, source_target_pairs={{0,4},{8,0},{16,8},{24,16},{28,24},{20,28},{12,20},{4,12},{1,5},{9... | collective-permute-start | bytes 3145736 | tf_op jit(solution)/shard_map/ppermute | solution.py:78
  163.3 18.1 %copy-start.3 = (bf16[512,1024]{1,0:T(8,128)(2,1)S(1)}, bf16[512,1024]{1,0:T(8,128)(2,1)}, u32[]{:S(2)}) copy-start(bf16[512,1024]{1,0:T(8,128)(2,1)} %param.12) | copy-start | bytes 3145732
  181.5 23.3 %collective-permute-start.15 = (bf16[512,1024]{1,0:T(8,128)(2,1)S(1)}, bf16[512,1024]{1,0:T(8,128)(2,1)S(1)}, u32[]{:S(2)}, u32[]{:S(2)}) collective-permute-start(bf16[512,1024]{1,0:T(8,128)(2,1)S(1)} %copy-done.3), channel_id=1, source_target_pairs={{0,4},{8,0},{16,8},{24,16},{28,24},{20,28},{12,20},{4,12},{1,5},{9... | collective-permute-start | bytes 3145736 | tf_op jit(solution)/shard_map/ppermute | solution.py:105
  181.5 23.3 %collective-permute-start.14 = (bf16[512,1024]{1,0:T(8,128)(2,1)S(1)}, bf16[512,1024]{1,0:T(8,128)(2,1)S(1)}, u32[]{:S(2)}, u32[]{:S(2)}) collective-permute-start(bf16[512,1024]{1,0:T(8,128)(2,1)S(1)} %copy-done.3), channel_id=1, source_target_pairs={{0,8},{8,16},{16,24},{24,28},{28,20},{20,12},{12,4},{4,0},{1,9},{9... | collective-permute-start | bytes 3145736 | tf_op jit(solution)/shard_map/ppermute | solution.py:104
  204.8 27.1 %collective-permute-start.17 = (bf16[512,1024]{1,0:T(8,128)(2,1)S(1)}, bf16[512,1024]{1,0:T(8,128)(2,1)S(1)}, u32[]{:S(2)}, u32[]{:S(2)}) collective-permute-start(bf16[512,1024]{1,0:T(8,128)(2,1)S(1)} %collective-permute-done.15), channel_id=1, source_target_pairs={{0,4},{8,0},{16,8},{24,16},{28,24},{20,28},{12,20},{4,12},{1,5},{9... | collective-permute-start | bytes 3145736 | tf_op jit(solution)/shard_map/ppermute | solution.py:105
  204.8 23.3 %collective-permute-start.16 = (bf16[512,1024]{1,0:T(8,128)(2,1)S(1)}, bf16[512,1024]{1,0:T(8,128)(2,1)S(1)}, u32[]{:S(2)}, u32[]{:S(2)}) collective-permute-start(bf16[512,1024]{1,0:T(8,128)(2,1)S(1)} %collective-permute-done.14), channel_id=1, source_target_pairs={{0,8},{8,16},{16,24},{24,28},{28,20},{20,12},{12,4},{4,0},{1,9},{9... | collective-permute-start | bytes 3145736 | tf_op jit(solution)/shard_map/ppermute | solution.py:104
  228.1 23.2 %collective-permute-start.18 = (bf16[512,1024]{1,0:T(8,128)(2,1)S(1)}, bf16[512,1024]{1,0:T(8,128)(2,1)S(1)}, u32[]{:S(2)}, u32[]{:S(2)}) collective-permute-start(bf16[512,1024]{1,0:T(8,128)(2,1)S(1)} %collective-permute-done.16), channel_id=1, source_target_pairs={{0,8},{8,16},{16,24},{24,28},{28,20},{20,12},{12,4},{4,0},{1,9},{9... | collective-permute-start | bytes 3145736 | tf_op jit(solution)/shard_map/ppermute | solution.py:104
  231.9 23.3 %collective-permute-start.19 = (bf16[512,1024]{1,0:T(8,128)(2,1)S(1)}, bf16[512,1024]{1,0:T(8,128)(2,1)S(1)}, u32[]{:S(2)}, u32[]{:S(2)}) collective-permute-start(bf16[512,1024]{1,0:T(8,128)(2,1)S(1)} %collective-permute-done.17), channel_id=1, source_target_pairs={{0,4},{8,0},{16,8},{24,16},{28,24},{20,28},{12,20},{4,12},{1,5},{9... | collective-permute-start | bytes 3145736 | tf_op jit(solution)/shard_map/ppermute | solution.py:105
  251.4 9.2 %collective-permute-start.20 = (bf16[256,1024]{1,0:T(8,128)(2,1)S(1)}, bf16[256,1024]{1,0:T(8,128)(2,1)S(1)}, u32[]{:S(2)}, u32[]{:S(2)}) collective-permute-start(bf16[256,1024]{1,0:T(8,128)(2,1)S(1)} %slice.30), channel_id=1, source_target_pairs={{0,8},{8,16},{16,24},{24,28},{28,20},{20,12},{12,4},{4,0},{1,9},{9... | collective-permute-start | bytes 1572872 | tf_op jit(solution)/shard_map/ppermute | solution.py:110
  255.3 9.2 %collective-permute-start.21 = (bf16[256,1024]{1,0:T(8,128)(2,1)S(1)}, bf16[256,1024]{1,0:T(8,128)(2,1)S(1)}, u32[]{:S(2)}, u32[]{:S(2)}) collective-permute-start(bf16[256,1024]{1,0:T(8,128)(2,1)S(1)} %slice.31), channel_id=1, source_target_pairs={{0,4},{8,0},{16,8},{24,16},{28,24},{20,28},{12,20},{4,12},{1,5},{9... | collective-permute-start | bytes 1572872 | tf_op jit(solution)/shard_map/ppermute | solution.py:111
  271.1 3.0 %copy-start.1 = (bf16[1024,1024]{1,0:T(8,128)(2,1)S(1)}, bf16[1024,1024]{1,0:T(8,128)(2,1)}, u32[]{:S(2)}) copy-start(bf16[1024,1024]{1,0:T(8,128)(2,1)} %param.11) | copy-start | bytes 6291460
  (1 other events, 2.5 us)

commit v14 on v13

--- a/solution.py
+++ b/solution.py
@@ -95,9 +95,12 @@
 
     def q_part(acc, piece, src, lo, n):
         cols = lax.dynamic_slice_in_dim(queries_in, src * wrows + lo, n, 1)
-        return lax.optimization_barrier(acc + jnp.dot(cols, piece, preferred_element_type=jnp.float32))
+        piece = piece.reshape(n, heads_here, HD)
+        part = jnp.einsum("rf,fhe->hre", cols, piece, preferred_element_type=jnp.float32)
+        return lax.optimization_barrier(acc + part)
 
-    acc = q_part(jnp.zeros((queries_in.shape[0], width), jnp.float32), q_piece, me, 0, wrows)
+    acc = jnp.zeros((heads_here, queries_in.shape[0], HD), jnp.float32)
+    acc = q_part(acc, q_piece, me, 0, wrows)
     fwd = q_piece
     bwd = q_piece
     for k in range(1, steps_bwd + 1):
@@ -113,14 +116,14 @@
     nslots = ncrop * CAP
     keys_all = incoming[..., :width].reshape(nslots * CT, heads_here, HD)
     vals_all = incoming[..., width:].reshape(nslots * CT, heads_here, HD)
-    query_row = query.reshape(rows_here, GR, heads_here, HD)
+    query_row = query.reshape(heads_here, rows_here, GR, HD)
     in_use = (jnp.arange(NB, dtype=jnp.int32)[None, :] < region_len[:, None])[:, :, None]
     hits = region_slots[:, :, None] == jnp.arange(nslots, dtype=jnp.int32)[None, None, :]
     member = jnp.any(hits & in_use, axis=1)
     member = jnp.repeat(member, CT, axis=1)
     scale = 1.0 / HD**0.5
     scores = (
-        jnp.einsum("rghe,khe->rhgk", query_row, keys_all, preferred_element_type=jnp.float32)
+        jnp.einsum("hrge,khe->rhgk", query_row, keys_all, preferred_element_type=jnp.float32)
         * scale
     )
     scores = jnp.where(member[:, None, None, :], scores, jnp.float32(-1e30))

time: 275 us -> 297 us (1.080)
  local copies, waits for them, and re-layouts: 33.8 us -> 59.1 us
  waiting for transfers between devices: 170 us -> 158 us
  matrix products: 21.6 us -> 30.4 us
  starting transfers between devices: 32.5 us -> 29.4 us
    all_to_all x1, waiting for transfers between devices: 5.94 us -> 32.7 us  [body(): lax.all_to_all(chosen, 'crop', split_axis=0, concat_axis=0, tiled=True)]
    ppermute x3, waiting for transfers between devices: 19.1 us -> 0.01 us  [body(): bwd = lax.ppermute(bwd, 'crop', bwd_perm)]
    ppermute x3, waiting for transfers between devices: 83.7 us -> 68.4 us  [ring_pieces(): fwd = lax.ppermute(fwd, 'crop', fwd_perm)]
    ppermute x0 -> x8, local copies, waits for them, and re-layouts: none -> 11.6 us  [the longest x3 4.63 us: body(): fwd = lax.ppermute(fwd, 'crop', fwd_perm)]
    unnamed x42 -> x59, local copies, waits for them, and re-layouts: 15.2 us -> 26 us
    dot_general x9 -> x10, matrix products: 15.2 us -> 21.2 us  [the longest x9 20.5 us: q_part(): jnp.einsum('rf,fhe->hre', cols, piece, preferred_element_type=jnp.float32)]
    ppermute x3, starting transfers between devices: 0.25 us -> 4.62 us  [body(): bwd = lax.ppermute(bwd, 'crop', bwd_perm)]
    ppermute x3, starting transfers between devices: 6.06 us -> 1.74 us  [body(): fwd = lax.ppermute(fwd, 'crop', fwd_perm)]
  transfers between devices with their start and end apart: 23 -> 23, of which waited for: 14 -> 12; matrix products, arithmetic and copies ran while one was open for 18% -> 28% of each run, Pallas kernels for 0% -> 0%
where the time goes in v14:
time: 297 us; the launch traced here: 295 us
  waiting for transfers between devices  158 us (53%)
  local copies, waits for them, and re-layouts  59.1 us (20%)
  matrix products  30.4 us (10%)
  starting transfers between devices  29.4 us (10%)
  between operations  9.32 us (3%)
  other arithmetic  8.86 us (3%)
    ppermute x3, waiting for transfers between devices, ring_pieces(): fwd = lax.ppermute(fwd, 'crop', fwd_perm)  68.4 us
    all_to_all x1, waiting for transfers between devices, body(): lax.all_to_all(chosen, 'crop', split_axis=0, concat_axis=0, tiled=True)  32.7 us
    ppermute x3, waiting for transfers between devices, body(): fwd = lax.ppermute(fwd, 'crop', fwd_perm)  29.7 us
    unnamed x59, local copies, waits for them, and re-layouts  26 us
    dot_general x9, matrix products, q_part(): jnp.einsum('rf,fhe->hre', cols, piece, preferred_element_type=jnp.float32)  20.5 us
    ppermute x6, waiting for transfers between devices, head_gather(): part = lax.ppermute(x, 'head', [(j, (j + k) % nhead) for j in range(nhead)])  12 us
    ppermute x1, waiting for transfers between devices, ring_pieces(): got.append((lax.ppermute(fwd[:split], 'crop', fwd_perm), src, 0, split))  11.6 us
    dot_general x1, matrix products, body(): jnp.dot(tokens_perm, kv_weight, preferred_element_type=jnp.float32)  8.27 us
  transfers between devices with their start and end apart: 23, of which 12 were waited for; matrix products, arithmetic and copies ran while one was open for 28% of the time, Pallas kernels for 0%

profile of v14, /device:TPU:0, one launch (start us, length us, event | category | flops | bytes accessed | tf_op | source)
XLA Modules:
  0.0 295.4 jit_solution(15488737477091963023)
XLA Ops:
  0.0 2.5 constant_dynamic-update-slice_fusion.11
  3.7 3.0 %collective-permute-start.3 = (bf16[512,2048]{1,0:T(8,128)(2,1)S(1)}, bf16[512,2048]{1,0:T(8,128)(2,1)}, u32[]{:S(2)}, u32[]{:S(2)}) collective-permute-start(bf16[512,2048]{1,0:T(8,128)(2,1)S(1)} %get-tuple-element.14), channel_id=1, source_target_pairs={{0,8},{8,16},{16,24},{24,28},{28,20},{20,12},{12,4},{4,0},{1,9},{9... | collective-permute-start | bytes 6291464 | tf_op jit(solution)/shard_map/ppermute | solution.py:71
  6.8 45.7 %collective-permute-done.3 = bf16[512,2048]{1,0:T(8,128)(2,1)} collective-permute-done((bf16[512,2048]{1,0:T(8,128)(2,1)S(1)}, bf16[512,2048]{1,0:T(8,128)(2,1)}, u32[]{:S(2)}, u32[]{:S(2)}) %collective-permute-start.3) | collective-permute-done | bytes 2097184 | tf_op jit(solution)/shard_map/ppermute | solution.py:71
  57.8 5.8 %all-to-all-start = ((bf16[8,2,16,1024]{3,2,1,0:T(8,128)(2,1)}), bf16[8,2,16,1024]{3,2,1,0:T(8,128)(2,1)S(1)}, u32[]{:S(2)}, u32[]{:S(2)}) async-start(bf16[8,2,16,1024]{3,2,1,0:T(8,128)(2,1)} %bitcast.2), calls=%async_computation | async-start | bytes 1048576 | tf_op jit(solution)/shard_map/all_to_all | solution.py:59
  75.4 2.5 broadcast_in_dim.35
  77.9 2.3 constant_dynamic-update-slice_fusion.15
  80.2 32.7 %all-to-all-done = bf16[8,2,16,1024]{3,2,1,0:T(8,128)(2,1)S(1)} async-done(((bf16[8,2,16,1024]{3,2,1,0:T(8,128)(2,1)}), bf16[8,2,16,1024]{3,2,1,0:T(8,128)(2,1)S(1)}, u32[]{:S(2)}, u32[]{:S(2)}) %all-to-all-start) | async-done | bytes 524320 | tf_op jit(solution)/shard_map/all_to_all | solution.py:59
  114.8 2.3 constant_dynamic-update-slice_fusion.14
  118.5 2.3 constant_dynamic-update-slice_fusion.13
  120.9 2.0 collective-permute-start.8
  122.9 2.4 constant_dynamic-update-slice_fusion.12
  128.1 9.3 %collective-permute-done.2 = bf16[256,1024]{1,0:T(8,128)(2,1)S(1)} collective-permute-done((bf16[256,1024]{1,0:T(8,128)(2,1)S(1)}, bf16[256,1024]{1,0:T(8,128)(2,1)S(1)}, u32[]{:S(2)}, u32[]{:S(2)}) %collective-permute-start.2) | collective-permute-done | bytes 524320 | tf_op jit(solution)/shard_map/ppermute | solution.py:51
  137.8 3.9 %constant_dynamic-update-slice_fusion.9 = bf16[4096,2048]{1,0:T(8,128)(2,1)} fusion(bf16[4096,2048]{1,0:T(8,128)(2,1)} %get-tuple-element.13, bf16[512,2048]{1,0:T(8,128)(2,1)} %collective-permute-done.3), kind=kLoop, calls=%fused_computation.70 | loop fusion | bytes 4194304
  141.7 3.2 %constant_dynamic-update-slice_fusion.8 = bf16[4096,2048]{1,0:T(8,128)(2,1)} fusion(bf16[4096,2048]{1,0:T(8,128)(2,1)} %constant_dynamic-update-slice_fusion.9, bf16[512,2048]{1,0:T(8,128)(2,1)} %collective-permute-done.4), kind=kLoop, calls=%fused_computation.69 | loop fusion | bytes 4194304
  144.9 22.8 %collective-permute-done.7 = bf16[512,2048]{1,0:T(8,128)(2,1)S(1)} collective-permute-done((bf16[512,2048]{1,0:T(8,128)(2,1)}, bf16[512,2048]{1,0:T(8,128)(2,1)S(1)}, u32[]{:S(2)}, u32[]{:S(2)}) %collective-permute-start.7) | collective-permute-done | bytes 2097184 | tf_op jit(solution)/shard_map/ppermute | solution.py:71
  170.0 3.2 %constant_dynamic-update-slice_fusion.7 = bf16[4096,2048]{1,0:T(8,128)(2,1)} fusion(bf16[4096,2048]{1,0:T(8,128)(2,1)} %constant_dynamic-update-slice_fusion.8, bf16[512,2048]{1,0:T(8,128)(2,1)} %collective-permute-done.5), kind=kLoop, calls=%fused_computation.68 | loop fusion | bytes 4194304
  173.3 3.2 %constant_dynamic-update-slice_fusion.6 = bf16[4096,2048]{1,0:T(8,128)(2,1)} fusion(bf16[4096,2048]{1,0:T(8,128)(2,1)} %constant_dynamic-update-slice_fusion.7, bf16[512,2048]{1,0:T(8,128)(2,1)} %collective-permute-done.6), kind=kLoop, calls=%fused_computation.67 | loop fusion | bytes 4194304
  179.4 11.6 %collective-permute-done.10 = bf16[256,2048]{1,0:T(8,128)(2,1)S(1)} collective-permute-done((bf16[256,2048]{1,0:T(8,128)(2,1)S(1)}, bf16[256,2048]{1,0:T(8,128)(2,1)S(1)}, u32[]{:S(2)}, u32[]{:S(2)}) %collective-permute-start.10) | collective-permute-done | bytes 1048608 | tf_op jit(solution)/shard_map/ppermute | solution.py:77
  197.3 8.3 %convolution_convert_fusion = bf16[256,2048]{1,0:T(8,128)(2,1)S(1)} fusion(bf16[256,4096]{1,0:T(8,128)(2,1)S(1)} %copy-done.13, bf16[4096,2048]{1,0:T(8,128)(2,1)} %constant_dynamic-update-slice_fusion.2), kind=kOutput, calls=%fused_computation.6 | convolution fusion | flops 4295491584 | bytes 19922944 | tf_op jit(solution)/shard_map/dot_general | solution.py:93
  205.5 12.1 %collective-permute-done.14 = bf16[512,1024]{1,0:T(8,128)(2,1)} collective-permute-done((bf16[512,1024]{1,0:T(8,128)(2,1)S(1)}, bf16[512,1024]{1,0:T(8,128)(2,1)}, u32[]{:S(2)}, u32[]{:S(2)}) %collective-permute-start.14) | collective-permute-done | bytes 1048608 | tf_op jit(solution)/shard_map/ppermute | solution.py:107
  218.2 3.1 %convolution_bitcast_fusion = f32[8,512,128]{1,2,0:T(8,128)} fusion(bf16[512,8,128]{0,2,1:T(8,128)(2,1)S(1)} %bitcast.121, bf16[512,4096]{1,0:T(8,128)(2,1)} %constant_dynamic-update-slice_fusion.12, s32[]{:T(128)S(6)} %select_n.168), kind=kOutput, calls=%fused_computation.19 | convolution fusion | flops 536870912 | bytes 3670020 | tf_op jit(solution)/shard_map/rf,fhe->hre/dot_general | solution.py:99
  226.2 2.5 bitcast_add_fusion.7
  232.0 9.0 %collective-permute-done.16 = bf16[512,1024]{1,0:T(8,128)(2,1)} collective-permute-done((bf16[512,1024]{1,0:T(8,128)(2,1)}, bf16[512,1024]{1,0:T(8,128)(2,1)}, u32[]{:S(2)}, u32[]{:S(2)}) %collective-permute-start.16) | collective-permute-done | bytes 1048608 | tf_op jit(solution)/shard_map/ppermute | solution.py:107
  246.8 3.1 %bitcast_add_fusion.5 = f32[8,512,128]{1,2,0:T(8,128)} fusion(f32[8,512,128]{1,2,0:T(8,128)S(1)} %copy-done.2, bf16[512,8,128]{0,2,1:T(8,128)(2,1)S(1)} %bitcast.122, bf16[512,4096]{1,0:T(8,128)(2,1)} %constant_dynamic-update-slice_fusion.12, s32[]{:T(128)S(6)} %select_n.178), kind=kOutput, calls=%fused_computation.12 | convolution fusion | flops 537395200 | bytes 5767172 | tf_op jit(solution)/shard_map/rf,fhe->hre/dot_general | solution.py:99
  251.4 1.9 fusion.11
  253.8 8.6 %collective-permute-done.18 = bf16[512,1024]{1,0:T(8,128)(2,1)} collective-permute-done((bf16[512,1024]{1,0:T(8,128)(2,1)}, bf16[512,1024]{1,0:T(8,128)(2,1)}, u32[]{:S(2)}, u32[]{:S(2)}) %collective-permute-start.18) | collective-permute-done | bytes 1048608 | tf_op jit(solution)/shard_map/ppermute | solution.py:107
  262.5 1.9 slice.30
  266.4 3.2 %bitcast_add_fusion.3 = f32[8,512,128]{1,2,0:T(8,128)} fusion(f32[8,512,128]{1,2,0:T(8,128)S(1)} %bitcast_add_fusion.4, bf16[512,8,128]{0,2,1:T(8,128)(2,1)S(1)} %bitcast.123, bf16[512,4096]{1,0:T(8,128)(2,1)} %constant_dynamic-update-slice_fusion.12, s32[]{:T(128)S(6)} %select_n.184), kind=kOutput, calls=%fused_computation.10 | convolution fusion | flops 537395200 | bytes 5767172 | tf_op jit(solution)/shard_map/rf,fhe->hre/dot_general | solution.py:99
  271.1 1.9 fusion.8
  278.8 1.8 bitcast_add_fusion.1
  280.6 3.3 %collective-permute-done.21 = bf16[256,1024]{1,0:T(8,128)(2,1)} collective-permute-done((bf16[256,1024]{1,0:T(8,128)(2,1)S(1)}, bf16[256,1024]{1,0:T(8,128)(2,1)}, u32[]{:S(2)}, u32[]{:S(2)}) %collective-permute-start.21) | collective-permute-done | bytes 524320 | tf_op jit(solution)/shard_map/ppermute | solution.py:114
  288.9 3.5 %fusion.49 = (f32[16,8,32]{2,0,1:T(8,128)S(1)}, f32[16,8,32,256]{3,2,0,1:T(8,128)S(1)}) fusion(f32[8,256,16,32]{1,3,2,0:T(8,128)S(1)} %fusion.18, pred[16,256]{1,0:T(8,128)(4,1)S(1)} %broadcast_in_dim.33), kind=kOutput, calls=%fused_computation.97 | output fusion | flops 6291711 | bytes 8409088 | tf_op jit(solution)/shard_map/sub | solution.py:131
  (130 shorter events, 60.9 us)
Async XLA Ops:
  0.0 56.4 %copy-start = (bf16[1024,1024]{1,0:T(8,128)(2,1)S(1)}, bf16[1024,1024]{1,0:T(8,128)(2,1)}, u32[]{:S(2)}) copy-start(bf16[1024,1024]{1,0:T(8,128)(2,1)} %param.11) | copy-start | bytes 6291460
  2.5 53.7 %copy-start.16 = (s32[1,8,2]{1,2,0:T(2,128)S(1)}, s32[1,8,2]{1,2,0:T(2,128)}, u32[]{:S(2)}) copy-start(s32[1,8,2]{1,2,0:T(2,128)} %param.15) | copy-start | bytes 196
  2.5 62.2 %copy-start.18 = (s32[8]{0:T(128)S(1)}, s32[8]{0:T(128)}, u32[]{:S(2)}) copy-start(s32[8]{0:T(128)} %constant.150.clone) | copy-start | bytes 100
  2.5 67.3 %copy-start.14 = (s32[8]{0:T(128)S(1)}, s32[8]{0:T(128)}, u32[]{:S(2)}) copy-start(s32[8]{0:T(128)} %constant.151.clone) | copy-start | bytes 100
  2.5 72.3 %copy-start.15 = (s32[16,8]{0,1:T(8,128)S(1)}, s32[16,8]{0,1:T(8,128)}, u32[]{:S(2)}) copy-start(s32[16,8]{0,1:T(8,128)} %param.16) | copy-start | bytes 1540
  2.5 72.4 %copy-start.17 = (s32[16]{0:T(128)S(1)}, s32[16]{0:T(128)}, u32[]{:S(2)}) copy-start(s32[16]{0:T(128)} %param.17) | copy-start | bytes 196
  3.7 48.7 %collective-permute-start.3 = (bf16[512,2048]{1,0:T(8,128)(2,1)S(1)}, bf16[512,2048]{1,0:T(8,128)(2,1)}, u32[]{:S(2)}, u32[]{:S(2)}) collective-permute-start(bf16[512,2048]{1,0:T(8,128)(2,1)S(1)} %get-tuple-element.14), channel_id=1, source_target_pairs={{0,8},{8,16},{16,24},{24,28},{28,20},{20,12},{12,4},{4,0},{1,9},{9... | collective-permute-start | bytes 6291464 | tf_op jit(solution)/shard_map/ppermute | solution.py:71
  6.8 47.5 %collective-permute-start.4 = (bf16[512,2048]{1,0:T(8,128)(2,1)S(1)}, bf16[512,2048]{1,0:T(8,128)(2,1)}, u32[]{:S(2)}, u32[]{:S(2)}) collective-permute-start(bf16[512,2048]{1,0:T(8,128)(2,1)S(1)} %get-tuple-element.14), channel_id=1, source_target_pairs={{0,4},{8,0},{16,8},{24,16},{28,24},{20,28},{12,20},{4,12},{1,5},{9... | collective-permute-start | bytes 6291464 | tf_op jit(solution)/shard_map/ppermute | solution.py:72
  52.4 68.4 %collective-permute-start.5 = (bf16[512,2048]{1,0:T(8,128)(2,1)}, bf16[512,2048]{1,0:T(8,128)(2,1)}, u32[]{:S(2)}, u32[]{:S(2)}) collective-permute-start(bf16[512,2048]{1,0:T(8,128)(2,1)} %collective-permute-done.3), channel_id=1, source_target_pairs={{0,8},{8,16},{16,24},{24,28},{28,20},{20,12},{12,4},{4,0},{1,9},{9... | collective-permute-start | bytes 6291464 | tf_op jit(solution)/shard_map/ppermute | solution.py:71
  54.2 66.6 %collective-permute-start.6 = (bf16[512,2048]{1,0:T(8,128)(2,1)}, bf16[512,2048]{1,0:T(8,128)(2,1)}, u32[]{:S(2)}, u32[]{:S(2)}) collective-permute-start(bf16[512,2048]{1,0:T(8,128)(2,1)} %collective-permute-done.4), channel_id=1, source_target_pairs={{0,4},{8,0},{16,8},{24,16},{28,24},{20,28},{12,20},{4,12},{1,5},{9... | collective-permute-start | bytes 6291464 | tf_op jit(solution)/shard_map/ppermute | solution.py:72
  54.5 58.5 %collective-permute-start.11 = (bf16[512,1024]{1,0:T(8,128)(2,1)}, bf16[512,1024]{1,0:T(8,128)(2,1)}, u32[]{:S(2)}, u32[]{:S(2)}) collective-permute-start(bf16[512,1024]{1,0:T(8,128)(2,1)} %param.10), channel_id=1, source_target_pairs={{0,1},{1,2},{2,3},{3,0},{4,5},{5,6},{6,7},{7,4},{8,9},{9,10},{10,1... | collective-permute-start | bytes 3145736 | tf_op jit(solution)/shard_map/ppermute | solution.py:51
  54.5 58.7 %collective-permute-start.12 = (bf16[512,1024]{1,0:T(8,128)(2,1)}, bf16[512,1024]{1,0:T(8,128)(2,1)}, u32[]{:S(2)}, u32[]{:S(2)}) collective-permute-start(bf16[512,1024]{1,0:T(8,128)(2,1)} %param.10), channel_id=1, source_target_pairs={{0,2},{1,3},{2,0},{3,1},{4,6},{5,7},{6,4},{7,5},{8,10},{9,11},{10,... | collective-permute-start | bytes 3145736 | tf_op jit(solution)/shard_map/ppermute | solution.py:51
  57.8 55.1 %all-to-all-start = ((bf16[8,2,16,1024]{3,2,1,0:T(8,128)(2,1)}), bf16[8,2,16,1024]{3,2,1,0:T(8,128)(2,1)S(1)}, u32[]{:S(2)}, u32[]{:S(2)}) async-start(bf16[8,2,16,1024]{3,2,1,0:T(8,128)(2,1)} %bitcast.2), calls=%async_computation | async-start | bytes 1048576 | tf_op jit(solution)/shard_map/all_to_all | solution.py:59
  63.6 53.5 %collective-permute-start.13 = (bf16[512,1024]{1,0:T(8,128)(2,1)}, bf16[512,1024]{1,0:T(8,128)(2,1)}, u32[]{:S(2)}, u32[]{:S(2)}) collective-permute-start(bf16[512,1024]{1,0:T(8,128)(2,1)} %param.10), channel_id=1, source_target_pairs={{0,3},{1,0},{2,1},{3,2},{4,7},{5,4},{6,5},{7,6},{8,11},{9,8},{10,9... | collective-permute-start | bytes 3145736 | tf_op jit(solution)/shard_map/ppermute | solution.py:51
  112.9 13.3 %collective-permute-start = (bf16[256,1024]{1,0:T(8,128)(2,1)S(1)}, bf16[256,1024]{1,0:T(8,128)(2,1)S(1)}, u32[]{:S(2)}, u32[]{:S(2)}) collective-permute-start(bf16[256,1024]{1,0:T(8,128)(2,1)S(1)} %bitcast.129), channel_id=1, source_target_pairs={{0,1},{1,2},{2,3},{3,0},{4,5},{5,6},{6,7},{7,4},{8,9},{9,10},{10,1... | collective-permute-start | bytes 1572872 | tf_op jit(solution)/shard_map/ppermute | solution.py:51
  113.2 14.9 %collective-permute-start.1 = (bf16[256,1024]{1,0:T(8,128)(2,1)S(1)}, bf16[256,1024]{1,0:T(8,128)(2,1)S(1)}, u32[]{:S(2)}, u32[]{:S(2)}) collective-permute-start(bf16[256,1024]{1,0:T(8,128)(2,1)S(1)} %bitcast.131), channel_id=1, source_target_pairs={{0,2},{1,3},{2,0},{3,1},{4,6},{5,7},{6,4},{7,5},{8,10},{9,11},{10,... | collective-permute-start | bytes 1572872 | tf_op jit(solution)/shard_map/ppermute | solution.py:51
  117.1 20.3 %collective-permute-start.2 = (bf16[256,1024]{1,0:T(8,128)(2,1)S(1)}, bf16[256,1024]{1,0:T(8,128)(2,1)S(1)}, u32[]{:S(2)}, u32[]{:S(2)}) collective-permute-start(bf16[256,1024]{1,0:T(8,128)(2,1)S(1)} %bitcast.132), channel_id=1, source_target_pairs={{0,3},{1,0},{2,1},{3,2},{4,7},{5,4},{6,5},{7,6},{8,11},{9,8},{10,9... | collective-permute-start | bytes 1572872 | tf_op jit(solution)/shard_map/ppermute | solution.py:51
  120.9 46.8 %collective-permute-start.7 = (bf16[512,2048]{1,0:T(8,128)(2,1)}, bf16[512,2048]{1,0:T(8,128)(2,1)S(1)}, u32[]{:S(2)}, u32[]{:S(2)}) collective-permute-start(bf16[512,2048]{1,0:T(8,128)(2,1)} %collective-permute-done.5), channel_id=1, source_target_pairs={{0,8},{8,16},{16,24},{24,28},{28,20},{20,12},{12,4},{4,0},{1,9},{9... | collective-permute-start | bytes 6291464 | tf_op jit(solution)/shard_map/ppermute | solution.py:71
  120.9 47.3 %collective-permute-start.8 = (bf16[512,2048]{1,0:T(8,128)(2,1)}, bf16[512,2048]{1,0:T(8,128)(2,1)S(1)}, u32[]{:S(2)}, u32[]{:S(2)}) collective-permute-start(bf16[512,2048]{1,0:T(8,128)(2,1)} %collective-permute-done.6), channel_id=1, source_target_pairs={{0,4},{8,0},{16,8},{24,16},{28,24},{20,28},{12,20},{4,12},{1,5},{9... | collective-permute-start | bytes 6291464 | tf_op jit(solution)/shard_map/ppermute | solution.py:72
  137.7 3.9 %copy-start.12 = (bf16[256,4096]{1,0:T(8,128)(2,1)}, bf16[256,4096]{1,0:T(8,128)(2,1)S(1)}, u32[]{:S(2)}) copy-start(bf16[256,4096]{1,0:T(8,128)(2,1)S(1)} %dynamic-slice_dynamic-update-slice_fusion.7) | copy-start | bytes 6291460
  167.8 23.3 %collective-permute-start.10 = (bf16[256,2048]{1,0:T(8,128)(2,1)S(1)}, bf16[256,2048]{1,0:T(8,128)(2,1)S(1)}, u32[]{:S(2)}, u32[]{:S(2)}) collective-permute-start(bf16[256,2048]{1,0:T(8,128)(2,1)S(1)} %slice.27), channel_id=1, source_target_pairs={{0,8},{8,16},{16,24},{24,28},{28,20},{20,12},{12,4},{4,0},{1,9},{9... | collective-permute-start | bytes 3145736 | tf_op jit(solution)/shard_map/ppermute | solution.py:77
  168.2 23.3 %collective-permute-start.9 = (bf16[256,2048]{1,0:T(8,128)(2,1)S(1)}, bf16[256,2048]{1,0:T(8,128)(2,1)S(1)}, u32[]{:S(2)}, u32[]{:S(2)}) collective-permute-start(bf16[256,2048]{1,0:T(8,128)(2,1)S(1)} %slice.26), channel_id=1, source_target_pairs={{0,4},{8,0},{16,8},{24,16},{28,24},{20,28},{12,20},{4,12},{1,5},{9... | collective-permute-start | bytes 3145736 | tf_op jit(solution)/shard_map/ppermute | solution.py:78
  178.0 14.5 %copy-start.8 = (bf16[512,1024]{1,0:T(8,128)(2,1)S(1)}, bf16[512,1024]{1,0:T(8,128)(2,1)}, u32[]{:S(2)}) copy-start(bf16[512,1024]{1,0:T(8,128)(2,1)} %param.12) | copy-start | bytes 3145732
  192.5 28.9 %collective-permute-start.15 = (bf16[512,1024]{1,0:T(8,128)(2,1)S(1)}, bf16[512,1024]{1,0:T(8,128)(2,1)}, u32[]{:S(2)}, u32[]{:S(2)}) collective-permute-start(bf16[512,1024]{1,0:T(8,128)(2,1)S(1)} %copy-done.8), channel_id=1, source_target_pairs={{0,4},{8,0},{16,8},{24,16},{28,24},{20,28},{12,20},{4,12},{1,5},{9... | collective-permute-start | bytes 3145736 | tf_op jit(solution)/shard_map/ppermute | solution.py:108
  194.5 23.2 %collective-permute-start.14 = (bf16[512,1024]{1,0:T(8,128)(2,1)S(1)}, bf16[512,1024]{1,0:T(8,128)(2,1)}, u32[]{:S(2)}, u32[]{:S(2)}) collective-permute-start(bf16[512,1024]{1,0:T(8,128)(2,1)S(1)} %copy-done.8), channel_id=1, source_target_pairs={{0,8},{8,16},{16,24},{24,28},{28,20},{20,12},{12,4},{4,0},{1,9},{9... | collective-permute-start | bytes 3145736 | tf_op jit(solution)/shard_map/ppermute | solution.py:107
  217.7 23.3 %collective-permute-start.16 = (bf16[512,1024]{1,0:T(8,128)(2,1)}, bf16[512,1024]{1,0:T(8,128)(2,1)}, u32[]{:S(2)}, u32[]{:S(2)}) collective-permute-start(bf16[512,1024]{1,0:T(8,128)(2,1)} %collective-permute-done.14), channel_id=1, source_target_pairs={{0,8},{8,16},{16,24},{24,28},{28,20},{20,12},{12,4},{4,0},{1,9},{9... | collective-permute-start | bytes 3145736 | tf_op jit(solution)/shard_map/ppermute | solution.py:107
  221.4 23.7 %collective-permute-start.17 = (bf16[512,1024]{1,0:T(8,128)(2,1)}, bf16[512,1024]{1,0:T(8,128)(2,1)}, u32[]{:S(2)}, u32[]{:S(2)}) collective-permute-start(bf16[512,1024]{1,0:T(8,128)(2,1)} %collective-permute-done.15), channel_id=1, source_target_pairs={{0,4},{8,0},{16,8},{24,16},{28,24},{20,28},{12,20},{4,12},{1,5},{9... | collective-permute-start | bytes 3145736 | tf_op jit(solution)/shard_map/ppermute | solution.py:108
  241.0 21.5 %collective-permute-start.18 = (bf16[512,1024]{1,0:T(8,128)(2,1)}, bf16[512,1024]{1,0:T(8,128)(2,1)}, u32[]{:S(2)}, u32[]{:S(2)}) collective-permute-start(bf16[512,1024]{1,0:T(8,128)(2,1)} %collective-permute-done.16), channel_id=1, source_target_pairs={{0,8},{8,16},{16,24},{24,28},{28,20},{20,12},{12,4},{4,0},{1,9},{9... | collective-permute-start | bytes 3145736 | tf_op jit(solution)/shard_map/ppermute | solution.py:107
  245.1 24.5 %collective-permute-start.19 = (bf16[512,1024]{1,0:T(8,128)(2,1)}, bf16[512,1024]{1,0:T(8,128)(2,1)}, u32[]{:S(2)}, u32[]{:S(2)}) collective-permute-start(bf16[512,1024]{1,0:T(8,128)(2,1)} %collective-permute-done.17), channel_id=1, source_target_pairs={{0,4},{8,0},{16,8},{24,16},{28,24},{20,28},{12,20},{4,12},{1,5},{9... | collective-permute-start | bytes 3145736 | tf_op jit(solution)/shard_map/ppermute | solution.py:108
  264.3 11.8 %collective-permute-start.20 = (bf16[256,1024]{1,0:T(8,128)(2,1)}, bf16[256,1024]{1,0:T(8,128)(2,1)}, u32[]{:S(2)}, u32[]{:S(2)}) collective-permute-start(bf16[256,1024]{1,0:T(8,128)(2,1)} %slice.30), channel_id=1, source_target_pairs={{0,8},{8,16},{16,24},{24,28},{28,20},{20,12},{12,4},{4,0},{1,9},{9... | collective-permute-start | bytes 1572872 | tf_op jit(solution)/shard_map/ppermute | solution.py:113
  274.6 9.3 %collective-permute-start.21 = (bf16[256,1024]{1,0:T(8,128)(2,1)S(1)}, bf16[256,1024]{1,0:T(8,128)(2,1)}, u32[]{:S(2)}, u32[]{:S(2)}) collective-permute-start(bf16[256,1024]{1,0:T(8,128)(2,1)S(1)} %slice.31), channel_id=1, source_target_pairs={{0,4},{8,0},{16,8},{24,16},{28,24},{20,28},{12,20},{4,12},{1,5},{9... | collective-permute-start | bytes 1572872 | tf_op jit(solution)/shard_map/ppermute | solution.py:114
  280.6 6.0 %copy-start.5 = (f32[8,512,128]{1,2,0:T(8,128)S(1)}, f32[8,512,128]{1,2,0:T(8,128)}, u32[]{:S(2)}) copy-start(f32[8,512,128]{1,2,0:T(8,128)} %bitcast_add_fusion.1) | copy-start | bytes 6291460
  (10 other events, 22.7 us)

commit v15 on v13

--- a/solution.py
+++ b/solution.py
@@ -78,7 +78,7 @@
             got.append((lax.ppermute(bwd[split:], "crop", bwd_perm), src, split, wrows - split))
         return got
 
-    kv_got = ring_pieces(jnp.concatenate([key_weight, value_weight], axis=1))
+    kv_got = ring_pieces(lax.optimization_barrier(jnp.concatenate([key_weight, value_weight], axis=1)))
     q_piece, last_a, last_b = lax.optimization_barrier(
         (query_weight, kv_got[-1][0], kv_got[-2][0])
     )

time: 275 us -> 275 us (level)
  waiting for transfers between devices: 170 us -> 165 us
    ppermute x3, waiting for transfers between devices: 83.7 us -> 79.6 us  [ring_pieces(): fwd = lax.ppermute(fwd, 'crop', fwd_perm)]
    unnamed x42 -> x41, local copies, waits for them, and re-layouts: 15.2 us -> 16.4 us
  transfers between devices with their start and end apart: 23 -> 23, of which waited for: 14 -> 14; matrix products, arithmetic and copies ran while one was open for 18% -> 20% of each run, Pallas kernels for 0% -> 0%
where the time goes in v15:
time: 275 us; the launch traced here: 274 us
  waiting for transfers between devices  165 us (60%)
  local copies, waits for them, and re-layouts  36.3 us (13%)
  starting transfers between devices  33.6 us (12%)
  matrix products  21.6 us (8%)
  between operations  9.33 us (3%)
  other arithmetic  8.19 us (3%)
    ppermute x3, waiting for transfers between devices, ring_pieces(): fwd = lax.ppermute(fwd, 'crop', fwd_perm)  79.6 us
    ppermute x3, waiting for transfers between devices, body(): fwd = lax.ppermute(fwd, 'crop', fwd_perm)  27 us
    ppermute x3, waiting for transfers between devices, body(): bwd = lax.ppermute(bwd, 'crop', bwd_perm)  17.4 us
    unnamed x41, local copies, waits for them, and re-layouts  16.4 us
    dot_general x9, matrix products, q_part(): jnp.dot(cols, piece, preferred_element_type=jnp.float32)  15.2 us
    ppermute x6, waiting for transfers between devices, head_gather(): part = lax.ppermute(x, 'head', [(j, (j + k) % nhead) for j in range(nhead)])  13.2 us
    ppermute x1, waiting for transfers between devices, ring_pieces(): got.append((lax.ppermute(fwd[:split], 'crop', fwd_perm), src, 0, split))  11.8 us
    dynamic_update_slice x6, local copies, waits for them, and re-layouts, head_gather(): lax.dynamic_update_slice(full, part, (0, (hme - k) % nhead * x.shape[1]))  7.97 us
  transfers between devices with their start and end apart: 23, of which 14 were waited for; matrix products, arithmetic and copies ran while one was open for 20% of the time, Pallas kernels for 0%

profile of v15, /device:TPU:0, one launch (start us, length us, event | category | flops | bytes accessed | tf_op | source)
XLA Modules:
  0.0 273.7 jit_solution(10839787488424447341)
XLA Ops:
  0.0 1.9 pad_maximum_fusion
  2.0 3.1 %collective-permute-start.3 = (bf16[512,2048]{1,0:T(8,128)(2,1)S(1)}, bf16[512,2048]{1,0:T(8,128)(2,1)}, u32[]{:S(2)}, u32[]{:S(2)}) collective-permute-start(bf16[512,2048]{1,0:T(8,128)(2,1)S(1)} %pad_maximum_fusion), channel_id=1, source_target_pairs={{0,8},{8,16},{16,24},{24,28},{28,20},{20,12},{12,4},{4,0},{1,9},{9... | collective-permute-start | bytes 6291464 | tf_op jit(solution)/shard_map/ppermute | solution.py:71
  6.2 44.5 %collective-permute-done.3 = bf16[512,2048]{1,0:T(8,128)(2,1)} collective-permute-done((bf16[512,2048]{1,0:T(8,128)(2,1)S(1)}, bf16[512,2048]{1,0:T(8,128)(2,1)}, u32[]{:S(2)}, u32[]{:S(2)}) %collective-permute-start.3) | collective-permute-done | bytes 2097184 | tf_op jit(solution)/shard_map/ppermute | solution.py:71
  56.8 5.1 %all-to-all-start = ((bf16[8,2,16,1024]{3,2,1,0:T(8,128)(2,1)}), bf16[8,2,16,1024]{3,2,1,0:T(8,128)(2,1)S(1)}, u32[]{:S(2)}, u32[]{:S(2)}) async-start(bf16[8,2,16,1024]{3,2,1,0:T(8,128)(2,1)} %bitcast.2), calls=%async_computation | async-start | bytes 1048576 | tf_op jit(solution)/shard_map/all_to_all | solution.py:59
  73.7 3.2 %constant_dynamic-update-slice_fusion.8 = bf16[4096,2048]{1,0:T(8,128)(2,1)} fusion(bf16[512,2048]{1,0:T(8,128)(2,1)} %copy-done.2), kind=kLoop, calls=%fused_computation.57 | loop fusion | bytes 4194304
  76.9 23.3 %collective-permute-done.5 = bf16[512,2048]{1,0:T(8,128)(2,1)} collective-permute-done((bf16[512,2048]{1,0:T(8,128)(2,1)}, bf16[512,2048]{1,0:T(8,128)(2,1)}, u32[]{:S(2)}, u32[]{:S(2)}) %collective-permute-start.5) | collective-permute-done | bytes 2097184 | tf_op jit(solution)/shard_map/ppermute | solution.py:71
  100.2 2.7 collective-permute-start.7
  102.9 2.5 broadcast_in_dim.35
  105.3 2.4 constant_dynamic-update-slice_fusion.12
  107.7 5.9 %all-to-all-done = bf16[8,2,16,1024]{3,2,1,0:T(8,128)(2,1)S(1)} async-done(((bf16[8,2,16,1024]{3,2,1,0:T(8,128)(2,1)}), bf16[8,2,16,1024]{3,2,1,0:T(8,128)(2,1)S(1)}, u32[]{:S(2)}, u32[]{:S(2)}) %all-to-all-start) | async-done | bytes 524320 | tf_op jit(solution)/shard_map/all_to_all | solution.py:59
  115.4 2.5 constant_dynamic-update-slice_fusion.11
  119.3 3.0 %constant_dynamic-update-slice_fusion.10 = bf16[512,4096]{1,0:T(8,128)(2,1)} fusion(bf16[512,4096]{1,0:T(8,128)(2,1)} %constant_dynamic-update-slice_fusion.11, bf16[512,1024]{1,0:T(8,128)(2,1)} %collective-permute-done.12, s32[]{:T(128)S(6)} %select_n.165), kind=kLoop, calls=%fused_computation.69 | loop fusion | bytes 2097156 | tf_op jit(solution)/shard_map/dynamic_update_slice | solution.py:52
  122.4 2.3 constant_dynamic-update-slice_fusion.9
  124.7 2.2 collective-permute-done
  128.8 9.3 %collective-permute-done.2 = bf16[256,1024]{1,0:T(8,128)(2,1)S(1)} collective-permute-done((bf16[256,1024]{1,0:T(8,128)(2,1)S(1)}, bf16[256,1024]{1,0:T(8,128)(2,1)S(1)}, u32[]{:S(2)}, u32[]{:S(2)}) %collective-permute-start.2) | collective-permute-done | bytes 524320 | tf_op jit(solution)/shard_map/ppermute | solution.py:51
  138.4 11.8 %collective-permute-done.7 = bf16[512,2048]{1,0:T(8,128)(2,1)} collective-permute-done((bf16[512,2048]{1,0:T(8,128)(2,1)}, bf16[512,2048]{1,0:T(8,128)(2,1)}, u32[]{:S(2)}, u32[]{:S(2)}) %collective-permute-start.7) | collective-permute-done | bytes 2097184 | tf_op jit(solution)/shard_map/ppermute | solution.py:71
  151.5 4.4 %collective-permute-start.10 = (bf16[256,2048]{1,0:T(8,128)(2,1)S(1)}, bf16[256,2048]{1,0:T(8,128)(2,1)S(1)}, u32[]{:S(2)}, u32[]{:S(2)}) collective-permute-start(bf16[256,2048]{1,0:T(8,128)(2,1)S(1)} %slice.27), channel_id=1, source_target_pairs={{0,8},{8,16},{16,24},{24,28},{28,20},{20,12},{12,4},{4,0},{1,9},{9... | collective-permute-start | bytes 3145736 | tf_op jit(solution)/shard_map/ppermute | solution.py:77
  159.2 1.8 constant_dynamic-update-slice_fusion.6
  162.9 1.9 constant_dynamic-update-slice_fusion.4
  164.8 11.8 %collective-permute-done.10 = bf16[256,2048]{1,0:T(8,128)(2,1)S(1)} collective-permute-done((bf16[256,2048]{1,0:T(8,128)(2,1)S(1)}, bf16[256,2048]{1,0:T(8,128)(2,1)S(1)}, u32[]{:S(2)}, u32[]{:S(2)}) %collective-permute-start.10) | collective-permute-done | bytes 1048608 | tf_op jit(solution)/shard_map/ppermute | solution.py:77
  176.6 4.5 %collective-permute-done.9 = bf16[256,2048]{1,0:T(8,128)(2,1)S(1)} collective-permute-done((bf16[256,2048]{1,0:T(8,128)(2,1)S(1)}, bf16[256,2048]{1,0:T(8,128)(2,1)S(1)}, u32[]{:S(2)}, u32[]{:S(2)}) %collective-permute-start.9) | collective-permute-done | bytes 1048608 | tf_op jit(solution)/shard_map/ppermute | solution.py:78
  181.1 2.0 collective-permute-start.14
  187.0 17.4 %collective-permute-done.15 = bf16[512,1024]{1,0:T(8,128)(2,1)S(1)} collective-permute-done((bf16[512,1024]{1,0:T(8,128)(2,1)S(1)}, bf16[512,1024]{1,0:T(8,128)(2,1)S(1)}, u32[]{:S(2)}, u32[]{:S(2)}) %collective-permute-start.15) | collective-permute-done | bytes 1048608 | tf_op jit(solution)/shard_map/ppermute | solution.py:105
  204.4 2.0 collective-permute-start.16
  206.5 4.6 %convolution_convert_fusion = bf16[256,2048]{1,0:T(8,128)(2,1)S(1)} fusion(bf16[256,4096]{1,0:T(8,128)(2,1)S(1)} %dynamic-slice_dynamic-update-slice_fusion.7, bf16[4096,2048]{1,0:T(8,128)(2,1)S(1)} %constant_dynamic-update-slice_fusion), kind=kOutput, calls=%fused_computation.6 | convolution fusion | flops 4295491584 | bytes 19922944 | tf_op jit(solution)/shard_map/dot_general | solution.py:93
  213.2 14.6 %collective-permute-done.16 = bf16[512,1024]{1,0:T(8,128)(2,1)S(1)} collective-permute-done((bf16[512,1024]{1,0:T(8,128)(2,1)S(1)}, bf16[512,1024]{1,0:T(8,128)(2,1)S(1)}, u32[]{:S(2)}, u32[]{:S(2)}) %collective-permute-start.16) | collective-permute-done | bytes 1048608 | tf_op jit(solution)/shard_map/ppermute | solution.py:104
  227.8 2.0 collective-permute-start.18
  238.6 12.4 %collective-permute-done.18 = bf16[512,1024]{1,0:T(8,128)(2,1)S(1)} collective-permute-done((bf16[512,1024]{1,0:T(8,128)(2,1)S(1)}, bf16[512,1024]{1,0:T(8,128)(2,1)S(1)}, u32[]{:S(2)}, u32[]{:S(2)}) %collective-permute-start.18) | collective-permute-done | bytes 1048608 | tf_op jit(solution)/shard_map/ppermute | solution.py:104
  251.0 2.1 collective-permute-start.20
  257.2 3.1 %collective-permute-done.20 = bf16[256,1024]{1,0:T(8,128)(2,1)S(1)} collective-permute-done((bf16[256,1024]{1,0:T(8,128)(2,1)S(1)}, bf16[256,1024]{1,0:T(8,128)(2,1)S(1)}, u32[]{:S(2)}, u32[]{:S(2)}) %collective-permute-start.20) | collective-permute-done | bytes 524320 | tf_op jit(solution)/shard_map/ppermute | solution.py:110
  262.1 2.1 collective-permute-done.21
  267.2 3.5 %fusion.42 = (f32[16,8,32]{2,0,1:T(8,128)S(1)}, f32[16,8,32,256]{3,2,0,1:T(8,128)S(1)}) fusion(f32[8,256,16,32]{1,3,2,0:T(8,128)S(1)} %bitcast.73, pred[16,256]{1,0:T(8,128)(4,1)S(1)} %broadcast_in_dim.33), kind=kOutput, calls=%fused_computation.82 | output fusion | flops 6291711 | bytes 8409088 | tf_op jit(solution)/shard_map/sub | solution.py:128
  (105 shorter events, 48.4 us)
Async XLA Ops:
  0.0 55.4 %copy-start = (bf16[1024,1024]{1,0:T(8,128)(2,1)S(1)}, bf16[1024,1024]{1,0:T(8,128)(2,1)}, u32[]{:S(2)}) copy-start(bf16[1024,1024]{1,0:T(8,128)(2,1)} %param.11) | copy-start | bytes 6291460
  0.0 55.2 %copy-start.7 = (s32[1,8,2]{1,2,0:T(2,128)S(1)}, s32[1,8,2]{1,2,0:T(2,128)}, u32[]{:S(2)}) copy-start(s32[1,8,2]{1,2,0:T(2,128)} %param.15) | copy-start | bytes 196
  1.9 3.1 %copy-start.2 = (bf16[512,2048]{1,0:T(8,128)(2,1)}, bf16[512,2048]{1,0:T(8,128)(2,1)S(1)}, u32[]{:S(2)}) copy-start(bf16[512,2048]{1,0:T(8,128)(2,1)S(1)} %pad_maximum_fusion) | copy-start | bytes 6291460
  1.9 61.1 %copy-start.9 = (s32[8]{0:T(128)S(1)}, s32[8]{0:T(128)}, u32[]{:S(2)}) copy-start(s32[8]{0:T(128)} %constant.150.clone) | copy-start | bytes 100
  1.9 66.1 %copy-start.5 = (s32[8]{0:T(128)S(1)}, s32[8]{0:T(128)}, u32[]{:S(2)}) copy-start(s32[8]{0:T(128)} %constant.151.clone) | copy-start | bytes 100
  2.0 71.2 %copy-start.6 = (s32[16,8]{0,1:T(8,128)S(1)}, s32[16,8]{0,1:T(8,128)}, u32[]{:S(2)}) copy-start(s32[16,8]{0,1:T(8,128)} %param.16) | copy-start | bytes 1540
  2.0 71.2 %copy-start.8 = (s32[16]{0:T(128)S(1)}, s32[16]{0:T(128)}, u32[]{:S(2)}) copy-start(s32[16]{0:T(128)} %param.17) | copy-start | bytes 196
  2.0 48.8 %collective-permute-start.3 = (bf16[512,2048]{1,0:T(8,128)(2,1)S(1)}, bf16[512,2048]{1,0:T(8,128)(2,1)}, u32[]{:S(2)}, u32[]{:S(2)}) collective-permute-start(bf16[512,2048]{1,0:T(8,128)(2,1)S(1)} %pad_maximum_fusion), channel_id=1, source_target_pairs={{0,8},{8,16},{16,24},{24,28},{28,20},{20,12},{12,4},{4,0},{1,9},{9... | collective-permute-start | bytes 6291464 | tf_op jit(solution)/shard_map/ppermute | solution.py:71
  5.1 47.5 %collective-permute-start.4 = (bf16[512,2048]{1,0:T(8,128)(2,1)S(1)}, bf16[512,2048]{1,0:T(8,128)(2,1)}, u32[]{:S(2)}, u32[]{:S(2)}) collective-permute-start(bf16[512,2048]{1,0:T(8,128)(2,1)S(1)} %pad_maximum_fusion), channel_id=1, source_target_pairs={{0,4},{8,0},{16,8},{24,16},{28,24},{20,28},{12,20},{4,12},{1,5},{9... | collective-permute-start | bytes 6291464 | tf_op jit(solution)/shard_map/ppermute | solution.py:72
  50.7 49.5 %collective-permute-start.5 = (bf16[512,2048]{1,0:T(8,128)(2,1)}, bf16[512,2048]{1,0:T(8,128)(2,1)}, u32[]{:S(2)}, u32[]{:S(2)}) collective-permute-start(bf16[512,2048]{1,0:T(8,128)(2,1)} %collective-permute-done.3), channel_id=1, source_target_pairs={{0,8},{8,16},{16,24},{24,28},{28,20},{20,12},{12,4},{4,0},{1,9},{9... | collective-permute-start | bytes 6291464 | tf_op jit(solution)/shard_map/ppermute | solution.py:71
  52.5 50.3 %collective-permute-start.6 = (bf16[512,2048]{1,0:T(8,128)(2,1)}, bf16[512,2048]{1,0:T(8,128)(2,1)}, u32[]{:S(2)}, u32[]{:S(2)}) collective-permute-start(bf16[512,2048]{1,0:T(8,128)(2,1)} %collective-permute-done.4), channel_id=1, source_target_pairs={{0,4},{8,0},{16,8},{24,16},{28,24},{20,28},{12,20},{4,12},{1,5},{9... | collective-permute-start | bytes 6291464 | tf_op jit(solution)/shard_map/ppermute | solution.py:72
  53.7 59.9 %collective-permute-start.11 = (bf16[512,1024]{1,0:T(8,128)(2,1)}, bf16[512,1024]{1,0:T(8,128)(2,1)}, u32[]{:S(2)}, u32[]{:S(2)}) collective-permute-start(bf16[512,1024]{1,0:T(8,128)(2,1)} %param.10), channel_id=1, source_target_pairs={{0,1},{1,2},{2,3},{3,0},{4,5},{5,6},{6,7},{7,4},{8,9},{9,10},{10,1... | collective-permute-start | bytes 3145736 | tf_op jit(solution)/shard_map/ppermute | solution.py:51
  53.7 60.2 %collective-permute-start.12 = (bf16[512,1024]{1,0:T(8,128)(2,1)}, bf16[512,1024]{1,0:T(8,128)(2,1)}, u32[]{:S(2)}, u32[]{:S(2)}) collective-permute-start(bf16[512,1024]{1,0:T(8,128)(2,1)} %param.10), channel_id=1, source_target_pairs={{0,2},{1,3},{2,0},{3,1},{4,6},{5,7},{6,4},{7,5},{8,10},{9,11},{10,... | collective-permute-start | bytes 3145736 | tf_op jit(solution)/shard_map/ppermute | solution.py:51
  56.8 56.8 %all-to-all-start = ((bf16[8,2,16,1024]{3,2,1,0:T(8,128)(2,1)}), bf16[8,2,16,1024]{3,2,1,0:T(8,128)(2,1)S(1)}, u32[]{:S(2)}, u32[]{:S(2)}) async-start(bf16[8,2,16,1024]{3,2,1,0:T(8,128)(2,1)} %bitcast.2), calls=%async_computation | async-start | bytes 1048576 | tf_op jit(solution)/shard_map/all_to_all | solution.py:59
  61.9 56.0 %collective-permute-start.13 = (bf16[512,1024]{1,0:T(8,128)(2,1)}, bf16[512,1024]{1,0:T(8,128)(2,1)}, u32[]{:S(2)}, u32[]{:S(2)}) collective-permute-start(bf16[512,1024]{1,0:T(8,128)(2,1)} %param.10), channel_id=1, source_target_pairs={{0,3},{1,0},{2,1},{3,2},{4,7},{5,4},{6,5},{7,6},{8,11},{9,8},{10,9... | collective-permute-start | bytes 3145736 | tf_op jit(solution)/shard_map/ppermute | solution.py:51
  100.2 50.0 %collective-permute-start.7 = (bf16[512,2048]{1,0:T(8,128)(2,1)}, bf16[512,2048]{1,0:T(8,128)(2,1)}, u32[]{:S(2)}, u32[]{:S(2)}) collective-permute-start(bf16[512,2048]{1,0:T(8,128)(2,1)} %collective-permute-done.5), channel_id=1, source_target_pairs={{0,8},{8,16},{16,24},{24,28},{28,20},{20,12},{12,4},{4,0},{1,9},{9... | collective-permute-start | bytes 6291464 | tf_op jit(solution)/shard_map/ppermute | solution.py:71
  102.9 53.1 %collective-permute-start.8 = (bf16[512,2048]{1,0:T(8,128)(2,1)}, bf16[512,2048]{1,0:T(8,128)(2,1)}, u32[]{:S(2)}, u32[]{:S(2)}) collective-permute-start(bf16[512,2048]{1,0:T(8,128)(2,1)} %collective-permute-done.6), channel_id=1, source_target_pairs={{0,4},{8,0},{16,8},{24,16},{28,24},{20,28},{12,20},{4,12},{1,5},{9... | collective-permute-start | bytes 6291464 | tf_op jit(solution)/shard_map/ppermute | solution.py:72
  113.6 13.3 %collective-permute-start = (bf16[256,1024]{1,0:T(8,128)(2,1)S(1)}, bf16[256,1024]{1,0:T(8,128)(2,1)S(1)}, u32[]{:S(2)}, u32[]{:S(2)}) collective-permute-start(bf16[256,1024]{1,0:T(8,128)(2,1)S(1)} %bitcast.77), channel_id=1, source_target_pairs={{0,1},{1,2},{2,3},{3,0},{4,5},{5,6},{6,7},{7,4},{8,9},{9,10},{10,1... | collective-permute-start | bytes 1572872 | tf_op jit(solution)/shard_map/ppermute | solution.py:51
  113.9 14.8 %collective-permute-start.1 = (bf16[256,1024]{1,0:T(8,128)(2,1)S(1)}, bf16[256,1024]{1,0:T(8,128)(2,1)S(1)}, u32[]{:S(2)}, u32[]{:S(2)}) collective-permute-start(bf16[256,1024]{1,0:T(8,128)(2,1)S(1)} %bitcast.79), channel_id=1, source_target_pairs={{0,2},{1,3},{2,0},{3,1},{4,6},{5,7},{6,4},{7,5},{8,10},{9,11},{10,... | collective-permute-start | bytes 1572872 | tf_op jit(solution)/shard_map/ppermute | solution.py:51
  115.4 41.9 %copy-start.4 = (bf16[4096,2048]{1,0:T(8,128)(2,1)S(1)}, bf16[4096,2048]{1,0:T(8,128)(2,1)}, u32[]{:S(2)}) copy-start(bf16[4096,2048]{1,0:T(8,128)(2,1)} %constant_dynamic-update-slice_fusion.8) | copy-start | bytes 50331652
  117.9 20.1 %collective-permute-start.2 = (bf16[256,1024]{1,0:T(8,128)(2,1)S(1)}, bf16[256,1024]{1,0:T(8,128)(2,1)S(1)}, u32[]{:S(2)}, u32[]{:S(2)}) collective-permute-start(bf16[256,1024]{1,0:T(8,128)(2,1)S(1)} %bitcast.80), channel_id=1, source_target_pairs={{0,3},{1,0},{2,1},{3,2},{4,7},{5,4},{6,5},{7,6},{8,11},{9,8},{10,9... | collective-permute-start | bytes 1572872 | tf_op jit(solution)/shard_map/ppermute | solution.py:51
  151.5 25.1 %collective-permute-start.10 = (bf16[256,2048]{1,0:T(8,128)(2,1)S(1)}, bf16[256,2048]{1,0:T(8,128)(2,1)S(1)}, u32[]{:S(2)}, u32[]{:S(2)}) collective-permute-start(bf16[256,2048]{1,0:T(8,128)(2,1)S(1)} %slice.27), channel_id=1, source_target_pairs={{0,8},{8,16},{16,24},{24,28},{28,20},{20,12},{12,4},{4,0},{1,9},{9... | collective-permute-start | bytes 3145736 | tf_op jit(solution)/shard_map/ppermute | solution.py:77
  157.3 23.8 %collective-permute-start.9 = (bf16[256,2048]{1,0:T(8,128)(2,1)S(1)}, bf16[256,2048]{1,0:T(8,128)(2,1)S(1)}, u32[]{:S(2)}, u32[]{:S(2)}) collective-permute-start(bf16[256,2048]{1,0:T(8,128)(2,1)S(1)} %slice.26), channel_id=1, source_target_pairs={{0,4},{8,0},{16,8},{24,16},{28,24},{20,28},{12,20},{4,12},{1,5},{9... | collective-permute-start | bytes 3145736 | tf_op jit(solution)/shard_map/ppermute | solution.py:78
  162.9 18.2 %copy-start.3 = (bf16[512,1024]{1,0:T(8,128)(2,1)S(1)}, bf16[512,1024]{1,0:T(8,128)(2,1)}, u32[]{:S(2)}) copy-start(bf16[512,1024]{1,0:T(8,128)(2,1)} %param.12) | copy-start | bytes 3145732
  181.1 23.3 %collective-permute-start.15 = (bf16[512,1024]{1,0:T(8,128)(2,1)S(1)}, bf16[512,1024]{1,0:T(8,128)(2,1)S(1)}, u32[]{:S(2)}, u32[]{:S(2)}) collective-permute-start(bf16[512,1024]{1,0:T(8,128)(2,1)S(1)} %copy-done.3), channel_id=1, source_target_pairs={{0,4},{8,0},{16,8},{24,16},{28,24},{20,28},{12,20},{4,12},{1,5},{9... | collective-permute-start | bytes 3145736 | tf_op jit(solution)/shard_map/ppermute | solution.py:105
  181.1 23.3 %collective-permute-start.14 = (bf16[512,1024]{1,0:T(8,128)(2,1)S(1)}, bf16[512,1024]{1,0:T(8,128)(2,1)S(1)}, u32[]{:S(2)}, u32[]{:S(2)}) collective-permute-start(bf16[512,1024]{1,0:T(8,128)(2,1)S(1)} %copy-done.3), channel_id=1, source_target_pairs={{0,8},{8,16},{16,24},{24,28},{28,20},{20,12},{12,4},{4,0},{1,9},{9... | collective-permute-start | bytes 3145736 | tf_op jit(solution)/shard_map/ppermute | solution.py:104
  204.4 27.1 %collective-permute-start.17 = (bf16[512,1024]{1,0:T(8,128)(2,1)S(1)}, bf16[512,1024]{1,0:T(8,128)(2,1)S(1)}, u32[]{:S(2)}, u32[]{:S(2)}) collective-permute-start(bf16[512,1024]{1,0:T(8,128)(2,1)S(1)} %collective-permute-done.15), channel_id=1, source_target_pairs={{0,4},{8,0},{16,8},{24,16},{28,24},{20,28},{12,20},{4,12},{1,5},{9... | collective-permute-start | bytes 3145736 | tf_op jit(solution)/shard_map/ppermute | solution.py:105
  204.4 23.3 %collective-permute-start.16 = (bf16[512,1024]{1,0:T(8,128)(2,1)S(1)}, bf16[512,1024]{1,0:T(8,128)(2,1)S(1)}, u32[]{:S(2)}, u32[]{:S(2)}) collective-permute-start(bf16[512,1024]{1,0:T(8,128)(2,1)S(1)} %collective-permute-done.14), channel_id=1, source_target_pairs={{0,8},{8,16},{16,24},{24,28},{28,20},{20,12},{12,4},{4,0},{1,9},{9... | collective-permute-start | bytes 3145736 | tf_op jit(solution)/shard_map/ppermute | solution.py:104
  227.8 23.2 %collective-permute-start.18 = (bf16[512,1024]{1,0:T(8,128)(2,1)S(1)}, bf16[512,1024]{1,0:T(8,128)(2,1)S(1)}, u32[]{:S(2)}, u32[]{:S(2)}) collective-permute-start(bf16[512,1024]{1,0:T(8,128)(2,1)S(1)} %collective-permute-done.16), channel_id=1, source_target_pairs={{0,8},{8,16},{16,24},{24,28},{28,20},{20,12},{12,4},{4,0},{1,9},{9... | collective-permute-start | bytes 3145736 | tf_op jit(solution)/shard_map/ppermute | solution.py:104
  231.6 23.3 %collective-permute-start.19 = (bf16[512,1024]{1,0:T(8,128)(2,1)S(1)}, bf16[512,1024]{1,0:T(8,128)(2,1)S(1)}, u32[]{:S(2)}, u32[]{:S(2)}) collective-permute-start(bf16[512,1024]{1,0:T(8,128)(2,1)S(1)} %collective-permute-done.17), channel_id=1, source_target_pairs={{0,4},{8,0},{16,8},{24,16},{28,24},{20,28},{12,20},{4,12},{1,5},{9... | collective-permute-start | bytes 3145736 | tf_op jit(solution)/shard_map/ppermute | solution.py:105
  251.0 9.2 %collective-permute-start.20 = (bf16[256,1024]{1,0:T(8,128)(2,1)S(1)}, bf16[256,1024]{1,0:T(8,128)(2,1)S(1)}, u32[]{:S(2)}, u32[]{:S(2)}) collective-permute-start(bf16[256,1024]{1,0:T(8,128)(2,1)S(1)} %slice.30), channel_id=1, source_target_pairs={{0,8},{8,16},{16,24},{24,28},{28,20},{20,12},{12,4},{4,0},{1,9},{9... | collective-permute-start | bytes 1572872 | tf_op jit(solution)/shard_map/ppermute | solution.py:110
  254.9 9.2 %collective-permute-start.21 = (bf16[256,1024]{1,0:T(8,128)(2,1)S(1)}, bf16[256,1024]{1,0:T(8,128)(2,1)S(1)}, u32[]{:S(2)}, u32[]{:S(2)}) collective-permute-start(bf16[256,1024]{1,0:T(8,128)(2,1)S(1)} %slice.31), channel_id=1, source_target_pairs={{0,4},{8,0},{16,8},{24,16},{28,24},{20,28},{12,20},{4,12},{1,5},{9... | collective-permute-start | bytes 1572872 | tf_op jit(solution)/shard_map/ppermute | solution.py:111
  (1 other events, 3.0 us)

commit v16 on v15

--- a/solution.py
+++ b/solution.py
@@ -78,20 +78,27 @@
             got.append((lax.ppermute(bwd[split:], "crop", bwd_perm), src, split, wrows - split))
         return got
 
-    kv_got = ring_pieces(lax.optimization_barrier(jnp.concatenate([key_weight, value_weight], axis=1)))
-    q_piece, last_a, last_b = lax.optimization_barrier(
-        (query_weight, kv_got[-1][0], kv_got[-2][0])
-    )
-    kv_got[-1] = (last_a,) + kv_got[-1][1:]
-    kv_got[-2] = (last_b,) + kv_got[-2][1:]
+    k_got = ring_pieces(key_weight)
+    v_piece, k_last, k_prev = lax.optimization_barrier((value_weight, k_got[-1][0], k_got[-2][0]))
+    k_got[-1] = (k_last,) + k_got[-1][1:]
+    k_got[-2] = (k_prev,) + k_got[-2][1:]
+    v_got = ring_pieces(v_piece)
+    q_piece, v_last, v_prev = lax.optimization_barrier((query_weight, v_got[-1][0], v_got[-2][0]))
+    v_got[-1] = (v_last,) + v_got[-1][1:]
+    v_got[-2] = (v_prev,) + v_got[-2][1:]
     tokens_in = head_gather(delivered)
-    kv_weight = jnp.concatenate([p for p, _, _, _ in kv_got], axis=0)
     tokens_perm = jnp.concatenate(
-        [lax.dynamic_slice_in_dim(tokens_in, src * wrows + lo, n, 1) for _, src, lo, n in kv_got],
+        [lax.dynamic_slice_in_dim(tokens_in, src * wrows + lo, n, 1) for _, src, lo, n in k_got],
         axis=1,
     )
-    kv = jnp.dot(tokens_perm, kv_weight, preferred_element_type=jnp.float32).astype(jnp.bfloat16)
-    incoming = kv.reshape(ncrop, CAP, CT, 2 * width)
+
+    def project(got):
+        weight = jnp.concatenate([p for p, _, _, _ in got], axis=0)
+        out = jnp.dot(tokens_perm, weight, preferred_element_type=jnp.float32)
+        return out.astype(jnp.bfloat16)
+
+    keys_all = project(k_got)
+    vals_all = project(v_got)
 
     def q_part(acc, piece, src, lo, n):
         cols = lax.dynamic_slice_in_dim(queries_in, src * wrows + lo, n, 1)
@@ -111,8 +118,8 @@
         acc = q_part(acc, lax.ppermute(bwd[split:], "crop", bwd_perm), src, split, wrows - split)
     query = acc.astype(jnp.bfloat16)
     nslots = ncrop * CAP
-    keys_all = incoming[..., :width].reshape(nslots * CT, heads_here, HD)
-    vals_all = incoming[..., width:].reshape(nslots * CT, heads_here, HD)
+    keys_all = keys_all.reshape(nslots * CT, heads_here, HD)
+    vals_all = vals_all.reshape(nslots * CT, heads_here, HD)
     query_row = query.reshape(rows_here, GR, heads_here, HD)
     in_use = (jnp.arange(NB, dtype=jnp.int32)[None, :] < region_len[:, None])[:, :, None]
     hits = region_slots[:, :, None] == jnp.arange(nslots, dtype=jnp.int32)[None, None, :]

time: 275 us -> 278 us (1.011)
  starting transfers between devices: 33.6 us -> 41.3 us
  waiting for transfers between devices: 165 us -> 160 us
    ppermute x3 -> x6, waiting for transfers between devices: 0.01 us -> 16.8 us  [ring_pieces(): bwd = lax.ppermute(bwd, 'crop', bwd_perm)]
    ppermute x1 -> x2, waiting for transfers between devices: 11.8 us -> 0.01 us  [ring_pieces(): got.append((lax.ppermute(fwd[:split], 'crop', fwd_perm), src, 0, split))]
    ppermute x3 -> x6, waiting for transfers between devices: 79.6 us -> 69.1 us  [ring_pieces(): fwd = lax.ppermute(fwd, 'crop', fwd_perm)]
    all_to_all x1, waiting for transfers between devices: 5.86 us -> 0.01 us  [body(): lax.all_to_all(chosen, 'crop', split_axis=0, concat_axis=0, tiled=True)]
    ppermute x3 -> x6, starting transfers between devices: 7.54 us -> 13.3 us  [ring_pieces(): fwd = lax.ppermute(fwd, 'crop', fwd_perm)]
    ppermute x1, waiting for transfers between devices: 3.12 us -> 6.51 us  [body(): lax.ppermute(fwd[:split], 'crop', fwd_perm)]
    ppermute x1 -> x2, waiting for transfers between devices: 4.51 us -> 7.21 us  [ring_pieces(): lax.ppermute(bwd[split:], 'crop', bwd_perm)]
    ppermute x1 -> x2, starting transfers between devices: 4.44 us -> 6.53 us  [ring_pieces(): got.append((lax.ppermute(fwd[:split], 'crop', fwd_perm), src, 0, split))]
  transfers between devices with their start and end apart: 23 -> 31, of which waited for: 14 -> 14; matrix products, arithmetic and copies ran while one was open for 20% -> 20% of each run, Pallas kernels for 0% -> 0%
where the time goes in v16:
time: 278 us; the launch traced here: 275 us
  waiting for transfers between devices  160 us (58%)
  starting transfers between devices  41.3 us (15%)
  local copies, waits for them, and re-layouts  35.6 us (13%)
  matrix products  21.5 us (8%)
  between operations  10.1 us (4%)
  other arithmetic  7.28 us (3%)
    ppermute x6, waiting for transfers between devices, ring_pieces(): fwd = lax.ppermute(fwd, 'crop', fwd_perm)  69.1 us
    ppermute x3, waiting for transfers between devices, body(): fwd = lax.ppermute(fwd, 'crop', fwd_perm)  28.4 us
    ppermute x3, waiting for transfers between devices, body(): bwd = lax.ppermute(bwd, 'crop', bwd_perm)  18 us
    ppermute x6, waiting for transfers between devices, ring_pieces(): bwd = lax.ppermute(bwd, 'crop', bwd_perm)  16.8 us
    unnamed x56, local copies, waits for them, and re-layouts  16.5 us
    dot_general x9, matrix products, q_part(): jnp.dot(cols, piece, preferred_element_type=jnp.float32)  15.1 us
    ppermute x6, starting transfers between devices, ring_pieces(): fwd = lax.ppermute(fwd, 'crop', fwd_perm)  13.3 us
    ppermute x6, waiting for transfers between devices, head_gather(): part = lax.ppermute(x, 'head', [(j, (j + k) % nhead) for j in range(nhead)])  11.2 us
  transfers between devices with their start and end apart: 31, of which 14 were waited for; matrix products, arithmetic and copies ran while one was open for 20% of the time, Pallas kernels for 0%

profile of v16, /device:TPU:0, one launch (start us, length us, event | category | flops | bytes accessed | tf_op | source)
XLA Modules:
  0.0 275.3 jit_solution(10305285360888035744)
XLA Ops:
  0.0 3.1 %collective-permute-start.7 = (bf16[512,1024]{1,0:T(8,128)(2,1)}, bf16[512,1024]{1,0:T(8,128)(2,1)S(1)}, u32[]{:S(2)}, u32[]{:S(2)}) collective-permute-start(bf16[512,1024]{1,0:T(8,128)(2,1)} %param.13), channel_id=1, source_target_pairs={{0,8},{8,16},{16,24},{24,28},{28,20},{20,12},{12,4},{4,0},{1,9},{9... | collective-permute-start | bytes 3145736 | tf_op jit(solution)/shard_map/ppermute | solution.py:71
  3.1 23.3 %collective-permute-done.7 = bf16[512,1024]{1,0:T(8,128)(2,1)S(1)} collective-permute-done((bf16[512,1024]{1,0:T(8,128)(2,1)}, bf16[512,1024]{1,0:T(8,128)(2,1)S(1)}, u32[]{:S(2)}, u32[]{:S(2)}) %collective-permute-start.7) | collective-permute-done | bytes 1048608 | tf_op jit(solution)/shard_map/ppermute | solution.py:71
  29.2 21.7 %collective-permute-done.8 = bf16[512,1024]{1,0:T(8,128)(2,1)} collective-permute-done((bf16[512,1024]{1,0:T(8,128)(2,1)S(1)}, bf16[512,1024]{1,0:T(8,128)(2,1)}, u32[]{:S(2)}, u32[]{:S(2)}) %collective-permute-start.8) | collective-permute-done | bytes 1048608 | tf_op jit(solution)/shard_map/ppermute | solution.py:71
  55.2 5.7 %all-to-all-start = ((bf16[8,2,16,1024]{3,2,1,0:T(8,128)(2,1)}), bf16[8,2,16,1024]{3,2,1,0:T(8,128)(2,1)S(1)}, u32[]{:S(2)}, u32[]{:S(2)}) async-start(bf16[8,2,16,1024]{3,2,1,0:T(8,128)(2,1)} %bitcast.82), calls=%async_computation | async-start | bytes 1048576 | tf_op jit(solution)/shard_map/all_to_all | solution.py:59
  63.9 13.6 %collective-permute-done.9 = bf16[512,1024]{1,0:T(8,128)(2,1)S(1)} collective-permute-done((bf16[512,1024]{1,0:T(8,128)(2,1)}, bf16[512,1024]{1,0:T(8,128)(2,1)S(1)}, u32[]{:S(2)}, u32[]{:S(2)}) %collective-permute-start.9) | collective-permute-done | bytes 1048608 | tf_op jit(solution)/shard_map/ppermute | solution.py:71
  78.3 4.2 %collective-permute-start.10 = (bf16[256,1024]{1,0:T(8,128)(2,1)}, bf16[256,1024]{1,0:T(8,128)(2,1)S(1)}, u32[]{:S(2)}, u32[]{:S(2)}) collective-permute-start(bf16[256,1024]{1,0:T(8,128)(2,1)} %slice.27), channel_id=1, source_target_pairs={{0,8},{8,16},{16,24},{24,28},{28,20},{20,12},{12,4},{4,0},{1,9},{9... | collective-permute-start | bytes 1572872 | tf_op jit(solution)/shard_map/ppermute | solution.py:77
  95.7 2.3 constant_dynamic-update-slice_fusion.17
  98.0 2.5 broadcast_in_dim.35
  101.7 2.9 %collective-permute-start.11 = (bf16[512,1024]{1,0:T(8,128)(2,1)}, bf16[512,1024]{1,0:T(8,128)(2,1)}, u32[]{:S(2)}, u32[]{:S(2)}) collective-permute-start(bf16[512,1024]{1,0:T(8,128)(2,1)} %param.14), channel_id=1, source_target_pairs={{0,8},{8,16},{16,24},{24,28},{28,20},{20,12},{12,4},{4,0},{1,9},{9... | collective-permute-start | bytes 3145736 | tf_op jit(solution)/shard_map/ppermute | solution.py:71
  104.8 2.3 constant_dynamic-update-slice_fusion.16
  109.6 2.3 constant_dynamic-update-slice_fusion.20
  113.3 2.3 constant_dynamic-update-slice_fusion.19
  115.6 2.5 constant_dynamic-update-slice_fusion.18
  119.7 3.4 %collective-permute-done.1 = bf16[256,1024]{1,0:T(8,128)(2,1)S(1)} collective-permute-done((bf16[256,1024]{1,0:T(8,128)(2,1)S(1)}, bf16[256,1024]{1,0:T(8,128)(2,1)S(1)}, u32[]{:S(2)}, u32[]{:S(2)}) %collective-permute-start.1) | collective-permute-done | bytes 524320 | tf_op jit(solution)/shard_map/ppermute | solution.py:51
  123.1 2.1 collective-permute-start.13
  125.2 6.3 %collective-permute-done.2 = bf16[256,1024]{1,0:T(8,128)(2,1)S(1)} collective-permute-done((bf16[256,1024]{1,0:T(8,128)(2,1)S(1)}, bf16[256,1024]{1,0:T(8,128)(2,1)S(1)}, u32[]{:S(2)}, u32[]{:S(2)}) %collective-permute-start.2) | collective-permute-done | bytes 524320 | tf_op jit(solution)/shard_map/ppermute | solution.py:51
  131.8 10.5 %collective-permute-done.13 = bf16[512,1024]{1,0:T(8,128)(2,1)S(1)} collective-permute-done((bf16[512,1024]{1,0:T(8,128)(2,1)}, bf16[512,1024]{1,0:T(8,128)(2,1)S(1)}, u32[]{:S(2)}, u32[]{:S(2)}) %collective-permute-start.13) | collective-permute-done | bytes 1048608 | tf_op jit(solution)/shard_map/ppermute | solution.py:71
  142.3 2.0 collective-permute-start.15
  150.9 16.8 %collective-permute-done.16 = bf16[512,1024]{1,0:T(8,128)(2,1)S(1)} collective-permute-done((bf16[512,1024]{1,0:T(8,128)(2,1)S(1)}, bf16[512,1024]{1,0:T(8,128)(2,1)S(1)}, u32[]{:S(2)}, u32[]{:S(2)}) %collective-permute-start.16) | collective-permute-done | bytes 1048608 | tf_op jit(solution)/shard_map/ppermute | solution.py:72
  167.9 2.4 collective-permute-start.18
  170.2 2.3 fusion.9
  172.6 7.2 %collective-permute-done.17 = bf16[256,1024]{1,0:T(8,128)(2,1)S(1)} collective-permute-done((bf16[256,1024]{1,0:T(8,128)(2,1)S(1)}, bf16[256,1024]{1,0:T(8,128)(2,1)S(1)}, u32[]{:S(2)}, u32[]{:S(2)}) %collective-permute-start.17) | collective-permute-done | bytes 524320 | tf_op jit(solution)/shard_map/ppermute | solution.py:78
  179.8 2.4 collective-permute-start.22
  185.1 18.0 %collective-permute-done.23 = bf16[512,1024]{1,0:T(8,128)(2,1)S(1)} collective-permute-done((bf16[512,1024]{1,0:T(8,128)(2,1)S(1)}, bf16[512,1024]{1,0:T(8,128)(2,1)S(1)}, u32[]{:S(2)}, u32[]{:S(2)}) %collective-permute-start.23) | collective-permute-done | bytes 1048608 | tf_op jit(solution)/shard_map/ppermute | solution.py:112
  203.1 2.3 collective-permute-start.24
  205.4 2.3 fusion.8
  209.6 16.1 %collective-permute-done.24 = bf16[512,1024]{1,0:T(8,128)(2,1)S(1)} collective-permute-done((bf16[512,1024]{1,0:T(8,128)(2,1)S(1)}, bf16[512,1024]{1,0:T(8,128)(2,1)S(1)}, u32[]{:S(2)}, u32[]{:S(2)}) %collective-permute-start.24) | collective-permute-done | bytes 1048608 | tf_op jit(solution)/shard_map/ppermute | solution.py:111
  236.7 12.3 %collective-permute-done.26 = bf16[512,1024]{1,0:T(8,128)(2,1)S(1)} collective-permute-done((bf16[512,1024]{1,0:T(8,128)(2,1)S(1)}, bf16[512,1024]{1,0:T(8,128)(2,1)S(1)}, u32[]{:S(2)}, u32[]{:S(2)}) %collective-permute-start.26) | collective-permute-done | bytes 1048608 | tf_op jit(solution)/shard_map/ppermute | solution.py:111
  249.1 2.1 collective-permute-start.28
  255.2 6.5 %collective-permute-done.28 = bf16[256,1024]{1,0:T(8,128)(2,1)S(1)} collective-permute-done((bf16[256,1024]{1,0:T(8,128)(2,1)S(1)}, bf16[256,1024]{1,0:T(8,128)(2,1)S(1)}, u32[]{:S(2)}, u32[]{:S(2)}) %collective-permute-start.28) | collective-permute-done | bytes 524320 | tf_op jit(solution)/shard_map/ppermute | solution.py:117
  263.5 2.3 collective-permute-done.29
  268.9 3.5 %fusion.44 = (f32[16,8,32]{2,0,1:T(8,128)S(1)}, f32[16,8,32,256]{3,2,0,1:T(8,128)S(1)}) fusion(f32[8,256,16,32]{1,3,2,0:T(8,128)S(1)} %bitcast.74, pred[16,256]{1,0:T(8,128)(4,1)S(1)} %broadcast_in_dim.33), kind=kOutput, calls=%fused_computation.93 | output fusion | flops 6291711 | bytes 8409088 | tf_op jit(solution)/shard_map/sub | solution.py:135
  (138 shorter events, 56.0 us)
Async XLA Ops:
  0.0 95.2 %copy-start.11 = (s32[16,8]{0,1:T(8,128)S(1)}, s32[16,8]{0,1:T(8,128)}, u32[]{:S(2)}) copy-start(s32[16,8]{0,1:T(8,128)} %param.16) | copy-start | bytes 1540
  0.0 26.4 %collective-permute-start.7 = (bf16[512,1024]{1,0:T(8,128)(2,1)}, bf16[512,1024]{1,0:T(8,128)(2,1)S(1)}, u32[]{:S(2)}, u32[]{:S(2)}) collective-permute-start(bf16[512,1024]{1,0:T(8,128)(2,1)} %param.13), channel_id=1, source_target_pairs={{0,8},{8,16},{16,24},{24,28},{28,20},{20,12},{12,4},{4,0},{1,9},{9... | collective-permute-start | bytes 3145736 | tf_op jit(solution)/shard_map/ppermute | solution.py:71
  3.1 25.1 %collective-permute-start.3 = (bf16[512,1024]{1,0:T(8,128)(2,1)}, bf16[512,1024]{1,0:T(8,128)(2,1)S(1)}, u32[]{:S(2)}, u32[]{:S(2)}) collective-permute-start(bf16[512,1024]{1,0:T(8,128)(2,1)} %param.13), channel_id=1, source_target_pairs={{0,4},{8,0},{16,8},{24,16},{28,24},{20,28},{12,20},{4,12},{1,5},{9... | collective-permute-start | bytes 3145736 | tf_op jit(solution)/shard_map/ppermute | solution.py:72
  26.4 24.5 %collective-permute-start.8 = (bf16[512,1024]{1,0:T(8,128)(2,1)S(1)}, bf16[512,1024]{1,0:T(8,128)(2,1)}, u32[]{:S(2)}, u32[]{:S(2)}) collective-permute-start(bf16[512,1024]{1,0:T(8,128)(2,1)S(1)} %collective-permute-done.7), channel_id=1, source_target_pairs={{0,8},{8,16},{16,24},{24,28},{28,20},{20,12},{12,4},{4,0},{1,9},{9... | collective-permute-start | bytes 3145736 | tf_op jit(solution)/shard_map/ppermute | solution.py:71
  28.2 24.1 %collective-permute-start.4 = (bf16[512,1024]{1,0:T(8,128)(2,1)S(1)}, bf16[512,1024]{1,0:T(8,128)(2,1)}, u32[]{:S(2)}, u32[]{:S(2)}) collective-permute-start(bf16[512,1024]{1,0:T(8,128)(2,1)S(1)} %collective-permute-done.3), channel_id=1, source_target_pairs={{0,4},{8,0},{16,8},{24,16},{28,24},{20,28},{12,20},{4,12},{1,5},{9... | collective-permute-start | bytes 3145736 | tf_op jit(solution)/shard_map/ppermute | solution.py:72
  50.9 26.6 %collective-permute-start.9 = (bf16[512,1024]{1,0:T(8,128)(2,1)}, bf16[512,1024]{1,0:T(8,128)(2,1)S(1)}, u32[]{:S(2)}, u32[]{:S(2)}) collective-permute-start(bf16[512,1024]{1,0:T(8,128)(2,1)} %collective-permute-done.8), channel_id=1, source_target_pairs={{0,8},{8,16},{16,24},{24,28},{28,20},{20,12},{12,4},{4,0},{1,9},{9... | collective-permute-start | bytes 3145736 | tf_op jit(solution)/shard_map/ppermute | solution.py:71
  52.4 30.1 %collective-permute-start.5 = (bf16[512,1024]{1,0:T(8,128)(2,1)}, bf16[512,1024]{1,0:T(8,128)(2,1)}, u32[]{:S(2)}, u32[]{:S(2)}) collective-permute-start(bf16[512,1024]{1,0:T(8,128)(2,1)} %collective-permute-done.4), channel_id=1, source_target_pairs={{0,4},{8,0},{16,8},{24,16},{28,24},{20,28},{12,20},{4,12},{1,5},{9... | collective-permute-start | bytes 3145736 | tf_op jit(solution)/shard_map/ppermute | solution.py:72
  55.2 49.4 %all-to-all-start = ((bf16[8,2,16,1024]{3,2,1,0:T(8,128)(2,1)}), bf16[8,2,16,1024]{3,2,1,0:T(8,128)(2,1)S(1)}, u32[]{:S(2)}, u32[]{:S(2)}) async-start(bf16[8,2,16,1024]{3,2,1,0:T(8,128)(2,1)} %bitcast.82), calls=%async_computation | async-start | bytes 1048576 | tf_op jit(solution)/shard_map/all_to_all | solution.py:59
  60.9 46.2 %collective-permute-start.19 = (bf16[512,1024]{1,0:T(8,128)(2,1)}, bf16[512,1024]{1,0:T(8,128)(2,1)}, u32[]{:S(2)}, u32[]{:S(2)}) collective-permute-start(bf16[512,1024]{1,0:T(8,128)(2,1)} %param.10), channel_id=1, source_target_pairs={{0,1},{1,2},{2,3},{3,0},{4,5},{5,6},{6,7},{7,4},{8,9},{9,10},{10,1... | collective-permute-start | bytes 3145736 | tf_op jit(solution)/shard_map/ppermute | solution.py:51
  60.9 47.2 %collective-permute-start.20 = (bf16[512,1024]{1,0:T(8,128)(2,1)}, bf16[512,1024]{1,0:T(8,128)(2,1)}, u32[]{:S(2)}, u32[]{:S(2)}) collective-permute-start(bf16[512,1024]{1,0:T(8,128)(2,1)} %param.10), channel_id=1, source_target_pairs={{0,2},{1,3},{2,0},{3,1},{4,6},{5,7},{6,4},{7,5},{8,10},{9,11},{10,... | collective-permute-start | bytes 3145736 | tf_op jit(solution)/shard_map/ppermute | solution.py:51
  62.5 49.4 %collective-permute-start.21 = (bf16[512,1024]{1,0:T(8,128)(2,1)}, bf16[512,1024]{1,0:T(8,128)(2,1)}, u32[]{:S(2)}, u32[]{:S(2)}) collective-permute-start(bf16[512,1024]{1,0:T(8,128)(2,1)} %param.10), channel_id=1, source_target_pairs={{0,3},{1,0},{2,1},{3,2},{4,7},{5,4},{6,5},{7,6},{8,11},{9,8},{10,9... | collective-permute-start | bytes 3145736 | tf_op jit(solution)/shard_map/ppermute | solution.py:51
  78.3 23.3 %collective-permute-start.10 = (bf16[256,1024]{1,0:T(8,128)(2,1)}, bf16[256,1024]{1,0:T(8,128)(2,1)S(1)}, u32[]{:S(2)}, u32[]{:S(2)}) collective-permute-start(bf16[256,1024]{1,0:T(8,128)(2,1)} %slice.27), channel_id=1, source_target_pairs={{0,8},{8,16},{16,24},{24,28},{28,20},{20,12},{12,4},{4,0},{1,9},{9... | collective-permute-start | bytes 1572872 | tf_op jit(solution)/shard_map/ppermute | solution.py:77
  84.3 17.3 %collective-permute-start.6 = (bf16[256,1024]{1,0:T(8,128)(2,1)}, bf16[256,1024]{1,0:T(8,128)(2,1)}, u32[]{:S(2)}, u32[]{:S(2)}) collective-permute-start(bf16[256,1024]{1,0:T(8,128)(2,1)} %slice.26), channel_id=1, source_target_pairs={{0,4},{8,0},{16,8},{24,16},{28,24},{20,28},{12,20},{4,12},{1,5},{9... | collective-permute-start | bytes 1572872 | tf_op jit(solution)/shard_map/ppermute | solution.py:78
  101.7 21.4 %collective-permute-start.11 = (bf16[512,1024]{1,0:T(8,128)(2,1)}, bf16[512,1024]{1,0:T(8,128)(2,1)}, u32[]{:S(2)}, u32[]{:S(2)}) collective-permute-start(bf16[512,1024]{1,0:T(8,128)(2,1)} %param.14), channel_id=1, source_target_pairs={{0,8},{8,16},{16,24},{24,28},{28,20},{20,12},{12,4},{4,0},{1,9},{9... | collective-permute-start | bytes 3145736 | tf_op jit(solution)/shard_map/ppermute | solution.py:71
  104.5 20.6 %collective-permute-start.12 = (bf16[512,1024]{1,0:T(8,128)(2,1)}, bf16[512,1024]{1,0:T(8,128)(2,1)}, u32[]{:S(2)}, u32[]{:S(2)}) collective-permute-start(bf16[512,1024]{1,0:T(8,128)(2,1)} %param.14), channel_id=1, source_target_pairs={{0,4},{8,0},{16,8},{24,16},{28,24},{20,28},{12,20},{4,12},{1,5},{9... | collective-permute-start | bytes 3145736 | tf_op jit(solution)/shard_map/ppermute | solution.py:72
  107.1 12.5 %collective-permute-start = (bf16[256,1024]{1,0:T(8,128)(2,1)S(1)}, bf16[256,1024]{1,0:T(8,128)(2,1)S(1)}, u32[]{:S(2)}, u32[]{:S(2)}) collective-permute-start(bf16[256,1024]{1,0:T(8,128)(2,1)S(1)} %bitcast.79), channel_id=1, source_target_pairs={{0,1},{1,2},{2,3},{3,0},{4,5},{5,6},{6,7},{7,4},{8,9},{9,10},{10,1... | collective-permute-start | bytes 1572872 | tf_op jit(solution)/shard_map/ppermute | solution.py:51
  108.2 14.9 %collective-permute-start.1 = (bf16[256,1024]{1,0:T(8,128)(2,1)S(1)}, bf16[256,1024]{1,0:T(8,128)(2,1)S(1)}, u32[]{:S(2)}, u32[]{:S(2)}) collective-permute-start(bf16[256,1024]{1,0:T(8,128)(2,1)S(1)} %bitcast.80), channel_id=1, source_target_pairs={{0,2},{1,3},{2,0},{3,1},{4,6},{5,7},{6,4},{7,5},{8,10},{9,11},{10,... | collective-permute-start | bytes 1572872 | tf_op jit(solution)/shard_map/ppermute | solution.py:51
  111.9 19.6 %collective-permute-start.2 = (bf16[256,1024]{1,0:T(8,128)(2,1)S(1)}, bf16[256,1024]{1,0:T(8,128)(2,1)S(1)}, u32[]{:S(2)}, u32[]{:S(2)}) collective-permute-start(bf16[256,1024]{1,0:T(8,128)(2,1)S(1)} %bitcast.81), channel_id=1, source_target_pairs={{0,3},{1,0},{2,1},{3,2},{4,7},{5,4},{6,5},{7,6},{8,11},{9,8},{10,9... | collective-permute-start | bytes 1572872 | tf_op jit(solution)/shard_map/ppermute | solution.py:51
  123.1 19.3 %collective-permute-start.13 = (bf16[512,1024]{1,0:T(8,128)(2,1)}, bf16[512,1024]{1,0:T(8,128)(2,1)S(1)}, u32[]{:S(2)}, u32[]{:S(2)}) collective-permute-start(bf16[512,1024]{1,0:T(8,128)(2,1)} %collective-permute-done.11), channel_id=1, source_target_pairs={{0,8},{8,16},{16,24},{24,28},{28,20},{20,12},{12,4},{4,0},{1,9},{9... | collective-permute-start | bytes 3145736 | tf_op jit(solution)/shard_map/ppermute | solution.py:71
  125.2 19.2 %collective-permute-start.14 = (bf16[512,1024]{1,0:T(8,128)(2,1)}, bf16[512,1024]{1,0:T(8,128)(2,1)S(1)}, u32[]{:S(2)}, u32[]{:S(2)}) collective-permute-start(bf16[512,1024]{1,0:T(8,128)(2,1)} %collective-permute-done.12), channel_id=1, source_target_pairs={{0,4},{8,0},{16,8},{24,16},{28,24},{20,28},{12,20},{4,12},{1,5},{9... | collective-permute-start | bytes 3145736 | tf_op jit(solution)/shard_map/ppermute | solution.py:72
  142.3 25.5 %collective-permute-start.15 = (bf16[512,1024]{1,0:T(8,128)(2,1)S(1)}, bf16[512,1024]{1,0:T(8,128)(2,1)S(1)}, u32[]{:S(2)}, u32[]{:S(2)}) collective-permute-start(bf16[512,1024]{1,0:T(8,128)(2,1)S(1)} %collective-permute-done.13), channel_id=1, source_target_pairs={{0,8},{8,16},{16,24},{24,28},{28,20},{20,12},{12,4},{4,0},{1,9},{9... | collective-permute-start | bytes 3145736 | tf_op jit(solution)/shard_map/ppermute | solution.py:71
  144.4 23.3 %collective-permute-start.16 = (bf16[512,1024]{1,0:T(8,128)(2,1)S(1)}, bf16[512,1024]{1,0:T(8,128)(2,1)S(1)}, u32[]{:S(2)}, u32[]{:S(2)}) collective-permute-start(bf16[512,1024]{1,0:T(8,128)(2,1)S(1)} %collective-permute-done.14), channel_id=1, source_target_pairs={{0,4},{8,0},{16,8},{24,16},{28,24},{20,28},{12,20},{4,12},{1,5},{9... | collective-permute-start | bytes 3145736 | tf_op jit(solution)/shard_map/ppermute | solution.py:72
  167.7 12.1 %collective-permute-start.17 = (bf16[256,1024]{1,0:T(8,128)(2,1)S(1)}, bf16[256,1024]{1,0:T(8,128)(2,1)S(1)}, u32[]{:S(2)}, u32[]{:S(2)}) collective-permute-start(bf16[256,1024]{1,0:T(8,128)(2,1)S(1)} %slice.28), channel_id=1, source_target_pairs={{0,4},{8,0},{16,8},{24,16},{28,24},{20,28},{12,20},{4,12},{1,5},{9... | collective-permute-start | bytes 1572872 | tf_op jit(solution)/shard_map/ppermute | solution.py:78
  167.9 11.9 %collective-permute-start.18 = (bf16[256,1024]{1,0:T(8,128)(2,1)S(1)}, bf16[256,1024]{1,0:T(8,128)(2,1)S(1)}, u32[]{:S(2)}, u32[]{:S(2)}) collective-permute-start(bf16[256,1024]{1,0:T(8,128)(2,1)S(1)} %slice.29), channel_id=1, source_target_pairs={{0,8},{8,16},{16,24},{24,28},{28,20},{20,12},{12,4},{4,0},{1,9},{9... | collective-permute-start | bytes 1572872 | tf_op jit(solution)/shard_map/ppermute | solution.py:77
  179.8 23.3 %collective-permute-start.23 = (bf16[512,1024]{1,0:T(8,128)(2,1)S(1)}, bf16[512,1024]{1,0:T(8,128)(2,1)S(1)}, u32[]{:S(2)}, u32[]{:S(2)}) collective-permute-start(bf16[512,1024]{1,0:T(8,128)(2,1)S(1)} %copy-done.6), channel_id=1, source_target_pairs={{0,4},{8,0},{16,8},{24,16},{28,24},{20,28},{12,20},{4,12},{1,5},{9... | collective-permute-start | bytes 3145736 | tf_op jit(solution)/shard_map/ppermute | solution.py:112
  179.8 23.3 %collective-permute-start.22 = (bf16[512,1024]{1,0:T(8,128)(2,1)S(1)}, bf16[512,1024]{1,0:T(8,128)(2,1)S(1)}, u32[]{:S(2)}, u32[]{:S(2)}) collective-permute-start(bf16[512,1024]{1,0:T(8,128)(2,1)S(1)} %copy-done.6), channel_id=1, source_target_pairs={{0,8},{8,16},{16,24},{24,28},{28,20},{20,12},{12,4},{4,0},{1,9},{9... | collective-permute-start | bytes 3145736 | tf_op jit(solution)/shard_map/ppermute | solution.py:111
  203.1 26.4 %collective-permute-start.25 = (bf16[512,1024]{1,0:T(8,128)(2,1)S(1)}, bf16[512,1024]{1,0:T(8,128)(2,1)S(1)}, u32[]{:S(2)}, u32[]{:S(2)}) collective-permute-start(bf16[512,1024]{1,0:T(8,128)(2,1)S(1)} %collective-permute-done.23), channel_id=1, source_target_pairs={{0,4},{8,0},{16,8},{24,16},{28,24},{20,28},{12,20},{4,12},{1,5},{9... | collective-permute-start | bytes 3145736 | tf_op jit(solution)/shard_map/ppermute | solution.py:112
  203.1 22.6 %collective-permute-start.24 = (bf16[512,1024]{1,0:T(8,128)(2,1)S(1)}, bf16[512,1024]{1,0:T(8,128)(2,1)S(1)}, u32[]{:S(2)}, u32[]{:S(2)}) collective-permute-start(bf16[512,1024]{1,0:T(8,128)(2,1)S(1)} %collective-permute-done.22), channel_id=1, source_target_pairs={{0,8},{8,16},{16,24},{24,28},{28,20},{20,12},{12,4},{4,0},{1,9},{9... | collective-permute-start | bytes 3145736 | tf_op jit(solution)/shard_map/ppermute | solution.py:111
  225.7 23.3 %collective-permute-start.26 = (bf16[512,1024]{1,0:T(8,128)(2,1)S(1)}, bf16[512,1024]{1,0:T(8,128)(2,1)S(1)}, u32[]{:S(2)}, u32[]{:S(2)}) collective-permute-start(bf16[512,1024]{1,0:T(8,128)(2,1)S(1)} %collective-permute-done.24), channel_id=1, source_target_pairs={{0,8},{8,16},{16,24},{24,28},{28,20},{20,12},{12,4},{4,0},{1,9},{9... | collective-permute-start | bytes 3145736 | tf_op jit(solution)/shard_map/ppermute | solution.py:111
  229.5 23.4 %collective-permute-start.27 = (bf16[512,1024]{1,0:T(8,128)(2,1)S(1)}, bf16[512,1024]{1,0:T(8,128)(2,1)S(1)}, u32[]{:S(2)}, u32[]{:S(2)}) collective-permute-start(bf16[512,1024]{1,0:T(8,128)(2,1)S(1)} %collective-permute-done.25), channel_id=1, source_target_pairs={{0,4},{8,0},{16,8},{24,16},{28,24},{20,28},{12,20},{4,12},{1,5},{9... | collective-permute-start | bytes 3145736 | tf_op jit(solution)/shard_map/ppermute | solution.py:112
  249.1 12.6 %collective-permute-start.28 = (bf16[256,1024]{1,0:T(8,128)(2,1)S(1)}, bf16[256,1024]{1,0:T(8,128)(2,1)S(1)}, u32[]{:S(2)}, u32[]{:S(2)}) collective-permute-start(bf16[256,1024]{1,0:T(8,128)(2,1)S(1)} %slice.30), channel_id=1, source_target_pairs={{0,8},{8,16},{16,24},{24,28},{28,20},{20,12},{12,4},{4,0},{1,9},{9... | collective-permute-start | bytes 1572872 | tf_op jit(solution)/shard_map/ppermute | solution.py:117
  253.0 12.8 %collective-permute-start.29 = (bf16[256,1024]{1,0:T(8,128)(2,1)S(1)}, bf16[256,1024]{1,0:T(8,128)(2,1)S(1)}, u32[]{:S(2)}, u32[]{:S(2)}) collective-permute-start(bf16[256,1024]{1,0:T(8,128)(2,1)S(1)} %slice.31), channel_id=1, source_target_pairs={{0,4},{8,0},{16,8},{24,16},{28,24},{20,28},{12,20},{4,12},{1,5},{9... | collective-permute-start | bytes 1572872 | tf_op jit(solution)/shard_map/ppermute | solution.py:118
  (13 other events, 401.3 us)

commit v17 on v15

--- a/solution.py
+++ b/solution.py
@@ -64,18 +64,19 @@
     split = wrows // 2
 
     def ring_pieces(piece):
+        two = piece.reshape(2, split, piece.shape[1])
         got = [(piece, me, 0, wrows)]
-        fwd = piece
-        bwd = piece
+        fwd = two
+        bwd = two
         for k in range(1, steps_bwd + 1):
             fwd = lax.ppermute(fwd, "crop", fwd_perm)
             bwd = lax.ppermute(bwd, "crop", bwd_perm)
-            got.append((fwd, ring_arr[(pos - k) % ncrop], 0, wrows))
-            got.append((bwd, ring_arr[(pos + k) % ncrop], 0, wrows))
+            got.append((fwd.reshape(wrows, -1), ring_arr[(pos - k) % ncrop], 0, wrows))
+            got.append((bwd.reshape(wrows, -1), ring_arr[(pos + k) % ncrop], 0, wrows))
         if steps_fwd > steps_bwd:
             src = ring_arr[(pos - steps_fwd) % ncrop]
-            got.append((lax.ppermute(fwd[:split], "crop", fwd_perm), src, 0, split))
-            got.append((lax.ppermute(bwd[split:], "crop", bwd_perm), src, split, wrows - split))
+            got.append((lax.ppermute(fwd[0], "crop", fwd_perm), src, 0, split))
+            got.append((lax.ppermute(bwd[1], "crop", bwd_perm), src, split, wrows - split))
         return got
 
     kv_got = ring_pieces(lax.optimization_barrier(jnp.concatenate([key_weight, value_weight], axis=1)))
@@ -98,17 +99,17 @@
         return lax.optimization_barrier(acc + jnp.dot(cols, piece, preferred_element_type=jnp.float32))
 
     acc = q_part(jnp.zeros((queries_in.shape[0], width), jnp.float32), q_piece, me, 0, wrows)
-    fwd = q_piece
-    bwd = q_piece
+    fwd = q_piece.reshape(2, split, width)
+    bwd = fwd
     for k in range(1, steps_bwd + 1):
         fwd = lax.ppermute(fwd, "crop", fwd_perm)
         bwd = lax.ppermute(bwd, "crop", bwd_perm)
-        acc = q_part(acc, fwd, ring_arr[(pos - k) % ncrop], 0, wrows)
-        acc = q_part(acc, bwd, ring_arr[(pos + k) % ncrop], 0, wrows)
+        acc = q_part(acc, fwd.reshape(wrows, width), ring_arr[(pos - k) % ncrop], 0, wrows)
+        acc = q_part(acc, bwd.reshape(wrows, width), ring_arr[(pos + k) % ncrop], 0, wrows)
     if steps_fwd > steps_bwd:
         src = ring_arr[(pos - steps_fwd) % ncrop]
-        acc = q_part(acc, lax.ppermute(fwd[:split], "crop", fwd_perm), src, 0, split)
-        acc = q_part(acc, lax.ppermute(bwd[split:], "crop", bwd_perm), src, split, wrows - split)
+        acc = q_part(acc, lax.ppermute(fwd[0], "crop", fwd_perm), src, 0, split)
+        acc = q_part(acc, lax.ppermute(bwd[1], "crop", bwd_perm), src, split, wrows - split)
     query = acc.astype(jnp.bfloat16)
     nslots = ncrop * CAP
     keys_all = incoming[..., :width].reshape(nslots * CT, heads_here, HD)

time: 275 us -> 283 us (1.029)
  waiting for transfers between devices: 165 us -> 171 us
  starting transfers between devices: 33.6 us -> 38.7 us
  local copies, waits for them, and re-layouts: 36.3 us -> 32.7 us
    ppermute x3, waiting for transfers between devices: 27 us -> 44.3 us  [body(): fwd = lax.ppermute(fwd, 'crop', fwd_perm)]
    ppermute x3, waiting for transfers between devices: 17.4 us -> 4.53 us  [body(): bwd = lax.ppermute(bwd, 'crop', bwd_perm)]
    ppermute x3, waiting for transfers between devices: 0.01 us -> 7.87 us  [ring_pieces(): bwd = lax.ppermute(bwd, 'crop', bwd_perm)]
    ppermute x4, waiting for transfers between devices: 21.5 us -> 17.5 us  [the longest x1 10.6 us: ring_pieces(): lax.ppermute(bwd[1], 'crop', bwd_perm)]
    ppermute x3, starting transfers between devices: 0.25 us -> 3.83 us  [body(): bwd = lax.ppermute(bwd, 'crop', bwd_perm)]
    ppermute x3, starting transfers between devices: 6.07 us -> 2.9 us  [body(): fwd = lax.ppermute(fwd, 'crop', fwd_perm)]
  transfers between devices with their start and end apart: 23 -> 23, of which waited for: 14 -> 16; matrix products, arithmetic and copies ran while one was open for 20% -> 18% of each run, Pallas kernels for 0% -> 0%
where the time goes in v17:
time: 283 us; the launch traced here: 282 us
  waiting for transfers between devices  171 us (60%)
  starting transfers between devices  38.7 us (14%)
  local copies, waits for them, and re-layouts  32.7 us (12%)
  matrix products  21.5 us (8%)
  between operations  9.31 us (3%)
  other arithmetic  8.03 us (3%)
    ppermute x3, waiting for transfers between devices, ring_pieces(): fwd = lax.ppermute(fwd, 'crop', fwd_perm)  82 us
    ppermute x3, waiting for transfers between devices, body(): fwd = lax.ppermute(fwd, 'crop', fwd_perm)  44.3 us
    dot_general x9, matrix products, q_part(): jnp.dot(cols, piece, preferred_element_type=jnp.float32)  15.2 us
    unnamed x41, local copies, waits for them, and re-layouts  14.8 us
    ppermute x6, waiting for transfers between devices, head_gather(): part = lax.ppermute(x, 'head', [(j, (j + k) % nhead) for j in range(nhead)])  11.7 us
    ppermute x1, waiting for transfers between devices, ring_pieces(): lax.ppermute(bwd[1], 'crop', bwd_perm)  10.6 us
    ppermute x3, waiting for transfers between devices, ring_pieces(): bwd = lax.ppermute(bwd, 'crop', bwd_perm)  7.87 us
    ppermute x3, starting transfers between devices, ring_pieces(): fwd = lax.ppermute(fwd, 'crop', fwd_perm)  7.54 us
  transfers between devices with their start and end apart: 23, of which 16 were waited for; matrix products, arithmetic and copies ran while one was open for 18% of the time, Pallas kernels for 0%

profile of v17, /device:TPU:0, one launch (start us, length us, event | category | flops | bytes accessed | tf_op | source)
XLA Modules:
  0.0 281.7 jit_solution(12051186754500300093)
XLA Ops:
  0.0 1.9 pad_maximum_fusion
  2.0 3.1 %collective-permute-start.3 = (bf16[2,256,2048]{2,1,0:T(8,128)(2,1)S(1)}, bf16[2,256,2048]{2,1,0:T(8,128)(2,1)}, u32[]{:S(2)}, u32[]{:S(2)}) collective-permute-start(bf16[2,256,2048]{2,1,0:T(8,128)(2,1)S(1)} %bitcast.94), channel_id=1, source_target_pairs={{0,8},{8,16},{16,24},{24,28},{28,20},{20,12},{12,4},{4,0},{1,9},{9... | collective-permute-start | bytes 6291464 | tf_op jit(solution)/shard_map/ppermute | solution.py:72
  6.2 44.5 %collective-permute-done.3 = bf16[2,256,2048]{2,1,0:T(8,128)(2,1)} collective-permute-done((bf16[2,256,2048]{2,1,0:T(8,128)(2,1)S(1)}, bf16[2,256,2048]{2,1,0:T(8,128)(2,1)}, u32[]{:S(2)}, u32[]{:S(2)}) %collective-permute-start.3) | collective-permute-done | bytes 2097184 | tf_op jit(solution)/shard_map/ppermute | solution.py:72
  56.8 5.1 %all-to-all-start = ((bf16[8,2,16,1024]{3,2,1,0:T(8,128)(2,1)}), bf16[8,2,16,1024]{3,2,1,0:T(8,128)(2,1)S(1)}, u32[]{:S(2)}, u32[]{:S(2)}) async-start(bf16[8,2,16,1024]{3,2,1,0:T(8,128)(2,1)} %bitcast.2), calls=%async_computation | async-start | bytes 1048576 | tf_op jit(solution)/shard_map/all_to_all | solution.py:59
  73.7 3.2 %constant_dynamic-update-slice_fusion.8 = bf16[4096,2048]{1,0:T(8,128)(2,1)} fusion(bf16[512,2048]{1,0:T(8,128)(2,1)} %copy-done.2), kind=kLoop, calls=%fused_computation.61 | loop fusion | bytes 4194304
  76.9 23.3 %collective-permute-done.5 = bf16[2,256,2048]{2,1,0:T(8,128)(2,1)} collective-permute-done((bf16[2,256,2048]{2,1,0:T(8,128)(2,1)}, bf16[2,256,2048]{2,1,0:T(8,128)(2,1)}, u32[]{:S(2)}, u32[]{:S(2)}) %collective-permute-start.5) | collective-permute-done | bytes 2097184 | tf_op jit(solution)/shard_map/ppermute | solution.py:72
  100.2 2.7 collective-permute-start.7
  102.9 2.5 broadcast_in_dim.35
  105.3 2.4 constant_dynamic-update-slice_fusion.12
  107.7 3.5 %all-to-all-done = bf16[8,2,16,1024]{3,2,1,0:T(8,128)(2,1)S(1)} async-done(((bf16[8,2,16,1024]{3,2,1,0:T(8,128)(2,1)}), bf16[8,2,16,1024]{3,2,1,0:T(8,128)(2,1)S(1)}, u32[]{:S(2)}, u32[]{:S(2)}) %all-to-all-start) | async-done | bytes 524320 | tf_op jit(solution)/shard_map/all_to_all | solution.py:59
  113.1 2.5 constant_dynamic-update-slice_fusion.11
  117.0 2.3 collective-permute-start.8
  119.3 2.3 constant_dynamic-update-slice_fusion.10
  121.6 2.3 constant_dynamic-update-slice_fusion.9
  126.4 9.3 %collective-permute-done.2 = bf16[256,1024]{1,0:T(8,128)(2,1)S(1)} collective-permute-done((bf16[256,1024]{1,0:T(8,128)(2,1)S(1)}, bf16[256,1024]{1,0:T(8,128)(2,1)S(1)}, u32[]{:S(2)}, u32[]{:S(2)}) %collective-permute-start.2) | collective-permute-done | bytes 524320 | tf_op jit(solution)/shard_map/ppermute | solution.py:51
  136.1 14.2 %collective-permute-done.7 = bf16[2,256,2048]{2,1,0:T(8,128)(2,1)} collective-permute-done((bf16[2,256,2048]{2,1,0:T(8,128)(2,1)}, bf16[2,256,2048]{2,1,0:T(8,128)(2,1)}, u32[]{:S(2)}, u32[]{:S(2)}) %collective-permute-start.7) | collective-permute-done | bytes 2097184 | tf_op jit(solution)/shard_map/ppermute | solution.py:72
  151.5 4.4 %collective-permute-start.10 = (bf16[256,2048]{1,0:T(8,128)(2,1)S(1)}, bf16[256,2048]{1,0:T(8,128)(2,1)S(1)}, u32[]{:S(2)}, u32[]{:S(2)}) collective-permute-start(bf16[256,2048]{1,0:T(8,128)(2,1)S(1)} %slice_bitcast_fusion), channel_id=1, source_target_pairs={{0,8},{8,16},{16,24},{24,28},{28,20},{20,12},{12,4},{4,0},{1,9},{9... | collective-permute-start | bytes 3145736 | tf_op jit(solution)/shard_map/ppermute | solution.py:78
  156.0 7.9 %collective-permute-done.8 = bf16[2,256,2048]{2,1,0:T(8,128)(2,1)S(1)} collective-permute-done((bf16[2,256,2048]{2,1,0:T(8,128)(2,1)}, bf16[2,256,2048]{2,1,0:T(8,128)(2,1)S(1)}, u32[]{:S(2)}, u32[]{:S(2)}) %collective-permute-start.8) | collective-permute-done | bytes 2097184 | tf_op jit(solution)/shard_map/ppermute | solution.py:73
  163.9 2.4 collective-permute-start.9
  166.3 1.8 constant_dynamic-update-slice_fusion.7
  168.2 1.8 constant_dynamic-update-slice_fusion.6
  170.0 1.8 constant_dynamic-update-slice_fusion.5
  171.9 1.9 constant_dynamic-update-slice_fusion.4
  173.8 2.8 %collective-permute-done.10 = bf16[256,2048]{1,0:T(8,128)(2,1)S(1)} collective-permute-done((bf16[256,2048]{1,0:T(8,128)(2,1)S(1)}, bf16[256,2048]{1,0:T(8,128)(2,1)S(1)}, u32[]{:S(2)}, u32[]{:S(2)}) %collective-permute-start.10) | collective-permute-done | bytes 1048608 | tf_op jit(solution)/shard_map/ppermute | solution.py:78
  176.6 10.6 %collective-permute-done.9 = bf16[256,2048]{1,0:T(8,128)(2,1)S(1)} collective-permute-done((bf16[256,2048]{1,0:T(8,128)(2,1)S(1)}, bf16[256,2048]{1,0:T(8,128)(2,1)S(1)}, u32[]{:S(2)}, u32[]{:S(2)}) %collective-permute-start.9) | collective-permute-done | bytes 1048608 | tf_op jit(solution)/shard_map/ppermute | solution.py:79
  191.9 18.9 %collective-permute-done.14 = bf16[2,256,1024]{2,1,0:T(8,128)(2,1)S(1)} collective-permute-done((bf16[2,256,1024]{2,1,0:T(8,128)(2,1)S(1)}, bf16[2,256,1024]{2,1,0:T(8,128)(2,1)S(1)}, u32[]{:S(2)}, u32[]{:S(2)}) %collective-permute-start.14) | collective-permute-done | bytes 1048608 | tf_op jit(solution)/shard_map/ppermute | solution.py:105
  211.7 4.6 %convolution_convert_fusion = bf16[256,2048]{1,0:T(8,128)(2,1)S(1)} fusion(bf16[256,4096]{1,0:T(8,128)(2,1)S(1)} %dynamic-slice_dynamic-update-slice_fusion.7, bf16[4096,2048]{1,0:T(8,128)(2,1)S(1)} %constant_dynamic-update-slice_fusion), kind=kOutput, calls=%fused_computation.6 | convolution fusion | flops 4295491584 | bytes 19922944 | tf_op jit(solution)/shard_map/dot_general | solution.py:94
  219.7 14.5 %collective-permute-done.16 = bf16[2,256,1024]{2,1,0:T(8,128)(2,1)S(1)} collective-permute-done((bf16[2,256,1024]{2,1,0:T(8,128)(2,1)S(1)}, bf16[2,256,1024]{2,1,0:T(8,128)(2,1)S(1)}, u32[]{:S(2)}, u32[]{:S(2)}) %collective-permute-start.16) | collective-permute-done | bytes 1048608 | tf_op jit(solution)/shard_map/ppermute | solution.py:105
  244.8 10.9 %collective-permute-done.18 = bf16[2,256,1024]{2,1,0:T(8,128)(2,1)S(1)} collective-permute-done((bf16[2,256,1024]{2,1,0:T(8,128)(2,1)S(1)}, bf16[2,256,1024]{2,1,0:T(8,128)(2,1)S(1)}, u32[]{:S(2)}, u32[]{:S(2)}) %collective-permute-start.18) | collective-permute-done | bytes 1048608 | tf_op jit(solution)/shard_map/ppermute | solution.py:105
  258.4 4.5 %collective-permute-done.19 = bf16[2,256,1024]{2,1,0:T(8,128)(2,1)S(1)} collective-permute-done((bf16[2,256,1024]{2,1,0:T(8,128)(2,1)S(1)}, bf16[2,256,1024]{2,1,0:T(8,128)(2,1)S(1)}, u32[]{:S(2)}, u32[]{:S(2)}) %collective-permute-start.19) | collective-permute-done | bytes 1048608 | tf_op jit(solution)/shard_map/ppermute | solution.py:106
  268.5 3.7 %collective-permute-done.21 = bf16[256,1024]{1,0:T(8,128)(2,1)S(1)} collective-permute-done((bf16[256,1024]{1,0:T(8,128)(2,1)S(1)}, bf16[256,1024]{1,0:T(8,128)(2,1)S(1)}, u32[]{:S(2)}, u32[]{:S(2)}) %collective-permute-start.21) | collective-permute-done | bytes 524320 | tf_op jit(solution)/shard_map/ppermute | solution.py:112
  275.2 3.5 %fusion.42 = (f32[16,8,32]{2,0,1:T(8,128)S(1)}, f32[16,8,32,256]{3,2,0,1:T(8,128)S(1)}) fusion(f32[8,256,16,32]{1,3,2,0:T(8,128)S(1)} %bitcast.98, pred[16,256]{1,0:T(8,128)(4,1)S(1)} %broadcast_in_dim.33), kind=kOutput, calls=%fused_computation.86 | output fusion | flops 6291711 | bytes 8409088 | tf_op jit(solution)/shard_map/sub | solution.py:129
  (105 shorter events, 51.2 us)
Async XLA Ops:
  0.0 55.4 %copy-start = (bf16[1024,1024]{1,0:T(8,128)(2,1)S(1)}, bf16[1024,1024]{1,0:T(8,128)(2,1)}, u32[]{:S(2)}) copy-start(bf16[1024,1024]{1,0:T(8,128)(2,1)} %param.11) | copy-start | bytes 6291460
  0.0 55.2 %copy-start.7 = (s32[1,8,2]{1,2,0:T(2,128)S(1)}, s32[1,8,2]{1,2,0:T(2,128)}, u32[]{:S(2)}) copy-start(s32[1,8,2]{1,2,0:T(2,128)} %param.15) | copy-start | bytes 196
  1.9 3.1 %copy-start.2 = (bf16[512,2048]{1,0:T(8,128)(2,1)}, bf16[512,2048]{1,0:T(8,128)(2,1)S(1)}, u32[]{:S(2)}) copy-start(bf16[512,2048]{1,0:T(8,128)(2,1)S(1)} %pad_maximum_fusion) | copy-start | bytes 6291460
  1.9 61.1 %copy-start.9 = (s32[8]{0:T(128)S(1)}, s32[8]{0:T(128)}, u32[]{:S(2)}) copy-start(s32[8]{0:T(128)} %constant.150.clone) | copy-start | bytes 100
  1.9 66.1 %copy-start.5 = (s32[8]{0:T(128)S(1)}, s32[8]{0:T(128)}, u32[]{:S(2)}) copy-start(s32[8]{0:T(128)} %constant.151.clone) | copy-start | bytes 100
  2.0 71.2 %copy-start.6 = (s32[16,8]{0,1:T(8,128)S(1)}, s32[16,8]{0,1:T(8,128)}, u32[]{:S(2)}) copy-start(s32[16,8]{0,1:T(8,128)} %param.16) | copy-start | bytes 1540
  2.0 71.2 %copy-start.8 = (s32[16]{0:T(128)S(1)}, s32[16]{0:T(128)}, u32[]{:S(2)}) copy-start(s32[16]{0:T(128)} %param.17) | copy-start | bytes 196
  2.0 48.8 %collective-permute-start.3 = (bf16[2,256,2048]{2,1,0:T(8,128)(2,1)S(1)}, bf16[2,256,2048]{2,1,0:T(8,128)(2,1)}, u32[]{:S(2)}, u32[]{:S(2)}) collective-permute-start(bf16[2,256,2048]{2,1,0:T(8,128)(2,1)S(1)} %bitcast.94), channel_id=1, source_target_pairs={{0,8},{8,16},{16,24},{24,28},{28,20},{20,12},{12,4},{4,0},{1,9},{9... | collective-permute-start | bytes 6291464 | tf_op jit(solution)/shard_map/ppermute | solution.py:72
  5.1 47.5 %collective-permute-start.4 = (bf16[2,256,2048]{2,1,0:T(8,128)(2,1)S(1)}, bf16[2,256,2048]{2,1,0:T(8,128)(2,1)}, u32[]{:S(2)}, u32[]{:S(2)}) collective-permute-start(bf16[2,256,2048]{2,1,0:T(8,128)(2,1)S(1)} %bitcast.95), channel_id=1, source_target_pairs={{0,4},{8,0},{16,8},{24,16},{28,24},{20,28},{12,20},{4,12},{1,5},{9... | collective-permute-start | bytes 6291464 | tf_op jit(solution)/shard_map/ppermute | solution.py:73
  50.7 49.5 %collective-permute-start.5 = (bf16[2,256,2048]{2,1,0:T(8,128)(2,1)}, bf16[2,256,2048]{2,1,0:T(8,128)(2,1)}, u32[]{:S(2)}, u32[]{:S(2)}) collective-permute-start(bf16[2,256,2048]{2,1,0:T(8,128)(2,1)} %collective-permute-done.3), channel_id=1, source_target_pairs={{0,8},{8,16},{16,24},{24,28},{28,20},{20,12},{12,4},{4,0},{1,9},{9... | collective-permute-start | bytes 6291464 | tf_op jit(solution)/shard_map/ppermute | solution.py:72
  52.5 64.5 %collective-permute-start.6 = (bf16[2,256,2048]{2,1,0:T(8,128)(2,1)}, bf16[2,256,2048]{2,1,0:T(8,128)(2,1)}, u32[]{:S(2)}, u32[]{:S(2)}) collective-permute-start(bf16[2,256,2048]{2,1,0:T(8,128)(2,1)} %collective-permute-done.4), channel_id=1, source_target_pairs={{0,4},{8,0},{16,8},{24,16},{28,24},{20,28},{12,20},{4,12},{1,5},{9... | collective-permute-start | bytes 6291464 | tf_op jit(solution)/shard_map/ppermute | solution.py:73
  53.7 57.5 %collective-permute-start.11 = (bf16[512,1024]{1,0:T(8,128)(2,1)}, bf16[512,1024]{1,0:T(8,128)(2,1)}, u32[]{:S(2)}, u32[]{:S(2)}) collective-permute-start(bf16[512,1024]{1,0:T(8,128)(2,1)} %param.10), channel_id=1, source_target_pairs={{0,1},{1,2},{2,3},{3,0},{4,5},{5,6},{6,7},{7,4},{8,9},{9,10},{10,1... | collective-permute-start | bytes 3145736 | tf_op jit(solution)/shard_map/ppermute | solution.py:51
  53.7 57.8 %collective-permute-start.12 = (bf16[512,1024]{1,0:T(8,128)(2,1)}, bf16[512,1024]{1,0:T(8,128)(2,1)}, u32[]{:S(2)}, u32[]{:S(2)}) collective-permute-start(bf16[512,1024]{1,0:T(8,128)(2,1)} %param.10), channel_id=1, source_target_pairs={{0,2},{1,3},{2,0},{3,1},{4,6},{5,7},{6,4},{7,5},{8,10},{9,11},{10,... | collective-permute-start | bytes 3145736 | tf_op jit(solution)/shard_map/ppermute | solution.py:51
  56.8 54.4 %all-to-all-start = ((bf16[8,2,16,1024]{3,2,1,0:T(8,128)(2,1)}), bf16[8,2,16,1024]{3,2,1,0:T(8,128)(2,1)S(1)}, u32[]{:S(2)}, u32[]{:S(2)}) async-start(bf16[8,2,16,1024]{3,2,1,0:T(8,128)(2,1)} %bitcast.2), calls=%async_computation | async-start | bytes 1048576 | tf_op jit(solution)/shard_map/all_to_all | solution.py:59
  61.9 53.7 %collective-permute-start.13 = (bf16[512,1024]{1,0:T(8,128)(2,1)}, bf16[512,1024]{1,0:T(8,128)(2,1)}, u32[]{:S(2)}, u32[]{:S(2)}) collective-permute-start(bf16[512,1024]{1,0:T(8,128)(2,1)} %param.10), channel_id=1, source_target_pairs={{0,3},{1,0},{2,1},{3,2},{4,7},{5,4},{6,5},{7,6},{8,11},{9,8},{10,9... | collective-permute-start | bytes 3145736 | tf_op jit(solution)/shard_map/ppermute | solution.py:51
  100.2 50.0 %collective-permute-start.7 = (bf16[2,256,2048]{2,1,0:T(8,128)(2,1)}, bf16[2,256,2048]{2,1,0:T(8,128)(2,1)}, u32[]{:S(2)}, u32[]{:S(2)}) collective-permute-start(bf16[2,256,2048]{2,1,0:T(8,128)(2,1)} %collective-permute-done.5), channel_id=1, source_target_pairs={{0,8},{8,16},{16,24},{24,28},{28,20},{20,12},{12,4},{4,0},{1,9},{9... | collective-permute-start | bytes 6291464 | tf_op jit(solution)/shard_map/ppermute | solution.py:72
  111.2 13.3 %collective-permute-start = (bf16[256,1024]{1,0:T(8,128)(2,1)S(1)}, bf16[256,1024]{1,0:T(8,128)(2,1)S(1)}, u32[]{:S(2)}, u32[]{:S(2)}) collective-permute-start(bf16[256,1024]{1,0:T(8,128)(2,1)S(1)} %bitcast.104), channel_id=1, source_target_pairs={{0,1},{1,2},{2,3},{3,0},{4,5},{5,6},{6,7},{7,4},{8,9},{9,10},{10,1... | collective-permute-start | bytes 1572872 | tf_op jit(solution)/shard_map/ppermute | solution.py:51
  111.5 14.8 %collective-permute-start.1 = (bf16[256,1024]{1,0:T(8,128)(2,1)S(1)}, bf16[256,1024]{1,0:T(8,128)(2,1)S(1)}, u32[]{:S(2)}, u32[]{:S(2)}) collective-permute-start(bf16[256,1024]{1,0:T(8,128)(2,1)S(1)} %bitcast.106), channel_id=1, source_target_pairs={{0,2},{1,3},{2,0},{3,1},{4,6},{5,7},{6,4},{7,5},{8,10},{9,11},{10,... | collective-permute-start | bytes 1572872 | tf_op jit(solution)/shard_map/ppermute | solution.py:51
  113.1 53.2 %copy-start.4 = (bf16[4096,2048]{1,0:T(8,128)(2,1)S(1)}, bf16[4096,2048]{1,0:T(8,128)(2,1)}, u32[]{:S(2)}) copy-start(bf16[4096,2048]{1,0:T(8,128)(2,1)} %constant_dynamic-update-slice_fusion.8) | copy-start | bytes 50331652
  115.6 20.1 %collective-permute-start.2 = (bf16[256,1024]{1,0:T(8,128)(2,1)S(1)}, bf16[256,1024]{1,0:T(8,128)(2,1)S(1)}, u32[]{:S(2)}, u32[]{:S(2)}) collective-permute-start(bf16[256,1024]{1,0:T(8,128)(2,1)S(1)} %bitcast.107), channel_id=1, source_target_pairs={{0,3},{1,0},{2,1},{3,2},{4,7},{5,4},{6,5},{7,6},{8,11},{9,8},{10,9... | collective-permute-start | bytes 1572872 | tf_op jit(solution)/shard_map/ppermute | solution.py:51
  117.0 46.8 %collective-permute-start.8 = (bf16[2,256,2048]{2,1,0:T(8,128)(2,1)}, bf16[2,256,2048]{2,1,0:T(8,128)(2,1)S(1)}, u32[]{:S(2)}, u32[]{:S(2)}) collective-permute-start(bf16[2,256,2048]{2,1,0:T(8,128)(2,1)} %collective-permute-done.6), channel_id=1, source_target_pairs={{0,4},{8,0},{16,8},{24,16},{28,24},{20,28},{12,20},{4,12},{1,5},{9... | collective-permute-start | bytes 6291464 | tf_op jit(solution)/shard_map/ppermute | solution.py:73
  151.5 25.1 %collective-permute-start.10 = (bf16[256,2048]{1,0:T(8,128)(2,1)S(1)}, bf16[256,2048]{1,0:T(8,128)(2,1)S(1)}, u32[]{:S(2)}, u32[]{:S(2)}) collective-permute-start(bf16[256,2048]{1,0:T(8,128)(2,1)S(1)} %slice_bitcast_fusion), channel_id=1, source_target_pairs={{0,8},{8,16},{16,24},{24,28},{28,20},{20,12},{12,4},{4,0},{1,9},{9... | collective-permute-start | bytes 3145736 | tf_op jit(solution)/shard_map/ppermute | solution.py:78
  163.9 23.3 %collective-permute-start.9 = (bf16[256,2048]{1,0:T(8,128)(2,1)S(1)}, bf16[256,2048]{1,0:T(8,128)(2,1)S(1)}, u32[]{:S(2)}, u32[]{:S(2)}) collective-permute-start(bf16[256,2048]{1,0:T(8,128)(2,1)S(1)} %slice_bitcast_fusion.1), channel_id=1, source_target_pairs={{0,4},{8,0},{16,8},{24,16},{28,24},{20,28},{12,20},{4,12},{1,5},{9... | collective-permute-start | bytes 3145736 | tf_op jit(solution)/shard_map/ppermute | solution.py:79
  171.8 15.4 %copy-start.3 = (bf16[512,1024]{1,0:T(8,128)(2,1)S(1)}, bf16[512,1024]{1,0:T(8,128)(2,1)}, u32[]{:S(2)}) copy-start(bf16[512,1024]{1,0:T(8,128)(2,1)} %param.12) | copy-start | bytes 3145732
  187.2 23.6 %collective-permute-start.14 = (bf16[2,256,1024]{2,1,0:T(8,128)(2,1)S(1)}, bf16[2,256,1024]{2,1,0:T(8,128)(2,1)S(1)}, u32[]{:S(2)}, u32[]{:S(2)}) collective-permute-start(bf16[2,256,1024]{2,1,0:T(8,128)(2,1)S(1)} %bitcast.112), channel_id=1, source_target_pairs={{0,8},{8,16},{16,24},{24,28},{28,20},{20,12},{12,4},{4,0},{1,9},{9... | collective-permute-start | bytes 3145736 | tf_op jit(solution)/shard_map/ppermute | solution.py:105
  190.5 25.9 %collective-permute-start.15 = (bf16[2,256,1024]{2,1,0:T(8,128)(2,1)S(1)}, bf16[2,256,1024]{2,1,0:T(8,128)(2,1)S(1)}, u32[]{:S(2)}, u32[]{:S(2)}) collective-permute-start(bf16[2,256,1024]{2,1,0:T(8,128)(2,1)S(1)} %bitcast.113), channel_id=1, source_target_pairs={{0,4},{8,0},{16,8},{24,16},{28,24},{20,28},{12,20},{4,12},{1,5},{9... | collective-permute-start | bytes 3145736 | tf_op jit(solution)/shard_map/ppermute | solution.py:106
  210.9 23.3 %collective-permute-start.16 = (bf16[2,256,1024]{2,1,0:T(8,128)(2,1)S(1)}, bf16[2,256,1024]{2,1,0:T(8,128)(2,1)S(1)}, u32[]{:S(2)}, u32[]{:S(2)}) collective-permute-start(bf16[2,256,1024]{2,1,0:T(8,128)(2,1)S(1)} %collective-permute-done.14), channel_id=1, source_target_pairs={{0,8},{8,16},{16,24},{24,28},{28,20},{20,12},{12,4},{4,0},{1,9},{9... | collective-permute-start | bytes 3145736 | tf_op jit(solution)/shard_map/ppermute | solution.py:105
  216.4 23.0 %collective-permute-start.17 = (bf16[2,256,1024]{2,1,0:T(8,128)(2,1)S(1)}, bf16[2,256,1024]{2,1,0:T(8,128)(2,1)S(1)}, u32[]{:S(2)}, u32[]{:S(2)}) collective-permute-start(bf16[2,256,1024]{2,1,0:T(8,128)(2,1)S(1)} %collective-permute-done.15), channel_id=1, source_target_pairs={{0,4},{8,0},{16,8},{24,16},{28,24},{20,28},{12,20},{4,12},{1,5},{9... | collective-permute-start | bytes 3145736 | tf_op jit(solution)/shard_map/ppermute | solution.py:106
  234.2 21.5 %collective-permute-start.18 = (bf16[2,256,1024]{2,1,0:T(8,128)(2,1)S(1)}, bf16[2,256,1024]{2,1,0:T(8,128)(2,1)S(1)}, u32[]{:S(2)}, u32[]{:S(2)}) collective-permute-start(bf16[2,256,1024]{2,1,0:T(8,128)(2,1)S(1)} %collective-permute-done.16), channel_id=1, source_target_pairs={{0,8},{8,16},{16,24},{24,28},{28,20},{20,12},{12,4},{4,0},{1,9},{9... | collective-permute-start | bytes 3145736 | tf_op jit(solution)/shard_map/ppermute | solution.py:105
  239.4 23.5 %collective-permute-start.19 = (bf16[2,256,1024]{2,1,0:T(8,128)(2,1)S(1)}, bf16[2,256,1024]{2,1,0:T(8,128)(2,1)S(1)}, u32[]{:S(2)}, u32[]{:S(2)}) collective-permute-start(bf16[2,256,1024]{2,1,0:T(8,128)(2,1)S(1)} %collective-permute-done.17), channel_id=1, source_target_pairs={{0,4},{8,0},{16,8},{24,16},{28,24},{20,28},{12,20},{4,12},{1,5},{9... | collective-permute-start | bytes 3145736 | tf_op jit(solution)/shard_map/ppermute | solution.py:106
  257.5 9.2 %collective-permute-start.20 = (bf16[256,1024]{1,0:T(8,128)(2,1)S(1)}, bf16[256,1024]{1,0:T(8,128)(2,1)S(1)}, u32[]{:S(2)}, u32[]{:S(2)}) collective-permute-start(bf16[256,1024]{1,0:T(8,128)(2,1)S(1)} %slice_bitcast_fusion.3), channel_id=1, source_target_pairs={{0,8},{8,16},{16,24},{24,28},{28,20},{20,12},{12,4},{4,0},{1,9},{9... | collective-permute-start | bytes 1572872 | tf_op jit(solution)/shard_map/ppermute | solution.py:111
  262.9 9.2 %collective-permute-start.21 = (bf16[256,1024]{1,0:T(8,128)(2,1)S(1)}, bf16[256,1024]{1,0:T(8,128)(2,1)S(1)}, u32[]{:S(2)}, u32[]{:S(2)}) collective-permute-start(bf16[256,1024]{1,0:T(8,128)(2,1)S(1)} %slice_bitcast_fusion.2), channel_id=1, source_target_pairs={{0,4},{8,0},{16,8},{24,16},{28,24},{20,28},{12,20},{4,12},{1,5},{9... | collective-permute-start | bytes 1572872 | tf_op jit(solution)/shard_map/ppermute | solution.py:112
  (1 other events, 3.0 us)

commit v18 on v15

--- a/solution.py
+++ b/solution.py
@@ -79,11 +79,12 @@
         return got
 
     kv_got = ring_pieces(lax.optimization_barrier(jnp.concatenate([key_weight, value_weight], axis=1)))
+    at = -3 if steps_fwd > steps_bwd else -1
     q_piece, last_a, last_b = lax.optimization_barrier(
-        (query_weight, kv_got[-1][0], kv_got[-2][0])
+        (query_weight, kv_got[at][0], kv_got[at - 1][0])
     )
-    kv_got[-1] = (last_a,) + kv_got[-1][1:]
-    kv_got[-2] = (last_b,) + kv_got[-2][1:]
+    kv_got[at] = (last_a,) + kv_got[at][1:]
+    kv_got[at - 1] = (last_b,) + kv_got[at - 1][1:]
     tokens_in = head_gather(delivered)
     kv_weight = jnp.concatenate([p for p, _, _, _ in kv_got], axis=0)
     tokens_perm = jnp.concatenate(

time: 275 us -> 288 us (1.047)
  waiting for transfers between devices: 165 us -> 188 us
  local copies, waits for them, and re-layouts: 36.3 us -> 27.4 us
    ppermute x3, waiting for transfers between devices: 79.6 us -> 2.1 us  [ring_pieces(): fwd = lax.ppermute(fwd, 'crop', fwd_perm)]
    ppermute x3, waiting for transfers between devices: 0.01 us -> 74.8 us  [ring_pieces(): bwd = lax.ppermute(bwd, 'crop', bwd_perm)]
    all_to_all x1, waiting for transfers between devices: 5.86 us -> 29.4 us  [body(): lax.all_to_all(chosen, 'crop', split_axis=0, concat_axis=0, tiled=True)]
    ppermute x1, waiting for transfers between devices: 11.8 us -> 20.8 us  [ring_pieces(): got.append((lax.ppermute(fwd[:split], 'crop', fwd_perm), src, 0, split))]
    ppermute x3, starting transfers between devices: 2.35 us -> 7.58 us  [ring_pieces(): bwd = lax.ppermute(bwd, 'crop', bwd_perm)]
    ppermute x3, starting transfers between devices: 7.54 us -> 2.6 us  [ring_pieces(): fwd = lax.ppermute(fwd, 'crop', fwd_perm)]
    ppermute x1, waiting for transfers between devices: 4.51 us -> 0.01 us  [ring_pieces(): lax.ppermute(bwd[split:], 'crop', bwd_perm)]
    ppermute x1, starting transfers between devices: 4.44 us -> 0.34 us  [ring_pieces(): got.append((lax.ppermute(fwd[:split], 'crop', fwd_perm), src, 0, split))]
  transfers between devices with their start and end apart: 23 -> 23, of which waited for: 14 -> 12; matrix products, arithmetic and copies ran while one was open for 20% -> 16% of each run, Pallas kernels for 0% -> 0%
where the time goes in v18:
time: 288 us; the launch traced here: 287 us
  waiting for transfers between devices  188 us (65%)
  starting transfers between devices  31.4 us (11%)
  local copies, waits for them, and re-layouts  27.4 us (10%)
  matrix products  21.5 us (7%)
  between operations  10.2 us (4%)
  other arithmetic  8.72 us (3%)
    ppermute x3, waiting for transfers between devices, ring_pieces(): bwd = lax.ppermute(bwd, 'crop', bwd_perm)  74.8 us
    all_to_all x1, waiting for transfers between devices, body(): lax.all_to_all(chosen, 'crop', split_axis=0, concat_axis=0, tiled=True)  29.4 us
    ppermute x3, waiting for transfers between devices, body(): fwd = lax.ppermute(fwd, 'crop', fwd_perm)  26.8 us
    ppermute x1, waiting for transfers between devices, ring_pieces(): got.append((lax.ppermute(fwd[:split], 'crop', fwd_perm), src, 0, split))  20.8 us
    ppermute x3, waiting for transfers between devices, body(): bwd = lax.ppermute(bwd, 'crop', bwd_perm)  17.6 us
    dot_general x9, matrix products, q_part(): jnp.dot(cols, piece, preferred_element_type=jnp.float32)  15.2 us
    unnamed x45, local copies, waits for them, and re-layouts  12.4 us
    ppermute x6, waiting for transfers between devices, head_gather(): part = lax.ppermute(x, 'head', [(j, (j + k) % nhead) for j in range(nhead)])  11.6 us
  transfers between devices with their start and end apart: 23, of which 12 were waited for; matrix products, arithmetic and copies ran while one was open for 16% of the time, Pallas kernels for 0%

profile of v18, /device:TPU:0, one launch (start us, length us, event | category | flops | bytes accessed | tf_op | source)
XLA Modules:
  0.0 286.9 jit_solution(14646124204891050425)
XLA Ops:
  0.0 1.9 pad_maximum_fusion
  2.0 3.0 %collective-permute-start.4 = (bf16[512,2048]{1,0:T(8,128)(2,1)S(1)}, bf16[512,2048]{1,0:T(8,128)(2,1)}, u32[]{:S(2)}, u32[]{:S(2)}) collective-permute-start(bf16[512,2048]{1,0:T(8,128)(2,1)S(1)} %pad_maximum_fusion), channel_id=1, source_target_pairs={{0,4},{8,0},{16,8},{24,16},{28,24},{20,28},{12,20},{4,12},{1,5},{9... | collective-permute-start | bytes 6291464 | tf_op jit(solution)/shard_map/ppermute | solution.py:72
  6.3 44.5 %collective-permute-done.4 = bf16[512,2048]{1,0:T(8,128)(2,1)} collective-permute-done((bf16[512,2048]{1,0:T(8,128)(2,1)S(1)}, bf16[512,2048]{1,0:T(8,128)(2,1)}, u32[]{:S(2)}, u32[]{:S(2)}) %collective-permute-start.4) | collective-permute-done | bytes 2097184 | tf_op jit(solution)/shard_map/ppermute | solution.py:72
  56.9 5.0 %all-to-all-start = ((bf16[8,2,16,1024]{3,2,1,0:T(8,128)(2,1)}), bf16[8,2,16,1024]{3,2,1,0:T(8,128)(2,1)S(1)}, u32[]{:S(2)}, u32[]{:S(2)}) async-start(bf16[8,2,16,1024]{3,2,1,0:T(8,128)(2,1)} %bitcast.2), calls=%async_computation | async-start | bytes 1048576 | tf_op jit(solution)/shard_map/all_to_all | solution.py:59
  74.6 2.5 broadcast_in_dim.35
  80.5 29.4 %all-to-all-done = bf16[8,2,16,1024]{3,2,1,0:T(8,128)(2,1)S(1)} async-done(((bf16[8,2,16,1024]{3,2,1,0:T(8,128)(2,1)}), bf16[8,2,16,1024]{3,2,1,0:T(8,128)(2,1)S(1)}, u32[]{:S(2)}, u32[]{:S(2)}) %all-to-all-start) | async-done | bytes 524320 | tf_op jit(solution)/shard_map/all_to_all | solution.py:59
  111.8 3.1 %constant_dynamic-update-slice_fusion.11 = bf16[512,4096]{1,0:T(8,128)(2,1)} fusion(bf16[512,4096]{1,0:T(8,128)(2,1)} %constant_dynamic-update-slice_fusion.12, bf16[512,1024]{1,0:T(8,128)(2,1)} %collective-permute-done.11, s32[]{:T(128)S(6)} %select_n.163), kind=kLoop, calls=%fused_computation.70 | loop fusion | bytes 2097156 | tf_op jit(solution)/shard_map/dynamic_update_slice | solution.py:52
  116.3 2.4 constant_dynamic-update-slice_fusion.10
  119.8 3.4 %collective-permute-done = bf16[256,1024]{1,0:T(8,128)(2,1)S(1)} collective-permute-done((bf16[256,1024]{1,0:T(8,128)(2,1)S(1)}, bf16[256,1024]{1,0:T(8,128)(2,1)S(1)}, u32[]{:S(2)}, u32[]{:S(2)}) %collective-permute-start) | collective-permute-done | bytes 524320 | tf_op jit(solution)/shard_map/ppermute | solution.py:51
  123.3 2.9 %collective-permute-start.7 = (bf16[512,2048]{1,0:T(8,128)(2,1)}, bf16[512,2048]{1,0:T(8,128)(2,1)S(1)}, u32[]{:S(2)}, u32[]{:S(2)}) collective-permute-start(bf16[512,2048]{1,0:T(8,128)(2,1)} %collective-permute-done.6), channel_id=1, source_target_pairs={{0,4},{8,0},{16,8},{24,16},{28,24},{20,28},{12,20},{4,12},{1,5},{9... | collective-permute-start | bytes 6291464 | tf_op jit(solution)/shard_map/ppermute | solution.py:72
  126.2 8.2 %collective-permute-done.2 = bf16[256,1024]{1,0:T(8,128)(2,1)S(1)} collective-permute-done((bf16[256,1024]{1,0:T(8,128)(2,1)S(1)}, bf16[256,1024]{1,0:T(8,128)(2,1)S(1)}, u32[]{:S(2)}, u32[]{:S(2)}) %collective-permute-start.2) | collective-permute-done | bytes 524320 | tf_op jit(solution)/shard_map/ppermute | solution.py:51
  134.8 1.8 constant_dynamic-update-slice_fusion.7
  136.6 1.8 constant_dynamic-update-slice_fusion.6
  138.4 1.9 constant_dynamic-update-slice_fusion.5
  140.4 30.3 %collective-permute-done.7 = bf16[512,2048]{1,0:T(8,128)(2,1)S(1)} collective-permute-done((bf16[512,2048]{1,0:T(8,128)(2,1)}, bf16[512,2048]{1,0:T(8,128)(2,1)S(1)}, u32[]{:S(2)}, u32[]{:S(2)}) %collective-permute-start.7) | collective-permute-done | bytes 2097184 | tf_op jit(solution)/shard_map/ppermute | solution.py:72
  170.6 2.1 collective-permute-done.8
  175.2 1.8 constant_dynamic-update-slice_fusion.4
  177.2 1.8 collective-permute-start.10
  178.9 1.8 fusion.21
  181.2 17.6 %collective-permute-done.15 = bf16[512,1024]{1,0:T(8,128)(2,1)S(1)} collective-permute-done((bf16[512,1024]{1,0:T(8,128)(2,1)S(1)}, bf16[512,1024]{1,0:T(8,128)(2,1)S(1)}, u32[]{:S(2)}, u32[]{:S(2)}) %collective-permute-start.15) | collective-permute-done | bytes 1048608 | tf_op jit(solution)/shard_map/ppermute | solution.py:106
  200.9 20.8 %collective-permute-done.9 = bf16[256,2048]{1,0:T(8,128)(2,1)S(1)} collective-permute-done((bf16[256,2048]{1,0:T(8,128)(2,1)S(1)}, bf16[256,2048]{1,0:T(8,128)(2,1)S(1)}, u32[]{:S(2)}, u32[]{:S(2)}) %collective-permute-start.9) | collective-permute-done | bytes 1048608 | tf_op jit(solution)/shard_map/ppermute | solution.py:77
  221.9 4.6 %convolution_convert_fusion = bf16[256,2048]{1,0:T(8,128)(2,1)S(1)} fusion(bf16[256,4096]{1,0:T(8,128)(2,1)S(1)} %dynamic-slice_dynamic-update-slice_fusion.7, bf16[4096,2048]{1,0:T(8,128)(2,1)S(1)} %constant_dynamic-update-slice_fusion), kind=kOutput, calls=%fused_computation.6 | convolution fusion | flops 4295491584 | bytes 19922944 | tf_op jit(solution)/shard_map/dot_general | solution.py:94
  226.5 1.8 fusion.17
  228.3 13.0 %collective-permute-done.16 = bf16[512,1024]{1,0:T(8,128)(2,1)S(1)} collective-permute-done((bf16[512,1024]{1,0:T(8,128)(2,1)S(1)}, bf16[512,1024]{1,0:T(8,128)(2,1)S(1)}, u32[]{:S(2)}, u32[]{:S(2)}) %collective-permute-start.16) | collective-permute-done | bytes 1048608 | tf_op jit(solution)/shard_map/ppermute | solution.py:105
  243.0 1.8 fusion.19
  246.7 1.8 convolution_add_fusion.1
  248.5 1.8 fusion.14
  250.9 13.7 %collective-permute-done.18 = bf16[512,1024]{1,0:T(8,128)(2,1)S(1)} collective-permute-done((bf16[512,1024]{1,0:T(8,128)(2,1)S(1)}, bf16[512,1024]{1,0:T(8,128)(2,1)S(1)}, u32[]{:S(2)}, u32[]{:S(2)}) %collective-permute-start.18) | collective-permute-done | bytes 1048608 | tf_op jit(solution)/shard_map/ppermute | solution.py:105
  266.4 1.8 convolution_add_fusion
  268.6 1.8 fusion.11
  270.9 3.8 %collective-permute-done.20 = bf16[256,1024]{1,0:T(8,128)(2,1)S(1)} collective-permute-done((bf16[256,1024]{1,0:T(8,128)(2,1)S(1)}, bf16[256,1024]{1,0:T(8,128)(2,1)S(1)}, u32[]{:S(2)}, u32[]{:S(2)}) %collective-permute-start.20) | collective-permute-done | bytes 524320 | tf_op jit(solution)/shard_map/ppermute | solution.py:111
  280.5 3.5 %fusion.42 = (f32[16,8,32]{2,0,1:T(8,128)S(1)}, f32[16,8,32,256]{3,2,0,1:T(8,128)S(1)}) fusion(f32[8,256,16,32]{1,3,2,0:T(8,128)S(1)} %bitcast.73, pred[16,256]{1,0:T(8,128)(4,1)S(1)} %broadcast_in_dim.33), kind=kOutput, calls=%fused_computation.82 | output fusion | flops 6291711 | bytes 8409088 | tf_op jit(solution)/shard_map/sub | solution.py:129
  (109 shorter events, 39.4 us)
Async XLA Ops:
  0.0 55.5 %copy-start = (bf16[1024,1024]{1,0:T(8,128)(2,1)S(1)}, bf16[1024,1024]{1,0:T(8,128)(2,1)}, u32[]{:S(2)}) copy-start(bf16[1024,1024]{1,0:T(8,128)(2,1)} %param.11) | copy-start | bytes 6291460
  0.0 53.8 %copy-start.4 = (bf16[512,1024]{1,0:T(8,128)(2,1)S(1)}, bf16[512,1024]{1,0:T(8,128)(2,1)}, u32[]{:S(2)}) copy-start(bf16[512,1024]{1,0:T(8,128)(2,1)} %param.10) | copy-start | bytes 3145732
  0.0 55.3 %copy-start.9 = (s32[1,8,2]{1,2,0:T(2,128)S(1)}, s32[1,8,2]{1,2,0:T(2,128)}, u32[]{:S(2)}) copy-start(s32[1,8,2]{1,2,0:T(2,128)} %param.15) | copy-start | bytes 196
  1.9 61.1 %copy-start.11 = (s32[8]{0:T(128)S(1)}, s32[8]{0:T(128)}, u32[]{:S(2)}) copy-start(s32[8]{0:T(128)} %constant.150.clone) | copy-start | bytes 100
  1.9 66.7 %copy-start.7 = (s32[8]{0:T(128)S(1)}, s32[8]{0:T(128)}, u32[]{:S(2)}) copy-start(s32[8]{0:T(128)} %constant.151.clone) | copy-start | bytes 100
  1.9 72.0 %copy-start.8 = (s32[16,8]{0,1:T(8,128)S(1)}, s32[16,8]{0,1:T(8,128)}, u32[]{:S(2)}) copy-start(s32[16,8]{0,1:T(8,128)} %param.16) | copy-start | bytes 1540
  2.0 72.1 %copy-start.10 = (s32[16]{0:T(128)S(1)}, s32[16]{0:T(128)}, u32[]{:S(2)}) copy-start(s32[16]{0:T(128)} %param.17) | copy-start | bytes 196
  2.0 48.8 %collective-permute-start.4 = (bf16[512,2048]{1,0:T(8,128)(2,1)S(1)}, bf16[512,2048]{1,0:T(8,128)(2,1)}, u32[]{:S(2)}, u32[]{:S(2)}) collective-permute-start(bf16[512,2048]{1,0:T(8,128)(2,1)S(1)} %pad_maximum_fusion), channel_id=1, source_target_pairs={{0,4},{8,0},{16,8},{24,16},{28,24},{20,28},{12,20},{4,12},{1,5},{9... | collective-permute-start | bytes 6291464 | tf_op jit(solution)/shard_map/ppermute | solution.py:72
  5.0 47.5 %collective-permute-start.3 = (bf16[512,2048]{1,0:T(8,128)(2,1)S(1)}, bf16[512,2048]{1,0:T(8,128)(2,1)}, u32[]{:S(2)}, u32[]{:S(2)}) collective-permute-start(bf16[512,2048]{1,0:T(8,128)(2,1)S(1)} %pad_maximum_fusion), channel_id=1, source_target_pairs={{0,8},{8,16},{16,24},{24,28},{28,20},{20,12},{12,4},{4,0},{1,9},{9... | collective-permute-start | bytes 6291464 | tf_op jit(solution)/shard_map/ppermute | solution.py:71
  50.8 72.5 %collective-permute-start.6 = (bf16[512,2048]{1,0:T(8,128)(2,1)}, bf16[512,2048]{1,0:T(8,128)(2,1)}, u32[]{:S(2)}, u32[]{:S(2)}) collective-permute-start(bf16[512,2048]{1,0:T(8,128)(2,1)} %collective-permute-done.4), channel_id=1, source_target_pairs={{0,4},{8,0},{16,8},{24,16},{28,24},{20,28},{12,20},{4,12},{1,5},{9... | collective-permute-start | bytes 6291464 | tf_op jit(solution)/shard_map/ppermute | solution.py:72
  52.5 73.7 %collective-permute-start.5 = (bf16[512,2048]{1,0:T(8,128)(2,1)}, bf16[512,2048]{1,0:T(8,128)(2,1)}, u32[]{:S(2)}, u32[]{:S(2)}) collective-permute-start(bf16[512,2048]{1,0:T(8,128)(2,1)} %collective-permute-done.3), channel_id=1, source_target_pairs={{0,8},{8,16},{16,24},{24,28},{28,20},{20,12},{12,4},{4,0},{1,9},{9... | collective-permute-start | bytes 6291464 | tf_op jit(solution)/shard_map/ppermute | solution.py:71
  53.8 56.1 %collective-permute-start.11 = (bf16[512,1024]{1,0:T(8,128)(2,1)S(1)}, bf16[512,1024]{1,0:T(8,128)(2,1)}, u32[]{:S(2)}, u32[]{:S(2)}) collective-permute-start(bf16[512,1024]{1,0:T(8,128)(2,1)S(1)} %copy-done.4), channel_id=1, source_target_pairs={{0,1},{1,2},{2,3},{3,0},{4,5},{5,6},{6,7},{7,4},{8,9},{9,10},{10,1... | collective-permute-start | bytes 3145736 | tf_op jit(solution)/shard_map/ppermute | solution.py:51
  53.8 56.4 %collective-permute-start.12 = (bf16[512,1024]{1,0:T(8,128)(2,1)S(1)}, bf16[512,1024]{1,0:T(8,128)(2,1)}, u32[]{:S(2)}, u32[]{:S(2)}) collective-permute-start(bf16[512,1024]{1,0:T(8,128)(2,1)S(1)} %copy-done.4), channel_id=1, source_target_pairs={{0,2},{1,3},{2,0},{3,1},{4,6},{5,7},{6,4},{7,5},{8,10},{9,11},{10,... | collective-permute-start | bytes 3145736 | tf_op jit(solution)/shard_map/ppermute | solution.py:51
  56.9 53.0 %all-to-all-start = ((bf16[8,2,16,1024]{3,2,1,0:T(8,128)(2,1)}), bf16[8,2,16,1024]{3,2,1,0:T(8,128)(2,1)S(1)}, u32[]{:S(2)}, u32[]{:S(2)}) async-start(bf16[8,2,16,1024]{3,2,1,0:T(8,128)(2,1)} %bitcast.2), calls=%async_computation | async-start | bytes 1048576 | tf_op jit(solution)/shard_map/all_to_all | solution.py:59
  61.9 52.9 %collective-permute-start.13 = (bf16[512,1024]{1,0:T(8,128)(2,1)S(1)}, bf16[512,1024]{1,0:T(8,128)(2,1)S(1)}, u32[]{:S(2)}, u32[]{:S(2)}) collective-permute-start(bf16[512,1024]{1,0:T(8,128)(2,1)S(1)} %copy-done.4), channel_id=1, source_target_pairs={{0,3},{1,0},{2,1},{3,2},{4,7},{5,4},{6,5},{7,6},{8,11},{9,8},{10,9... | collective-permute-start | bytes 3145736 | tf_op jit(solution)/shard_map/ppermute | solution.py:51
  109.9 13.3 %collective-permute-start = (bf16[256,1024]{1,0:T(8,128)(2,1)S(1)}, bf16[256,1024]{1,0:T(8,128)(2,1)S(1)}, u32[]{:S(2)}, u32[]{:S(2)}) collective-permute-start(bf16[256,1024]{1,0:T(8,128)(2,1)S(1)} %bitcast.77), channel_id=1, source_target_pairs={{0,1},{1,2},{2,3},{3,0},{4,5},{5,6},{6,7},{7,4},{8,9},{9,10},{10,1... | collective-permute-start | bytes 1572872 | tf_op jit(solution)/shard_map/ppermute | solution.py:51
  109.9 24.8 %copy-start.6 = (bf16[4096,2048]{1,0:T(8,128)(2,1)S(1)}, bf16[4096,2048]{1,0:T(8,128)(2,1)}, u32[]{:S(2)}) copy-start(bf16[4096,2048]{1,0:T(8,128)(2,1)} %constant_dynamic-update-slice_fusion.8) | copy-start | bytes 50331652
  110.2 15.9 %collective-permute-start.1 = (bf16[256,1024]{1,0:T(8,128)(2,1)S(1)}, bf16[256,1024]{1,0:T(8,128)(2,1)S(1)}, u32[]{:S(2)}, u32[]{:S(2)}) collective-permute-start(bf16[256,1024]{1,0:T(8,128)(2,1)S(1)} %bitcast.79), channel_id=1, source_target_pairs={{0,2},{1,3},{2,0},{3,1},{4,6},{5,7},{6,4},{7,5},{8,10},{9,11},{10,... | collective-permute-start | bytes 1572872 | tf_op jit(solution)/shard_map/ppermute | solution.py:51
  114.9 19.5 %collective-permute-start.2 = (bf16[256,1024]{1,0:T(8,128)(2,1)S(1)}, bf16[256,1024]{1,0:T(8,128)(2,1)S(1)}, u32[]{:S(2)}, u32[]{:S(2)}) collective-permute-start(bf16[256,1024]{1,0:T(8,128)(2,1)S(1)} %bitcast.80), channel_id=1, source_target_pairs={{0,3},{1,0},{2,1},{3,2},{4,7},{5,4},{6,5},{7,6},{8,11},{9,8},{10,9... | collective-permute-start | bytes 1572872 | tf_op jit(solution)/shard_map/ppermute | solution.py:51
  123.3 47.4 %collective-permute-start.7 = (bf16[512,2048]{1,0:T(8,128)(2,1)}, bf16[512,2048]{1,0:T(8,128)(2,1)S(1)}, u32[]{:S(2)}, u32[]{:S(2)}) collective-permute-start(bf16[512,2048]{1,0:T(8,128)(2,1)} %collective-permute-done.6), channel_id=1, source_target_pairs={{0,4},{8,0},{16,8},{24,16},{28,24},{20,28},{12,20},{4,12},{1,5},{9... | collective-permute-start | bytes 6291464 | tf_op jit(solution)/shard_map/ppermute | solution.py:72
  126.1 46.6 %collective-permute-start.8 = (bf16[512,2048]{1,0:T(8,128)(2,1)}, bf16[512,2048]{1,0:T(8,128)(2,1)S(1)}, u32[]{:S(2)}, u32[]{:S(2)}) collective-permute-start(bf16[512,2048]{1,0:T(8,128)(2,1)} %collective-permute-done.5), channel_id=1, source_target_pairs={{0,8},{8,16},{16,24},{24,28},{28,20},{20,12},{12,4},{4,0},{1,9},{9... | collective-permute-start | bytes 6291464 | tf_op jit(solution)/shard_map/ppermute | solution.py:71
  138.4 34.3 %copy-start.5 = (bf16[512,1024]{1,0:T(8,128)(2,1)S(1)}, bf16[512,1024]{1,0:T(8,128)(2,1)}, u32[]{:S(2)}) copy-start(bf16[512,1024]{1,0:T(8,128)(2,1)} %param.12) | copy-start | bytes 3145732
  172.7 26.1 %collective-permute-start.15 = (bf16[512,1024]{1,0:T(8,128)(2,1)S(1)}, bf16[512,1024]{1,0:T(8,128)(2,1)S(1)}, u32[]{:S(2)}, u32[]{:S(2)}) collective-permute-start(bf16[512,1024]{1,0:T(8,128)(2,1)S(1)} %copy-done.5), channel_id=1, source_target_pairs={{0,4},{8,0},{16,8},{24,16},{28,24},{20,28},{12,20},{4,12},{1,5},{9... | collective-permute-start | bytes 3145736 | tf_op jit(solution)/shard_map/ppermute | solution.py:106
  173.1 26.1 %collective-permute-start.14 = (bf16[512,1024]{1,0:T(8,128)(2,1)S(1)}, bf16[512,1024]{1,0:T(8,128)(2,1)S(1)}, u32[]{:S(2)}, u32[]{:S(2)}) collective-permute-start(bf16[512,1024]{1,0:T(8,128)(2,1)S(1)} %copy-done.5), channel_id=1, source_target_pairs={{0,8},{8,16},{16,24},{24,28},{28,20},{20,12},{12,4},{4,0},{1,9},{9... | collective-permute-start | bytes 3145736 | tf_op jit(solution)/shard_map/ppermute | solution.py:105
  174.9 46.8 %collective-permute-start.9 = (bf16[256,2048]{1,0:T(8,128)(2,1)S(1)}, bf16[256,2048]{1,0:T(8,128)(2,1)S(1)}, u32[]{:S(2)}, u32[]{:S(2)}) collective-permute-start(bf16[256,2048]{1,0:T(8,128)(2,1)S(1)} %slice.26), channel_id=1, source_target_pairs={{0,8},{8,16},{16,24},{24,28},{28,20},{20,12},{12,4},{4,0},{1,9},{9... | collective-permute-start | bytes 3145736 | tf_op jit(solution)/shard_map/ppermute | solution.py:77
  177.2 44.6 %collective-permute-start.10 = (bf16[256,2048]{1,0:T(8,128)(2,1)S(1)}, bf16[256,2048]{1,0:T(8,128)(2,1)S(1)}, u32[]{:S(2)}, u32[]{:S(2)}) collective-permute-start(bf16[256,2048]{1,0:T(8,128)(2,1)S(1)} %slice.27), channel_id=1, source_target_pairs={{0,4},{8,0},{16,8},{24,16},{28,24},{20,28},{12,20},{4,12},{1,5},{9... | collective-permute-start | bytes 3145736 | tf_op jit(solution)/shard_map/ppermute | solution.py:78
  198.8 46.0 %collective-permute-start.17 = (bf16[512,1024]{1,0:T(8,128)(2,1)S(1)}, bf16[512,1024]{1,0:T(8,128)(2,1)S(1)}, u32[]{:S(2)}, u32[]{:S(2)}) collective-permute-start(bf16[512,1024]{1,0:T(8,128)(2,1)S(1)} %collective-permute-done.15), channel_id=1, source_target_pairs={{0,4},{8,0},{16,8},{24,16},{28,24},{20,28},{12,20},{4,12},{1,5},{9... | collective-permute-start | bytes 3145736 | tf_op jit(solution)/shard_map/ppermute | solution.py:106
  199.2 42.2 %collective-permute-start.16 = (bf16[512,1024]{1,0:T(8,128)(2,1)S(1)}, bf16[512,1024]{1,0:T(8,128)(2,1)S(1)}, u32[]{:S(2)}, u32[]{:S(2)}) collective-permute-start(bf16[512,1024]{1,0:T(8,128)(2,1)S(1)} %collective-permute-done.14), channel_id=1, source_target_pairs={{0,8},{8,16},{16,24},{24,28},{28,20},{20,12},{12,4},{4,0},{1,9},{9... | collective-permute-start | bytes 3145736 | tf_op jit(solution)/shard_map/ppermute | solution.py:105
  241.4 23.2 %collective-permute-start.18 = (bf16[512,1024]{1,0:T(8,128)(2,1)S(1)}, bf16[512,1024]{1,0:T(8,128)(2,1)S(1)}, u32[]{:S(2)}, u32[]{:S(2)}) collective-permute-start(bf16[512,1024]{1,0:T(8,128)(2,1)S(1)} %collective-permute-done.16), channel_id=1, source_target_pairs={{0,8},{8,16},{16,24},{24,28},{28,20},{20,12},{12,4},{4,0},{1,9},{9... | collective-permute-start | bytes 3145736 | tf_op jit(solution)/shard_map/ppermute | solution.py:105
  244.8 23.3 %collective-permute-start.19 = (bf16[512,1024]{1,0:T(8,128)(2,1)S(1)}, bf16[512,1024]{1,0:T(8,128)(2,1)S(1)}, u32[]{:S(2)}, u32[]{:S(2)}) collective-permute-start(bf16[512,1024]{1,0:T(8,128)(2,1)S(1)} %collective-permute-done.17), channel_id=1, source_target_pairs={{0,4},{8,0},{16,8},{24,16},{28,24},{20,28},{12,20},{4,12},{1,5},{9... | collective-permute-start | bytes 3145736 | tf_op jit(solution)/shard_map/ppermute | solution.py:106
  264.6 10.1 %collective-permute-start.20 = (bf16[256,1024]{1,0:T(8,128)(2,1)S(1)}, bf16[256,1024]{1,0:T(8,128)(2,1)S(1)}, u32[]{:S(2)}, u32[]{:S(2)}) collective-permute-start(bf16[256,1024]{1,0:T(8,128)(2,1)S(1)} %slice.30), channel_id=1, source_target_pairs={{0,8},{8,16},{16,24},{24,28},{28,20},{20,12},{12,4},{4,0},{1,9},{9... | collective-permute-start | bytes 1572872 | tf_op jit(solution)/shard_map/ppermute | solution.py:111
  268.2 9.2 %collective-permute-start.21 = (bf16[256,1024]{1,0:T(8,128)(2,1)S(1)}, bf16[256,1024]{1,0:T(8,128)(2,1)S(1)}, u32[]{:S(2)}, u32[]{:S(2)}) collective-permute-start(bf16[256,1024]{1,0:T(8,128)(2,1)S(1)} %slice.31), channel_id=1, source_target_pairs={{0,4},{8,0},{16,8},{24,16},{28,24},{20,28},{12,20},{4,12},{1,5},{9... | collective-permute-start | bytes 1572872 | tf_op jit(solution)/shard_map/ppermute | solution.py:112
  (3 other events, 8.0 us)

commit v19 on v15

--- a/solution.py
+++ b/solution.py
@@ -120,14 +120,14 @@
     member = jnp.repeat(member, CT, axis=1)
     scale = 1.0 / HD**0.5
     scores = (
-        jnp.einsum("rghe,khe->rhgk", query_row, keys_all, preferred_element_type=jnp.float32)
+        jnp.einsum("rghe,khe->rghk", query_row, keys_all, preferred_element_type=jnp.float32)
         * scale
     )
     scores = jnp.where(member[:, None, None, :], scores, jnp.float32(-1e30))
     top = jnp.max(scores, axis=-1, keepdims=True)
     expo = jnp.exp(scores - top)
     weights = (expo / jnp.sum(expo, axis=-1, keepdims=True)).astype(jnp.bfloat16)
-    result = jnp.einsum("rhgk,khe->rghe", weights, vals_all, preferred_element_type=jnp.float32)
+    result = jnp.einsum("rghk,khe->rghe", weights, vals_all, preferred_element_type=jnp.float32)
     return result.astype(jnp.bfloat16).reshape(rows_here * GR, width)
 
 

time: 275 us -> 275 us (level)
  no operation moved by 1% of the time
where the time goes in v19:
time: 275 us; the launch traced here: 274 us
  waiting for transfers between devices  165 us (60%)
  local copies, waits for them, and re-layouts  35.6 us (13%)
  starting transfers between devices  33.6 us (12%)
  matrix products  21.2 us (8%)
  between operations  9.32 us (3%)
  other arithmetic  9.14 us (3%)
    ppermute x3, waiting for transfers between devices, ring_pieces(): fwd = lax.ppermute(fwd, 'crop', fwd_perm)  79.6 us
    ppermute x3, waiting for transfers between devices, body(): fwd = lax.ppermute(fwd, 'crop', fwd_perm)  27 us
    ppermute x3, waiting for transfers between devices, body(): bwd = lax.ppermute(bwd, 'crop', bwd_perm)  17.7 us
    unnamed x41, local copies, waits for them, and re-layouts  15.8 us
    dot_general x9, matrix products, q_part(): jnp.dot(cols, piece, preferred_element_type=jnp.float32)  15.2 us
    ppermute x6, waiting for transfers between devices, head_gather(): part = lax.ppermute(x, 'head', [(j, (j + k) % nhead) for j in range(nhead)])  13.2 us
    ppermute x1, waiting for transfers between devices, ring_pieces(): got.append((lax.ppermute(fwd[:split], 'crop', fwd_perm), src, 0, split))  12.2 us
    dynamic_update_slice x6, local copies, waits for them, and re-layouts, head_gather(): lax.dynamic_update_slice(full, part, (0, (hme - k) % nhead * x.shape[1]))  7.97 us
  transfers between devices with their start and end apart: 23, of which 14 were waited for; matrix products, arithmetic and copies ran while one was open for 20% of the time, Pallas kernels for 0%

profile of v19, /device:TPU:0, one launch (start us, length us, event | category | flops | bytes accessed | tf_op | source)
XLA Modules:
  0.0 274.3 jit_solution(12408441465103024194)
XLA Ops:
  0.0 1.9 pad_maximum_fusion
  2.0 3.1 %collective-permute-start.3 = (bf16[512,2048]{1,0:T(8,128)(2,1)S(1)}, bf16[512,2048]{1,0:T(8,128)(2,1)}, u32[]{:S(2)}, u32[]{:S(2)}) collective-permute-start(bf16[512,2048]{1,0:T(8,128)(2,1)S(1)} %pad_maximum_fusion), channel_id=1, source_target_pairs={{0,8},{8,16},{16,24},{24,28},{28,20},{20,12},{12,4},{4,0},{1,9},{9... | collective-permute-start | bytes 6291464 | tf_op jit(solution)/shard_map/ppermute | solution.py:71
  6.2 44.5 %collective-permute-done.3 = bf16[512,2048]{1,0:T(8,128)(2,1)} collective-permute-done((bf16[512,2048]{1,0:T(8,128)(2,1)S(1)}, bf16[512,2048]{1,0:T(8,128)(2,1)}, u32[]{:S(2)}, u32[]{:S(2)}) %collective-permute-start.3) | collective-permute-done | bytes 2097184 | tf_op jit(solution)/shard_map/ppermute | solution.py:71
  56.8 5.1 %all-to-all-start = ((bf16[8,2,16,1024]{3,2,1,0:T(8,128)(2,1)}), bf16[8,2,16,1024]{3,2,1,0:T(8,128)(2,1)S(1)}, u32[]{:S(2)}, u32[]{:S(2)}) async-start(bf16[8,2,16,1024]{3,2,1,0:T(8,128)(2,1)} %bitcast.2), calls=%async_computation | async-start | bytes 1048576 | tf_op jit(solution)/shard_map/all_to_all | solution.py:59
  73.7 3.2 %constant_dynamic-update-slice_fusion.8 = bf16[4096,2048]{1,0:T(8,128)(2,1)} fusion(bf16[512,2048]{1,0:T(8,128)(2,1)} %copy-done.2), kind=kLoop, calls=%fused_computation.56 | loop fusion | bytes 4194304
  76.9 23.3 %collective-permute-done.5 = bf16[512,2048]{1,0:T(8,128)(2,1)} collective-permute-done((bf16[512,2048]{1,0:T(8,128)(2,1)}, bf16[512,2048]{1,0:T(8,128)(2,1)}, u32[]{:S(2)}, u32[]{:S(2)}) %collective-permute-start.5) | collective-permute-done | bytes 2097184 | tf_op jit(solution)/shard_map/ppermute | solution.py:71
  100.2 2.7 collective-permute-start.7
  102.9 2.5 broadcast_in_dim.35
  105.3 2.4 constant_dynamic-update-slice_fusion.12
  107.7 5.9 %all-to-all-done = bf16[8,2,16,1024]{3,2,1,0:T(8,128)(2,1)S(1)} async-done(((bf16[8,2,16,1024]{3,2,1,0:T(8,128)(2,1)}), bf16[8,2,16,1024]{3,2,1,0:T(8,128)(2,1)S(1)}, u32[]{:S(2)}, u32[]{:S(2)}) %all-to-all-start) | async-done | bytes 524320 | tf_op jit(solution)/shard_map/all_to_all | solution.py:59
  115.4 2.5 constant_dynamic-update-slice_fusion.11
  119.3 3.0 %constant_dynamic-update-slice_fusion.10 = bf16[512,4096]{1,0:T(8,128)(2,1)} fusion(bf16[512,4096]{1,0:T(8,128)(2,1)} %constant_dynamic-update-slice_fusion.11, bf16[512,1024]{1,0:T(8,128)(2,1)} %collective-permute-done.12, s32[]{:T(128)S(6)} %select_n.165), kind=kLoop, calls=%fused_computation.68 | loop fusion | bytes 2097156 | tf_op jit(solution)/shard_map/dynamic_update_slice | solution.py:52
  122.4 2.3 constant_dynamic-update-slice_fusion.9
  124.7 2.2 collective-permute-done
  126.9 1.8 collective-permute-done.1
  128.8 9.3 %collective-permute-done.2 = bf16[256,1024]{1,0:T(8,128)(2,1)S(1)} collective-permute-done((bf16[256,1024]{1,0:T(8,128)(2,1)S(1)}, bf16[256,1024]{1,0:T(8,128)(2,1)S(1)}, u32[]{:S(2)}, u32[]{:S(2)}) %collective-permute-start.2) | collective-permute-done | bytes 524320 | tf_op jit(solution)/shard_map/ppermute | solution.py:51
  138.4 11.8 %collective-permute-done.7 = bf16[512,2048]{1,0:T(8,128)(2,1)} collective-permute-done((bf16[512,2048]{1,0:T(8,128)(2,1)}, bf16[512,2048]{1,0:T(8,128)(2,1)}, u32[]{:S(2)}, u32[]{:S(2)}) %collective-permute-start.7) | collective-permute-done | bytes 2097184 | tf_op jit(solution)/shard_map/ppermute | solution.py:71
  151.5 4.4 %collective-permute-start.10 = (bf16[256,2048]{1,0:T(8,128)(2,1)S(1)}, bf16[256,2048]{1,0:T(8,128)(2,1)S(1)}, u32[]{:S(2)}, u32[]{:S(2)}) collective-permute-start(bf16[256,2048]{1,0:T(8,128)(2,1)S(1)} %slice.27), channel_id=1, source_target_pairs={{0,8},{8,16},{16,24},{24,28},{28,20},{20,12},{12,4},{4,0},{1,9},{9... | collective-permute-start | bytes 3145736 | tf_op jit(solution)/shard_map/ppermute | solution.py:77
  162.6 1.8 constant_dynamic-update-slice_fusion.4
  164.4 12.2 %collective-permute-done.10 = bf16[256,2048]{1,0:T(8,128)(2,1)S(1)} collective-permute-done((bf16[256,2048]{1,0:T(8,128)(2,1)S(1)}, bf16[256,2048]{1,0:T(8,128)(2,1)S(1)}, u32[]{:S(2)}, u32[]{:S(2)}) %collective-permute-start.10) | collective-permute-done | bytes 1048608 | tf_op jit(solution)/shard_map/ppermute | solution.py:77
  176.6 4.5 %collective-permute-done.9 = bf16[256,2048]{1,0:T(8,128)(2,1)S(1)} collective-permute-done((bf16[256,2048]{1,0:T(8,128)(2,1)S(1)}, bf16[256,2048]{1,0:T(8,128)(2,1)S(1)}, u32[]{:S(2)}, u32[]{:S(2)}) %collective-permute-start.9) | collective-permute-done | bytes 1048608 | tf_op jit(solution)/shard_map/ppermute | solution.py:78
  181.1 2.0 collective-permute-start.14
  186.8 17.7 %collective-permute-done.15 = bf16[512,1024]{1,0:T(8,128)(2,1)S(1)} collective-permute-done((bf16[512,1024]{1,0:T(8,128)(2,1)S(1)}, bf16[512,1024]{1,0:T(8,128)(2,1)S(1)}, u32[]{:S(2)}, u32[]{:S(2)}) %collective-permute-start.15) | collective-permute-done | bytes 1048608 | tf_op jit(solution)/shard_map/ppermute | solution.py:105
  204.4 2.0 collective-permute-start.16
  206.5 4.6 %convolution_convert_fusion = bf16[256,2048]{1,0:T(8,128)(2,1)S(1)} fusion(bf16[256,4096]{1,0:T(8,128)(2,1)S(1)} %dynamic-slice_dynamic-update-slice_fusion.7, bf16[4096,2048]{1,0:T(8,128)(2,1)S(1)} %constant_dynamic-update-slice_fusion), kind=kOutput, calls=%fused_computation.6 | convolution fusion | flops 4295491584 | bytes 19922944 | tf_op jit(solution)/shard_map/dot_general | solution.py:93
  213.2 14.6 %collective-permute-done.16 = bf16[512,1024]{1,0:T(8,128)(2,1)S(1)} collective-permute-done((bf16[512,1024]{1,0:T(8,128)(2,1)S(1)}, bf16[512,1024]{1,0:T(8,128)(2,1)S(1)}, u32[]{:S(2)}, u32[]{:S(2)}) %collective-permute-start.16) | collective-permute-done | bytes 1048608 | tf_op jit(solution)/shard_map/ppermute | solution.py:104
  227.8 2.0 collective-permute-start.18
  238.6 12.4 %collective-permute-done.18 = bf16[512,1024]{1,0:T(8,128)(2,1)S(1)} collective-permute-done((bf16[512,1024]{1,0:T(8,128)(2,1)S(1)}, bf16[512,1024]{1,0:T(8,128)(2,1)S(1)}, u32[]{:S(2)}, u32[]{:S(2)}) %collective-permute-start.18) | collective-permute-done | bytes 1048608 | tf_op jit(solution)/shard_map/ppermute | solution.py:104
  251.0 2.1 collective-permute-start.20
  257.2 3.1 %collective-permute-done.20 = bf16[256,1024]{1,0:T(8,128)(2,1)S(1)} collective-permute-done((bf16[256,1024]{1,0:T(8,128)(2,1)S(1)}, bf16[256,1024]{1,0:T(8,128)(2,1)S(1)}, u32[]{:S(2)}, u32[]{:S(2)}) %collective-permute-start.20) | collective-permute-done | bytes 524320 | tf_op jit(solution)/shard_map/ppermute | solution.py:110
  262.1 2.1 collective-permute-done.21
  267.2 3.5 %fusion.40 = (f32[16,32,8]{1,0,2:T(8,128)S(1)}, f32[16,32,8,256]{3,1,0,2:T(8,128)S(1)}) fusion(f32[8,256,16,32]{1,3,2,0:T(8,128)S(1)} %bitcast.78, pred[16,256]{1,0:T(8,128)(4,1)S(1)} %broadcast_in_dim.33), kind=kOutput, calls=%fused_computation.81 | output fusion | flops 6291711 | bytes 8409088 | tf_op jit(solution)/shard_map/sub | solution.py:128
  (107 shorter events, 48.5 us)
Async XLA Ops:
  0.0 55.4 %copy-start = (bf16[1024,1024]{1,0:T(8,128)(2,1)S(1)}, bf16[1024,1024]{1,0:T(8,128)(2,1)}, u32[]{:S(2)}) copy-start(bf16[1024,1024]{1,0:T(8,128)(2,1)} %param.11) | copy-start | bytes 6291460
  0.0 55.2 %copy-start.7 = (s32[1,8,2]{1,2,0:T(2,128)S(1)}, s32[1,8,2]{1,2,0:T(2,128)}, u32[]{:S(2)}) copy-start(s32[1,8,2]{1,2,0:T(2,128)} %param.15) | copy-start | bytes 196
  1.9 3.1 %copy-start.2 = (bf16[512,2048]{1,0:T(8,128)(2,1)}, bf16[512,2048]{1,0:T(8,128)(2,1)S(1)}, u32[]{:S(2)}) copy-start(bf16[512,2048]{1,0:T(8,128)(2,1)S(1)} %pad_maximum_fusion) | copy-start | bytes 6291460
  1.9 61.1 %copy-start.9 = (s32[8]{0:T(128)S(1)}, s32[8]{0:T(128)}, u32[]{:S(2)}) copy-start(s32[8]{0:T(128)} %constant.150.clone) | copy-start | bytes 100
  1.9 66.1 %copy-start.5 = (s32[8]{0:T(128)S(1)}, s32[8]{0:T(128)}, u32[]{:S(2)}) copy-start(s32[8]{0:T(128)} %constant.151.clone) | copy-start | bytes 100
  2.0 71.2 %copy-start.6 = (s32[16,8]{0,1:T(8,128)S(1)}, s32[16,8]{0,1:T(8,128)}, u32[]{:S(2)}) copy-start(s32[16,8]{0,1:T(8,128)} %param.16) | copy-start | bytes 1540
  2.0 71.2 %copy-start.8 = (s32[16]{0:T(128)S(1)}, s32[16]{0:T(128)}, u32[]{:S(2)}) copy-start(s32[16]{0:T(128)} %param.17) | copy-start | bytes 196
  2.0 48.8 %collective-permute-start.3 = (bf16[512,2048]{1,0:T(8,128)(2,1)S(1)}, bf16[512,2048]{1,0:T(8,128)(2,1)}, u32[]{:S(2)}, u32[]{:S(2)}) collective-permute-start(bf16[512,2048]{1,0:T(8,128)(2,1)S(1)} %pad_maximum_fusion), channel_id=1, source_target_pairs={{0,8},{8,16},{16,24},{24,28},{28,20},{20,12},{12,4},{4,0},{1,9},{9... | collective-permute-start | bytes 6291464 | tf_op jit(solution)/shard_map/ppermute | solution.py:71
  5.1 47.5 %collective-permute-start.4 = (bf16[512,2048]{1,0:T(8,128)(2,1)S(1)}, bf16[512,2048]{1,0:T(8,128)(2,1)}, u32[]{:S(2)}, u32[]{:S(2)}) collective-permute-start(bf16[512,2048]{1,0:T(8,128)(2,1)S(1)} %pad_maximum_fusion), channel_id=1, source_target_pairs={{0,4},{8,0},{16,8},{24,16},{28,24},{20,28},{12,20},{4,12},{1,5},{9... | collective-permute-start | bytes 6291464 | tf_op jit(solution)/shard_map/ppermute | solution.py:72
  50.7 49.5 %collective-permute-start.5 = (bf16[512,2048]{1,0:T(8,128)(2,1)}, bf16[512,2048]{1,0:T(8,128)(2,1)}, u32[]{:S(2)}, u32[]{:S(2)}) collective-permute-start(bf16[512,2048]{1,0:T(8,128)(2,1)} %collective-permute-done.3), channel_id=1, source_target_pairs={{0,8},{8,16},{16,24},{24,28},{28,20},{20,12},{12,4},{4,0},{1,9},{9... | collective-permute-start | bytes 6291464 | tf_op jit(solution)/shard_map/ppermute | solution.py:71
  52.5 50.3 %collective-permute-start.6 = (bf16[512,2048]{1,0:T(8,128)(2,1)}, bf16[512,2048]{1,0:T(8,128)(2,1)}, u32[]{:S(2)}, u32[]{:S(2)}) collective-permute-start(bf16[512,2048]{1,0:T(8,128)(2,1)} %collective-permute-done.4), channel_id=1, source_target_pairs={{0,4},{8,0},{16,8},{24,16},{28,24},{20,28},{12,20},{4,12},{1,5},{9... | collective-permute-start | bytes 6291464 | tf_op jit(solution)/shard_map/ppermute | solution.py:72
  53.7 59.9 %collective-permute-start.11 = (bf16[512,1024]{1,0:T(8,128)(2,1)}, bf16[512,1024]{1,0:T(8,128)(2,1)}, u32[]{:S(2)}, u32[]{:S(2)}) collective-permute-start(bf16[512,1024]{1,0:T(8,128)(2,1)} %param.10), channel_id=1, source_target_pairs={{0,1},{1,2},{2,3},{3,0},{4,5},{5,6},{6,7},{7,4},{8,9},{9,10},{10,1... | collective-permute-start | bytes 3145736 | tf_op jit(solution)/shard_map/ppermute | solution.py:51
  53.7 60.2 %collective-permute-start.12 = (bf16[512,1024]{1,0:T(8,128)(2,1)}, bf16[512,1024]{1,0:T(8,128)(2,1)}, u32[]{:S(2)}, u32[]{:S(2)}) collective-permute-start(bf16[512,1024]{1,0:T(8,128)(2,1)} %param.10), channel_id=1, source_target_pairs={{0,2},{1,3},{2,0},{3,1},{4,6},{5,7},{6,4},{7,5},{8,10},{9,11},{10,... | collective-permute-start | bytes 3145736 | tf_op jit(solution)/shard_map/ppermute | solution.py:51
  56.8 56.8 %all-to-all-start = ((bf16[8,2,16,1024]{3,2,1,0:T(8,128)(2,1)}), bf16[8,2,16,1024]{3,2,1,0:T(8,128)(2,1)S(1)}, u32[]{:S(2)}, u32[]{:S(2)}) async-start(bf16[8,2,16,1024]{3,2,1,0:T(8,128)(2,1)} %bitcast.2), calls=%async_computation | async-start | bytes 1048576 | tf_op jit(solution)/shard_map/all_to_all | solution.py:59
  61.9 56.0 %collective-permute-start.13 = (bf16[512,1024]{1,0:T(8,128)(2,1)}, bf16[512,1024]{1,0:T(8,128)(2,1)}, u32[]{:S(2)}, u32[]{:S(2)}) collective-permute-start(bf16[512,1024]{1,0:T(8,128)(2,1)} %param.10), channel_id=1, source_target_pairs={{0,3},{1,0},{2,1},{3,2},{4,7},{5,4},{6,5},{7,6},{8,11},{9,8},{10,9... | collective-permute-start | bytes 3145736 | tf_op jit(solution)/shard_map/ppermute | solution.py:51
  100.2 50.0 %collective-permute-start.7 = (bf16[512,2048]{1,0:T(8,128)(2,1)}, bf16[512,2048]{1,0:T(8,128)(2,1)}, u32[]{:S(2)}, u32[]{:S(2)}) collective-permute-start(bf16[512,2048]{1,0:T(8,128)(2,1)} %collective-permute-done.5), channel_id=1, source_target_pairs={{0,8},{8,16},{16,24},{24,28},{28,20},{20,12},{12,4},{4,0},{1,9},{9... | collective-permute-start | bytes 6291464 | tf_op jit(solution)/shard_map/ppermute | solution.py:71
  102.9 53.1 %collective-permute-start.8 = (bf16[512,2048]{1,0:T(8,128)(2,1)}, bf16[512,2048]{1,0:T(8,128)(2,1)}, u32[]{:S(2)}, u32[]{:S(2)}) collective-permute-start(bf16[512,2048]{1,0:T(8,128)(2,1)} %collective-permute-done.6), channel_id=1, source_target_pairs={{0,4},{8,0},{16,8},{24,16},{28,24},{20,28},{12,20},{4,12},{1,5},{9... | collective-permute-start | bytes 6291464 | tf_op jit(solution)/shard_map/ppermute | solution.py:72
  113.6 13.3 %collective-permute-start = (bf16[256,1024]{1,0:T(8,128)(2,1)S(1)}, bf16[256,1024]{1,0:T(8,128)(2,1)S(1)}, u32[]{:S(2)}, u32[]{:S(2)}) collective-permute-start(bf16[256,1024]{1,0:T(8,128)(2,1)S(1)} %bitcast.83), channel_id=1, source_target_pairs={{0,1},{1,2},{2,3},{3,0},{4,5},{5,6},{6,7},{7,4},{8,9},{9,10},{10,1... | collective-permute-start | bytes 1572872 | tf_op jit(solution)/shard_map/ppermute | solution.py:51
  113.9 14.8 %collective-permute-start.1 = (bf16[256,1024]{1,0:T(8,128)(2,1)S(1)}, bf16[256,1024]{1,0:T(8,128)(2,1)S(1)}, u32[]{:S(2)}, u32[]{:S(2)}) collective-permute-start(bf16[256,1024]{1,0:T(8,128)(2,1)S(1)} %bitcast.85), channel_id=1, source_target_pairs={{0,2},{1,3},{2,0},{3,1},{4,6},{5,7},{6,4},{7,5},{8,10},{9,11},{10,... | collective-permute-start | bytes 1572872 | tf_op jit(solution)/shard_map/ppermute | solution.py:51
  115.4 41.9 %copy-start.4 = (bf16[4096,2048]{1,0:T(8,128)(2,1)S(1)}, bf16[4096,2048]{1,0:T(8,128)(2,1)}, u32[]{:S(2)}) copy-start(bf16[4096,2048]{1,0:T(8,128)(2,1)} %constant_dynamic-update-slice_fusion.8) | copy-start | bytes 50331652
  117.9 20.1 %collective-permute-start.2 = (bf16[256,1024]{1,0:T(8,128)(2,1)S(1)}, bf16[256,1024]{1,0:T(8,128)(2,1)S(1)}, u32[]{:S(2)}, u32[]{:S(2)}) collective-permute-start(bf16[256,1024]{1,0:T(8,128)(2,1)S(1)} %bitcast.86), channel_id=1, source_target_pairs={{0,3},{1,0},{2,1},{3,2},{4,7},{5,4},{6,5},{7,6},{8,11},{9,8},{10,9... | collective-permute-start | bytes 1572872 | tf_op jit(solution)/shard_map/ppermute | solution.py:51
  151.5 25.1 %collective-permute-start.10 = (bf16[256,2048]{1,0:T(8,128)(2,1)S(1)}, bf16[256,2048]{1,0:T(8,128)(2,1)S(1)}, u32[]{:S(2)}, u32[]{:S(2)}) collective-permute-start(bf16[256,2048]{1,0:T(8,128)(2,1)S(1)} %slice.27), channel_id=1, source_target_pairs={{0,8},{8,16},{16,24},{24,28},{28,20},{20,12},{12,4},{4,0},{1,9},{9... | collective-permute-start | bytes 3145736 | tf_op jit(solution)/shard_map/ppermute | solution.py:77
  157.3 23.8 %collective-permute-start.9 = (bf16[256,2048]{1,0:T(8,128)(2,1)S(1)}, bf16[256,2048]{1,0:T(8,128)(2,1)S(1)}, u32[]{:S(2)}, u32[]{:S(2)}) collective-permute-start(bf16[256,2048]{1,0:T(8,128)(2,1)S(1)} %slice.26), channel_id=1, source_target_pairs={{0,4},{8,0},{16,8},{24,16},{28,24},{20,28},{12,20},{4,12},{1,5},{9... | collective-permute-start | bytes 3145736 | tf_op jit(solution)/shard_map/ppermute | solution.py:78
  162.5 18.6 %copy-start.3 = (bf16[512,1024]{1,0:T(8,128)(2,1)S(1)}, bf16[512,1024]{1,0:T(8,128)(2,1)}, u32[]{:S(2)}) copy-start(bf16[512,1024]{1,0:T(8,128)(2,1)} %param.12) | copy-start | bytes 3145732
  181.1 23.3 %collective-permute-start.15 = (bf16[512,1024]{1,0:T(8,128)(2,1)S(1)}, bf16[512,1024]{1,0:T(8,128)(2,1)S(1)}, u32[]{:S(2)}, u32[]{:S(2)}) collective-permute-start(bf16[512,1024]{1,0:T(8,128)(2,1)S(1)} %copy-done.3), channel_id=1, source_target_pairs={{0,4},{8,0},{16,8},{24,16},{28,24},{20,28},{12,20},{4,12},{1,5},{9... | collective-permute-start | bytes 3145736 | tf_op jit(solution)/shard_map/ppermute | solution.py:105
  181.1 23.3 %collective-permute-start.14 = (bf16[512,1024]{1,0:T(8,128)(2,1)S(1)}, bf16[512,1024]{1,0:T(8,128)(2,1)S(1)}, u32[]{:S(2)}, u32[]{:S(2)}) collective-permute-start(bf16[512,1024]{1,0:T(8,128)(2,1)S(1)} %copy-done.3), channel_id=1, source_target_pairs={{0,8},{8,16},{16,24},{24,28},{28,20},{20,12},{12,4},{4,0},{1,9},{9... | collective-permute-start | bytes 3145736 | tf_op jit(solution)/shard_map/ppermute | solution.py:104
  204.4 27.1 %collective-permute-start.17 = (bf16[512,1024]{1,0:T(8,128)(2,1)S(1)}, bf16[512,1024]{1,0:T(8,128)(2,1)S(1)}, u32[]{:S(2)}, u32[]{:S(2)}) collective-permute-start(bf16[512,1024]{1,0:T(8,128)(2,1)S(1)} %collective-permute-done.15), channel_id=1, source_target_pairs={{0,4},{8,0},{16,8},{24,16},{28,24},{20,28},{12,20},{4,12},{1,5},{9... | collective-permute-start | bytes 3145736 | tf_op jit(solution)/shard_map/ppermute | solution.py:105
  204.4 23.3 %collective-permute-start.16 = (bf16[512,1024]{1,0:T(8,128)(2,1)S(1)}, bf16[512,1024]{1,0:T(8,128)(2,1)S(1)}, u32[]{:S(2)}, u32[]{:S(2)}) collective-permute-start(bf16[512,1024]{1,0:T(8,128)(2,1)S(1)} %collective-permute-done.14), channel_id=1, source_target_pairs={{0,8},{8,16},{16,24},{24,28},{28,20},{20,12},{12,4},{4,0},{1,9},{9... | collective-permute-start | bytes 3145736 | tf_op jit(solution)/shard_map/ppermute | solution.py:104
  227.8 23.2 %collective-permute-start.18 = (bf16[512,1024]{1,0:T(8,128)(2,1)S(1)}, bf16[512,1024]{1,0:T(8,128)(2,1)S(1)}, u32[]{:S(2)}, u32[]{:S(2)}) collective-permute-start(bf16[512,1024]{1,0:T(8,128)(2,1)S(1)} %collective-permute-done.16), channel_id=1, source_target_pairs={{0,8},{8,16},{16,24},{24,28},{28,20},{20,12},{12,4},{4,0},{1,9},{9... | collective-permute-start | bytes 3145736 | tf_op jit(solution)/shard_map/ppermute | solution.py:104
  231.6 23.3 %collective-permute-start.19 = (bf16[512,1024]{1,0:T(8,128)(2,1)S(1)}, bf16[512,1024]{1,0:T(8,128)(2,1)S(1)}, u32[]{:S(2)}, u32[]{:S(2)}) collective-permute-start(bf16[512,1024]{1,0:T(8,128)(2,1)S(1)} %collective-permute-done.17), channel_id=1, source_target_pairs={{0,4},{8,0},{16,8},{24,16},{28,24},{20,28},{12,20},{4,12},{1,5},{9... | collective-permute-start | bytes 3145736 | tf_op jit(solution)/shard_map/ppermute | solution.py:105
  251.0 9.2 %collective-permute-start.20 = (bf16[256,1024]{1,0:T(8,128)(2,1)S(1)}, bf16[256,1024]{1,0:T(8,128)(2,1)S(1)}, u32[]{:S(2)}, u32[]{:S(2)}) collective-permute-start(bf16[256,1024]{1,0:T(8,128)(2,1)S(1)} %slice.29), channel_id=1, source_target_pairs={{0,8},{8,16},{16,24},{24,28},{28,20},{20,12},{12,4},{4,0},{1,9},{9... | collective-permute-start | bytes 1572872 | tf_op jit(solution)/shard_map/ppermute | solution.py:110
  254.9 9.2 %collective-permute-start.21 = (bf16[256,1024]{1,0:T(8,128)(2,1)S(1)}, bf16[256,1024]{1,0:T(8,128)(2,1)S(1)}, u32[]{:S(2)}, u32[]{:S(2)}) collective-permute-start(bf16[256,1024]{1,0:T(8,128)(2,1)S(1)} %slice.30), channel_id=1, source_target_pairs={{0,4},{8,0},{16,8},{24,16},{28,24},{20,28},{12,20},{4,12},{1,5},{9... | collective-permute-start | bytes 1572872 | tf_op jit(solution)/shard_map/ppermute | solution.py:111
  (1 other events, 2.2 us)
